TPU v7x, 32 devices: a whole 2x2x4 slice. The times are simulated.
32 devices in a mesh: ctx: 8 (over y, x, core), fsdp: 4 (over z).
Axes of the slice: x: 2, y: 2, z: 4, core: 2. Of those that a mesh axis runs over, the one named last changes fastest.
Arguments:
- hidden_in: float32 [4, 1024, 2048], P('fsdp', 'ctx'), may hold values from -6 to 6
- block_map: int32 [16], replicated, may hold values from 0 to 15, each once
- doc_ids: int32 [4, 1024], P('fsdp'), may hold values from 0 to 3, never falling along the last dimension, each value on 1 to 512 neighbouring positions
- routes: int32 [4, 1024, 8], P('fsdp', 'ctx'), may hold values from 0 to 15, all different within a row; in each aligned block of 128 rows (0 to 127, 128 to 255, ..., all dimensions but the last counted through in order) at most 96 rows name the same one
- attn_gain: float32 [2048], replicated, may hold values from 0.5 to 1.5
- query_proj: bfloat16 [2048, 4096], P('fsdp'), may hold values from -0.125 to 0.125
- key_proj: bfloat16 [2048, 512], P('fsdp'), may hold values from -0.125 to 0.125
- value_proj: bfloat16 [2048, 512], P('fsdp'), may hold values from -0.125 to 0.125
- query_gain: float32 [128], replicated, may hold values from 0.1 to 1.9
- key_gain: float32 [128], replicated, may hold values from 0.1 to 1.9
- out_proj: bfloat16 [4096, 2048], P('fsdp'), may hold values from -0.375 to 0.375
- ffn_gain: float32 [2048], replicated, may hold values from 0.5 to 1.5
- router_proj: bfloat16 [2048, 16], P('fsdp'), may hold values from -0.125 to 0.125
- expert_gate: bfloat16 [16, 2048, 768], P('ctx', 'fsdp'), may hold values from -0.125 to 0.125
- expert_up: bfloat16 [16, 2048, 768], P('ctx', 'fsdp'), may hold values from -0.125 to 0.125
- expert_down: bfloat16 [16, 768, 2048], P('ctx', 'fsdp'), may hold values from -0.4375 to 0.4375
- cotangent: float32 [4, 1024, 2048], P('fsdp', 'ctx'), may hold values from -6 to 6
Outputs:
- layer_out: float32 [4, 1024, 2048], P('fsdp', 'ctx')
- input_grad: float32 [4, 1024, 2048], P('fsdp', 'ctx')
- attn_gain_grad: float32 [2048], replicated
- query_proj_grad: float32 [2048, 4096], P('fsdp')
- key_proj_grad: float32 [2048, 512], P('fsdp')
- value_proj_grad: float32 [2048, 512], P('fsdp')
- query_gain_grad: float32 [128], replicated
- key_gain_grad: float32 [128], replicated
- out_proj_grad: float32 [4096, 2048], P('fsdp')
- ffn_gain_grad: float32 [2048], replicated
- router_grad: float32 [2048, 16], P('fsdp')
- gate_grad: float32 [16, 2048, 768], P('ctx', 'fsdp')
- up_grad: float32 [16, 2048, 768], P('ctx', 'fsdp')
- down_grad: float32 [16, 768, 2048], P('ctx', 'fsdp')
Inputs may be any that keep to these rules, and one draw needn't show every extreme that they name: `block_map`: A permutation: every block of positions is held by exactly one stored block. `doc_ids`: along the positions of a sequence the document numbers never fall; each document is 1 to 512 positions long and one is exactly that long. `routes`: each token names 8 different experts. Within the 128 stored rows of one device (aligned blocks of rows), no expert is named by more than 96 of them, and in every draw some expert is named by exactly 96.
All inputs are finite; a program needn't handle non-finite values.
Results may differ from a plain program's by a relative error of at most 0.024.
Values may be sent and summed in bfloat16 or wider, within the bound.
No kernel may reach another device: no remote copies, remote signals or barrier semaphores. Data moves between devices by JAX's collectives and lax.ppermute only.
A program may use at most 320 MiB of HBM per device.

v0:
```python
import jax
import jax.numpy as jnp
from jax import lax
from jax.sharding import PartitionSpec as P

D = 2048
HEADS = 32
KV_HEADS = 4
HEAD_DIM = 128
TOP = 8


EPSILON = 1e-06
ROPE_BASE = 1000000.0
NEG_FILL = -1e30


def matmul(left, right):
    return jnp.dot(left, right, preferred_element_type=jnp.float32)


def contract(form, left, right):
    return jnp.einsum(form, left, right, preferred_element_type=jnp.float32)


def rms_scale(field):
    return lax.rsqrt(jnp.mean(field * field, axis=-1, keepdims=True) + EPSILON)


def rotary(positions):
    halfway = HEAD_DIM // 2
    inverse = ROPE_BASE ** (-2.0 * jnp.arange(halfway, dtype=jnp.float32) / HEAD_DIM)
    angle = positions.astype(jnp.float32)[:, None] * inverse[None, :]
    return (jnp.cos(angle), jnp.sin(angle))


def rotate(field, cosine, sine_table):
    halfway = field.shape[-1] // 2
    former = field[..., :halfway]
    latter = field[..., halfway:]
    cos_b = cosine[:, None, :]
    sin_b = sine_table[:, None, :]
    return jnp.concatenate(
        [former * cos_b - latter * sin_b, latter * cos_b + former * sin_b], axis=-1
    )


def rotate_back(field, cosine, sine_table):
    halfway = field.shape[-1] // 2
    former = field[..., :halfway]
    latter = field[..., halfway:]
    cos_b = cosine[:, None, :]
    sin_b = sine_table[:, None, :]
    return jnp.concatenate(
        [former * cos_b + latter * sin_b, latter * cos_b - former * sin_b], axis=-1
    )


def norm_back(grad, normed, inv_scale, factor):
    lead_axes = tuple(range(grad.ndim - 1))
    factor_grad = jnp.sum(grad * normed, axis=lead_axes)
    scaled = grad * factor
    return (
        inv_scale * (scaled - normed * jnp.mean(scaled * normed, axis=-1, keepdims=True)),
        factor_grad,
    )


def per_device(
    hidden_in,
    block_map,
    doc_ids,
    routes,
    attn_gain,
    query_proj,
    key_proj,
    value_proj,
    query_gain,
    key_gain,
    out_proj,
    ffn_gain,
    router_proj,
    expert_gate,
    expert_up,
    expert_down,
    cotangent,
):
    tokens = hidden_in.shape[1]
    ctx_size = lax.axis_size("ctx")
    local_experts = expert_gate.shape[0]
    experts = local_experts * ctx_size
    capacity = min(tokens, 3 * tokens * TOP // (2 * experts))
    block_len = tokens // 2
    group_size = HEADS // KV_HEADS
    score_scale = HEAD_DIM ** (-0.5)
    ctx_index = lax.axis_index("ctx")
    own_blocks = lax.dynamic_slice_in_dim(block_map, 2 * ctx_index, 2, 0)
    offsets = jnp.arange(block_len, dtype=jnp.int32)
    local_pos = (own_blocks[:, None] * block_len + offsets[None, :]).reshape(-1)
    all_pos = (block_map[:, None] * block_len + offsets[None, :]).reshape(-1)
    doc_row = doc_ids[0]
    same_doc = jnp.take(doc_row, all_pos)[None, :] == jnp.take(doc_row, local_pos)[:, None]
    visible = (all_pos[None, :] <= local_pos[:, None]) & same_doc
    cosine, sine_table = rotary(local_pos)
    hidden = hidden_in[0]
    first_scale = rms_scale(hidden)
    first_normed = hidden * first_scale
    first_input = (first_normed * attn_gain).astype(jnp.bfloat16)
    w_query, w_key, w_value, w_out = (
        lax.all_gather(query_proj, "fsdp", axis=0, tiled=True),
        lax.all_gather(key_proj, "fsdp", axis=0, tiled=True),
        lax.all_gather(value_proj, "fsdp", axis=0, tiled=True),
        lax.all_gather(out_proj, "fsdp", axis=0, tiled=True),
    )
    query_raw = matmul(first_input, w_query).reshape(tokens, HEADS, HEAD_DIM)
    key_raw = matmul(first_input, w_key).reshape(tokens, KV_HEADS, HEAD_DIM)
    value_low = matmul(first_input, w_value).astype(jnp.bfloat16)
    query_scale = rms_scale(query_raw)
    query_normed = query_raw * query_scale
    query_rot = rotate(query_normed * query_gain, cosine, sine_table).astype(jnp.bfloat16)
    key_scale = rms_scale(key_raw)
    key_normed = key_raw * key_scale
    key_rot = (
        rotate(key_normed * key_gain, cosine, sine_table)
        .reshape(tokens, KV_HEADS * HEAD_DIM)
        .astype(jnp.bfloat16)
    )
    keys_all, values_all = (
        lax.all_gather(key_rot, "ctx", axis=0, tiled=True),
        lax.all_gather(value_low, "ctx", axis=0, tiled=True),
    )

    def split_keys(flat):
        return flat.reshape(-1, KV_HEADS, HEAD_DIM).transpose(1, 0, 2)

    def join_keys(stacked):
        return stacked.transpose(1, 0, 2).reshape(-1, KV_HEADS * HEAD_DIM)

    def split_queries(flat):
        return flat.reshape(tokens, KV_HEADS, group_size, HEAD_DIM).transpose(1, 2, 0, 3)

    def join_queries(stacked):
        return stacked.transpose(2, 0, 1, 3).reshape(tokens, HEADS * HEAD_DIM)

    def masked_scores(q_block, k_block):
        scores = contract("gtd,sd->gts", q_block, k_block) * score_scale
        return jnp.where(visible[None], scores, NEG_FILL)

    def head_forward(items):
        q_block, k_block, v_block = items
        scores = masked_scores(q_block, k_block)
        peak = jnp.max(scores, axis=-1, keepdims=True)
        expo = jnp.exp(scores - peak)
        total = jnp.sum(expo, axis=-1, keepdims=True)
        probs = (expo / total).astype(jnp.bfloat16)
        mixed = contract("gts,sd->gtd", probs, v_block)
        return (mixed, (peak + jnp.log(total))[..., 0])

    query_groups = split_queries(query_rot)
    attn_out, log_sums = lax.map(
        head_forward, (query_groups, split_keys(keys_all), split_keys(values_all))
    )
    attended = join_queries(attn_out).astype(jnp.bfloat16)
    middle = hidden + matmul(attended, w_out)
    second_scale = rms_scale(middle)
    second_normed = middle * second_scale
    second_input = (second_normed * ffn_gain).astype(jnp.bfloat16)
    w_gate, w_up, w_down, w_router = (
        lax.all_gather(expert_gate, "fsdp", axis=1, tiled=True),
        lax.all_gather(expert_up, "fsdp", axis=1, tiled=True),
        lax.all_gather(expert_down, "fsdp", axis=1, tiled=True),
        lax.all_gather(router_proj, "fsdp", axis=0, tiled=True),
    )
    logits = matmul(second_input, w_router)
    route_ids = routes[0]
    chosen = jnp.take_along_axis(logits, route_ids, axis=1)
    route_weights = jax.nn.softmax(chosen, axis=-1)
    flat_ids = route_ids.reshape(-1)
    expert_range = jnp.arange(experts, dtype=jnp.int32)
    one_hot = (flat_ids[:, None] == expert_range[None, :]).astype(jnp.int32)
    earlier = jnp.cumsum(one_hot, axis=0) - one_hot
    slot_index = jnp.sum(earlier * one_hot, axis=1)
    target = flat_ids * capacity + slot_index

    def dispatch(route_rows):
        buffer = jnp.zeros((experts * capacity, D), jnp.bfloat16).at[target].set(route_rows)
        return buffer.reshape(ctx_size, local_experts, capacity, D)

    def collect(returned):
        return jnp.take(returned.reshape(experts * capacity, D), target, axis=0)

    received = lax.all_to_all(
        dispatch(jnp.repeat(second_input, TOP, axis=0)),
        "ctx",
        split_axis=0,
        concat_axis=2,
        tiled=True,
    )[0]
    gate_val = contract("erd,edf->erf", received, w_gate)
    up_val = contract("erd,edf->erf", received, w_up)
    gate_sig = jax.nn.sigmoid(gate_val)
    hid_low = (gate_val * gate_sig * up_val).astype(jnp.bfloat16)
    expert_out = contract("erf,efd->erd", hid_low, w_down).astype(jnp.bfloat16)
    route_out = (
        collect(lax.all_to_all(expert_out[None], "ctx", split_axis=2, concat_axis=0, tiled=True))
        .reshape(tokens, TOP, D)
        .astype(jnp.float32)
    )
    layer_out = middle + jnp.einsum("tr,trd->td", route_weights, route_out)
    grad_out = cotangent[0]
    grad_weights = jnp.einsum("td,trd->tr", grad_out, route_out)
    grad_routes = (
        (route_weights[:, :, None] * grad_out[:, None, :])
        .astype(jnp.bfloat16)
        .reshape(tokens * TOP, D)
    )
    grad_expert = lax.all_to_all(
        dispatch(grad_routes), "ctx", split_axis=0, concat_axis=2, tiled=True
    )[0]
    grad_hid = contract("erd,efd->erf", grad_expert, w_down)
    down_grad_full = contract("erf,erd->efd", hid_low, grad_expert)
    grad_gate = (grad_hid * up_val * gate_sig * (1.0 + gate_val * (1.0 - gate_sig))).astype(
        jnp.bfloat16
    )
    grad_up = (grad_hid * gate_val * gate_sig).astype(jnp.bfloat16)
    gate_grad_full = contract("erd,erf->edf", received, grad_gate)
    up_grad_full = contract("erd,erf->edf", received, grad_up)
    grad_rows = (
        contract("erf,edf->erd", grad_gate, w_gate) + contract("erf,edf->erd", grad_up, w_up)
    ).astype(jnp.bfloat16)
    grad_copies = collect(
        lax.all_to_all(grad_rows[None], "ctx", split_axis=2, concat_axis=0, tiled=True)
    ).reshape(tokens, TOP, D)
    grad_chosen = route_weights * (
        grad_weights - jnp.sum(route_weights * grad_weights, axis=-1, keepdims=True)
    )
    route_hot = (route_ids[:, :, None] == expert_range[None, None, :]).astype(jnp.float32)
    grad_logits = jnp.einsum("tr,tre->te", grad_chosen, route_hot).astype(jnp.bfloat16)
    router_grad_full = contract("td,te->de", second_input, grad_logits)
    grad_second = jnp.sum(grad_copies.astype(jnp.float32), axis=1) + contract(
        "te,de->td", grad_logits, w_router
    )
    grad_middle, ffn_gain_grad = norm_back(grad_second, second_normed, second_scale, ffn_gain)
    grad_middle = grad_middle + grad_out
    w_query, w_key, w_value, w_out = (
        lax.all_gather(query_proj, "fsdp", axis=0, tiled=True),
        lax.all_gather(key_proj, "fsdp", axis=0, tiled=True),
        lax.all_gather(value_proj, "fsdp", axis=0, tiled=True),
        lax.all_gather(out_proj, "fsdp", axis=0, tiled=True),
    )
    keys_all, values_all = (
        lax.all_gather(key_rot, "ctx", axis=0, tiled=True),
        lax.all_gather(value_low, "ctx", axis=0, tiled=True),
    )
    grad_branch = grad_middle.astype(jnp.bfloat16)
    out_grad_full = contract("tq,td->qd", attended, grad_branch)
    grad_attended = contract("td,qd->tq", grad_branch, w_out).astype(jnp.bfloat16)

    def head_backward(items):
        q_block, k_block, v_block, g_block, lse_block = items
        probs = jnp.exp(masked_scores(q_block, k_block) - lse_block[..., None])
        grad_probs = contract("gtd,sd->gts", g_block, v_block)
        delta = jnp.sum(probs * grad_probs, axis=-1, keepdims=True)
        grad_scores = (probs * (grad_probs - delta)).astype(jnp.bfloat16)
        grad_q = contract("gts,sd->gtd", grad_scores, k_block) * score_scale
        grad_k = contract("gts,gtd->sd", grad_scores, q_block) * score_scale
        grad_v = contract("gts,gtd->sd", probs.astype(jnp.bfloat16), g_block)
        return (grad_q, grad_k, grad_v)

    grad_qgroups, grad_kheads, grad_vheads = lax.map(
        head_backward,
        (
            query_groups,
            split_keys(keys_all),
            split_keys(values_all),
            split_queries(grad_attended),
            log_sums,
        ),
    )
    grad_key_rot, grad_value = (
        lax.psum_scatter(
            join_keys(grad_kheads).astype(jnp.bfloat16), "ctx", scatter_dimension=0, tiled=True
        ).astype(jnp.float32),
        lax.psum_scatter(
            join_keys(grad_vheads).astype(jnp.bfloat16), "ctx", scatter_dimension=0, tiled=True
        ).astype(jnp.float32),
    )
    grad_query_rot = join_queries(grad_qgroups).reshape(tokens, HEADS, HEAD_DIM)
    grad_query, query_gain_grad = norm_back(
        rotate_back(grad_query_rot, cosine, sine_table), query_normed, query_scale, query_gain
    )
    grad_key, key_gain_grad = norm_back(
        rotate_back(grad_key_rot.reshape(tokens, KV_HEADS, HEAD_DIM), cosine, sine_table),
        key_normed,
        key_scale,
        key_gain,
    )
    grad_query = grad_query.reshape(tokens, HEADS * HEAD_DIM).astype(jnp.bfloat16)
    grad_key = grad_key.reshape(tokens, KV_HEADS * HEAD_DIM).astype(jnp.bfloat16)
    grad_value = grad_value.astype(jnp.bfloat16)
    query_grad_full = contract("td,tq->dq", first_input, grad_query)
    key_grad_full = contract("td,tq->dq", first_input, grad_key)
    value_grad_full = contract("td,tq->dq", first_input, grad_value)
    grad_first = (
        contract("tq,dq->td", grad_query, w_query)
        + contract("tq,dq->td", grad_key, w_key)
        + contract("tq,dq->td", grad_value, w_value)
    )
    grad_hidden, attn_gain_grad = norm_back(grad_first, first_normed, first_scale, attn_gain)
    grad_hidden = grad_hidden + grad_middle
    gate_grad, up_grad, down_grad = (
        lax.psum_scatter(
            gate_grad_full.astype(jnp.bfloat16), "fsdp", scatter_dimension=1, tiled=True
        ).astype(jnp.float32),
        lax.psum_scatter(
            up_grad_full.astype(jnp.bfloat16), "fsdp", scatter_dimension=1, tiled=True
        ).astype(jnp.float32),
        lax.psum_scatter(
            down_grad_full.astype(jnp.bfloat16), "fsdp", scatter_dimension=1, tiled=True
        ).astype(jnp.float32),
    )
    shard_grads = (
        lax.psum_scatter(
            query_grad_full.astype(jnp.bfloat16), "fsdp", scatter_dimension=0, tiled=True
        ).astype(jnp.float32),
        lax.psum_scatter(
            key_grad_full.astype(jnp.bfloat16), "fsdp", scatter_dimension=0, tiled=True
        ).astype(jnp.float32),
        lax.psum_scatter(
            value_grad_full.astype(jnp.bfloat16), "fsdp", scatter_dimension=0, tiled=True
        ).astype(jnp.float32),
        lax.psum_scatter(
            out_grad_full.astype(jnp.bfloat16), "fsdp", scatter_dimension=0, tiled=True
        ).astype(jnp.float32),
        lax.psum_scatter(
            router_grad_full.astype(jnp.bfloat16), "fsdp", scatter_dimension=0, tiled=True
        ).astype(jnp.float32),
    )
    query_grad, key_grad, value_grad, out_grad, router_grad = (
        lax.psum(shard_grads[0].astype(jnp.bfloat16), "ctx").astype(jnp.float32),
        lax.psum(shard_grads[1].astype(jnp.bfloat16), "ctx").astype(jnp.float32),
        lax.psum(shard_grads[2].astype(jnp.bfloat16), "ctx").astype(jnp.float32),
        lax.psum(shard_grads[3].astype(jnp.bfloat16), "ctx").astype(jnp.float32),
        lax.psum(shard_grads[4].astype(jnp.bfloat16), "ctx").astype(jnp.float32),
    )
    attn_gain_total, query_gain_total, key_gain_total, ffn_gain_total = lax.psum(
        (attn_gain_grad, query_gain_grad, key_gain_grad, ffn_gain_grad), ("ctx", "fsdp")
    )
    return (
        layer_out[None],
        grad_hidden[None],
        attn_gain_total,
        query_grad,
        key_grad,
        value_grad,
        query_gain_total,
        key_gain_total,
        out_grad,
        ffn_gain_total,
        router_grad,
        gate_grad,
        up_grad,
        down_grad,
    )


def solution(mesh):
    placed = (
        P("fsdp", "ctx", None),
        P(),
        P("fsdp", None),
        P("fsdp", "ctx", None),
        P(),
        P("fsdp", None),
        P("fsdp", None),
        P("fsdp", None),
        P(),
        P(),
        P("fsdp", None),
        P(),
        P("fsdp", None),
        P("ctx", "fsdp", None),
        P("ctx", "fsdp", None),
        P("ctx", "fsdp", None),
        P("fsdp", "ctx", None),
    )
    return jax.shard_map(
        per_device,
        mesh=mesh,
        in_specs=placed,
        out_specs=(
            P("fsdp", "ctx", None),
            P("fsdp", "ctx", None),
            P(),
            P("fsdp", None),
            P("fsdp", None),
            P("fsdp", None),
            P(),
            P(),
            P("fsdp", None),
            P(),
            P("fsdp", None),
            P("ctx", "fsdp", None),
            P("ctx", "fsdp", None),
            P("ctx", "fsdp", None),
        ),
        check_vma=False,
    )
```

profile of v0, /device:TPU:0, one launch (start us, length us, event | category | flops | bytes accessed | tf_op | source)
XLA Modules:
  0.0 2629.0 jit_solution(3409406196270798106)
XLA Ops:
  14.3 43.7 %all-gather.12.cloned.1.call-done = bf16[2048,512]{1,0:T(8,128)(2,1)} async-done(((bf16[512,512]{1,0:T(8,128)(2,1)}), bf16[2048,512]{1,0:T(8,128)(2,1)}) %all-gather.12.cloned.1.call-update) | async-done | bytes 2097168 | tf_op jit(solution)/shard_map/all_gather | solution.py:111
  65.3 38.8 %all-gather.16.cloned.1.call-done = bf16[2048,512]{1,0:T(8,128)(2,1)} async-done(((bf16[512,512]{1,0:T(8,128)(2,1)}), bf16[2048,512]{1,0:T(8,128)(2,1)}) %all-gather.16.cloned.1.call-update) | async-done | bytes 2097168 | tf_op jit(solution)/shard_map/all_gather | solution.py:112
  114.7 13.3 all_gather.42
  135.1 19.4 all-gather.18.cloned.1.call-done
  156.9 285.8 %all-gather.10.cloned.1.call-done = bf16[2048,4096]{1,0:T(8,128)(2,1)} async-done(((bf16[512,4096]{1,0:T(8,128)(2,1)}), bf16[2048,4096]{1,0:T(8,128)(2,1)}) %all-gather.10.cloned.1.call-update) | async-done | bytes 16777232 | tf_op jit(solution)/shard_map/all_gather | solution.py:110
  442.7 23.1 copy.78
  465.9 8.3 multiply_reduce_fusion.3
  480.9 27.0 %while.28 = (s32[]{:T(128)}, bf16[4,8,128,128]{2,3,1,0:T(8,128)(2,1)}, f32[4,8,128]{2,1,0:T(8,128)}, bf16[4,8,128,128]{3,2,1,0:T(8,128)(2,1)S(1)}, bf16[4,1024,1...) while((s32[]{:T(128)}, ...), condition=%wide.region_6.7_spmd.clone, body=%wide.region_3.6_spmd.clone.sunk | while | flops 549846016 | bytes 14462573 | solution.py:160
  508.0 221.2 %all-gather.20.cloned.1.call-done = bf16[4096,2048]{1,0:T(8,128)(2,1)} async-done(((bf16[1024,2048]{1,0:T(8,128)(2,1)}), bf16[4096,2048]{1,0:T(8,128)(2,1)}) %all-gather.20.cloned.1.call-update) | async-done | bytes 16777232 | tf_op jit(solution)/shard_map/all_gather | solution.py:113
  729.1 8.6 multiply_reduce_fusion.8
  747.4 10.7 scatter_custom_fusion.1
  763.6 10.4 scatter_custom_fusion
  774.0 60.4 %all-to-all-done.2 = bf16[8,2,96,2048]{3,2,1,0:T(8,128)(2,1)} async-done(((bf16[8,2,96,2048]{3,2,1,0:T(8,128)(2,1)}), bf16[8,2,96,2048]{3,2,1,0:T(8,128)(2,1)}, u32[]{:S(2)}, u32[]{:S(2)}) %all-to-all-start.2) | async-done | bytes 6291488 | tf_op jit(solution)/shard_map/all_to_all | solution.py:217
  845.8 65.0 %all-to-all-done = bf16[8,2,96,2048]{3,2,1,0:T(8,128)(2,1)} async-done(((bf16[8,2,96,2048]{3,2,1,0:T(8,128)(2,1)}), bf16[8,2,96,2048]{3,2,1,0:T(8,128)(2,1)}, u32[]{:S(2)}, u32[]{:S(2)}) %all-to-all-start) | async-done | bytes 6291488 | tf_op jit(solution)/shard_map/all_to_all | solution.py:192
  917.4 10.4 fusion.103
  927.8 31.6 %all-gather.24.cloned.1.call-done = bf16[2,2048,768]{2,1,0:T(8,128)(2,1)} async-done(((bf16[2,512,768]{2,1,0:T(8,128)(2,1)}), bf16[2,2048,768]{2,1,0:T(8,128)(2,1)}) %all-gather.24.cloned.1.call-update) | async-done | bytes 6291472 | tf_op jit(solution)/shard_map/all_gather | solution.py:170
  959.4 10.4 fusion.104
  969.8 104.8 %all-gather.26.cloned.1.call-done = bf16[2,768,2048]{2,1,0:T(8,128)(2,1)} async-done(((bf16[2,192,2048]{2,1,0:T(8,128)(2,1)}), bf16[2,768,2048]{2,1,0:T(8,128)(2,1)}) %all-gather.26.cloned.1.call-update) | async-done | bytes 6291472 | tf_op jit(solution)/shard_map/all_gather | solution.py:171
  1074.5 13.9 multiply_convert_fusion.1
  1095.3 18.8 copy.93
  1119.2 10.7 fusion.105
  1129.9 10.2 fusion.58
  1140.1 18.8 copy.96
  1158.9 31.8 %all-to-all-done.1 = bf16[1,2,768,2048]{3,1,0,2:T(2,128)(2,1)} async-done(((bf16[1,2,768,2048]{3,1,0,2:T(2,128)(2,1)}), bf16[1,2,768,2048]{3,1,0,2:T(2,128)(2,1)}, u32[]{:S(2)}, u32[]{:S(2)}) %all-to-all-start.1) | async-done | bytes 6291488 | tf_op jit(solution)/shard_map/all_to_all | solution.py:205
  1203.9 12.9 gather_fusion.3
  1224.8 42.2 %all-to-all-done.3 = bf16[1,2,768,2048]{3,1,0,2:T(2,128)(2,1)} async-done(((bf16[1,2,768,2048]{3,1,0,2:T(2,128)(2,1)}), bf16[1,2,768,2048]{3,1,0,2:T(2,128)(2,1)}, u32[]{:S(2)}, u32[]{:S(2)}) %all-to-all-start.3) | async-done | bytes 6291488 | tf_op jit(solution)/shard_map/all_to_all | solution.py:232
  1267.1 8.3 copy.97
  1275.3 12.5 gather_fusion.4
  1298.0 12.7 fusion.72
  1313.7 60.1 %while.29 = (s32[]{:T(128)}, f32[4,8,128,128]{3,2,1,0:T(8,128)}, bf16[4,1024,128]{1,2,0:T(8,128)(2,1)}, bf16[4,1024,128]{1,2,0:T(8,128)(2,1)}, bf16[4,8,128,128]...) while((s32[]{:T(128)}, f32[4,8,128,128]{3,2,1,0:T(8,128)}, ...), condition=%wide.region_20.22_spmd.clone, body=%wide.region_18.21_spmd.clone.sunk | while | flops 1358691328 | bytes 52995752 | solution.py:270
  1378.7 30.1 %reduce-scatter.31.cloned.1.call-done = bf16[128,512]{1,0:T(8,128)(2,1)} async-done(((bf16[1024,512]{1,0:T(8,128)(2,1)}), bf16[128,512]{1,0:T(8,128)(2,1)}) %reduce-scatter.31.cloned.1.call-update) | async-done | bytes 131088
  1412.3 35.6 %reduce-scatter.33.cloned.1.call-done = bf16[128,512]{1,0:T(8,128)(2,1)} async-done(((bf16[1024,512]{1,0:T(8,128)(2,1)}), bf16[128,512]{1,0:T(8,128)(2,1)}) %reduce-scatter.33.cloned.1.call-update) | async-done | bytes 131088
  1451.1 9.4 convolution_convert_fusion
  1468.6 11.7 convolution_convert_fusion.1
  1482.3 9.7 convolution_convert_fusion.3
  1492.0 9.7 convolution_convert_fusion.5
  1501.8 9.8 convolution_convert_fusion.4
  1511.8 27.1 %reduce-scatter.19.cloned.1.call-done = bf16[512,512]{1,0:T(8,128)(2,1)} async-done(((bf16[2048,512]{1,0:T(8,128)(2,1)}), bf16[512,512]{1,0:T(8,128)(2,1)}) %reduce-scatter.19.cloned.1.call-update) | async-done | bytes 524304 | tf_op jit(solution)/shard_map/reduce_scatter | solution.py:329
  1538.9 281.9 %reduce-scatter.21.cloned.1.call-done = bf16[1024,2048]{1,0:T(8,128)(2,1)} async-done(((bf16[4096,2048]{1,0:T(8,128)(2,1)}), bf16[1024,2048]{1,0:T(8,128)(2,1)}) %reduce-scatter.21.cloned.1.call-update) | async-done | bytes 4194320 | tf_op jit(solution)/shard_map/reduce_scatter | solution.py:332
  1820.8 283.3 %reduce-scatter.15.cloned.1.call-done = bf16[512,4096]{1,0:T(8,128)(2,1)} async-done(((bf16[2048,4096]{1,0:T(8,128)(2,1)}), bf16[512,4096]{1,0:T(8,128)(2,1)}) %reduce-scatter.15.cloned.1.call-update) | async-done | bytes 4194320 | tf_op jit(solution)/shard_map/reduce_scatter | solution.py:323
  2105.3 11.5 fusion.106
  2116.8 9.9 reduce-scatter.23.cloned.1.call-done
  2126.7 23.7 psum.71
  2154.6 42.7 %all-reduce = (f32[2048]{0:T(1024)}, f32[128]{0:T(128)}, f32[128]{0:T(128)}, f32[2048]{0:T(1024)}) all-reduce(f32[2048]{0:T(1024)S(1)} %get-tuple-element.220, f32[128]{0:T(128)S(1)} %get-tuple-element.216, f32[128]{0:T(128)S(1)} %get-tuple-element.222, f32[2048]{0:T(1024)S(1)} %copy-done.57), channel_id=1, replica_groups=mesh['ctx'=8,'fsdp'=4] {'ctx','fsdp'}, use_global_device_ids=true, to_apply=%region_27.29 | all-reduce | flops 4352 | bytes 34816 | tf_op jit(solution)/shard_map/psum | solution.py:346
  2198.5 40.3 %reduce-scatter.29.cloned.1.call-done = bf16[2,192,2048]{2,1,0:T(8,128)(2,1)} async-done(((bf16[2,768,2048]{2,1,0:T(8,128)(2,1)}), bf16[2,192,2048]{2,1,0:T(8,128)(2,1)}) %reduce-scatter.29.cloned.1.call-update) | async-done | bytes 1572880 | tf_op jit(solution)/shard_map/reduce_scatter | solution.py:318
  2242.3 110.6 %reduce-scatter.25.cloned.1.call-done = bf16[2,512,768]{2,1,0:T(8,128)(2,1)} async-done(((bf16[2,2048,768]{2,1,0:T(8,128)(2,1)}), bf16[2,512,768]{2,1,0:T(8,128)(2,1)}) %reduce-scatter.25.cloned.1.call-update) | async-done | bytes 1572880 | tf_op jit(solution)/shard_map/reduce_scatter | solution.py:312
  2356.1 110.3 %reduce-scatter.27.cloned.1.call-done = bf16[2,512,768]{2,1,0:T(8,128)(2,1)} async-done(((bf16[2,2048,768]{2,1,0:T(8,128)(2,1)}), bf16[2,512,768]{2,1,0:T(8,128)(2,1)}) %reduce-scatter.27.cloned.1.call-update) | async-done | bytes 1572880 | tf_op jit(solution)/shard_map/reduce_scatter | solution.py:315
  2469.8 138.7 %all-reduce.4.cloned.1.call-done = (bf16[512,4096]{1,0:T(8,128)(2,1)}, bf16[512,512]{1,0:T(8,128)(2,1)}, bf16[512,512]{1,0:T(8,128)(2,1)}, bf16[1024,2048]{1,0:T(8,128)(2,1)}) async-done(((bf16[512,4096]{1,0:T(8,128)(2,1)}, bf16[512,512]{1,0:T(8,128)(2,1)}, bf16[512,512]{1,0:T(8,128)(2,1)}, bf16[1024,2048]{1,0:T(8,128)(2,1)}), (bf16[512,4096]{1,0:T(8,128)(2,1)}, bf16[512,512]{1,0:T(8,128)(2,1)}, ...) | async-done | bytes 9437200 | tf_op jit(solution)/shard_map/psum | solution.py:340
  (370 shorter events, 258.3 us)
Async XLA Ops:
  7.2 50.8 %all-gather.12.cloned.1.call-start = ((), (), s32[]{:S(2)}) async-start(), calls=%async_computation.15 | async-start | bytes 2621440 | tf_op jit(solution)/shard_map/all_gather | solution.py:111
  7.9 96.1 %all-gather.16.cloned.1.call-start = ((), (), s32[]{:S(2)}) async-start(), calls=%async_computation.17 | async-start | bytes 2621440 | tf_op jit(solution)/shard_map/all_gather | solution.py:112
  8.7 124.8 %all-gather.14.cloned.1.call-start = ((), (), s32[]{:S(2)}) async-start(), calls=%async_computation.16 | async-start | bytes 1179648 | tf_op jit(solution)/shard_map/all_gather | solution.py:129
  12.1 91.9 %copy-start.59 = (f32[128]{0:T(128)}, f32[128]{0:T(128)S(1)}, u32[]{:S(2)}) copy-start(f32[128]{0:T(128)S(1)} %add_rsqrt_fusion.3) | copy-start | bytes 1540
  12.9 463.0 %copy-start.29 = (f32[128,64]{0,1:T(8,128)}, f32[128,64]{0,1:T(8,128)S(1)}, u32[]{:S(2)}) copy-start(f32[128,64]{0,1:T(8,128)S(1)} %get-tuple-element.297) | copy-start | bytes 98308
  12.9 463.0 %copy-start.31 = (f32[128,64]{0,1:T(8,128)}, f32[128,64]{0,1:T(8,128)S(1)}, u32[]{:S(2)}) copy-start(f32[128,64]{0,1:T(8,128)S(1)} %get-tuple-element.298) | copy-start | bytes 98308
  12.9 51.5 %copy-start.61 = (f32[128]{0:T(128)S(1)}, f32[128]{0:T(128)}, u32[]{:S(2)}) copy-start(f32[128]{0:T(128)} %param.32) | copy-start | bytes 1540
  14.3 451.5 %copy-start.13 = (bf16[1,128,2048]{2,1,0:T(8,128)(2,1)}, bf16[1,128,2048]{2,1,0:T(8,128)(2,1)S(1)}, u32[]{:S(2)}) copy-start(bf16[1,128,2048]{2,1,0:T(8,128)(2,1)S(1)} %multiply_convert_fusion.7) | copy-start | bytes 1572868
  58.0 46.1 %copy-start.3 = (f32[1,128,2048]{2,1,0:T(8,128)S(1)}, f32[1,128,2048]{2,1,0:T(8,128)}, u32[]{:S(2)}) copy-start(f32[1,128,2048]{2,1,0:T(8,128)} %param.23) | copy-start | bytes 3145732
  58.0 46.1 %copy-start.46 = (f32[2048]{0:T(1024)S(1)}, f32[2048]{0:T(1024)}, u32[]{:S(2)}) copy-start(f32[2048]{0:T(1024)} %param.27) | copy-start | bytes 24580
  64.3 43.1 %copy-start.23 = (f32[128,4,128]{0,2,1:T(8,128)}, f32[128,4,128]{0,2,1:T(8,128)S(1)}, u32[]{:S(2)}) copy-start(f32[128,4,128]{0,2,1:T(8,128)S(1)} %get-tuple-element.304) | copy-start | bytes 786436
  64.4 43.1 %copy-start.55 = (f32[128,4]{0,1:T(4,128)}, f32[128,4]{0,1:T(4,128)S(1)}, u32[]{:S(2)}) copy-start(f32[128,4]{0,1:T(4,128)S(1)} %add_rsqrt_fusion.1) | copy-start | bytes 6148
  65.2 89.3 %all-gather.18.cloned.1.call-start = ((), (), s32[]{:S(2)}) async-start(), calls=%async_computation.18 | async-start | bytes 1179648 | tf_op jit(solution)/shard_map/all_gather | solution.py:130
  106.9 335.9 %all-gather.10.cloned.1.call-start = ((), (), s32[]{:S(2)}) async-start(), calls=%async_computation.14 | async-start | bytes 20971520 | tf_op jit(solution)/shard_map/all_gather | solution.py:110
  107.5 621.6 %all-gather.20.cloned.1.call-start = ((), (), s32[]{:S(2)}) async-start(), calls=%async_computation.19 | async-start | bytes 20971520 | tf_op jit(solution)/shard_map/all_gather | solution.py:113
  108.1 809.3 %all-gather.22.cloned.1.call-start = ((), (), s32[]{:S(2)}) async-start(), calls=%async_computation.20 | async-start | bytes 7864320 | tf_op jit(solution)/shard_map/all_gather | solution.py:169
  108.8 850.6 %all-gather.24.cloned.1.call-start = ((), (), s32[]{:S(2)}) async-start(), calls=%async_computation.21 | async-start | bytes 7864320 | tf_op jit(solution)/shard_map/all_gather | solution.py:170
  128.0 610.9 %copy-start.33 = (bf16[2048,16]{0,1:T(8,128)(2,1)}, bf16[2048,16]{0,1:T(8,128)(2,1)S(1)}, u32[]{:S(2)}) copy-start(bf16[2048,16]{0,1:T(8,128)(2,1)S(1)} %all_gather.42) | copy-start | bytes 196612
  133.4 332.4 %copy-start.50 = (s32[1024]{0:T(1024)}, s32[1024]{0:T(1024)S(1)}, u32[]{:S(2)}) copy-start(s32[1024]{0:T(1024)S(1)} %fusion.88) | copy-start | bytes 12292
  507.9 229.8 %copy-start.7 = (bf16[4,1024,128]{2,1,0:T(8,128)(2,1)}, bf16[4,1024,128]{2,1,0:T(8,128)(2,1)S(1)}, u32[]{:S(2)}) copy-start(bf16[4,1024,128]{2,1,0:T(8,128)(2,1)S(1)} %get-tuple-element.573) | copy-start | bytes 3145732
  507.9 229.8 %copy-start.15 = (bf16[4,8,128,128]{3,2,1,0:T(8,128)(2,1)}, bf16[4,8,128,128]{3,2,1,0:T(8,128)(2,1)S(1)}, u32[]{:S(2)}) copy-start(bf16[4,8,128,128]{3,2,1,0:T(8,128)(2,1)S(1)} %get-tuple-element.574) | copy-start | bytes 3145732
  507.9 229.8 %copy-start.35 = (s32[1024]{0:T(1024)}, s32[1024]{0:T(1024)S(1)}, u32[]{:S(2)}) copy-start(s32[1024]{0:T(1024)S(1)} %get-tuple-element.615) | copy-start | bytes 12292
  507.9 229.8 %copy-start.40 = (s32[1024]{0:T(1024)}, s32[1024]{0:T(1024)S(1)}, u32[]{:S(2)}) copy-start(s32[1024]{0:T(1024)S(1)} %get-tuple-element.631) | copy-start | bytes 12292
  507.9 229.8 %copy-start.52 = (s32[128]{0:T(128)}, s32[128]{0:T(128)S(1)}, u32[]{:S(2)}) copy-start(s32[128]{0:T(128)S(1)} %get-tuple-element.635) | copy-start | bytes 1540
  758.1 76.3 %all-to-all-start.2 = ((bf16[8,2,96,2048]{3,2,1,0:T(8,128)(2,1)}), bf16[8,2,96,2048]{3,2,1,0:T(8,128)(2,1)}, u32[]{:S(2)}, u32[]{:S(2)}) async-start(bf16[8,2,96,2048]{3,2,1,0:T(8,128)(2,1)} %bitcast.321), calls=%async_computation.2 | async-start | bytes 12582912 | tf_op jit(solution)/shard_map/all_to_all | solution.py:217
  762.8 311.7 %all-gather.26.cloned.1.call-start = ((), (), s32[]{:S(2)}) async-start(), calls=%async_computation.22 | async-start | bytes 7864320 | tf_op jit(solution)/shard_map/all_gather | solution.py:171
  834.4 76.4 %all-to-all-start = ((bf16[8,2,96,2048]{3,2,1,0:T(8,128)(2,1)}), bf16[8,2,96,2048]{3,2,1,0:T(8,128)(2,1)}, u32[]{:S(2)}, u32[]{:S(2)}) async-start(bf16[8,2,96,2048]{3,2,1,0:T(8,128)(2,1)} %bitcast.322), calls=%async_computation | async-start | bytes 12582912 | tf_op jit(solution)/shard_map/all_to_all | solution.py:192
  1114.1 76.6 %all-to-all-start.1 = ((bf16[1,2,768,2048]{3,1,0,2:T(2,128)(2,1)}), bf16[1,2,768,2048]{3,1,0,2:T(2,128)(2,1)}, u32[]{:S(2)}, u32[]{:S(2)}) async-start(bf16[1,2,768,2048]{3,1,0,2:T(2,128)(2,1)} %copy.93), calls=%async_computation.1 | async-start | bytes 12582912 | tf_op jit(solution)/shard_map/all_to_all | solution.py:205
  1158.9 36.7 %copy-start.51 = (s32[1024]{0:T(1024)S(1)}, s32[1024]{0:T(1024)}, u32[]{:S(2)}) copy-start(s32[1024]{0:T(1024)} %copy-done.50) | copy-start | bytes 12292
  1190.7 76.3 %all-to-all-start.3 = ((bf16[1,2,768,2048]{3,1,0,2:T(2,128)(2,1)}), bf16[1,2,768,2048]{3,1,0,2:T(2,128)(2,1)}, u32[]{:S(2)}, u32[]{:S(2)}) async-start(bf16[1,2,768,2048]{3,1,0,2:T(2,128)(2,1)} %copy.96), calls=%async_computation.3 | async-start | bytes 12582912 | tf_op jit(solution)/shard_map/all_to_all | solution.py:232
  1195.5 213.2 %reduce-scatter.31.cloned.1.call-start = ((), (), s32[]{:S(2)}) async-start(), calls=%async_computation.31 | async-start | bytes 1179648
  1298.0 153.1 %copy-start.9 = (f32[128,2048]{1,0:T(8,128)}, f32[128,2048]{1,0:T(8,128)S(1)}, u32[]{:S(2)}) copy-start(f32[128,2048]{1,0:T(8,128)S(1)} %get-tuple-element.291) | copy-start | bytes 3145732
  1373.8 36.3 %copy-start.14 = (bf16[1,128,2048]{2,1,0:T(8,128)(2,1)S(1)}, bf16[1,128,2048]{2,1,0:T(8,128)(2,1)}, u32[]{:S(2)}) copy-start(bf16[1,128,2048]{2,1,0:T(8,128)(2,1)} %copy-done.13) | copy-start | bytes 1572868
  1376.2 71.7 %reduce-scatter.33.cloned.1.call-start = ((), (), s32[]{:S(2)}) async-start(), calls=%async_computation.32 | async-start | bytes 1179648
  1378.6 69.3 %copy-start.4 = (f32[1,128,2048]{2,1,0:T(8,128)S(1)}, f32[1,128,2048]{2,1,0:T(8,128)}, u32[]{:S(2)}) copy-start(f32[1,128,2048]{2,1,0:T(8,128)} %param.23) | copy-start | bytes 3145732
  1378.6 69.3 %copy-start.47 = (f32[2048]{0:T(1024)S(1)}, f32[2048]{0:T(1024)}, u32[]{:S(2)}) copy-start(f32[2048]{0:T(1024)} %param.27) | copy-start | bytes 24580
  1378.6 69.3 %copy-start.60 = (f32[128]{0:T(128)S(1)}, f32[128]{0:T(128)}, u32[]{:S(2)}) copy-start(f32[128]{0:T(128)} %copy-done.59) | copy-start | bytes 1540
  1378.6 133.2 %reduce-scatter.17.cloned.1.call-start = ((), (), s32[]{:S(2)}) async-start(), calls=%async_computation.24 | async-start | bytes 2621440 | tf_op jit(solution)/shard_map/reduce_scatter | solution.py:326
  1412.3 126.6 %reduce-scatter.19.cloned.1.call-start = ((), (), s32[]{:S(2)}) async-start(), calls=%async_computation.25 | async-start | bytes 2621440 | tf_op jit(solution)/shard_map/reduce_scatter | solution.py:329
  1451.0 369.7 %reduce-scatter.21.cloned.1.call-start = ((), (), s32[]{:S(2)}) async-start(), calls=%async_computation.26 | async-start | bytes 20971520 | tf_op jit(solution)/shard_map/reduce_scatter | solution.py:332
  1460.5 643.5 %reduce-scatter.15.cloned.1.call-start = ((), (), s32[]{:S(2)}) async-start(), calls=%async_computation.23 | async-start | bytes 20971520 | tf_op jit(solution)/shard_map/reduce_scatter | solution.py:323
  1480.3 646.3 %reduce-scatter.23.cloned.1.call-start = ((), (), s32[]{:S(2)}) async-start(), calls=%async_computation.27 | async-start | bytes 81920 | tf_op jit(solution)/shard_map/reduce_scatter | solution.py:335
  1482.2 756.6 %reduce-scatter.29.cloned.1.call-start = ((), (), s32[]{:S(2)}) async-start(), calls=%async_computation.30 | async-start | bytes 7864320 | tf_op jit(solution)/shard_map/reduce_scatter | solution.py:318
  1492.0 860.8 %reduce-scatter.25.cloned.1.call-start = ((), (), s32[]{:S(2)}) async-start(), calls=%async_computation.28 | async-start | bytes 7864320 | tf_op jit(solution)/shard_map/reduce_scatter | solution.py:312
  1501.8 964.7 %reduce-scatter.27.cloned.1.call-start = ((), (), s32[]{:S(2)}) async-start(), calls=%async_computation.29 | async-start | bytes 7864320 | tf_op jit(solution)/shard_map/reduce_scatter | solution.py:315
  1511.7 1096.8 %all-reduce.4.cloned.1.call-start = ((), (), s32[]{:S(2)}) async-start(), calls=%async_computation.33 | async-start | bytes 18874368 | tf_op jit(solution)/shard_map/psum | solution.py:340
  2116.8 36.8 %copy-start.39 = (bf16[128,512]{1,0:T(8,128)(2,1)S(1)}, bf16[128,512]{1,0:T(8,128)(2,1)}, u32[]{:S(2)}) copy-start(bf16[128,512]{1,0:T(8,128)(2,1)} %reduce-scatter.33.cloned.1.call-done) | copy-start | bytes 393220
  2151.0 46.2 %copy-start.10 = (f32[128,2048]{1,0:T(8,128)S(1)}, f32[128,2048]{1,0:T(8,128)}, u32[]{:S(2)}) copy-start(f32[128,2048]{1,0:T(8,128)} %copy-done.9) | copy-start | bytes 3145732
  (49 other events, 433.0 us)
Sparse Core Ops, SparseCore 0:
  9.6 48.3 all-gather.11
  59.6 44.4 all-gather.15
  106.5 22.2 all-gather.13
  131.1 23.3 all-gather.17
  156.0 286.7 all-gather.9
  444.2 284.9 all-gather.19
  730.7 113.5 all-gather.21
  845.8 113.5 all-gather.23
  961.0 113.5 all-gather.25
  1376.4 32.3 reduce-scatter.30
  1411.9 35.9 reduce-scatter.32
  1450.1 43.6 reduce-scatter.16
  1496.0 42.8 reduce-scatter.18
  1541.1 279.6 reduce-scatter.20
  1823.0 281.0 reduce-scatter.14
  2106.7 19.9 reduce-scatter.22
  2128.8 109.9 reduce-scatter.28
  2241.5 111.2 reduce-scatter.24
  2355.1 111.2 reduce-scatter.26
  2470.3 138.1 all-reduce.3
where the time goes:
time: 2630 us
  waiting for transfers between devices  2020 us (77%)
  matrix products  236 us (9%)
  local copies, waits for them, and re-layouts  178 us (7%)
  other arithmetic  81.3 us (3%)
  blocking collectives  79.7 us (3%)
    all_gather x1, waiting for transfers between devices, per_device(): lax.all_gather(query_proj, 'fsdp', axis=0, tiled=True)  286 us
    reduce_scatter x1, waiting for transfers between devices, per_device(): lax.psum_scatter(query_grad_full.astype(jnp.bfloat16), 'fsdp', scatter_di...  283 us
    reduce_scatter x1, waiting for transfers between devices, per_device(): lax.psum_scatter(out_grad_full.astype(jnp.bfloat16), 'fsdp', scatter_dime...  282 us
    all_gather x1, waiting for transfers between devices, per_device(): lax.all_gather(out_proj, 'fsdp', axis=0, tiled=True)  221 us
    dot_general x47, matrix products, contract(): return jnp.einsum(form, left, right, preferred_element_type=jnp.float32)  206 us
    psum x1, waiting for transfers between devices, per_device(): lax.psum(shard_grads[0].astype(jnp.bfloat16), 'ctx').astype(jnp.float32)  139 us
    reduce_scatter x1, waiting for transfers between devices, per_device(): lax.psum_scatter(gate_grad_full.astype(jnp.bfloat16), 'fsdp', scatter_dim...  111 us
    reduce_scatter x1, waiting for transfers between devices, per_device(): lax.psum_scatter(up_grad_full.astype(jnp.bfloat16), 'fsdp', scatter_dimen...  110 us
  transfers between devices with their start and end apart: 24, of which 21 were waited for; matrix products, arithmetic and copies ran while one was open for 13% of the time, Pallas kernels for 0%

commit v1 on v0

--- a/solution.py
+++ b/solution.py
@@ -87,34 +87,58 @@
 ):
     tokens = hidden_in.shape[1]
     ctx_size = lax.axis_size("ctx")
+    fsdp_size = lax.axis_size("fsdp")
+    fsdp_index = lax.axis_index("fsdp")
     local_experts = expert_gate.shape[0]
     experts = local_experts * ctx_size
     capacity = min(tokens, 3 * tokens * TOP // (2 * experts))
     block_len = tokens // 2
     group_size = HEADS // KV_HEADS
     score_scale = HEAD_DIM ** (-0.5)
+    heads_dev = HEADS // fsdp_size
+    share = max(1, fsdp_size // KV_HEADS)
+    kv_dev = max(1, heads_dev // group_size)
+    group_dev = heads_dev // kv_dev
+    d_part = D // fsdp_size
+    seqs = fsdp_size
+    group_rows = seqs * tokens
+
     ctx_index = lax.axis_index("ctx")
     own_blocks = lax.dynamic_slice_in_dim(block_map, 2 * ctx_index, 2, 0)
     offsets = jnp.arange(block_len, dtype=jnp.int32)
     local_pos = (own_blocks[:, None] * block_len + offsets[None, :]).reshape(-1)
     all_pos = (block_map[:, None] * block_len + offsets[None, :]).reshape(-1)
-    doc_row = doc_ids[0]
-    same_doc = jnp.take(doc_row, all_pos)[None, :] == jnp.take(doc_row, local_pos)[:, None]
-    visible = (all_pos[None, :] <= local_pos[:, None]) & same_doc
+    doc_rows = lax.all_gather(doc_ids[0], "fsdp", axis=0, tiled=False)
+    docs_query = jnp.take(doc_rows, local_pos, axis=1)
+    docs_key = jnp.take(doc_rows, all_pos, axis=1)
+    visible = (all_pos[None, None, :] <= local_pos[None, :, None]) & (
+        docs_key[:, None, :] == docs_query[:, :, None]
+    )
     cosine, sine_table = rotary(local_pos)
     hidden = hidden_in[0]
     first_scale = rms_scale(hidden)
     first_normed = hidden * first_scale
     first_input = (first_normed * attn_gain).astype(jnp.bfloat16)
-    w_query, w_key, w_value, w_out = (
-        lax.all_gather(query_proj, "fsdp", axis=0, tiled=True),
-        lax.all_gather(key_proj, "fsdp", axis=0, tiled=True),
-        lax.all_gather(value_proj, "fsdp", axis=0, tiled=True),
-        lax.all_gather(out_proj, "fsdp", axis=0, tiled=True),
-    )
-    query_raw = matmul(first_input, w_query).reshape(tokens, HEADS, HEAD_DIM)
-    key_raw = matmul(first_input, w_key).reshape(tokens, KV_HEADS, HEAD_DIM)
-    value_low = matmul(first_input, w_value).astype(jnp.bfloat16)
+    group_input = lax.all_gather(first_input, "fsdp", axis=0, tiled=True)
+    w_query_cols = lax.all_to_all(query_proj, "fsdp", 1, 0, tiled=True)
+    if share == 1:
+        w_key_cols = lax.all_to_all(key_proj, "fsdp", 1, 0, tiled=True)
+        w_value_cols = lax.all_to_all(value_proj, "fsdp", 1, 0, tiled=True)
+    else:
+        kv_start = (fsdp_index // share) * HEAD_DIM
+        w_key_cols = lax.dynamic_slice_in_dim(
+            lax.all_gather(key_proj, "fsdp", axis=0, tiled=True), kv_start, HEAD_DIM, 1
+        )
+        w_value_cols = lax.dynamic_slice_in_dim(
+            lax.all_gather(value_proj, "fsdp", axis=0, tiled=True), kv_start, HEAD_DIM, 1
+        )
+    query_raw = matmul(group_input, w_query_cols).reshape(seqs, tokens, heads_dev, HEAD_DIM)
+    key_raw = matmul(group_input, w_key_cols).reshape(seqs, tokens, kv_dev, HEAD_DIM)
+    value_low = (
+        matmul(group_input, w_value_cols)
+        .astype(jnp.bfloat16)
+        .reshape(seqs, tokens, kv_dev * HEAD_DIM)
+    )
     query_scale = rms_scale(query_raw)
     query_normed = query_raw * query_scale
     query_rot = rotate(query_normed * query_gain, cosine, sine_table).astype(jnp.bfloat16)
@@ -122,46 +146,35 @@
     key_normed = key_raw * key_scale
     key_rot = (
         rotate(key_normed * key_gain, cosine, sine_table)
-        .reshape(tokens, KV_HEADS * HEAD_DIM)
+        .reshape(seqs, tokens, kv_dev * HEAD_DIM)
         .astype(jnp.bfloat16)
     )
-    keys_all, values_all = (
-        lax.all_gather(key_rot, "ctx", axis=0, tiled=True),
-        lax.all_gather(value_low, "ctx", axis=0, tiled=True),
-    )
-
-    def split_keys(flat):
-        return flat.reshape(-1, KV_HEADS, HEAD_DIM).transpose(1, 0, 2)
-
-    def join_keys(stacked):
-        return stacked.transpose(1, 0, 2).reshape(-1, KV_HEADS * HEAD_DIM)
-
-    def split_queries(flat):
-        return flat.reshape(tokens, KV_HEADS, group_size, HEAD_DIM).transpose(1, 2, 0, 3)
-
-    def join_queries(stacked):
-        return stacked.transpose(2, 0, 1, 3).reshape(tokens, HEADS * HEAD_DIM)
-
-    def masked_scores(q_block, k_block):
-        scores = contract("gtd,sd->gts", q_block, k_block) * score_scale
-        return jnp.where(visible[None], scores, NEG_FILL)
-
-    def head_forward(items):
-        q_block, k_block, v_block = items
-        scores = masked_scores(q_block, k_block)
-        peak = jnp.max(scores, axis=-1, keepdims=True)
-        expo = jnp.exp(scores - peak)
-        total = jnp.sum(expo, axis=-1, keepdims=True)
-        probs = (expo / total).astype(jnp.bfloat16)
-        mixed = contract("gts,sd->gtd", probs, v_block)
-        return (mixed, (peak + jnp.log(total))[..., 0])
-
-    query_groups = split_queries(query_rot)
-    attn_out, log_sums = lax.map(
-        head_forward, (query_groups, split_keys(keys_all), split_keys(values_all))
-    )
-    attended = join_queries(attn_out).astype(jnp.bfloat16)
-    middle = hidden + matmul(attended, w_out)
+    keys_all = lax.all_gather(key_rot, "ctx", axis=1, tiled=True).reshape(
+        seqs, -1, kv_dev, HEAD_DIM
+    )
+    values_all = lax.all_gather(value_low, "ctx", axis=1, tiled=True).reshape(
+        seqs, -1, kv_dev, HEAD_DIM
+    )
+    query_groups = query_rot.reshape(seqs, tokens, kv_dev, group_dev, HEAD_DIM)
+
+    def masked_scores():
+        scores = contract("stkgd,sjkd->skgtj", query_groups, keys_all) * score_scale
+        return jnp.where(visible[:, None, None], scores, NEG_FILL)
+
+    scores = masked_scores()
+    peak = jnp.max(scores, axis=-1, keepdims=True)
+    expo = jnp.exp(scores - peak)
+    total = jnp.sum(expo, axis=-1, keepdims=True)
+    probs = (expo / total).astype(jnp.bfloat16)
+    log_sums = peak + jnp.log(total)
+    attended = (
+        contract("skgtj,sjkd->stkgd", probs, values_all)
+        .astype(jnp.bfloat16)
+        .reshape(group_rows, heads_dev * HEAD_DIM)
+    )
+    branch_parts = matmul(attended, out_proj).reshape(seqs, tokens, D)
+    branch = lax.psum_scatter(branch_parts, "fsdp", scatter_dimension=0, tiled=True)[0]
+    middle = hidden + branch
     second_scale = rms_scale(middle)
     second_normed = middle * second_scale
     second_input = (second_normed * ffn_gain).astype(jnp.bfloat16)
@@ -242,70 +255,75 @@
     )
     grad_middle, ffn_gain_grad = norm_back(grad_second, second_normed, second_scale, ffn_gain)
     grad_middle = grad_middle + grad_out
-    w_query, w_key, w_value, w_out = (
-        lax.all_gather(query_proj, "fsdp", axis=0, tiled=True),
-        lax.all_gather(key_proj, "fsdp", axis=0, tiled=True),
-        lax.all_gather(value_proj, "fsdp", axis=0, tiled=True),
-        lax.all_gather(out_proj, "fsdp", axis=0, tiled=True),
-    )
-    keys_all, values_all = (
-        lax.all_gather(key_rot, "ctx", axis=0, tiled=True),
-        lax.all_gather(value_low, "ctx", axis=0, tiled=True),
-    )
-    grad_branch = grad_middle.astype(jnp.bfloat16)
-    out_grad_full = contract("tq,td->qd", attended, grad_branch)
-    grad_attended = contract("td,qd->tq", grad_branch, w_out).astype(jnp.bfloat16)
-
-    def head_backward(items):
-        q_block, k_block, v_block, g_block, lse_block = items
-        probs = jnp.exp(masked_scores(q_block, k_block) - lse_block[..., None])
-        grad_probs = contract("gtd,sd->gts", g_block, v_block)
-        delta = jnp.sum(probs * grad_probs, axis=-1, keepdims=True)
-        grad_scores = (probs * (grad_probs - delta)).astype(jnp.bfloat16)
-        grad_q = contract("gts,sd->gtd", grad_scores, k_block) * score_scale
-        grad_k = contract("gts,gtd->sd", grad_scores, q_block) * score_scale
-        grad_v = contract("gts,gtd->sd", probs.astype(jnp.bfloat16), g_block)
-        return (grad_q, grad_k, grad_v)
-
-    grad_qgroups, grad_kheads, grad_vheads = lax.map(
-        head_backward,
-        (
-            query_groups,
-            split_keys(keys_all),
-            split_keys(values_all),
-            split_queries(grad_attended),
-            log_sums,
-        ),
-    )
-    grad_key_rot, grad_value = (
-        lax.psum_scatter(
-            join_keys(grad_kheads).astype(jnp.bfloat16), "ctx", scatter_dimension=0, tiled=True
-        ).astype(jnp.float32),
-        lax.psum_scatter(
-            join_keys(grad_vheads).astype(jnp.bfloat16), "ctx", scatter_dimension=0, tiled=True
-        ).astype(jnp.float32),
-    )
-    grad_query_rot = join_queries(grad_qgroups).reshape(tokens, HEADS, HEAD_DIM)
+
+    grad_branch = lax.all_gather(grad_middle.astype(jnp.bfloat16), "fsdp", axis=0, tiled=True)
+    out_grad_part = contract("tq,td->qd", attended, grad_branch)
+    grad_attended = contract("td,qd->tq", grad_branch, out_proj).astype(jnp.bfloat16)
+    grad_groups = grad_attended.reshape(seqs, tokens, kv_dev, group_dev, HEAD_DIM)
+
+    probs_back = jnp.exp(masked_scores() - log_sums)
+    grad_probs = contract("stkgd,sjkd->skgtj", grad_groups, values_all)
+    delta = jnp.sum(probs_back * grad_probs, axis=-1, keepdims=True)
+    grad_scores = (probs_back * (grad_probs - delta)).astype(jnp.bfloat16)
+    grad_qgroups = contract("skgtj,sjkd->stkgd", grad_scores, keys_all) * score_scale
+    grad_kheads = contract("skgtj,stkgd->sjkd", grad_scores, query_groups) * score_scale
+    grad_vheads = contract("skgtj,stkgd->sjkd", probs_back.astype(jnp.bfloat16), grad_groups)
+
+    def kv_reduce(grads):
+        summed = lax.psum_scatter(
+            grads.reshape(seqs, -1, kv_dev * HEAD_DIM).astype(jnp.bfloat16),
+            "ctx",
+            scatter_dimension=1,
+            tiled=True,
+        ).astype(jnp.float32)
+        total = summed
+        for step in range(1, share):
+            pairs = [
+                (i, (i // share) * share + (i % share + step) % share) for i in range(fsdp_size)
+            ]
+            total = total + lax.ppermute(summed, "fsdp", pairs)
+        return total
+
+    grad_key_rot = kv_reduce(grad_kheads)
+    grad_value = kv_reduce(grad_vheads)
+    grad_query_rot = grad_qgroups.reshape(seqs, tokens, heads_dev, HEAD_DIM)
     grad_query, query_gain_grad = norm_back(
         rotate_back(grad_query_rot, cosine, sine_table), query_normed, query_scale, query_gain
     )
     grad_key, key_gain_grad = norm_back(
-        rotate_back(grad_key_rot.reshape(tokens, KV_HEADS, HEAD_DIM), cosine, sine_table),
+        rotate_back(grad_key_rot.reshape(seqs, tokens, kv_dev, HEAD_DIM), cosine, sine_table),
         key_normed,
         key_scale,
         key_gain,
     )
-    grad_query = grad_query.reshape(tokens, HEADS * HEAD_DIM).astype(jnp.bfloat16)
-    grad_key = grad_key.reshape(tokens, KV_HEADS * HEAD_DIM).astype(jnp.bfloat16)
-    grad_value = grad_value.astype(jnp.bfloat16)
-    query_grad_full = contract("td,tq->dq", first_input, grad_query)
-    key_grad_full = contract("td,tq->dq", first_input, grad_key)
-    value_grad_full = contract("td,tq->dq", first_input, grad_value)
-    grad_first = (
-        contract("tq,dq->td", grad_query, w_query)
-        + contract("tq,dq->td", grad_key, w_key)
-        + contract("tq,dq->td", grad_value, w_value)
-    )
+    if share > 1:
+        key_gain_grad = key_gain_grad * (fsdp_index % share == 0).astype(jnp.float32)
+    grad_query = grad_query.reshape(group_rows, heads_dev * HEAD_DIM).astype(jnp.bfloat16)
+    grad_key = grad_key.reshape(group_rows, kv_dev * HEAD_DIM).astype(jnp.bfloat16)
+    grad_value = grad_value.reshape(group_rows, kv_dev * HEAD_DIM).astype(jnp.bfloat16)
+
+    def gather_heads(grads):
+        whole = lax.all_gather(grads, "fsdp", axis=1, tiled=True)
+        if share > 1:
+            whole = whole.reshape(group_rows, KV_HEADS, share, HEAD_DIM)[:, :, 0]
+            whole = whole.reshape(group_rows, KV_HEADS * HEAD_DIM)
+        return whole
+
+    query_all = lax.all_gather(grad_query, "fsdp", axis=1, tiled=True)
+    key_all = gather_heads(grad_key)
+    value_all = gather_heads(grad_value)
+    input_part = lax.dynamic_slice_in_dim(group_input, fsdp_index * d_part, d_part, 1)
+    query_grad_part = contract("td,tq->dq", input_part, query_all)
+    key_grad_part = contract("td,tq->dq", input_part, key_all)
+    value_grad_part = contract("td,tq->dq", input_part, value_all)
+    grad_first_cols = (
+        contract("tq,dq->td", query_all, query_proj)
+        + contract("tq,dq->td", key_all, key_proj)
+        + contract("tq,dq->td", value_all, value_proj)
+    )
+    grad_first = lax.all_to_all(
+        grad_first_cols.reshape(seqs, tokens, d_part), "fsdp", 0, 2, tiled=True
+    )[0]
     grad_hidden, attn_gain_grad = norm_back(grad_first, first_normed, first_scale, attn_gain)
     grad_hidden = grad_hidden + grad_middle
     gate_grad, up_grad, down_grad = (
@@ -319,29 +337,15 @@
             down_grad_full.astype(jnp.bfloat16), "fsdp", scatter_dimension=1, tiled=True
         ).astype(jnp.float32),
     )
-    shard_grads = (
-        lax.psum_scatter(
-            query_grad_full.astype(jnp.bfloat16), "fsdp", scatter_dimension=0, tiled=True
-        ).astype(jnp.float32),
-        lax.psum_scatter(
-            key_grad_full.astype(jnp.bfloat16), "fsdp", scatter_dimension=0, tiled=True
-        ).astype(jnp.float32),
-        lax.psum_scatter(
-            value_grad_full.astype(jnp.bfloat16), "fsdp", scatter_dimension=0, tiled=True
-        ).astype(jnp.float32),
-        lax.psum_scatter(
-            out_grad_full.astype(jnp.bfloat16), "fsdp", scatter_dimension=0, tiled=True
-        ).astype(jnp.float32),
-        lax.psum_scatter(
-            router_grad_full.astype(jnp.bfloat16), "fsdp", scatter_dimension=0, tiled=True
-        ).astype(jnp.float32),
-    )
+    router_shard = lax.psum_scatter(
+        router_grad_full.astype(jnp.bfloat16), "fsdp", scatter_dimension=0, tiled=True
+    ).astype(jnp.float32)
     query_grad, key_grad, value_grad, out_grad, router_grad = (
-        lax.psum(shard_grads[0].astype(jnp.bfloat16), "ctx").astype(jnp.float32),
-        lax.psum(shard_grads[1].astype(jnp.bfloat16), "ctx").astype(jnp.float32),
-        lax.psum(shard_grads[2].astype(jnp.bfloat16), "ctx").astype(jnp.float32),
-        lax.psum(shard_grads[3].astype(jnp.bfloat16), "ctx").astype(jnp.float32),
-        lax.psum(shard_grads[4].astype(jnp.bfloat16), "ctx").astype(jnp.float32),
+        lax.psum(query_grad_part.astype(jnp.bfloat16), "ctx").astype(jnp.float32),
+        lax.psum(key_grad_part.astype(jnp.bfloat16), "ctx").astype(jnp.float32),
+        lax.psum(value_grad_part.astype(jnp.bfloat16), "ctx").astype(jnp.float32),
+        lax.psum(out_grad_part.astype(jnp.bfloat16), "ctx").astype(jnp.float32),
+        lax.psum(router_shard.astype(jnp.bfloat16), "ctx").astype(jnp.float32),
     )
     attn_gain_total, query_gain_total, key_gain_total, ffn_gain_total = lax.psum(
         (attn_gain_grad, query_gain_grad, key_gain_grad, ffn_gain_grad), ("ctx", "fsdp")

time: 2630 us -> 1710 us (0.65)
  waiting for transfers between devices: 2020 us -> 927 us
  blocking collectives: 79.7 us -> 260 us
  matrix products: 236 us -> 192 us
    reduce_scatter x4 -> x2, waiting for transfers between devices: 592 us -> 66.1 us  [the longest x1 56.2 us: per_device(): lax.psum_scatter(branch_parts, 'fsdp', scatter_dimension=0, tiled=True)[0]]
    all_gather x6 -> x5, waiting for transfers between devices: 609 us -> 85.4 us  [the longest x1 42.1 us: per_device(): lax.all_gather(grad_middle.astype(jnp.bfloat16), 'fsdp', axis=0, tiled=True)]
    all_gather x0 -> x3, blocking collectives: none -> 179 us  [the longest x1 130 us: per_device(): doc_rows = lax.all_gather(doc_ids[0], 'fsdp', axis=0, tiled=False)]
    unnamed x22 -> x17, waiting for transfers between devices: 70.4 us -> 1.97 us
    reduce_scatter x1, waiting for transfers between devices: 40.3 us -> 96.3 us  [per_device(): lax.psum_scatter(down_grad_full.astype(jnp.bfloat16), 'fsdp', scatter_dim...]
    psum x1, waiting for transfers between devices: 139 us -> 92.6 us  [per_device(): lax.psum(query_grad_part.astype(jnp.bfloat16), 'ctx').astype(jnp.float32)]
    all_gather x1, waiting for transfers between devices: 0.01 us -> 40.9 us  [per_device(): lax.all_gather(expert_gate, 'fsdp', axis=1, tiled=True)]
    dot_general x47 -> x25, matrix products: 206 us -> 171 us  [contract(): return jnp.einsum(form, left, right, preferred_element_type=jnp.float32)]
  transfers between devices with their start and end apart: 24 -> 24, of which waited for: 21 -> 18; matrix products, arithmetic and copies ran while one was open for 13% -> 18% of each run, Pallas kernels for 0% -> 0%
where the time goes in v1:
time: 1710 us; the launch traced here: 1700 us
  waiting for transfers between devices  927 us (54%)
  blocking collectives  260 us (15%)
  matrix products  192 us (11%)
  local copies, waits for them, and re-layouts  176 us (10%)
  other arithmetic  94.4 us (6%)
  starting transfers between devices  38.6 us (2%)
    dot_general x25, matrix products, contract(): return jnp.einsum(form, left, right, preferred_element_type=jnp.float32)  171 us
    all_gather x1, blocking collectives, per_device(): doc_rows = lax.all_gather(doc_ids[0], 'fsdp', axis=0, tiled=False)  130 us
    reduce_scatter x1, waiting for transfers between devices, per_device(): lax.psum_scatter(up_grad_full.astype(jnp.bfloat16), 'fsdp', scatter_dimen...  114 us
    reduce_scatter x1, waiting for transfers between devices, per_device(): lax.psum_scatter(gate_grad_full.astype(jnp.bfloat16), 'fsdp', scatter_dim...  111 us
    all_gather x1, waiting for transfers between devices, per_device(): lax.all_gather(expert_down, 'fsdp', axis=1, tiled=True)  105 us
    reduce_scatter x1, waiting for transfers between devices, per_device(): lax.psum_scatter(down_grad_full.astype(jnp.bfloat16), 'fsdp', scatter_dim...  96.3 us
    psum x1, waiting for transfers between devices, per_device(): lax.psum(query_grad_part.astype(jnp.bfloat16), 'ctx').astype(jnp.float32)  92.6 us
    all_to_all x1, waiting for transfers between devices, per_device(): lax.all_to_all(dispatch(jnp.repeat(second_input, TOP, axis=0)), 'ctx', sp...  65.1 us
  transfers between devices with their start and end apart: 24, of which 18 were waited for; matrix products, arithmetic and copies ran while one was open for 18% of the time, Pallas kernels for 0%

profile of v1, /device:TPU:0, one launch (start us, length us, event | category | flops | bytes accessed | tf_op | source)
XLA Modules:
  0.0 1704.3 jit_solution(12288966190104806452)
XLA Ops:
  17.6 12.4 all-to-all-done.1
  55.4 129.7 %all-gather.1 = s32[4,1,1024]{2,1,0:T(1,128)S(1)} all-gather(s32[1,1,1024]{2,1,0:T(1,128)S(1)} %bitcast.379), channel_id=1, replica_groups=mesh['ctx'=8,'fsdp'=4] {'fsdp'}, dimensions={0}, use_global_device_ids=true | all-gather | bytes 20480 | tf_op jit(solution)/shard_map/all_gather | solution.py:111
  220.0 8.6 fusion.76
  228.7 8.4 fusion.3
  241.0 9.4 fusion.27
  262.5 15.0 all_gather.40
  277.6 56.2 %reduce-scatter.10.cloned.1.call-done = f32[1,128,2048]{2,1,0:T(8,128)} async-done(((f32[4,128,2048]{2,1,0:T(8,128)}), f32[1,128,2048]{2,1,0:T(8,128)}) %reduce-scatter.10.cloned.1.call-update) | async-done | bytes 1048592 | tf_op jit(solution)/shard_map/reduce_scatter | solution.py:176
  336.7 7.0 gather_fusion.2
  344.5 10.7 scatter_custom_fusion.1
  360.7 10.2 scatter_custom_fusion
  371.0 60.6 %all-to-all-done.5 = bf16[8,2,96,2048]{3,2,1,0:T(8,128)(2,1)} async-done(((bf16[8,2,96,2048]{3,2,1,0:T(8,128)(2,1)}), bf16[8,2,96,2048]{3,2,1,0:T(8,128)(2,1)}, u32[]{:S(2)}, u32[]{:S(2)}) %all-to-all-start.5) | async-done | bytes 6291488 | tf_op jit(solution)/shard_map/all_to_all | solution.py:230
  443.0 65.1 %all-to-all-done.3 = bf16[8,2,96,2048]{3,2,1,0:T(8,128)(2,1)} async-done(((bf16[8,2,96,2048]{3,2,1,0:T(8,128)(2,1)}), bf16[8,2,96,2048]{3,2,1,0:T(8,128)(2,1)}, u32[]{:S(2)}, u32[]{:S(2)}) %all-to-all-start.3) | async-done | bytes 6291488 | tf_op jit(solution)/shard_map/all_to_all | solution.py:205
  514.7 10.4 fusion.79
  525.2 40.9 %all-gather.15.cloned.1.call-done = bf16[2,2048,768]{2,1,0:T(8,128)(2,1)} async-done(((bf16[2,512,768]{2,1,0:T(8,128)(2,1)}), bf16[2,2048,768]{2,1,0:T(8,128)(2,1)}) %all-gather.15.cloned.1.call-update) | async-done | bytes 6291472 | tf_op jit(solution)/shard_map/all_gather | solution.py:182
  566.1 10.4 fusion.78
  576.4 104.8 %all-gather.19.cloned.1.call-done = bf16[2,768,2048]{2,1,0:T(8,128)(2,1)} async-done(((bf16[2,192,2048]{2,1,0:T(8,128)(2,1)}), bf16[2,768,2048]{2,1,0:T(8,128)(2,1)}) %all-gather.19.cloned.1.call-update) | async-done | bytes 6291472 | tf_op jit(solution)/shard_map/all_gather | solution.py:184
  681.2 13.9 multiply_convert_fusion
  695.1 6.9 convert_bitcast_fusion
  702.0 18.8 %copy.197 = bf16[1,2,768,2048]{3,1,0,2:T(2,128)(2,1)} copy(bf16[1,2,768,2048]{3,2,1,0:T(8,128)(2,1)S(1)} %convert_bitcast_fusion) | data formatting | bytes 12582912 | tf_op jit(solution)/shard_map/broadcast_in_dim | solution.py:218
  725.8 10.8 fusion.80
  736.6 9.9 fusion.10
  746.5 18.8 %copy.200 = bf16[1,2,768,2048]{3,1,0,2:T(2,128)(2,1)} copy(bf16[1,2,768,2048]{3,2,1,0:T(8,128)(2,1)S(1)} %fusion.10) | data formatting | bytes 12582912 | tf_op jit(solution)/shard_map/broadcast_in_dim | solution.py:245
  765.3 32.1 %all-to-all-done.4 = bf16[1,2,768,2048]{3,1,0,2:T(2,128)(2,1)} async-done(((bf16[1,2,768,2048]{3,1,0,2:T(2,128)(2,1)}), bf16[1,2,768,2048]{3,1,0,2:T(2,128)(2,1)}, u32[]{:S(2)}, u32[]{:S(2)}) %all-to-all-start.4) | async-done | bytes 6291488 | tf_op jit(solution)/shard_map/all_to_all | solution.py:218
  802.2 8.4 copy.198
  810.6 12.8 gather_fusion.3
  830.6 43.1 %all-to-all-done.6 = bf16[1,2,768,2048]{3,1,0,2:T(2,128)(2,1)} async-done(((bf16[1,2,768,2048]{3,1,0,2:T(2,128)(2,1)}), bf16[1,2,768,2048]{3,1,0,2:T(2,128)(2,1)}, u32[]{:S(2)}, u32[]{:S(2)}) %all-to-all-start.6) | async-done | bytes 6291488 | tf_op jit(solution)/shard_map/all_to_all | solution.py:245
  873.7 8.4 copy.201
  882.1 12.6 gather_fusion.4
  894.7 6.7 convert_reduce_fusion
  904.6 42.1 %all-gather.21.cloned.1.call-done = bf16[512,2048]{1,0:T(8,128)(2,1)} async-done(((bf16[128,2048]{1,0:T(8,128)(2,1)}), bf16[512,2048]{1,0:T(8,128)(2,1)}) %all-gather.21.cloned.1.call-update) | async-done | bytes 2097168 | tf_op jit(solution)/shard_map/all_gather | solution.py:259
  952.2 11.1 fusion
  963.3 17.2 %fusion.5 = (bf16[4,8,128,1024]{2,3,1,0:T(8,128)(2,1)}, bf16[4,8,128,1024]{2,3,1,0:T(8,128)(2,1)}) fusion(f32[4,1,8,128,1024]{3,4,2,0,1:T(8,128)} %get-tuple-element.60, f32[4,8,128]{2,1,0:T(8,128)S(1)} %log_add_fusion, f32[4,8,128]{2,1,0:T(8,128)S(1)} %get-tuple-element.62, f32[4,1024,128,8]{2,1,3,0:T(8,128)} %get-tuple-element.63), kind=kLoop, calls=%fused_computation.19 | loop fusion | flops 20971520 | bytes 50364416 | tf_op jit(solution)/shard_map/reshape.89
  980.5 12.4 copy.209
  999.7 6.8 fusion.31
  1017.7 10.1 convolution_convert_fusion.1
  1029.5 11.9 convolution_convert_fusion.2
  1043.0 12.0 convolution_convert_fusion.3
  1064.3 9.9 reduce-scatter.12.cloned.1.call-done
  1075.9 16.6 all_gather.46
  1092.5 32.4 %all_gather.47 = bf16[512,512]{1,0:T(8,128)(2,1)S(1)} all-gather(bf16[512,128]{1,0:T(8,128)(2,1)S(1)} %bitcast.364), channel_id=1, replica_groups=mesh['ctx'=8,'fsdp'=4] {'fsdp'}, dimensions={1}, use_global_device_ids=true | all-gather | bytes 655360 | tf_op jit(solution)/shard_map/all_gather | solution.py:306
  1127.5 39.4 %all-gather.23.cloned.1.call-done = bf16[512,4096]{1,0:T(8,128)(2,1)} async-done(((bf16[512,1024]{1,0:T(8,128)(2,1)}), bf16[512,4096]{1,0:T(8,128)(2,1)}) %all-gather.23.cloned.1.call-update) | async-done | bytes 4194320 | tf_op jit(solution)/shard_map/all_gather | solution.py:312
  1186.5 23.9 %psum.71 = bf16[512,16]{0,1:T(8,128)(2,1)S(1)} all-reduce(bf16[512,16]{0,1:T(8,128)(2,1)} %reduce-scatter.14.cloned.1.call-done), channel_id=1, replica_groups=mesh['ctx'=8,'fsdp'=4] {'ctx'}, use_global_device_ids=true, to_apply=%region_36.38 | all-reduce | flops 8192 | bytes 32768 | tf_op jit(solution)/shard_map/psum | solution.py:348
  1211.0 96.3 %reduce-scatter.20.cloned.1.call-done = bf16[2,192,2048]{2,1,0:T(8,128)(2,1)} async-done(((bf16[2,768,2048]{2,1,0:T(8,128)(2,1)}), bf16[2,192,2048]{2,1,0:T(8,128)(2,1)}) %reduce-scatter.20.cloned.1.call-update) | async-done | bytes 1572880 | tf_op jit(solution)/shard_map/reduce_scatter | solution.py:336
  1310.7 114.0 %reduce-scatter.18.cloned.1.call-done = bf16[2,512,768]{2,1,0:T(8,128)(2,1)} async-done(((bf16[2,2048,768]{2,1,0:T(8,128)(2,1)}), bf16[2,512,768]{2,1,0:T(8,128)(2,1)}) %reduce-scatter.18.cloned.1.call-update) | async-done | bytes 1572880 | tf_op jit(solution)/shard_map/reduce_scatter | solution.py:333
  1428.1 110.7 %reduce-scatter.16.cloned.1.call-done = bf16[2,512,768]{2,1,0:T(8,128)(2,1)} async-done(((bf16[2,2048,768]{2,1,0:T(8,128)(2,1)}), bf16[2,512,768]{2,1,0:T(8,128)(2,1)}) %reduce-scatter.16.cloned.1.call-update) | async-done | bytes 1572880 | tf_op jit(solution)/shard_map/reduce_scatter | solution.py:330
  1544.7 42.4 %all-reduce = (f32[2048]{0:T(1024)}, f32[128]{0:T(128)}, f32[128]{0:T(128)}, f32[2048]{0:T(1024)}) all-reduce(f32[2048]{0:T(1024)S(1)} %bitcast.376, f32[128]{0:T(128)S(1)} %get-tuple-element.15, f32[128]{0:T(128)S(1)} %get-tuple-element.21, f32[2048]{0:T(1024)S(1)} %get-tuple-element.17), channel_id=1, replica_groups=mesh['ctx'=8,'fsdp'=4] {'ctx','fsdp'}, use_global_device_ids=true, to_apply=%region_24.26 | all-reduce | flops 4352 | bytes 34816 | tf_op jit(solution)/shard_map/psum | solution.py:350
  1589.5 92.6 %all-reduce.4.cloned.1.call-done = (bf16[512,4096]{1,0:T(8,128)(2,1)}, bf16[512,512]{1,0:T(8,128)(2,1)}, bf16[512,512]{1,0:T(8,128)(2,1)}, bf16[1024,2048]{1,0:T(8,128)(2,1)}) async-done(((bf16[512,4096]{1,0:T(8,128)(2,1)}, bf16[512,512]{1,0:T(8,128)(2,1)}, bf16[512,512]{1,0:T(8,128)(2,1)}, bf16[1024,2048]{1,0:T(8,128)(2,1)}), (bf16[512,4096]{1,0:T(8,128)(2,1)}, bf16[512,512]{1,0:T(8,128)(2,1)}, ...) | async-done | bytes 9437200 | tf_op jit(solution)/shard_map/psum | solution.py:344
  1686.3 6.8 convert_element_type.211
  (318 shorter events, 217.6 us)
Async XLA Ops:
  9.2 20.8 %all-to-all-start.1 = ((bf16[512,4,128]{0,2,1:T(8,128)(2,1)}), bf16[512,4,128]{0,2,1:T(8,128)(2,1)S(1)}, u32[]{:S(2)}, u32[]{:S(2)}) async-start(bf16[512,4,128]{0,2,1:T(8,128)(2,1)} %bitcast.13), calls=%async_computation.1 | async-start | bytes 1048576 | tf_op jit(solution)/shard_map/all_to_all | solution.py:125
  30.1 17.5 %all-to-all-start = ((bf16[512,4,128]{0,2,1:T(8,128)(2,1)}), bf16[512,4,128]{0,2,1:T(8,128)(2,1)S(1)}, u32[]{:S(2)}, u32[]{:S(2)}) async-start(bf16[512,4,128]{0,2,1:T(8,128)(2,1)} %bitcast.1), calls=%async_computation | async-start | bytes 1048576 | tf_op jit(solution)/shard_map/all_to_all | solution.py:126
  46.4 8.9 copy-start.60
  48.4 158.6 %all-to-all-start.2 = ((bf16[512,4,1024]{2,0,1:T(8,128)(2,1)}), bf16[512,4,1024]{2,0,1:T(8,128)(2,1)}, u32[]{:S(2)}, u32[]{:S(2)}) async-start(bf16[512,4,1024]{2,0,1:T(8,128)(2,1)} %copy.184), calls=%async_computation.2 | async-start | bytes 8388608 | tf_op jit(solution)/shard_map/all_to_all | solution.py:123
  53.2 137.1 %copy-start.52 = (f32[128]{0:T(128)S(1)}, f32[128]{0:T(128)}, u32[]{:S(2)}) copy-start(f32[128]{0:T(128)} %param.28) | copy-start | bytes 1540
  53.3 133.8 %all-gather.11.cloned.1.call-start = ((), (), s32[]{:S(2)}) async-start(), calls=%async_computation.15 | async-start | bytes 2621440 | tf_op jit(solution)/shard_map/all_gather | solution.py:122
  54.3 165.7 %all-gather.25.cloned.1.call-start = ((), (), s32[]{:S(2)}) async-start(), calls=%async_computation.28 | async-start | bytes 1179648 | tf_op jit(solution)/shard_map/all_gather | solution.py:152
  55.1 164.5 %copy-start.35 = (f32[128,64]{0,1:T(8,128)}, f32[128,64]{0,1:T(8,128)S(1)}, u32[]{:S(2)}) copy-start(f32[128,64]{0,1:T(8,128)S(1)} %get-tuple-element.53) | copy-start | bytes 98308
  55.1 164.5 %copy-start.37 = (f32[128,64]{0,1:T(8,128)}, f32[128,64]{0,1:T(8,128)S(1)}, u32[]{:S(2)}) copy-start(f32[128,64]{0,1:T(8,128)S(1)} %get-tuple-element.54) | copy-start | bytes 98308
  55.3 144.7 %copy-start.29 = (f32[128,64]{1,0:T(8,128)}, f32[128,64]{1,0:T(8,128)S(1)}, u32[]{:S(2)}) copy-start(f32[128,64]{1,0:T(8,128)S(1)} %copy.181) | copy-start | bytes 98308
  55.4 144.6 %copy-start.31 = (f32[128,64]{1,0:T(8,128)}, f32[128,64]{1,0:T(8,128)S(1)}, u32[]{:S(2)}) copy-start(f32[128,64]{1,0:T(8,128)S(1)} %copy.182) | copy-start | bytes 98308
  187.0 17.2 %copy-start.6 = (bf16[512,2048]{1,0:T(8,128)(2,1)S(1)}, bf16[512,2048]{1,0:T(8,128)(2,1)}, u32[]{:S(2)}) copy-start(bf16[512,2048]{1,0:T(8,128)(2,1)} %all-gather.11.cloned.1.call-done) | copy-start | bytes 6291460
  191.5 49.5 %all-gather.13.cloned.1.call-start = ((), (), s32[]{:S(2)}) async-start(), calls=%async_computation.16 | async-start | bytes 1179648 | tf_op jit(solution)/shard_map/all_gather | solution.py:155
  206.7 127.1 %reduce-scatter.10.cloned.1.call-start = ((), (), s32[]{:S(2)}) async-start(), calls=%async_computation.17 | async-start | bytes 5242880 | tf_op jit(solution)/shard_map/reduce_scatter | solution.py:176
  217.9 10.8 copy-start.39
  228.7 12.3 copy-start.41
  237.1 13.3 copy-start.47
  241.0 10.4 copy-start.10
  255.8 80.4 %copy-start.43 = (f32[2048]{0:T(1024)S(1)}, f32[2048]{0:T(1024)}, u32[]{:S(2)}) copy-start(f32[2048]{0:T(1024)} %param.30) | copy-start | bytes 24580
  255.8 258.9 %all-gather.17.cloned.1.call-start = ((), (), s32[]{:S(2)}) async-start(), calls=%async_computation.19 | async-start | bytes 7864320 | tf_op jit(solution)/shard_map/all_gather | solution.py:183
  256.4 309.7 %all-gather.15.cloned.1.call-start = ((), (), s32[]{:S(2)}) async-start(), calls=%async_computation.18 | async-start | bytes 7864320 | tf_op jit(solution)/shard_map/all_gather | solution.py:182
  277.5 58.9 %copy-start.33 = (bf16[2048,16]{0,1:T(8,128)(2,1)}, bf16[2048,16]{0,1:T(8,128)(2,1)S(1)}, u32[]{:S(2)}) copy-start(bf16[2048,16]{0,1:T(8,128)(2,1)S(1)} %all_gather.40) | copy-start | bytes 196612
  336.4 24.3 %copy-start.8 = (bf16[128,2048]{1,0:T(8,128)(2,1)}, bf16[128,2048]{1,0:T(8,128)(2,1)S(1)}, u32[]{:S(2)}) copy-start(bf16[128,2048]{1,0:T(8,128)(2,1)S(1)} %multiply_convert_fusion.4) | copy-start | bytes 1572868
  355.1 76.4 %all-to-all-start.5 = ((bf16[8,2,96,2048]{3,2,1,0:T(8,128)(2,1)}), bf16[8,2,96,2048]{3,2,1,0:T(8,128)(2,1)}, u32[]{:S(2)}, u32[]{:S(2)}) async-start(bf16[8,2,96,2048]{3,2,1,0:T(8,128)(2,1)} %bitcast.328), calls=%async_computation.6 | async-start | bytes 12582912 | tf_op jit(solution)/shard_map/all_to_all | solution.py:230
  360.0 321.2 %all-gather.19.cloned.1.call-start = ((), (), s32[]{:S(2)}) async-start(), calls=%async_computation.20 | async-start | bytes 7864320 | tf_op jit(solution)/shard_map/all_gather | solution.py:184
  431.5 76.5 %all-to-all-start.3 = ((bf16[8,2,96,2048]{3,2,1,0:T(8,128)(2,1)}), bf16[8,2,96,2048]{3,2,1,0:T(8,128)(2,1)}, u32[]{:S(2)}, u32[]{:S(2)}) async-start(bf16[8,2,96,2048]{3,2,1,0:T(8,128)(2,1)} %bitcast.329), calls=%async_computation.4 | async-start | bytes 12582912 | tf_op jit(solution)/shard_map/all_to_all | solution.py:205
  681.2 13.9 copy-start.61
  720.8 76.6 %all-to-all-start.4 = ((bf16[1,2,768,2048]{3,1,0,2:T(2,128)(2,1)}), bf16[1,2,768,2048]{3,1,0,2:T(2,128)(2,1)}, u32[]{:S(2)}, u32[]{:S(2)}) async-start(bf16[1,2,768,2048]{3,1,0,2:T(2,128)(2,1)} %copy.197), calls=%async_computation.5 | async-start | bytes 12582912 | tf_op jit(solution)/shard_map/all_to_all | solution.py:218
  725.8 10.8 copy-start.63
  797.4 76.3 %all-to-all-start.6 = ((bf16[1,2,768,2048]{3,1,0,2:T(2,128)(2,1)}), bf16[1,2,768,2048]{3,1,0,2:T(2,128)(2,1)}, u32[]{:S(2)}, u32[]{:S(2)}) async-start(bf16[1,2,768,2048]{3,1,0,2:T(2,128)(2,1)} %copy.200), calls=%async_computation.7 | async-start | bytes 12582912 | tf_op jit(solution)/shard_map/all_to_all | solution.py:245
  802.1 144.6 %all-gather.21.cloned.1.call-start = ((), (), s32[]{:S(2)}) async-start(), calls=%async_computation.21 | async-start | bytes 2621440 | tf_op jit(solution)/shard_map/all_gather | solution.py:259
  904.5 158.6 %reduce-scatter.22.cloned.1.call-start = ((), (), s32[]{:S(2)}) async-start(), calls=%async_computation.29 | async-start | bytes 1179648
  904.6 47.6 %copy-start.19 = (bf16[4,1024,128]{1,2,0:T(8,128)(2,1)S(1)}, bf16[4,1024,128]{1,2,0:T(8,128)(2,1)}, u32[]{:S(2)}) copy-start(bf16[4,1024,128]{1,2,0:T(8,128)(2,1)} %all-gather.13.cloned.1.call-done) | copy-start | bytes 3145732
  999.7 74.5 %reduce-scatter.12.cloned.1.call-start = ((), (), s32[]{:S(2)}) async-start(), calls=%async_computation.23 | async-start | bytes 1179648 | tf_op jit(solution)/shard_map/reduce_scatter | solution.py:273
  1006.6 160.3 %all-gather.23.cloned.1.call-start = ((), (), s32[]{:S(2)}) async-start(), calls=%async_computation.22 | async-start | bytes 5242880 | tf_op jit(solution)/shard_map/all_gather | solution.py:312
  1016.8 169.7 %reduce-scatter.14.cloned.1.call-start = ((), (), s32[]{:S(2)}) async-start(), calls=%async_computation.24 | async-start | bytes 81920 | tf_op jit(solution)/shard_map/reduce_scatter | solution.py:340
  1017.7 289.6 %reduce-scatter.20.cloned.1.call-start = ((), (), s32[]{:S(2)}) async-start(), calls=%async_computation.27 | async-start | bytes 7864320 | tf_op jit(solution)/shard_map/reduce_scatter | solution.py:336
  1027.8 396.9 %reduce-scatter.18.cloned.1.call-start = ((), (), s32[]{:S(2)}) async-start(), calls=%async_computation.26 | async-start | bytes 7864320 | tf_op jit(solution)/shard_map/reduce_scatter | solution.py:333
  1041.4 497.4 %reduce-scatter.16.cloned.1.call-start = ((), (), s32[]{:S(2)}) async-start(), calls=%async_computation.25 | async-start | bytes 7864320 | tf_op jit(solution)/shard_map/reduce_scatter | solution.py:330
  1055.0 627.0 %all-reduce.4.cloned.1.call-start = ((), (), s32[]{:S(2)}) async-start(), calls=%async_computation.30 | async-start | bytes 18874368 | tf_op jit(solution)/shard_map/psum | solution.py:344
  1056.9 18.2 %copy-start.30 = (f32[128,64]{1,0:T(8,128)S(1)}, f32[128,64]{1,0:T(8,128)}, u32[]{:S(2)}) copy-start(f32[128,64]{1,0:T(8,128)} %copy-done.29) | copy-start | bytes 98308
  1056.9 18.2 %copy-start.32 = (f32[128,64]{1,0:T(8,128)S(1)}, f32[128,64]{1,0:T(8,128)}, u32[]{:S(2)}) copy-start(f32[128,64]{1,0:T(8,128)} %copy-done.31) | copy-start | bytes 98308
  1056.9 18.4 %copy-start.16 = (f32[512,128]{1,0:T(8,128)S(1)}, f32[512,128]{1,0:T(8,128)}, u32[]{:S(2)}) copy-start(f32[512,128]{1,0:T(8,128)} %copy-done.15) | copy-start | bytes 786436
  1057.0 18.4 %copy-start.50 = (f32[512]{0:T(512)S(1)}, f32[512]{0:T(512)}, u32[]{:S(2)}) copy-start(f32[512]{0:T(512)} %get-tuple-element.51) | copy-start | bytes 6148
  1057.0 18.4 %copy-start.53 = (f32[128]{0:T(128)S(1)}, f32[128]{0:T(128)}, u32[]{:S(2)}) copy-start(f32[128]{0:T(128)} %param.28) | copy-start | bytes 1540
  1063.2 61.7 %copy-start.7 = (bf16[512,2048]{1,0:T(8,128)(2,1)S(1)}, bf16[512,2048]{1,0:T(8,128)(2,1)}, u32[]{:S(2)}) copy-start(bf16[512,2048]{1,0:T(8,128)(2,1)} %all-gather.11.cloned.1.call-done) | copy-start | bytes 6291460
  1181.3 360.8 %all-to-all-start.7 = ((f32[4,128,512]{2,1,0:T(8,128)}), f32[4,128,512]{2,1,0:T(8,128)S(1)}, u32[]{:S(2)}, u32[]{:S(2)}) async-start(f32[4,128,512]{2,1,0:T(8,128)} %bitcast.102), calls=%async_computation.9 | async-start | bytes 2097152 | tf_op jit(solution)/shard_map/all_to_all | solution.py:324
  1428.1 114.4 %copy-start.57 = (f32[128]{0:T(128)S(1)}, f32[128]{0:T(128)}, u32[]{:S(2)}) copy-start(f32[128]{0:T(128)} %copy-done.56) | copy-start | bytes 1540
  (42 other events, 179.0 us)
Sparse Core Ops, SparseCore 0:
  56.2 77.1 all-gather.10
  191.6 23.3 all-gather.24
  217.5 23.4 all-gather.12
  255.9 77.8 reduce-scatter.9
  335.2 115.8 all-gather.16
  452.5 113.4 all-gather.14
  567.6 113.5 all-gather.18
  904.7 42.0 all-gather.20
  999.8 34.7 reduce-scatter.21
  1038.2 35.9 reduce-scatter.11
  1076.4 90.4 all-gather.22
  1168.9 17.4 reduce-scatter.13
  1188.8 118.4 reduce-scatter.19
  1310.0 114.7 reduce-scatter.17
  1427.5 111.2 reduce-scatter.15
  1542.6 139.3 all-reduce.3

commit v2 on v1

--- a/solution.py
+++ b/solution.py
@@ -64,6 +64,18 @@
         inv_scale * (scaled - normed * jnp.mean(scaled * normed, axis=-1, keepdims=True)),
         factor_grad,
     )
+
+
+def gather_a2a(x, axis_name, size, axis):
+    rep = jnp.broadcast_to(x[None], (size,) + x.shape)
+    got = jnp.moveaxis(lax.all_to_all(rep, axis_name, 0, 0, tiled=True), 0, axis)
+    return got.reshape(x.shape[:axis] + (size * x.shape[axis],) + x.shape[axis + 1 :])
+
+
+def scatter_sum_a2a(x, axis_name, size, axis):
+    parts = x.reshape(x.shape[:axis] + (size, x.shape[axis] // size) + x.shape[axis + 1 :])
+    got = lax.all_to_all(parts, axis_name, axis, axis, tiled=True)
+    return jnp.sum(got.astype(jnp.float32), axis=axis)
 
 
 def per_device(
@@ -108,7 +120,7 @@
     offsets = jnp.arange(block_len, dtype=jnp.int32)
     local_pos = (own_blocks[:, None] * block_len + offsets[None, :]).reshape(-1)
     all_pos = (block_map[:, None] * block_len + offsets[None, :]).reshape(-1)
-    doc_rows = lax.all_gather(doc_ids[0], "fsdp", axis=0, tiled=False)
+    doc_rows = gather_a2a(doc_ids.astype(jnp.float32), "fsdp", fsdp_size, 0)
     docs_query = jnp.take(doc_rows, local_pos, axis=1)
     docs_key = jnp.take(doc_rows, all_pos, axis=1)
     visible = (all_pos[None, None, :] <= local_pos[None, :, None]) & (
@@ -149,12 +161,8 @@
         .reshape(seqs, tokens, kv_dev * HEAD_DIM)
         .astype(jnp.bfloat16)
     )
-    keys_all = lax.all_gather(key_rot, "ctx", axis=1, tiled=True).reshape(
-        seqs, -1, kv_dev, HEAD_DIM
-    )
-    values_all = lax.all_gather(value_low, "ctx", axis=1, tiled=True).reshape(
-        seqs, -1, kv_dev, HEAD_DIM
-    )
+    keys_all = gather_a2a(key_rot, "ctx", ctx_size, 1).reshape(seqs, -1, kv_dev, HEAD_DIM)
+    values_all = gather_a2a(value_low, "ctx", ctx_size, 1).reshape(seqs, -1, kv_dev, HEAD_DIM)
     query_groups = query_rot.reshape(seqs, tokens, kv_dev, group_dev, HEAD_DIM)
 
     def masked_scores():
@@ -182,7 +190,7 @@
         lax.all_gather(expert_gate, "fsdp", axis=1, tiled=True),
         lax.all_gather(expert_up, "fsdp", axis=1, tiled=True),
         lax.all_gather(expert_down, "fsdp", axis=1, tiled=True),
-        lax.all_gather(router_proj, "fsdp", axis=0, tiled=True),
+        gather_a2a(router_proj, "fsdp", fsdp_size, 0),
     )
     logits = matmul(second_input, w_router)
     route_ids = routes[0]
@@ -270,12 +278,9 @@
     grad_vheads = contract("skgtj,stkgd->sjkd", probs_back.astype(jnp.bfloat16), grad_groups)
 
     def kv_reduce(grads):
-        summed = lax.psum_scatter(
-            grads.reshape(seqs, -1, kv_dev * HEAD_DIM).astype(jnp.bfloat16),
-            "ctx",
-            scatter_dimension=1,
-            tiled=True,
-        ).astype(jnp.float32)
+        summed = scatter_sum_a2a(
+            grads.reshape(seqs, -1, kv_dev * HEAD_DIM).astype(jnp.bfloat16), "ctx", ctx_size, 1
+        )
         total = summed
         for step in range(1, share):
             pairs = [
@@ -302,16 +307,20 @@
     grad_key = grad_key.reshape(group_rows, kv_dev * HEAD_DIM).astype(jnp.bfloat16)
     grad_value = grad_value.reshape(group_rows, kv_dev * HEAD_DIM).astype(jnp.bfloat16)
 
-    def gather_heads(grads):
-        whole = lax.all_gather(grads, "fsdp", axis=1, tiled=True)
+    def gather_heads(parts):
+        whole = parts.reshape(group_rows, -1)
         if share > 1:
             whole = whole.reshape(group_rows, KV_HEADS, share, HEAD_DIM)[:, :, 0]
             whole = whole.reshape(group_rows, KV_HEADS * HEAD_DIM)
         return whole
 
-    query_all = lax.all_gather(grad_query, "fsdp", axis=1, tiled=True)
-    key_all = gather_heads(grad_key)
-    value_all = gather_heads(grad_value)
+    q_width, kv_width = heads_dev * HEAD_DIM, kv_dev * HEAD_DIM
+    joined = lax.all_gather(
+        jnp.concatenate([grad_query, grad_key, grad_value], axis=1), "fsdp", axis=1, tiled=False
+    )
+    query_all = joined[:, :, :q_width].reshape(group_rows, -1)
+    key_all = gather_heads(joined[:, :, q_width : q_width + kv_width])
+    value_all = gather_heads(joined[:, :, q_width + kv_width :])
     input_part = lax.dynamic_slice_in_dim(group_input, fsdp_index * d_part, d_part, 1)
     query_grad_part = contract("td,tq->dq", input_part, query_all)
     key_grad_part = contract("td,tq->dq", input_part, key_all)
@@ -337,19 +346,17 @@
             down_grad_full.astype(jnp.bfloat16), "fsdp", scatter_dimension=1, tiled=True
         ).astype(jnp.float32),
     )
-    router_shard = lax.psum_scatter(
-        router_grad_full.astype(jnp.bfloat16), "fsdp", scatter_dimension=0, tiled=True
-    ).astype(jnp.float32)
-    query_grad, key_grad, value_grad, out_grad, router_grad = (
+    query_grad, key_grad, value_grad, out_grad = (
         lax.psum(query_grad_part.astype(jnp.bfloat16), "ctx").astype(jnp.float32),
         lax.psum(key_grad_part.astype(jnp.bfloat16), "ctx").astype(jnp.float32),
         lax.psum(value_grad_part.astype(jnp.bfloat16), "ctx").astype(jnp.float32),
         lax.psum(out_grad_part.astype(jnp.bfloat16), "ctx").astype(jnp.float32),
-        lax.psum(router_shard.astype(jnp.bfloat16), "ctx").astype(jnp.float32),
-    )
-    attn_gain_total, query_gain_total, key_gain_total, ffn_gain_total = lax.psum(
-        (attn_gain_grad, query_gain_grad, key_gain_grad, ffn_gain_grad), ("ctx", "fsdp")
-    )
+    )
+    attn_gain_total, query_gain_total, key_gain_total, ffn_gain_total, router_total = lax.psum(
+        (attn_gain_grad, query_gain_grad, key_gain_grad, ffn_gain_grad, router_grad_full),
+        ("ctx", "fsdp"),
+    )
+    router_grad = lax.dynamic_slice_in_dim(router_total, fsdp_index * d_part, d_part, 0)
     return (
         layer_out[None],
         grad_hidden[None],

time: 1710 us -> 1800 us (1.053)
  waiting for transfers between devices: 927 us -> 1180 us
  blocking collectives: 260 us -> 42.4 us
  local copies, waits for them, and re-layouts: 176 us -> 208 us
  starting transfers between devices: 38.6 us -> 61.8 us
    all_gather x4 -> x0, blocking collectives: 194 us -> none  [the longest x1 130 us: per_device(): doc_rows = lax.all_gather(doc_ids[0], 'fsdp', axis=0, tiled=False)]
    psum x0 -> x1, waiting for transfers between devices: none -> 99.9 us  [per_device(): lax.psum((attn_gain_grad, query_gain_grad, key_gain_grad, ffn_gain_grad,...]
    all_to_all x1, waiting for transfers between devices: 0.01 us -> 72.3 us  [per_device(): w_query_cols = lax.all_to_all(query_proj, 'fsdp', 1, 0, tiled=True)]
    all_to_all x0 -> x6, waiting for transfers between devices: none -> 33.7 us  [the longest x4 16.9 us: gather_a2a(): lax.all_to_all(rep, axis_name, 0, 0, tiled=True)]
    psum x2 -> x1, blocking collectives: 66.3 us -> 42.4 us  [per_device(): lax.psum((attn_gain_grad, query_gain_grad, key_gain_grad, ffn_gain_grad,...]
    all_to_all x0 -> x6, starting transfers between devices: none -> 23.5 us  [the longest x4 15 us: gather_a2a(): lax.all_to_all(rep, axis_name, 0, 0, tiled=True)]
    all_to_all x1, waiting for transfers between devices: 1.11 us -> 23.3 us  [per_device(): w_value_cols = lax.all_to_all(value_proj, 'fsdp', 1, 0, tiled=True)]
    all_gather x3 -> x1, waiting for transfers between devices: 43.3 us -> 49.4 us  [per_device(): lax.all_gather(jnp.concatenate([grad_query, grad_key, grad_value], axis=1...]
  transfers between devices with their start and end apart: 24 -> 26, of which waited for: 18 -> 23; matrix products, arithmetic and copies ran while one was open for 18% -> 16% of each run, Pallas kernels for 0% -> 0%
where the time goes in v2:
time: 1800 us
  waiting for transfers between devices  1180 us (66%)
  local copies, waits for them, and re-layouts  208 us (12%)
  matrix products  188 us (10%)
  other arithmetic  97.9 us (5%)
  starting transfers between devices  61.8 us (3%)
  blocking collectives  42.4 us (2%)
    dot_general x25, matrix products, contract(): return jnp.einsum(form, left, right, preferred_element_type=jnp.float32)  165 us
    reduce_scatter x1, waiting for transfers between devices, per_device(): lax.psum_scatter(gate_grad_full.astype(jnp.bfloat16), 'fsdp', scatter_dim...  111 us
    reduce_scatter x1, waiting for transfers between devices, per_device(): lax.psum_scatter(down_grad_full.astype(jnp.bfloat16), 'fsdp', scatter_dim...  111 us
    reduce_scatter x1, waiting for transfers between devices, per_device(): lax.psum_scatter(up_grad_full.astype(jnp.bfloat16), 'fsdp', scatter_dimen...  111 us
    all_gather x1, waiting for transfers between devices, per_device(): lax.all_gather(expert_down, 'fsdp', axis=1, tiled=True)  105 us
    psum x1, waiting for transfers between devices, per_device(): lax.psum((attn_gain_grad, query_gain_grad, key_gain_grad, ffn_gain_grad,...  99.9 us
    psum x1, waiting for transfers between devices, per_device(): lax.psum(query_grad_part.astype(jnp.bfloat16), 'ctx').astype(jnp.float32)  92.5 us
    all_to_all x1, waiting for transfers between devices, per_device(): w_query_cols = lax.all_to_all(query_proj, 'fsdp', 1, 0, tiled=True)  72.3 us
  transfers between devices with their start and end apart: 26, of which 23 were waited for; matrix products, arithmetic and copies ran while one was open for 16% of the time, Pallas kernels for 0%

profile of v2, /device:TPU:0, one launch (start us, length us, event | category | flops | bytes accessed | tf_op | source)
XLA Modules:
  0.0 1795.8 jit_solution(5644299006329081928)
XLA Ops:
  20.8 27.5 %all-to-all-done.3 = bf16[512,4,128]{0,2,1:T(8,128)(2,1)S(1)} async-done(((bf16[512,4,128]{0,2,1:T(8,128)(2,1)}), bf16[512,4,128]{0,2,1:T(8,128)(2,1)S(1)}, u32[]{:S(2)}, u32[]{:S(2)}) %all-to-all-start.3) | async-done | bytes 524320 | tf_op jit(solution)/shard_map/all_to_all | solution.py:137
  53.3 23.3 %all-to-all-done = bf16[512,4,128]{0,2,1:T(8,128)(2,1)S(1)} async-done(((bf16[512,4,128]{0,2,1:T(8,128)(2,1)}), bf16[512,4,128]{0,2,1:T(8,128)(2,1)S(1)}, u32[]{:S(2)}, u32[]{:S(2)}) %all-to-all-start) | async-done | bytes 524320 | tf_op jit(solution)/shard_map/all_to_all | solution.py:138
  97.8 8.7 all-to-all-done.1
  152.1 72.3 %all-to-all-done.5 = bf16[512,4,1024]{2,0,1:T(8,128)(2,1)} async-done(((bf16[512,4,1024]{2,0,1:T(8,128)(2,1)}), bf16[512,4,1024]{2,0,1:T(8,128)(2,1)}, u32[]{:S(2)}, u32[]{:S(2)}) %all-to-all-start.5) | async-done | bytes 4194336 | tf_op jit(solution)/shard_map/all_to_all | solution.py:135
  237.2 7.2 fusion.84
  244.4 8.4 fusion.3
  252.9 7.8 fusion.27
  280.3 63.3 %reduce-scatter.5.cloned.1.call-done = f32[1,128,2048]{2,1,0:T(8,128)} async-done(((f32[4,128,2048]{2,1,0:T(8,128)}), f32[1,128,2048]{2,1,0:T(8,128)}) %reduce-scatter.5.cloned.1.call-update) | async-done | bytes 1048592 | tf_op jit(solution)/shard_map/reduce_scatter | solution.py:184
  346.6 7.0 gather_fusion.2
  354.5 10.7 scatter_custom_fusion.1
  370.7 10.2 scatter_custom_fusion
  380.9 60.6 %all-to-all-done.9 = bf16[8,2,96,2048]{3,2,1,0:T(8,128)(2,1)} async-done(((bf16[8,2,96,2048]{3,2,1,0:T(8,128)(2,1)}), bf16[8,2,96,2048]{3,2,1,0:T(8,128)(2,1)}, u32[]{:S(2)}, u32[]{:S(2)}) %all-to-all-start.9) | async-done | bytes 6291488 | tf_op jit(solution)/shard_map/all_to_all | solution.py:238
  452.9 65.1 %all-to-all-done.7 = bf16[8,2,96,2048]{3,2,1,0:T(8,128)(2,1)} async-done(((bf16[8,2,96,2048]{3,2,1,0:T(8,128)(2,1)}), bf16[8,2,96,2048]{3,2,1,0:T(8,128)(2,1)}, u32[]{:S(2)}, u32[]{:S(2)}) %all-to-all-start.7) | async-done | bytes 6291488 | tf_op jit(solution)/shard_map/all_to_all | solution.py:213
  524.6 10.4 fusion.86
  535.0 41.1 %all-gather.10.cloned.1.call-done = bf16[2,2048,768]{2,1,0:T(8,128)(2,1)} async-done(((bf16[2,512,768]{2,1,0:T(8,128)(2,1)}), bf16[2,2048,768]{2,1,0:T(8,128)(2,1)}) %all-gather.10.cloned.1.call-update) | async-done | bytes 6291472 | tf_op jit(solution)/shard_map/all_gather | solution.py:190
  576.1 10.4 fusion.85
  586.5 104.6 %all-gather.14.cloned.1.call-done = bf16[2,768,2048]{2,1,0:T(8,128)(2,1)} async-done(((bf16[2,192,2048]{2,1,0:T(8,128)(2,1)}), bf16[2,768,2048]{2,1,0:T(8,128)(2,1)}) %all-gather.14.cloned.1.call-update) | async-done | bytes 6291472 | tf_op jit(solution)/shard_map/all_gather | solution.py:192
  691.1 13.9 multiply_convert_fusion
  704.9 7.0 convert_bitcast_fusion
  711.9 18.8 %copy.202 = bf16[1,2,768,2048]{3,1,0,2:T(2,128)(2,1)} copy(bf16[1,2,768,2048]{3,2,1,0:T(8,128)(2,1)S(1)} %convert_bitcast_fusion) | data formatting | bytes 12582912 | tf_op jit(solution)/shard_map/broadcast_in_dim | solution.py:226
  735.7 10.9 fusion.87
  746.5 9.9 fusion.10
  756.5 18.8 %copy.205 = bf16[1,2,768,2048]{3,1,0,2:T(2,128)(2,1)} copy(bf16[1,2,768,2048]{3,2,1,0:T(8,128)(2,1)S(1)} %fusion.10) | data formatting | bytes 12582912 | tf_op jit(solution)/shard_map/broadcast_in_dim | solution.py:253
  775.2 32.0 %all-to-all-done.8 = bf16[1,2,768,2048]{3,1,0,2:T(2,128)(2,1)} async-done(((bf16[1,2,768,2048]{3,1,0,2:T(2,128)(2,1)}), bf16[1,2,768,2048]{3,1,0,2:T(2,128)(2,1)}, u32[]{:S(2)}, u32[]{:S(2)}) %all-to-all-start.8) | async-done | bytes 6291488 | tf_op jit(solution)/shard_map/all_to_all | solution.py:226
  812.1 8.4 copy.203
  820.5 12.9 gather_fusion.3
  841.4 42.1 %all-to-all-done.10 = bf16[1,2,768,2048]{3,1,0,2:T(2,128)(2,1)} async-done(((bf16[1,2,768,2048]{3,1,0,2:T(2,128)(2,1)}), bf16[1,2,768,2048]{3,1,0,2:T(2,128)(2,1)}, u32[]{:S(2)}, u32[]{:S(2)}) %all-to-all-start.10) | async-done | bytes 6291488 | tf_op jit(solution)/shard_map/all_to_all | solution.py:253
  883.6 8.4 copy.206
  892.0 12.6 gather_fusion.4
  904.5 6.7 convert_reduce_fusion
  916.4 40.3 %all-gather.16.cloned.1.call-done = bf16[512,2048]{1,0:T(8,128)(2,1)} async-done(((bf16[128,2048]{1,0:T(8,128)(2,1)}), bf16[512,2048]{1,0:T(8,128)(2,1)}) %all-gather.16.cloned.1.call-update) | async-done | bytes 2097168 | tf_op jit(solution)/shard_map/all_gather | solution.py:267
  962.2 14.3 fusion
  978.9 13.0 fusion.6
  991.9 12.7 copy.217
  1027.3 7.8 all-to-all-done.11
  1045.7 9.0 all-to-all-done.12
  1059.4 9.7 convolution_convert_fusion.1
  1070.8 11.9 convolution_convert_fusion.2
  1084.3 11.9 convolution_convert_fusion.3
  1104.4 49.4 %all-gather.18.cloned.1.call-done = bf16[512,5120]{1,0:T(8,128)(2,1)} async-done(((bf16[512,1280]{1,0:T(8,128)(2,1)}), bf16[512,5120]{1,0:T(8,128)(2,1)}) %all-gather.18.cloned.1.call-update) | async-done | bytes 5242896 | tf_op jit(solution)/shard_map/all_gather | solution.py:318
  1153.8 10.3 reshape.817
  1189.6 99.9 %all-reduce.5.cloned.1.call-done = f32[2048,16]{0,1:T(8,128)} async-done(((f32[2048,16]{0,1:T(8,128)}), f32[2048,16]{0,1:T(8,128)}) %all-reduce.5.cloned.1.call-update) | async-done | bytes 131088 | tf_op jit(solution)/shard_map/psum | solution.py:355
  1290.8 110.8 %reduce-scatter.11.cloned.1.call-done = bf16[2,192,2048]{2,1,0:T(8,128)(2,1)} async-done(((bf16[2,768,2048]{2,1,0:T(8,128)(2,1)}), bf16[2,192,2048]{2,1,0:T(8,128)(2,1)}) %reduce-scatter.11.cloned.1.call-update) | async-done | bytes 1572880 | tf_op jit(solution)/shard_map/reduce_scatter | solution.py:345
  1405.1 110.6 %reduce-scatter.9.cloned.1.call-done = bf16[2,512,768]{2,1,0:T(8,128)(2,1)} async-done(((bf16[2,2048,768]{2,1,0:T(8,128)(2,1)}), bf16[2,512,768]{2,1,0:T(8,128)(2,1)}) %reduce-scatter.9.cloned.1.call-update) | async-done | bytes 1572880 | tf_op jit(solution)/shard_map/reduce_scatter | solution.py:342
  1519.0 110.9 %reduce-scatter.7.cloned.1.call-done = bf16[2,512,768]{2,1,0:T(8,128)(2,1)} async-done(((bf16[2,2048,768]{2,1,0:T(8,128)(2,1)}), bf16[2,512,768]{2,1,0:T(8,128)(2,1)}) %reduce-scatter.7.cloned.1.call-update) | async-done | bytes 1572880 | tf_op jit(solution)/shard_map/reduce_scatter | solution.py:339
  1635.7 42.4 %all-reduce = (f32[2048]{0:T(1024)}, f32[128]{0:T(128)}, f32[128]{0:T(128)}, f32[2048]{0:T(1024)}) all-reduce(f32[2048]{0:T(1024)S(1)} %bitcast.408, f32[128]{0:T(128)S(1)} %get-tuple-element.15, f32[128]{0:T(128)S(1)} %get-tuple-element.21, f32[2048]{0:T(1024)S(1)} %get-tuple-element.17), channel_id=1, replica_groups=mesh['ctx'=8,'fsdp'=4] {'ctx','fsdp'}, use_global_device_ids=true, to_apply=%region_24.26 | all-reduce | flops 4352 | bytes 34816 | tf_op jit(solution)/shard_map/psum | solution.py:355
  1680.6 92.5 %all-reduce.7.cloned.1.call-done = (bf16[512,4096]{1,0:T(8,128)(2,1)}, bf16[512,512]{1,0:T(8,128)(2,1)}, bf16[512,512]{1,0:T(8,128)(2,1)}, bf16[1024,2048]{1,0:T(8,128)(2,1)}) async-done(((bf16[512,4096]{1,0:T(8,128)(2,1)}, bf16[512,512]{1,0:T(8,128)(2,1)}, bf16[512,512]{1,0:T(8,128)(2,1)}, bf16[1024,2048]{1,0:T(8,128)(2,1)}), (bf16[512,4096]{1,0:T(8,128)(2,1)}, bf16[512,512]{1,0:T(8,128)(2,1)}, ...) | async-done | bytes 9437200 | tf_op jit(solution)/shard_map/psum | solution.py:350
  1777.4 6.8 convert_element_type.223
  (341 shorter events, 275.1 us)
Async XLA Ops:
  7.2 44.6 %copy-start.59 = (s32[16]{0:T(128)S(1)}, s32[16]{0:T(128)}, u32[]{:S(2)}) copy-start(s32[16]{0:T(128)} %param.20) | copy-start | bytes 196
  7.2 44.9 %copy-start.57 = (s32[1,1024]{1,0:T(1,128)S(1)}, s32[1,1024]{1,0:T(1,128)}, u32[]{:S(2)}) copy-start(s32[1,1024]{1,0:T(1,128)} %param.21) | copy-start | bytes 12292
  7.2 73.6 %all-gather.8.cloned.1.call-start = ((), (), s32[]{:S(2)}) async-start(), calls=%async_computation.18 | async-start | bytes 2621440 | tf_op jit(solution)/shard_map/all_gather | solution.py:134
  13.5 34.9 %all-to-all-start.3 = ((bf16[512,4,128]{0,2,1:T(8,128)(2,1)}), bf16[512,4,128]{0,2,1:T(8,128)(2,1)S(1)}, u32[]{:S(2)}, u32[]{:S(2)}) async-start(bf16[512,4,128]{0,2,1:T(8,128)(2,1)} %bitcast.13), calls=%async_computation.3 | async-start | bytes 1048576 | tf_op jit(solution)/shard_map/all_to_all | solution.py:137
  48.3 28.3 %all-to-all-start = ((bf16[512,4,128]{0,2,1:T(8,128)(2,1)}), bf16[512,4,128]{0,2,1:T(8,128)(2,1)S(1)}, u32[]{:S(2)}, u32[]{:S(2)}) async-start(bf16[512,4,128]{0,2,1:T(8,128)(2,1)} %bitcast.1), calls=%async_computation | async-start | bytes 1048576 | tf_op jit(solution)/shard_map/all_to_all | solution.py:138
  52.3 184.5 %copy-start.32 = (f32[128,64]{0,1:T(8,128)}, f32[128,64]{0,1:T(8,128)S(1)}, u32[]{:S(2)}) copy-start(f32[128,64]{0,1:T(8,128)S(1)} %get-tuple-element.55) | copy-start | bytes 98308
  52.3 184.5 %copy-start.34 = (f32[128,64]{0,1:T(8,128)}, f32[128,64]{0,1:T(8,128)S(1)}, u32[]{:S(2)}) copy-start(f32[128,64]{0,1:T(8,128)S(1)} %get-tuple-element.56) | copy-start | bytes 98308
  77.3 8.8 all-to-all-start.2
  80.8 13.5 copy-start.51
  87.3 19.1 %all-to-all-start.1 = ((bf16[8,4,128,128]{2,3,1,0:T(8,128)(2,1)}), bf16[8,4,128,128]{2,3,1,0:T(8,128)(2,1)S(1)}, u32[]{:S(2)}, u32[]{:S(2)}) async-start(bf16[8,4,128,128]{2,3,1,0:T(8,128)(2,1)} %broadcast_in_dim.74), calls=%async_computation.1 | async-start | bytes 2097152 | tf_op jit(solution)/shard_map/all_to_all | solution.py:71
  92.9 26.4 %copy-start.24 = (f32[512,128]{1,0:T(8,128)}, f32[512,128]{1,0:T(8,128)S(1)}, u32[]{:S(2)}) copy-start(f32[512,128]{1,0:T(8,128)S(1)} %get-tuple-element.58) | copy-start | bytes 786436
  106.4 42.5 %copy-start.8 = (bf16[8,4,128,128]{2,3,1,0:T(8,128)(2,1)}, bf16[8,4,128,128]{2,3,1,0:T(8,128)(2,1)S(1)}, u32[]{:S(2)}) copy-start(bf16[8,4,128,128]{2,3,1,0:T(8,128)(2,1)S(1)} %all-to-all-done.1) | copy-start | bytes 3145732
  108.7 19.6 %all-to-all-start.4 = ((bf16[8,4,128,128]{3,2,1,0:T(8,128)(2,1)}), bf16[8,4,128,128]{3,2,1,0:T(8,128)(2,1)}, u32[]{:S(2)}, u32[]{:S(2)}) async-start(bf16[8,4,128,128]{3,2,1,0:T(8,128)(2,1)} %broadcast_in_dim.82), calls=%async_computation.4 | async-start | bytes 2097152 | tf_op jit(solution)/shard_map/all_to_all | solution.py:71
  128.3 96.1 %all-to-all-start.5 = ((bf16[512,4,1024]{2,0,1:T(8,128)(2,1)}), bf16[512,4,1024]{2,0,1:T(8,128)(2,1)}, u32[]{:S(2)}, u32[]{:S(2)}) async-start(bf16[512,4,1024]{2,0,1:T(8,128)(2,1)} %copy.188), calls=%async_computation.5 | async-start | bytes 8388608 | tf_op jit(solution)/shard_map/all_to_all | solution.py:135
  133.2 210.4 %reduce-scatter.5.cloned.1.call-start = ((), (), s32[]{:S(2)}) async-start(), calls=%async_computation.19 | async-start | bytes 5242880 | tf_op jit(solution)/shard_map/reduce_scatter | solution.py:184
  266.1 77.5 %copy-start.1 = (f32[1,128,2048]{2,1,0:T(8,128)S(1)}, f32[1,128,2048]{2,1,0:T(8,128)}, u32[]{:S(2)}) copy-start(f32[1,128,2048]{2,1,0:T(8,128)} %param.19) | copy-start | bytes 3145732
  266.1 78.9 %copy-start.44 = (f32[2048]{0:T(1024)S(1)}, f32[2048]{0:T(1024)}, u32[]{:S(2)}) copy-start(f32[2048]{0:T(1024)} %param.30) | copy-start | bytes 24580
  266.1 258.5 %all-gather.12.cloned.1.call-start = ((), (), s32[]{:S(2)}) async-start(), calls=%async_computation.21 | async-start | bytes 7864320 | tf_op jit(solution)/shard_map/all_gather | solution.py:191
  266.9 309.3 %all-gather.10.cloned.1.call-start = ((), (), s32[]{:S(2)}) async-start(), calls=%async_computation.20 | async-start | bytes 7864320 | tf_op jit(solution)/shard_map/all_gather | solution.py:190
  268.1 12.2 all-to-all-start.6
  280.3 64.7 %copy-start.36 = (bf16[4,2,8,512]{3,2,0,1:T(8,128)(2,1)}, bf16[4,2,8,512]{3,2,0,1:T(8,128)(2,1)S(1)}, u32[]{:S(2)}) copy-start(bf16[4,2,8,512]{3,2,0,1:T(8,128)(2,1)S(1)} %copy.256) | copy-start | bytes 196612
  365.1 76.3 %all-to-all-start.9 = ((bf16[8,2,96,2048]{3,2,1,0:T(8,128)(2,1)}), bf16[8,2,96,2048]{3,2,1,0:T(8,128)(2,1)}, u32[]{:S(2)}, u32[]{:S(2)}) async-start(bf16[8,2,96,2048]{3,2,1,0:T(8,128)(2,1)} %bitcast.341), calls=%async_computation.10 | async-start | bytes 12582912 | tf_op jit(solution)/shard_map/all_to_all | solution.py:238
  369.9 321.2 %all-gather.14.cloned.1.call-start = ((), (), s32[]{:S(2)}) async-start(), calls=%async_computation.22 | async-start | bytes 7864320 | tf_op jit(solution)/shard_map/all_gather | solution.py:192
  370.6 70.8 %copy-start.20 = (bf16[128,2048]{1,0:T(8,128)(2,1)}, bf16[128,2048]{1,0:T(8,128)(2,1)S(1)}, u32[]{:S(2)}) copy-start(bf16[128,2048]{1,0:T(8,128)(2,1)S(1)} %multiply_convert_fusion.4) | copy-start | bytes 1572868
  441.5 76.5 %all-to-all-start.7 = ((bf16[8,2,96,2048]{3,2,1,0:T(8,128)(2,1)}), bf16[8,2,96,2048]{3,2,1,0:T(8,128)(2,1)}, u32[]{:S(2)}, u32[]{:S(2)}) async-start(bf16[8,2,96,2048]{3,2,1,0:T(8,128)(2,1)} %bitcast.342), calls=%async_computation.8 | async-start | bytes 12582912 | tf_op jit(solution)/shard_map/all_to_all | solution.py:213
  691.1 13.9 copy-start.58
  730.7 76.6 %all-to-all-start.8 = ((bf16[1,2,768,2048]{3,1,0,2:T(2,128)(2,1)}), bf16[1,2,768,2048]{3,1,0,2:T(2,128)(2,1)}, u32[]{:S(2)}, u32[]{:S(2)}) async-start(bf16[1,2,768,2048]{3,1,0,2:T(2,128)(2,1)} %copy.202), calls=%async_computation.9 | async-start | bytes 12582912 | tf_op jit(solution)/shard_map/all_to_all | solution.py:226
  807.2 76.3 %all-to-all-start.10 = ((bf16[1,2,768,2048]{3,1,0,2:T(2,128)(2,1)}), bf16[1,2,768,2048]{3,1,0,2:T(2,128)(2,1)}, u32[]{:S(2)}, u32[]{:S(2)}) async-start(bf16[1,2,768,2048]{3,1,0,2:T(2,128)(2,1)} %copy.205), calls=%async_computation.11 | async-start | bytes 12582912 | tf_op jit(solution)/shard_map/all_to_all | solution.py:253
  812.0 144.7 %all-gather.16.cloned.1.call-start = ((), (), s32[]{:S(2)}) async-start(), calls=%async_computation.23 | async-start | bytes 2621440 | tf_op jit(solution)/shard_map/all_gather | solution.py:267
  962.1 14.3 slice-start
  962.2 14.3 slice-start.1
  962.2 15.6 slice-start.2
  962.2 16.8 slice-start.3
  1015.5 19.6 %all-to-all-start.11 = ((bf16[4,8,128,128]{2,3,0,1:T(8,128)(2,1)}), bf16[4,8,128,128]{2,3,0,1:T(8,128)(2,1)}, u32[]{:S(2)}, u32[]{:S(2)}) async-start(bf16[4,8,128,128]{2,3,0,1:T(8,128)(2,1)} %copy.213), calls=%async_computation.12 | async-start | bytes 2097152 | tf_op jit(solution)/shard_map/all_to_all | solution.py:77
  1035.1 19.6 %all-to-all-start.12 = ((bf16[4,8,128,128]{2,3,0,1:T(8,128)(2,1)}), bf16[4,8,128,128]{2,3,0,1:T(8,128)(2,1)}, u32[]{:S(2)}, u32[]{:S(2)}) async-start(bf16[4,8,128,128]{2,3,0,1:T(8,128)(2,1)} %copy.218), calls=%async_computation.13 | async-start | bytes 2097152 | tf_op jit(solution)/shard_map/all_to_all | solution.py:77
  1039.4 114.4 %all-gather.18.cloned.1.call-start = ((), (), s32[]{:S(2)}) async-start(), calls=%async_computation.28 | async-start | bytes 6553600 | tf_op jit(solution)/shard_map/all_gather | solution.py:318
  1042.2 14.3 copy-start.25
  1042.2 14.3 copy-start.49
  1042.2 14.3 copy-start.52
  1045.6 12.8 copy-start.21
  1045.7 12.8 copy-start.41
  1058.4 231.1 %all-reduce.5.cloned.1.call-start = ((), (), s32[]{:S(2)}) async-start(), calls=%async_computation.24 | async-start | bytes 262144 | tf_op jit(solution)/shard_map/psum | solution.py:355
  1059.4 342.3 %reduce-scatter.11.cloned.1.call-start = ((), (), s32[]{:S(2)}) async-start(), calls=%async_computation.27 | async-start | bytes 7864320 | tf_op jit(solution)/shard_map/reduce_scatter | solution.py:345
  1069.1 446.6 %reduce-scatter.9.cloned.1.call-start = ((), (), s32[]{:S(2)}) async-start(), calls=%async_computation.26 | async-start | bytes 7864320 | tf_op jit(solution)/shard_map/reduce_scatter | solution.py:342
  1082.7 547.2 %reduce-scatter.7.cloned.1.call-start = ((), (), s32[]{:S(2)}) async-start(), calls=%async_computation.25 | async-start | bytes 7864320 | tf_op jit(solution)/shard_map/reduce_scatter | solution.py:339
  1096.2 676.9 %all-reduce.7.cloned.1.call-start = ((), (), s32[]{:S(2)}) async-start(), calls=%async_computation.29 | async-start | bytes 18874368 | tf_op jit(solution)/shard_map/psum | solution.py:350
  1184.5 448.7 %all-to-all-start.13 = ((f32[4,128,512]{2,1,0:T(8,128)}), f32[4,128,512]{2,1,0:T(8,128)S(1)}, u32[]{:S(2)}, u32[]{:S(2)}) async-start(f32[4,128,512]{2,1,0:T(8,128)} %bitcast.104), calls=%async_computation.14 | async-start | bytes 2097152 | tf_op jit(solution)/shard_map/all_to_all | solution.py:333
  1519.0 114.5 %copy-start.54 = (f32[128]{0:T(128)S(1)}, f32[128]{0:T(128)}, u32[]{:S(2)}) copy-start(f32[128]{0:T(128)} %copy-done.53) | copy-start | bytes 1540
  (48 other events, 225.2 us)
Sparse Core Ops, SparseCore 0:
  11.5 68.1 all-gather.7
  266.2 77.3 reduce-scatter.4
  345.2 115.9 all-gather.11
  462.6 113.5 all-gather.9
  577.5 113.5 all-gather.13
  914.6 42.0 all-gather.15
  1058.5 95.1 all-gather.17
  1159.3 130.1 all-reduce.4
  1291.8 109.8 reduce-scatter.10
  1404.4 111.2 reduce-scatter.8
  1518.6 111.2 reduce-scatter.6
  1633.7 139.3 all-reduce.6

commit v3 on v2

--- a/solution.py
+++ b/solution.py
@@ -131,7 +131,7 @@
     first_scale = rms_scale(hidden)
     first_normed = hidden * first_scale
     first_input = (first_normed * attn_gain).astype(jnp.bfloat16)
-    group_input = lax.all_gather(first_input, "fsdp", axis=0, tiled=True)
+    group_input = gather_a2a(first_input, "fsdp", fsdp_size, 0)
     w_query_cols = lax.all_to_all(query_proj, "fsdp", 1, 0, tiled=True)
     if share == 1:
         w_key_cols = lax.all_to_all(key_proj, "fsdp", 1, 0, tiled=True)
@@ -181,7 +181,7 @@
         .reshape(group_rows, heads_dev * HEAD_DIM)
     )
     branch_parts = matmul(attended, out_proj).reshape(seqs, tokens, D)
-    branch = lax.psum_scatter(branch_parts, "fsdp", scatter_dimension=0, tiled=True)[0]
+    branch = scatter_sum_a2a(branch_parts, "fsdp", fsdp_size, 0)[0]
     middle = hidden + branch
     second_scale = rms_scale(middle)
     second_normed = middle * second_scale
@@ -264,7 +264,7 @@
     grad_middle, ffn_gain_grad = norm_back(grad_second, second_normed, second_scale, ffn_gain)
     grad_middle = grad_middle + grad_out
 
-    grad_branch = lax.all_gather(grad_middle.astype(jnp.bfloat16), "fsdp", axis=0, tiled=True)
+    grad_branch = gather_a2a(grad_middle.astype(jnp.bfloat16), "fsdp", fsdp_size, 0)
     out_grad_part = contract("tq,td->qd", attended, grad_branch)
     grad_attended = contract("td,qd->tq", grad_branch, out_proj).astype(jnp.bfloat16)
     grad_groups = grad_attended.reshape(seqs, tokens, kv_dev, group_dev, HEAD_DIM)
@@ -315,8 +315,8 @@
         return whole
 
     q_width, kv_width = heads_dev * HEAD_DIM, kv_dev * HEAD_DIM
-    joined = lax.all_gather(
-        jnp.concatenate([grad_query, grad_key, grad_value], axis=1), "fsdp", axis=1, tiled=False
+    joined = gather_a2a(
+        jnp.concatenate([grad_query, grad_key, grad_value], axis=1)[:, None], "fsdp", fsdp_size, 1
     )
     query_all = joined[:, :, :q_width].reshape(group_rows, -1)
     key_all = gather_heads(joined[:, :, q_width : q_width + kv_width])
@@ -346,17 +346,17 @@
             down_grad_full.astype(jnp.bfloat16), "fsdp", scatter_dimension=1, tiled=True
         ).astype(jnp.float32),
     )
-    query_grad, key_grad, value_grad, out_grad = (
+    router_shard = scatter_sum_a2a(router_grad_full, "fsdp", fsdp_size, 0)
+    query_grad, key_grad, value_grad, out_grad, router_grad = (
         lax.psum(query_grad_part.astype(jnp.bfloat16), "ctx").astype(jnp.float32),
         lax.psum(key_grad_part.astype(jnp.bfloat16), "ctx").astype(jnp.float32),
         lax.psum(value_grad_part.astype(jnp.bfloat16), "ctx").astype(jnp.float32),
         lax.psum(out_grad_part.astype(jnp.bfloat16), "ctx").astype(jnp.float32),
-    )
-    attn_gain_total, query_gain_total, key_gain_total, ffn_gain_total, router_total = lax.psum(
-        (attn_gain_grad, query_gain_grad, key_gain_grad, ffn_gain_grad, router_grad_full),
-        ("ctx", "fsdp"),
-    )
-    router_grad = lax.dynamic_slice_in_dim(router_total, fsdp_index * d_part, d_part, 0)
+        jnp.sum(gather_a2a(router_shard[None], "ctx", ctx_size, 0), axis=0),
+    )
+    attn_gain_total, query_gain_total, key_gain_total, ffn_gain_total = lax.psum(
+        (attn_gain_grad, query_gain_grad, key_gain_grad, ffn_gain_grad), ("ctx", "fsdp")
+    )
     return (
         layer_out[None],
         grad_hidden[None],

time: 1800 us -> 1520 us (0.84)
  waiting for transfers between devices: 1180 us -> 860 us
  starting transfers between devices: 61.8 us -> 85.4 us
    all_to_all x4 -> x8, waiting for transfers between devices: 16.9 us -> 240 us  [gather_a2a(): lax.all_to_all(rep, axis_name, 0, 0, tiled=True)]
    all_to_all x2 -> x3, waiting for transfers between devices: 16.8 us -> 189 us  [scatter_sum_a2a(): got = lax.all_to_all(parts, axis_name, axis, axis, tiled=True)]
    reduce_scatter x1, waiting for transfers between devices: 111 us -> 0.01 us  [per_device(): lax.psum_scatter(gate_grad_full.astype(jnp.bfloat16), 'fsdp', scatter_dim...]
    reduce_scatter x1, waiting for transfers between devices: 111 us -> 0.01 us  [per_device(): lax.psum_scatter(down_grad_full.astype(jnp.bfloat16), 'fsdp', scatter_dim...]
    reduce_scatter x1, waiting for transfers between devices: 111 us -> 0.01 us  [per_device(): lax.psum_scatter(up_grad_full.astype(jnp.bfloat16), 'fsdp', scatter_dimen...]
    all_gather x1, waiting for transfers between devices: 105 us -> 0.01 us  [per_device(): lax.all_gather(expert_down, 'fsdp', axis=1, tiled=True)]
    psum x1 -> x0, waiting for transfers between devices: 99.9 us -> none  [per_device(): lax.psum((attn_gain_grad, query_gain_grad, key_gain_grad, ffn_gain_grad,...]
    all_to_all x1, waiting for transfers between devices: 72.3 us -> 167 us  [per_device(): w_query_cols = lax.all_to_all(query_proj, 'fsdp', 1, 0, tiled=True)]
  transfers between devices with their start and end apart: 26 -> 26, of which waited for: 23 -> 19; matrix products, arithmetic and copies ran while one was open for 16% -> 30% of each run, Pallas kernels for 0% -> 0%
where the time goes in v3:
time: 1520 us; the launch traced here: 1510 us
  waiting for transfers between devices  860 us (57%)
  local copies, waits for them, and re-layouts  211 us (14%)
  matrix products  189 us (12%)
  other arithmetic  98.5 us (6%)
  starting transfers between devices  85.4 us (6%)
  blocking collectives  47.6 us (3%)
  between operations  15.6 us (1%)
    all_to_all x8, waiting for transfers between devices, gather_a2a(): lax.all_to_all(rep, axis_name, 0, 0, tiled=True)  240 us
    all_to_all x3, waiting for transfers between devices, scatter_sum_a2a(): got = lax.all_to_all(parts, axis_name, axis, axis, tiled=True)  189 us
    dot_general x25, matrix products, contract(): return jnp.einsum(form, left, right, preferred_element_type=jnp.float32)  170 us
    all_to_all x1, waiting for transfers between devices, per_device(): w_query_cols = lax.all_to_all(query_proj, 'fsdp', 1, 0, tiled=True)  167 us
    all_to_all x1, waiting for transfers between devices, per_device(): lax.all_to_all(dispatch(grad_routes), 'ctx', split_axis=0, concat_axis=2,...  64.9 us
    all_to_all x1, waiting for transfers between devices, per_device(): lax.all_to_all(dispatch(jnp.repeat(second_input, TOP, axis=0)), 'ctx', sp...  51.2 us
    psum x1, waiting for transfers between devices, per_device(): lax.psum(query_grad_part.astype(jnp.bfloat16), 'ctx').astype(jnp.float32)  43.9 us
    all_to_all x1, waiting for transfers between devices, per_device(): lax.all_to_all(grad_rows[None], 'ctx', split_axis=2, concat_axis=0, tiled...  43.9 us
  transfers between devices with their start and end apart: 26, of which 19 were waited for; matrix products, arithmetic and copies ran while one was open for 30% of the time, Pallas kernels for 0%

profile of v3, /device:TPU:0, one launch (start us, length us, event | category | flops | bytes accessed | tf_op | source)
XLA Modules:
  0.0 1507.2 jit_solution(1178998891978333765)
XLA Ops:
  18.4 11.6 all-to-all-done.4
  37.1 45.9 %all-to-all-done = bf16[4,128,2048]{2,1,0:T(8,128)(2,1)S(1)} async-done(((bf16[4,128,2048]{2,1,0:T(8,128)(2,1)}), bf16[4,128,2048]{2,1,0:T(8,128)(2,1)S(1)}, u32[]{:S(2)}, u32[]{:S(2)}) %all-to-all-start) | async-done | bytes 2097184 | tf_op jit(solution)/shard_map/all_to_all | solution.py:71
  96.9 12.0 all-to-all-done.1
  119.3 9.9 all-to-all-done.5
  134.0 6.4 copy.201
  174.0 167.2 %all-to-all-done.6 = bf16[512,4,1024]{2,0,1:T(8,128)(2,1)} async-done(((bf16[512,4,1024]{2,0,1:T(8,128)(2,1)}), bf16[512,4,1024]{2,0,1:T(8,128)(2,1)}, u32[]{:S(2)}, u32[]{:S(2)}) %all-to-all-start.6) | async-done | bytes 4194336 | tf_op jit(solution)/shard_map/all_to_all | solution.py:135
  341.1 6.4 copy.203
  354.0 7.1 fusion.89
  361.1 8.4 fusion.3
  369.6 7.8 fusion.32
  394.1 180.1 %all-to-all-done.7 = f32[4,1,128,2048]{3,2,1,0:T(8,128)} async-done(((f32[4,1,128,2048]{3,2,1,0:T(8,128)}), f32[4,1,128,2048]{3,2,1,0:T(8,128)}, u32[]{:S(2)}, u32[]{:S(2)}) %all-to-all-start.7) | async-done | bytes 4194336 | tf_op jit(solution)/shard_map/all_to_all | solution.py:77
  582.1 10.2 scatter_custom_fusion
  599.0 7.0 gather_fusion.2
  606.8 10.7 scatter_custom_fusion.1
  617.5 51.2 %all-to-all-done.9 = bf16[8,2,96,2048]{3,2,1,0:T(8,128)(2,1)} async-done(((bf16[8,2,96,2048]{3,2,1,0:T(8,128)(2,1)}), bf16[8,2,96,2048]{3,2,1,0:T(8,128)(2,1)}, u32[]{:S(2)}, u32[]{:S(2)}) %all-to-all-start.9) | async-done | bytes 6291488 | tf_op jit(solution)/shard_map/all_to_all | solution.py:213
  673.5 6.6 copy.216
  680.1 64.9 %all-to-all-done.11 = bf16[8,2,96,2048]{3,2,1,0:T(8,128)(2,1)} async-done(((bf16[8,2,96,2048]{3,2,1,0:T(8,128)(2,1)}), bf16[8,2,96,2048]{3,2,1,0:T(8,128)(2,1)}, u32[]{:S(2)}, u32[]{:S(2)}) %all-to-all-start.11) | async-done | bytes 6291488 | tf_op jit(solution)/shard_map/all_to_all | solution.py:238
  745.0 6.6 copy.219
  751.6 10.5 fusion.91
  762.2 10.5 fusion.90
  772.7 13.5 multiply_convert_fusion
  787.6 7.0 convolution_convert_fusion.1
  794.6 7.9 convert_bitcast_fusion
  802.5 19.0 %copy.217 = bf16[1,2,768,2048]{3,1,0,2:T(2,128)(2,1)} copy(bf16[1,2,768,2048]{3,2,1,0:T(8,128)(2,1)S(1)} %convert_bitcast_fusion) | data formatting | bytes 12582912 | tf_op jit(solution)/shard_map/broadcast_in_dim | solution.py:226
  826.3 9.6 convolution_convert_fusion.2
  836.0 10.8 fusion.92
  846.8 9.9 fusion.10
  856.7 18.8 %copy.220 = bf16[1,2,768,2048]{3,1,0,2:T(2,128)(2,1)} copy(bf16[1,2,768,2048]{3,2,1,0:T(8,128)(2,1)S(1)} %fusion.10) | data formatting | bytes 12582912 | tf_op jit(solution)/shard_map/broadcast_in_dim | solution.py:253
  875.5 22.3 %all-to-all-done.10 = bf16[1,2,768,2048]{3,1,0,2:T(2,128)(2,1)} async-done(((bf16[1,2,768,2048]{3,1,0,2:T(2,128)(2,1)}), bf16[1,2,768,2048]{3,1,0,2:T(2,128)(2,1)}, u32[]{:S(2)}, u32[]{:S(2)}) %all-to-all-start.10) | async-done | bytes 6291488 | tf_op jit(solution)/shard_map/all_to_all | solution.py:226
  903.0 8.5 copy.218
  911.6 13.0 gather_fusion.3
  930.7 43.9 %all-to-all-done.12 = bf16[1,2,768,2048]{3,1,0,2:T(2,128)(2,1)} async-done(((bf16[1,2,768,2048]{3,1,0,2:T(2,128)(2,1)}), bf16[1,2,768,2048]{3,1,0,2:T(2,128)(2,1)}, u32[]{:S(2)}, u32[]{:S(2)}) %all-to-all-start.12) | async-done | bytes 6291488 | tf_op jit(solution)/shard_map/all_to_all | solution.py:253
  974.6 8.4 copy.221
  982.9 12.6 gather_fusion.4
  995.6 6.8 convert_reduce_fusion
  1015.8 9.6 convolution_convert_fusion.3
  1025.5 69.3 %all-to-all-done.13 = bf16[4,128,2048]{2,1,0:T(8,128)(2,1)} async-done(((bf16[4,128,2048]{2,1,0:T(8,128)(2,1)}), bf16[4,128,2048]{2,1,0:T(8,128)(2,1)}, u32[]{:S(2)}, u32[]{:S(2)}) %all-to-all-start.13) | async-done | bytes 2097184 | tf_op jit(solution)/shard_map/all_to_all | solution.py:71
  1101.3 16.8 %fusion = (f32[4,8,128]{2,1,0:T(8,128)}, f32[4,1024,128,8]{2,1,3,0:T(8,128)}) fusion(f32[4,1,8,128,1024]{3,4,2,0,1:T(8,128)} %get-tuple-element.62, f32[4,8,128]{2,1,0:T(8,128)} %log_add_fusion, bf16[4,1024,128,1]{2,1,3,0:T(8,128)(2,1)} %bitcast.389, bf16[4,128,8,128]{3,2,1,0:T(8,128)(2,1)} %bitcast.382), kind=kOutput, calls=%fused_computation.10 | convolution fusion | flops 1086320640 | bytes 35684352 | tf_op jit(solution)/shard_map/stkgd,sjkd->skgtj/dot_general | solution.py:23
  1118.0 13.0 fusion.6
  1131.1 12.6 copy.232
  1182.9 6.9 all-to-all-done.14
  1207.5 106.1 %all-to-all-done.16 = bf16[4,512,1,1280]{3,1,2,0:T(8,128)(2,1)} async-done(((bf16[4,512,1,1280]{3,1,2,0:T(8,128)(2,1)}), bf16[4,512,1,1280]{3,1,2,0:T(8,128)(2,1)}, u32[]{:S(2)}, u32[]{:S(2)}) %all-to-all-start.16) | async-done | bytes 5242912 | tf_op jit(solution)/shard_map/all_to_all | solution.py:71
  1335.6 6.6 convolution_convert_fusion
  1343.5 8.5 all_to_all.192
  1383.8 12.5 all-to-all-done.17
  1399.1 39.1 %all-reduce = (f32[2048]{0:T(1024)}, f32[128]{0:T(128)}, f32[128]{0:T(128)}, f32[2048]{0:T(1024)}) all-reduce(f32[2048]{0:T(1024)S(1)} %bitcast.444, f32[128]{0:T(128)S(1)} %copy-done.63, f32[128]{0:T(128)S(1)} %copy-done.64, f32[2048]{0:T(1024)S(1)} %copy-done.50), channel_id=1, replica_groups=mesh['ctx'=8,'fsdp'=4] {'ctx','fsdp'}, use_global_device_ids=true, to_apply=%region_24.26 | all-reduce | flops 4352 | bytes 34816 | tf_op jit(solution)/shard_map/psum | solution.py:357
  1440.7 43.9 %all-reduce.4.cloned.1.call-done = (bf16[512,4096]{1,0:T(8,128)(2,1)}, bf16[512,512]{1,0:T(8,128)(2,1)}, bf16[512,512]{1,0:T(8,128)(2,1)}, bf16[1024,2048]{1,0:T(8,128)(2,1)}) async-done(((bf16[512,4096]{1,0:T(8,128)(2,1)}, bf16[512,512]{1,0:T(8,128)(2,1)}, bf16[512,512]{1,0:T(8,128)(2,1)}, bf16[1024,2048]{1,0:T(8,128)(2,1)}), (bf16[512,4096]{1,0:T(8,128)(2,1)}, bf16[512,512]{1,0:T(8,128)(2,1)}, ...) | async-done | bytes 9437200 | tf_op jit(solution)/shard_map/psum | solution.py:351
  1488.9 6.8 convert_element_type.224
  (356 shorter events, 286.7 us)
Async XLA Ops:
  9.2 20.8 %all-to-all-start.4 = ((bf16[512,4,128]{0,2,1:T(8,128)(2,1)}), bf16[512,4,128]{0,2,1:T(8,128)(2,1)S(1)}, u32[]{:S(2)}, u32[]{:S(2)}) async-start(bf16[512,4,128]{0,2,1:T(8,128)(2,1)} %bitcast.15), calls=%async_computation.4 | async-start | bytes 1048576 | tf_op jit(solution)/shard_map/all_to_all | solution.py:137
  17.0 18.3 %copy-start.65 = (s32[16]{0:T(128)S(1)}, s32[16]{0:T(128)}, u32[]{:S(2)}) copy-start(s32[16]{0:T(128)} %param.20) | copy-start | bytes 196
  17.0 18.6 %copy-start.62 = (s32[1,1024]{1,0:T(1,128)S(1)}, s32[1,1024]{1,0:T(1,128)}, u32[]{:S(2)}) copy-start(s32[1,1024]{1,0:T(1,128)} %param.21) | copy-start | bytes 12292
  17.0 18.6 %copy-start.32 = (bf16[512,512]{1,0:T(8,128)(2,1)S(1)}, bf16[512,512]{1,0:T(8,128)(2,1)}, u32[]{:S(2)}) copy-start(bf16[512,512]{1,0:T(8,128)(2,1)} %param.26) | copy-start | bytes 1572868
  31.7 51.3 %all-to-all-start = ((bf16[4,128,2048]{2,1,0:T(8,128)(2,1)}), bf16[4,128,2048]{2,1,0:T(8,128)(2,1)S(1)}, u32[]{:S(2)}, u32[]{:S(2)}) async-start(bf16[4,128,2048]{2,1,0:T(8,128)(2,1)} %broadcast_in_dim.84), calls=%async_computation | async-start | bytes 4194304 | tf_op jit(solution)/shard_map/all_to_all | solution.py:71
  35.3 61.3 %copy-start.56 = (f32[128]{0:T(128)S(1)}, f32[128]{0:T(128)}, u32[]{:S(2)}) copy-start(f32[128]{0:T(128)} %param.28) | copy-start | bytes 1540
  36.8 316.8 %copy-start.34 = (f32[128,64]{0,1:T(8,128)}, f32[128,64]{0,1:T(8,128)S(1)}, u32[]{:S(2)}) copy-start(f32[128,64]{0,1:T(8,128)S(1)} %get-tuple-element.55) | copy-start | bytes 98308
  36.8 316.8 %copy-start.36 = (f32[128,64]{0,1:T(8,128)}, f32[128,64]{0,1:T(8,128)S(1)}, u32[]{:S(2)}) copy-start(f32[128,64]{0,1:T(8,128)S(1)} %get-tuple-element.56) | copy-start | bytes 98308
  83.0 264.5 %copy-start.4 = (bf16[4,128,2048]{2,1,0:T(8,128)(2,1)}, bf16[4,128,2048]{2,1,0:T(8,128)(2,1)S(1)}, u32[]{:S(2)}) copy-start(bf16[4,128,2048]{2,1,0:T(8,128)(2,1)S(1)} %all-to-all-done) | copy-start | bytes 6291460
  83.7 8.8 all-to-all-start.3
  87.7 30.5 %copy-start.24 = (f32[512,128]{1,0:T(8,128)}, f32[512,128]{1,0:T(8,128)S(1)}, u32[]{:S(2)}) copy-start(f32[512,128]{1,0:T(8,128)S(1)} %get-tuple-element.58) | copy-start | bytes 786436
  92.5 16.3 %all-to-all-start.1 = ((bf16[512,4,128]{0,2,1:T(8,128)(2,1)}), bf16[512,4,128]{0,2,1:T(8,128)(2,1)S(1)}, u32[]{:S(2)}, u32[]{:S(2)}) async-start(bf16[512,4,128]{0,2,1:T(8,128)(2,1)} %bitcast.3), calls=%async_computation.1 | async-start | bytes 1048576 | tf_op jit(solution)/shard_map/all_to_all | solution.py:138
  110.1 19.1 %all-to-all-start.5 = ((bf16[8,4,128,128]{3,2,1,0:T(8,128)(2,1)}), bf16[8,4,128,128]{3,2,1,0:T(8,128)(2,1)S(1)}, u32[]{:S(2)}, u32[]{:S(2)}) async-start(bf16[8,4,128,128]{3,2,1,0:T(8,128)(2,1)} %broadcast_in_dim.94), calls=%async_computation.5 | async-start | bytes 2097152 | tf_op jit(solution)/shard_map/all_to_all | solution.py:71
  130.5 18.9 %all-to-all-start.2 = ((bf16[8,4,128,128]{2,3,1,0:T(8,128)(2,1)}), bf16[8,4,128,128]{2,3,1,0:T(8,128)(2,1)S(1)}, u32[]{:S(2)}, u32[]{:S(2)}) async-start(bf16[8,4,128,128]{2,3,1,0:T(8,128)(2,1)} %broadcast_in_dim.86), calls=%async_computation.2 | async-start | bytes 2097152 | tf_op jit(solution)/shard_map/all_to_all | solution.py:71
  149.4 21.4 %copy-start.9 = (bf16[8,4,128,128]{2,3,1,0:T(8,128)(2,1)}, bf16[8,4,128,128]{2,3,1,0:T(8,128)(2,1)S(1)}, u32[]{:S(2)}) copy-start(bf16[8,4,128,128]{2,3,1,0:T(8,128)(2,1)S(1)} %all-to-all-done.2) | copy-start | bytes 3145732
  149.4 191.7 %all-to-all-start.6 = ((bf16[512,4,1024]{2,0,1:T(8,128)(2,1)}), bf16[512,4,1024]{2,0,1:T(8,128)(2,1)}, u32[]{:S(2)}, u32[]{:S(2)}) async-start(bf16[512,4,1024]{2,0,1:T(8,128)(2,1)} %copy.202), calls=%async_computation.6 | async-start | bytes 8388608 | tf_op jit(solution)/shard_map/all_to_all | solution.py:135
  154.3 597.4 %all-gather.6.cloned.1.call-start = ((), (), s32[]{:S(2)}) async-start(), calls=%async_computation.24 | async-start | bytes 7864320 | tf_op jit(solution)/shard_map/all_gather | solution.py:191
  382.8 191.3 %copy-start.52 = (bf16[512,16]{0,1:T(8,128)(2,1)S(1)}, bf16[512,16]{0,1:T(8,128)(2,1)}, u32[]{:S(2)}) copy-start(bf16[512,16]{0,1:T(8,128)(2,1)} %param.31) | copy-start | bytes 49156
  382.8 191.3 %all-to-all-start.7 = ((f32[4,1,128,2048]{3,2,1,0:T(8,128)}), f32[4,1,128,2048]{3,2,1,0:T(8,128)}, u32[]{:S(2)}, u32[]{:S(2)}) async-start(f32[4,1,128,2048]{3,2,1,0:T(8,128)} %fusion.23), calls=%async_computation.7 | async-start | bytes 8388608 | tf_op jit(solution)/shard_map/all_to_all | solution.py:77
  387.8 192.9 %copy-start = (f32[1,128,2048]{2,1,0:T(8,128)S(1)}, f32[1,128,2048]{2,1,0:T(8,128)}, u32[]{:S(2)}) copy-start(f32[1,128,2048]{2,1,0:T(8,128)} %param.19) | copy-start | bytes 3145732
  387.8 374.3 %all-gather.4.cloned.1.call-start = ((), (), s32[]{:S(2)}) async-start(), calls=%async_computation.23 | async-start | bytes 7864320 | tf_op jit(solution)/shard_map/all_gather | solution.py:190
  574.8 17.6 %all-to-all-start.8 = ((bf16[4,512,16]{1,2,0:T(8,128)(2,1)}), bf16[4,512,16]{1,2,0:T(8,128)(2,1)S(1)}, u32[]{:S(2)}, u32[]{:S(2)}) async-start(bf16[4,512,16]{1,2,0:T(8,128)(2,1)} %broadcast_in_dim.96), calls=%async_computation.8 | async-start | bytes 131072 | tf_op jit(solution)/shard_map/all_to_all | solution.py:71
  581.0 17.1 %copy-start.53 = (f32[128]{0:T(128)}, f32[128]{0:T(128)S(1)}, u32[]{:S(2)}) copy-start(f32[128]{0:T(128)S(1)} %add_rsqrt_fusion.2) | copy-start | bytes 1540
  592.3 76.4 %all-to-all-start.9 = ((bf16[8,2,96,2048]{3,2,1,0:T(8,128)(2,1)}), bf16[8,2,96,2048]{3,2,1,0:T(8,128)(2,1)}, u32[]{:S(2)}, u32[]{:S(2)}) async-start(bf16[8,2,96,2048]{3,2,1,0:T(8,128)(2,1)} %bitcast.379), calls=%async_computation.9 | async-start | bytes 12582912 | tf_op jit(solution)/shard_map/all_to_all | solution.py:213
  597.1 175.6 %all-gather.8.cloned.1.call-start = ((), (), s32[]{:S(2)}) async-start(), calls=%async_computation.25 | async-start | bytes 7864320 | tf_op jit(solution)/shard_map/all_gather | solution.py:192
  668.7 76.3 %all-to-all-start.11 = ((bf16[8,2,96,2048]{3,2,1,0:T(8,128)(2,1)}), bf16[8,2,96,2048]{3,2,1,0:T(8,128)(2,1)}, u32[]{:S(2)}, u32[]{:S(2)}) async-start(bf16[8,2,96,2048]{3,2,1,0:T(8,128)(2,1)} %bitcast.380), calls=%async_computation.11 | async-start | bytes 12582912 | tf_op jit(solution)/shard_map/all_to_all | solution.py:238
  673.4 700.1 %reduce-scatter.8.cloned.1.call-start = ((), (), s32[]{:S(2)}) async-start(), calls=%async_computation.28 | async-start | bytes 7864320 | tf_op jit(solution)/shard_map/reduce_scatter | solution.py:345
  762.2 25.4 %slice-start.4 = ((s8[6291456]{0:T(1024)(128)(4,1)}), s8[2097152]{0:T(1024)(128)(4,1)S(1)}, s32[]{:S(2)}) async-start(s8[6291456]{0:T(1024)(128)(4,1)} %bitcast.395), calls=%async_computation.34 | async-start | bytes 4194304
  821.5 76.3 %all-to-all-start.10 = ((bf16[1,2,768,2048]{3,1,0,2:T(2,128)(2,1)}), bf16[1,2,768,2048]{3,1,0,2:T(2,128)(2,1)}, u32[]{:S(2)}, u32[]{:S(2)}) async-start(bf16[1,2,768,2048]{3,1,0,2:T(2,128)(2,1)} %copy.217), calls=%async_computation.10 | async-start | bytes 12582912 | tf_op jit(solution)/shard_map/all_to_all | solution.py:226
  826.2 550.9 %reduce-scatter.6.cloned.1.call-start = ((), (), s32[]{:S(2)}) async-start(), calls=%async_computation.27 | async-start | bytes 7864320 | tf_op jit(solution)/shard_map/reduce_scatter | solution.py:342
  897.8 76.7 %all-to-all-start.12 = ((bf16[1,2,768,2048]{3,1,0,2:T(2,128)(2,1)}), bf16[1,2,768,2048]{3,1,0,2:T(2,128)(2,1)}, u32[]{:S(2)}, u32[]{:S(2)}) async-start(bf16[1,2,768,2048]{3,1,0,2:T(2,128)(2,1)} %copy.220), calls=%async_computation.12 | async-start | bytes 12582912 | tf_op jit(solution)/shard_map/all_to_all | solution.py:253
  982.9 19.4 %copy-start.39 = (bf16[4,2,8,512]{3,2,0,1:T(8,128)(2,1)S(1)}, bf16[4,2,8,512]{3,2,0,1:T(8,128)(2,1)}, u32[]{:S(2)}) copy-start(bf16[4,2,8,512]{3,2,0,1:T(8,128)(2,1)} %copy-done.38) | copy-start | bytes 196612
  982.9 19.5 %copy-start.43 = (f32[2048]{0:T(1024)S(1)}, f32[2048]{0:T(1024)}, u32[]{:S(2)}) copy-start(f32[2048]{0:T(1024)} %param.30) | copy-start | bytes 24580
  1008.6 86.2 %all-to-all-start.13 = ((bf16[4,128,2048]{2,1,0:T(8,128)(2,1)}), bf16[4,128,2048]{2,1,0:T(8,128)(2,1)}, u32[]{:S(2)}, u32[]{:S(2)}) async-start(bf16[4,128,2048]{2,1,0:T(8,128)(2,1)} %broadcast_in_dim.174), calls=%async_computation.13 | async-start | bytes 4194304 | tf_op jit(solution)/shard_map/all_to_all | solution.py:71
  1013.6 366.8 %reduce-scatter.4.cloned.1.call-start = ((), (), s32[]{:S(2)}) async-start(), calls=%async_computation.26 | async-start | bytes 7864320 | tf_op jit(solution)/shard_map/reduce_scatter | solution.py:339
  1101.2 16.8 %slice-start = ((s8[16777216]{0:T(1024)(128)(4,1)}), s8[4194304]{0:T(1024)(128)(4,1)S(1)}, s32[]{:S(2)}) async-start(s8[16777216]{0:T(1024)(128)(4,1)} %bitcast.370), calls=%async_computation.30 | async-start | bytes 8388608
  1101.3 16.8 %slice-start.1 = ((s8[16777216]{0:T(1024)(128)(4,1)}), s8[4194304]{0:T(1024)(128)(4,1)S(1)}, s32[]{:S(2)}) async-start(s8[16777216]{0:T(1024)(128)(4,1)} %bitcast.370), calls=%async_computation.31 | async-start | bytes 8388608
  1101.3 16.8 %slice-start.2 = ((s8[16777216]{0:T(1024)(128)(4,1)}), s8[4194304]{0:T(1024)(128)(4,1)S(1)}, s32[]{:S(2)}) async-start(s8[16777216]{0:T(1024)(128)(4,1)} %bitcast.370), calls=%async_computation.32 | async-start | bytes 8388608
  1101.3 16.8 %slice-start.3 = ((s8[16777216]{0:T(1024)(128)(4,1)}), s8[4194304]{0:T(1024)(128)(4,1)S(1)}, s32[]{:S(2)}) async-start(s8[16777216]{0:T(1024)(128)(4,1)} %bitcast.370), calls=%async_computation.33 | async-start | bytes 8388608
  1150.1 20.1 %all-to-all-start.15 = ((bf16[4,8,128,128]{2,3,0,1:T(8,128)(2,1)}), bf16[4,8,128,128]{2,3,0,1:T(8,128)(2,1)}, u32[]{:S(2)}, u32[]{:S(2)}) async-start(bf16[4,8,128,128]{2,3,0,1:T(8,128)(2,1)} %copy.233), calls=%async_computation.15 | async-start | bytes 2097152 | tf_op jit(solution)/shard_map/all_to_all | solution.py:77
  1170.1 19.7 %all-to-all-start.14 = ((bf16[4,8,128,128]{2,3,0,1:T(8,128)(2,1)}), bf16[4,8,128,128]{2,3,0,1:T(8,128)(2,1)}, u32[]{:S(2)}, u32[]{:S(2)}) async-start(bf16[4,8,128,128]{2,3,0,1:T(8,128)(2,1)} %copy.228), calls=%async_computation.14 | async-start | bytes 2097152 | tf_op jit(solution)/shard_map/all_to_all | solution.py:77
  1195.4 118.2 %all-to-all-start.16 = ((bf16[4,512,1,1280]{3,1,2,0:T(8,128)(2,1)}), bf16[4,512,1,1280]{3,1,2,0:T(8,128)(2,1)}, u32[]{:S(2)}, u32[]{:S(2)}) async-start(bf16[4,512,1,1280]{3,1,2,0:T(8,128)(2,1)} %broadcast_in_dim.175), calls=%async_computation.16 | async-start | bytes 10485760 | tf_op jit(solution)/shard_map/all_to_all | solution.py:71
  1200.6 284.0 %all-reduce.4.cloned.1.call-start = ((), (), s32[]{:S(2)}) async-start(), calls=%async_computation.29 | async-start | bytes 18874368 | tf_op jit(solution)/shard_map/psum | solution.py:351
  1352.7 15.1 %all-to-all-start.19 = ((f32[8,1,512,16]{2,3,1,0:T(8,128)}), f32[8,1,512,16]{2,3,1,0:T(8,128)S(1)}, u32[]{:S(2)}, u32[]{:S(2)}) async-start(f32[8,1,512,16]{2,3,1,0:T(8,128)} %broadcast_in_dim.177), calls=%async_computation.19 | async-start | bytes 524288 | tf_op jit(solution)/shard_map/all_to_all | solution.py:71
  1367.8 28.5 %all-to-all-start.17 = ((f32[4,128,512]{2,1,0:T(8,128)}), f32[4,128,512]{2,1,0:T(8,128)S(1)}, u32[]{:S(2)}, u32[]{:S(2)}) async-start(f32[4,128,512]{2,1,0:T(8,128)} %bitcast.113), calls=%async_computation.17 | async-start | bytes 2097152 | tf_op jit(solution)/shard_map/all_to_all | solution.py:333
  1380.5 16.1 %copy-start.59 = (f32[128]{0:T(128)S(1)}, f32[128]{0:T(128)}, u32[]{:S(2)}) copy-start(f32[128]{0:T(128)} %copy-done.58) | copy-start | bytes 1540
  1383.8 15.3 %copy-start.63 = (f32[128]{0:T(128)S(1)}, f32[128]{0:T(128)}, u32[]{:S(2)}) copy-start(f32[128]{0:T(128)} %get-tuple-element.15) | copy-start | bytes 1540
  1383.8 15.3 %copy-start.64 = (f32[128]{0:T(128)S(1)}, f32[128]{0:T(128)}, u32[]{:S(2)}) copy-start(f32[128]{0:T(128)} %get-tuple-element.21) | copy-start | bytes 1540
  (52 other events, 357.2 us)
Sparse Core Ops, SparseCore 0:
  156.6 190.2 all-gather.5
  390.2 190.4 all-gather.3
  599.5 117.3 all-gather.7
  794.8 110.3 reduce-scatter.7
  907.3 114.7 reduce-scatter.5
  1025.6 129.4 reduce-scatter.3
  1342.4 142.2 all-reduce.3

commit v4 on v3

--- a/solution.py
+++ b/solution.py
@@ -132,22 +132,45 @@
     first_normed = hidden * first_scale
     first_input = (first_normed * attn_gain).astype(jnp.bfloat16)
     group_input = gather_a2a(first_input, "fsdp", fsdp_size, 0)
-    w_query_cols = lax.all_to_all(query_proj, "fsdp", 1, 0, tiled=True)
+    q_width, kv_width = heads_dev * HEAD_DIM, kv_dev * HEAD_DIM
     if share == 1:
-        w_key_cols = lax.all_to_all(key_proj, "fsdp", 1, 0, tiled=True)
-        w_value_cols = lax.all_to_all(value_proj, "fsdp", 1, 0, tiled=True)
+        blocks = jnp.concatenate(
+            [
+                query_proj.reshape(d_part, fsdp_size, q_width),
+                key_proj.reshape(d_part, fsdp_size, kv_width),
+                value_proj.reshape(d_part, fsdp_size, kv_width),
+            ],
+            axis=2,
+        )
+        half = d_part // 2
+        core = ctx_index % 2
+        mine = lax.all_to_all(
+            lax.dynamic_slice_in_dim(blocks, core * half, half, 0), "fsdp", 1, 0, tiled=True
+        ).reshape(fsdp_size, half, -1)
+        other = lax.ppermute(mine, "ctx", [(i, i ^ 1) for i in range(ctx_size)])
+        w_cols = jnp.where(
+            core == 0, jnp.stack([mine, other], axis=1), jnp.stack([other, mine], axis=1)
+        ).reshape(D, -1)
     else:
         kv_start = (fsdp_index // share) * HEAD_DIM
-        w_key_cols = lax.dynamic_slice_in_dim(
-            lax.all_gather(key_proj, "fsdp", axis=0, tiled=True), kv_start, HEAD_DIM, 1
+        w_cols = jnp.concatenate(
+            [
+                lax.all_to_all(query_proj, "fsdp", 1, 0, tiled=True),
+                lax.dynamic_slice_in_dim(
+                    lax.all_gather(key_proj, "fsdp", axis=0, tiled=True), kv_start, HEAD_DIM, 1
+                ),
+                lax.dynamic_slice_in_dim(
+                    lax.all_gather(value_proj, "fsdp", axis=0, tiled=True), kv_start, HEAD_DIM, 1
+                ),
+            ],
+            axis=1,
         )
-        w_value_cols = lax.dynamic_slice_in_dim(
-            lax.all_gather(value_proj, "fsdp", axis=0, tiled=True), kv_start, HEAD_DIM, 1
-        )
-    query_raw = matmul(group_input, w_query_cols).reshape(seqs, tokens, heads_dev, HEAD_DIM)
-    key_raw = matmul(group_input, w_key_cols).reshape(seqs, tokens, kv_dev, HEAD_DIM)
+    w_cols, expert_gate, expert_up = lax.optimization_barrier((w_cols, expert_gate, expert_up))
+    projected = matmul(group_input, w_cols)
+    query_raw = projected[:, :q_width].reshape(seqs, tokens, heads_dev, HEAD_DIM)
+    key_raw = projected[:, q_width : q_width + kv_width].reshape(seqs, tokens, kv_dev, HEAD_DIM)
     value_low = (
-        matmul(group_input, w_value_cols)
+        projected[:, q_width + kv_width :]
         .astype(jnp.bfloat16)
         .reshape(seqs, tokens, kv_dev * HEAD_DIM)
     )
@@ -181,7 +204,8 @@
         .reshape(group_rows, heads_dev * HEAD_DIM)
     )
     branch_parts = matmul(attended, out_proj).reshape(seqs, tokens, D)
-    branch = scatter_sum_a2a(branch_parts, "fsdp", fsdp_size, 0)[0]
+    branch = scatter_sum_a2a(branch_parts.astype(jnp.bfloat16), "fsdp", fsdp_size, 0)[0]
+    branch, expert_down = lax.optimization_barrier((branch, expert_down))
     middle = hidden + branch
     second_scale = rms_scale(middle)
     second_normed = middle * second_scale
@@ -314,7 +338,6 @@
             whole = whole.reshape(group_rows, KV_HEADS * HEAD_DIM)
         return whole
 
-    q_width, kv_width = heads_dev * HEAD_DIM, kv_dev * HEAD_DIM
     joined = gather_a2a(
         jnp.concatenate([grad_query, grad_key, grad_value], axis=1)[:, None], "fsdp", fsdp_size, 1
     )

time: 1520 us -> 1390 us (0.914)
  waiting for transfers between devices: 860 us -> 672 us
  blocking collectives: 47.6 us -> 113 us
    all_to_all x3 -> x0, waiting for transfers between devices: 191 us -> none  [the longest x1 167 us: per_device(): w_query_cols = lax.all_to_all(query_proj, 'fsdp', 1, 0, tiled=True)]
    all_to_all x3, waiting for transfers between devices: 189 us -> 99.8 us  [scatter_sum_a2a(): got = lax.all_to_all(parts, axis_name, axis, axis, tiled=True)]
    all_to_all x0 -> x1, blocking collectives: none -> 65.6 us  [per_device(): lax.all_to_all(lax.dynamic_slice_in_dim(blocks, core * half, half, 0), 'f...]
    all_to_all x8, waiting for transfers between devices: 240 us -> 299 us  [gather_a2a(): lax.all_to_all(rep, axis_name, 0, 0, tiled=True)]
    all_to_all x1, waiting for transfers between devices: 43.9 us -> 63.2 us  [per_device(): lax.all_to_all(grad_rows[None], 'ctx', split_axis=2, concat_axis=0, tiled...]
  transfers between devices with their start and end apart: 26 -> 24, of which waited for: 19 -> 17; matrix products, arithmetic and copies ran while one was open for 30% -> 32% of each run, Pallas kernels for 0% -> 0%
where the time goes in v4:
time: 1390 us; the launch traced here: 1370 us
  waiting for transfers between devices  672 us (48%)
  local copies, waits for them, and re-layouts  208 us (15%)
  matrix products  185 us (13%)
  blocking collectives  113 us (8%)
  other arithmetic  110 us (8%)
  starting transfers between devices  71 us (5%)
  between operations  16.2 us (1%)
    all_to_all x8, waiting for transfers between devices, gather_a2a(): lax.all_to_all(rep, axis_name, 0, 0, tiled=True)  299 us
    dot_general x25, matrix products, contract(): return jnp.einsum(form, left, right, preferred_element_type=jnp.float32)  167 us
    all_to_all x3, waiting for transfers between devices, scatter_sum_a2a(): got = lax.all_to_all(parts, axis_name, axis, axis, tiled=True)  99.8 us
    all_to_all x1, blocking collectives, per_device(): lax.all_to_all(lax.dynamic_slice_in_dim(blocks, core * half, half, 0), 'f...  65.6 us
    all_to_all x1, waiting for transfers between devices, per_device(): lax.all_to_all(dispatch(jnp.repeat(second_input, TOP, axis=0)), 'ctx', sp...  64.8 us
    all_to_all x1, waiting for transfers between devices, per_device(): lax.all_to_all(grad_rows[None], 'ctx', split_axis=2, concat_axis=0, tiled...  63.2 us
    all_to_all x1, waiting for transfers between devices, per_device(): lax.all_to_all(dispatch(grad_routes), 'ctx', split_axis=0, concat_axis=2,...  60.4 us
    psum x1, waiting for transfers between devices, per_device(): lax.psum(query_grad_part.astype(jnp.bfloat16), 'ctx').astype(jnp.float32)  44 us
  transfers between devices with their start and end apart: 24, of which 17 were waited for; matrix products, arithmetic and copies ran while one was open for 32% of the time, Pallas kernels for 0%

profile of v4, /device:TPU:0, one launch (start us, length us, event | category | flops | bytes accessed | tf_op | source)
XLA Modules:
  0.0 1375.0 jit_solution(9205919005732167322)
XLA Ops:
  9.8 6.4 copy.387
  18.0 65.6 %all_to_all.150 = bf16[256,4,1280]{0,2,1:T(8,128)(2,1)S(1)} all-to-all(bf16[256,4,1280]{0,2,1:T(8,128)(2,1)S(1)} %fusion.32), channel_id=1, replica_groups=mesh['ctx'=8,'fsdp'=4] {'fsdp'}, dimensions={1} | all-to-all | bytes 5242880 | tf_op jit(solution)/shard_map/all_to_all | solution.py:147
  94.6 7.9 copy.390
  125.8 96.5 %all-to-all-done = bf16[4,128,2048]{2,1,0:T(8,128)(2,1)S(1)} async-done(((bf16[4,128,2048]{2,1,0:T(8,128)(2,1)}), bf16[4,128,2048]{2,1,0:T(8,128)(2,1)S(1)}, u32[]{:S(2)}, u32[]{:S(2)}) %all-to-all-start) | async-done | bytes 2097184 | tf_op jit(solution)/shard_map/all_to_all | solution.py:71
  244.5 8.4 all-to-all-done.4
  264.0 9.7 all-to-all-done.2
  283.0 9.2 fusion.92
  292.2 8.5 fusion.3
  300.8 7.8 fusion.40
  324.7 90.9 %all-to-all-done.5 = bf16[4,1,128,2048]{3,2,1,0:T(8,128)(2,1)} async-done(((bf16[4,1,128,2048]{3,2,1,0:T(8,128)(2,1)}), bf16[4,1,128,2048]{3,2,1,0:T(8,128)(2,1)}, u32[]{:S(2)}, u32[]{:S(2)}) %all-to-all-start.5) | async-done | bytes 2097184 | tf_op jit(solution)/shard_map/all_to_all | solution.py:77
  418.7 7.0 gather_fusion.2
  427.1 10.7 scatter_custom_fusion.1
  443.2 10.4 scatter_custom_fusion
  453.7 60.4 %all-to-all-done.9 = bf16[8,2,96,2048]{3,2,1,0:T(8,128)(2,1)} async-done(((bf16[8,2,96,2048]{3,2,1,0:T(8,128)(2,1)}), bf16[8,2,96,2048]{3,2,1,0:T(8,128)(2,1)}, u32[]{:S(2)}, u32[]{:S(2)}) %all-to-all-start.9) | async-done | bytes 6291488 | tf_op jit(solution)/shard_map/all_to_all | solution.py:262
  518.9 6.7 copy.418
  525.5 64.8 %all-to-all-done.7 = bf16[8,2,96,2048]{3,2,1,0:T(8,128)(2,1)} async-done(((bf16[8,2,96,2048]{3,2,1,0:T(8,128)(2,1)}), bf16[8,2,96,2048]{3,2,1,0:T(8,128)(2,1)}, u32[]{:S(2)}, u32[]{:S(2)}) %all-to-all-start.7) | async-done | bytes 6291488 | tf_op jit(solution)/shard_map/all_to_all | solution.py:237
  590.4 6.6 copy.414
  597.0 10.6 fusion.96
  607.6 10.6 fusion.95
  618.2 13.5 multiply_convert_fusion
  633.0 7.1 convolution_convert_fusion.1
  640.2 7.9 convert_bitcast_fusion
  648.0 19.2 %copy.415 = bf16[1,2,768,2048]{3,1,0,2:T(2,128)(2,1)} copy(bf16[1,2,768,2048]{3,2,1,0:T(8,128)(2,1)S(1)} %convert_bitcast_fusion) | data formatting | bytes 12582912 | tf_op jit(solution)/shard_map/broadcast_in_dim | solution.py:250
  672.1 9.8 convolution_convert_fusion.2
  682.0 10.7 fusion.97
  692.7 10.1 fusion.10
  702.7 18.8 %copy.419 = bf16[1,2,768,2048]{3,1,0,2:T(2,128)(2,1)} copy(bf16[1,2,768,2048]{3,2,1,0:T(8,128)(2,1)S(1)} %fusion.10) | data formatting | bytes 12582912 | tf_op jit(solution)/shard_map/broadcast_in_dim | solution.py:277
  721.5 22.1 %all-to-all-done.8 = bf16[1,2,768,2048]{3,1,0,2:T(2,128)(2,1)} async-done(((bf16[1,2,768,2048]{3,1,0,2:T(2,128)(2,1)}), bf16[1,2,768,2048]{3,1,0,2:T(2,128)(2,1)}, u32[]{:S(2)}, u32[]{:S(2)}) %all-to-all-start.8) | async-done | bytes 6291488 | tf_op jit(solution)/shard_map/all_to_all | solution.py:250
  748.6 8.3 copy.416
  756.9 63.2 %all-to-all-done.10 = bf16[1,2,768,2048]{3,1,0,2:T(2,128)(2,1)} async-done(((bf16[1,2,768,2048]{3,1,0,2:T(2,128)(2,1)}), bf16[1,2,768,2048]{3,1,0,2:T(2,128)(2,1)}, u32[]{:S(2)}, u32[]{:S(2)}) %all-to-all-start.10) | async-done | bytes 6291488 | tf_op jit(solution)/shard_map/all_to_all | solution.py:277
  820.1 8.4 copy.420
  828.5 12.4 gather_fusion.3
  840.9 12.6 gather_fusion.4
  877.7 9.7 convolution_convert_fusion.3
  887.4 71.0 %all-to-all-done.11 = bf16[4,128,2048]{2,1,0:T(8,128)(2,1)S(1)} async-done(((bf16[4,128,2048]{2,1,0:T(8,128)(2,1)}), bf16[4,128,2048]{2,1,0:T(8,128)(2,1)S(1)}, u32[]{:S(2)}, u32[]{:S(2)}) %all-to-all-start.11) | async-done | bytes 2097184 | tf_op jit(solution)/shard_map/all_to_all | solution.py:71
  964.0 14.4 %fusion = (f32[4,8,128]{2,1,0:T(8,128)}, f32[4,1024,128,8]{2,1,3,0:T(8,128)}) fusion(f32[4,1,8,128,1024]{3,4,2,0,1:T(8,128)} %get-tuple-element.72, f32[4,8,128]{2,1,0:T(8,128)} %log_add_fusion, bf16[4,1024,128,1]{2,1,3,0:T(8,128)(2,1)} %bitcast.391, bf16[4,128,8,128]{3,2,1,0:T(8,128)(2,1)S(1)} %bitcast.381), kind=kOutput, calls=%fused_computation.10 | convolution fusion | flops 1086320640 | bytes 35684352 | tf_op jit(solution)/shard_map/stkgd,sjkd->skgtj/dot_general | solution.py:23
  980.9 13.2 fusion.6
  1000.1 12.6 copy.434
  1026.2 6.4 multiply_bitcast_fusion
  1035.4 6.2 all-to-all-done.13
  1080.4 106.4 %all-to-all-done.14 = bf16[4,512,1,1280]{3,1,2,0:T(8,128)(2,1)} async-done(((bf16[4,512,1,1280]{3,1,2,0:T(8,128)(2,1)}), bf16[4,512,1,1280]{3,1,2,0:T(8,128)(2,1)}, u32[]{:S(2)}, u32[]{:S(2)}) %all-to-all-start.14) | async-done | bytes 5242912 | tf_op jit(solution)/shard_map/all_to_all | solution.py:71
  1191.4 6.2 copy.438
  1203.9 6.6 convolution_convert_fusion
  1211.8 8.4 all_to_all.151
  1251.3 12.4 all-to-all-done.15
  1266.4 39.2 %all-reduce = (f32[2048]{0:T(1024)}, f32[128]{0:T(128)}, f32[128]{0:T(128)}, f32[2048]{0:T(1024)}) all-reduce(f32[2048]{0:T(1024)S(1)} %bitcast.451, f32[128]{0:T(128)S(1)} %bitcast_reduce_fusion, f32[128]{0:T(128)S(1)} %get-tuple-element.25, f32[2048]{0:T(1024)S(1)} %get-tuple-element.27), channel_id=1, replica_groups=mesh['ctx'=8,'fsdp'=4] {'ctx','fsdp'}, use_global_device_ids=true, to_apply=%region_24.26 | all-reduce | flops 4352 | bytes 34816 | tf_op jit(solution)/shard_map/psum | solution.py:380
  1308.1 44.0 %all-reduce.4.cloned.1.call-done = (bf16[512,4096]{1,0:T(8,128)(2,1)}, bf16[512,512]{1,0:T(8,128)(2,1)}, bf16[512,512]{1,0:T(8,128)(2,1)}, bf16[1024,2048]{1,0:T(8,128)(2,1)}) async-done(((bf16[512,4096]{1,0:T(8,128)(2,1)}, bf16[512,512]{1,0:T(8,128)(2,1)}, bf16[512,512]{1,0:T(8,128)(2,1)}, bf16[1024,2048]{1,0:T(8,128)(2,1)}), (bf16[512,4096]{1,0:T(8,128)(2,1)}, bf16[512,512]{1,0:T(8,128)(2,1)}, ...) | async-done | bytes 9437200 | tf_op jit(solution)/shard_map/psum | solution.py:374
  1356.4 6.8 convert_element_type.218
  (385 shorter events, 272.4 us)
Async XLA Ops:
  7.2 589.8 %all-gather.6.cloned.1.call-start = ((), (), s32[]{:S(2)}) async-start(), calls=%async_computation.22 | async-start | bytes 7864320 | tf_op jit(solution)/shard_map/all_gather | solution.py:215
  83.5 5.0 collective-permute-start
  103.2 8.8 all-to-all-start.3
  113.6 108.7 %all-to-all-start = ((bf16[4,128,2048]{2,1,0:T(8,128)(2,1)}), bf16[4,128,2048]{2,1,0:T(8,128)(2,1)S(1)}, u32[]{:S(2)}, u32[]{:S(2)}) async-start(bf16[4,128,2048]{2,1,0:T(8,128)(2,1)} %broadcast_in_dim.84), calls=%async_computation | async-start | bytes 4194304 | tf_op jit(solution)/shard_map/all_to_all | solution.py:71
  118.0 104.3 %copy-start.41 = (f32[128,64]{0,1:T(8,128)}, f32[128,64]{0,1:T(8,128)S(1)}, u32[]{:S(2)}) copy-start(f32[128,64]{0,1:T(8,128)S(1)} %get-tuple-element.69) | copy-start | bytes 98308
  118.0 104.3 %copy-start.43 = (f32[128,64]{0,1:T(8,128)}, f32[128,64]{0,1:T(8,128)S(1)}, u32[]{:S(2)}) copy-start(f32[128,64]{0,1:T(8,128)S(1)} %get-tuple-element.70) | copy-start | bytes 98308
  118.1 142.2 %copy-start.34 = (f32[128,64]{1,0:T(8,128)}, f32[128,64]{1,0:T(8,128)S(1)}, u32[]{:S(2)}) copy-start(f32[128,64]{1,0:T(8,128)S(1)} %copy.401) | copy-start | bytes 98308
  118.2 142.2 %copy-start.36 = (f32[128,64]{1,0:T(8,128)}, f32[128,64]{1,0:T(8,128)S(1)}, u32[]{:S(2)}) copy-start(f32[128,64]{1,0:T(8,128)S(1)} %copy.402) | copy-start | bytes 98308
  233.2 19.7 %all-to-all-start.4 = ((bf16[8,4,128,128]{3,2,1,0:T(8,128)(2,1)}), bf16[8,4,128,128]{3,2,1,0:T(8,128)(2,1)}, u32[]{:S(2)}, u32[]{:S(2)}) async-start(bf16[8,4,128,128]{3,2,1,0:T(8,128)(2,1)} %broadcast_in_dim.94), calls=%async_computation.4 | async-start | bytes 2097152 | tf_op jit(solution)/shard_map/all_to_all | solution.py:71
  244.5 15.9 %copy-start = (f32[64,8,8,128]{3,2,1,0:T(8,128)}, f32[64,8,8,128]{3,2,1,0:T(8,128)S(1)}, u32[]{:S(2)}) copy-start(f32[64,8,8,128]{3,2,1,0:T(8,128)S(1)} %copy.482) | copy-start | bytes 6291460
  254.0 19.6 %all-to-all-start.2 = ((bf16[8,4,128,128]{2,3,1,0:T(8,128)(2,1)}), bf16[8,4,128,128]{2,3,1,0:T(8,128)(2,1)}, u32[]{:S(2)}, u32[]{:S(2)}) async-start(bf16[8,4,128,128]{2,3,1,0:T(8,128)(2,1)} %broadcast_in_dim.86), calls=%async_computation.2 | async-start | bytes 2097152 | tf_op jit(solution)/shard_map/all_to_all | solution.py:71
  258.3 349.3 %all-gather.4.cloned.1.call-start = ((), (), s32[]{:S(2)}) async-start(), calls=%async_computation.21 | async-start | bytes 7864320 | tf_op jit(solution)/shard_map/all_gather | solution.py:214
  260.4 13.3 copy-start.61
  262.6 20.4 %copy-start.11 = (bf16[4,128,8,64]{3,1,2,0:T(8,128)(2,1)S(1)}, bf16[4,128,8,64]{3,1,2,0:T(8,128)(2,1)}, u32[]{:S(2)}) copy-start(bf16[4,128,8,64]{3,1,2,0:T(8,128)(2,1)} %get-tuple-element.60) | copy-start | bytes 1572868
  263.9 28.3 %copy-start.7 = (bf16[4,8,128,128]{3,2,1,0:T(8,128)(2,1)}, bf16[4,8,128,128]{3,2,1,0:T(8,128)(2,1)S(1)}, u32[]{:S(2)}) copy-start(bf16[4,8,128,128]{3,2,1,0:T(8,128)(2,1)S(1)} %copy.398) | copy-start | bytes 3145732
  274.3 38.9 %all-to-all-start.6 = ((bf16[4,512,16]{1,2,0:T(8,128)(2,1)}), bf16[4,512,16]{1,2,0:T(8,128)(2,1)S(1)}, u32[]{:S(2)}, u32[]{:S(2)}) async-start(bf16[4,512,16]{1,2,0:T(8,128)(2,1)} %broadcast_in_dim.96), calls=%async_computation.6 | async-start | bytes 131072 | tf_op jit(solution)/shard_map/all_to_all | solution.py:71
  313.3 102.4 %all-to-all-start.5 = ((bf16[4,1,128,2048]{3,2,1,0:T(8,128)(2,1)}), bf16[4,1,128,2048]{3,2,1,0:T(8,128)(2,1)}, u32[]{:S(2)}, u32[]{:S(2)}) async-start(bf16[4,1,128,2048]{3,2,1,0:T(8,128)(2,1)} %fusion.28), calls=%async_computation.5 | async-start | bytes 4194304 | tf_op jit(solution)/shard_map/all_to_all | solution.py:77
  319.0 99.0 %copy-start.53 = (f32[2048]{0:T(1024)S(1)}, f32[2048]{0:T(1024)}, u32[]{:S(2)}) copy-start(f32[2048]{0:T(1024)} %param.30) | copy-start | bytes 24580
  319.1 106.9 %copy-start.22 = (s32[1,128,8]{2,1,0:T(8,128)}, s32[1,128,8]{2,1,0:T(8,128)S(1)}, u32[]{:S(2)}) copy-start(s32[1,128,8]{2,1,0:T(8,128)S(1)} %copy.406) | copy-start | bytes 12292
  324.7 93.5 %copy-start.38 = (bf16[4,2,8,512]{3,2,0,1:T(8,128)(2,1)}, bf16[4,2,8,512]{3,2,0,1:T(8,128)(2,1)S(1)}, u32[]{:S(2)}) copy-start(bf16[4,2,8,512]{3,2,0,1:T(8,128)(2,1)S(1)} %copy.481) | copy-start | bytes 196612
  418.2 25.0 %copy-start.14 = (bf16[128,2048]{1,0:T(8,128)(2,1)}, bf16[128,2048]{1,0:T(8,128)(2,1)S(1)}, u32[]{:S(2)}) copy-start(bf16[128,2048]{1,0:T(8,128)(2,1)S(1)} %multiply_convert_fusion.3) | copy-start | bytes 1572868
  437.7 76.3 %all-to-all-start.9 = ((bf16[8,2,96,2048]{3,2,1,0:T(8,128)(2,1)}), bf16[8,2,96,2048]{3,2,1,0:T(8,128)(2,1)}, u32[]{:S(2)}, u32[]{:S(2)}) async-start(bf16[8,2,96,2048]{3,2,1,0:T(8,128)(2,1)} %bitcast.378), calls=%async_computation.9 | async-start | bytes 12582912 | tf_op jit(solution)/shard_map/all_to_all | solution.py:262
  442.5 175.7 %all-gather.8.cloned.1.call-start = ((), (), s32[]{:S(2)}) async-start(), calls=%async_computation.23 | async-start | bytes 7864320 | tf_op jit(solution)/shard_map/all_gather | solution.py:216
  514.0 76.4 %all-to-all-start.7 = ((bf16[8,2,96,2048]{3,2,1,0:T(8,128)(2,1)}), bf16[8,2,96,2048]{3,2,1,0:T(8,128)(2,1)}, u32[]{:S(2)}, u32[]{:S(2)}) async-start(bf16[8,2,96,2048]{3,2,1,0:T(8,128)(2,1)} %bitcast.379), calls=%async_computation.7 | async-start | bytes 12582912 | tf_op jit(solution)/shard_map/all_to_all | solution.py:237
  518.8 722.2 %reduce-scatter.8.cloned.1.call-start = ((), (), s32[]{:S(2)}) async-start(), calls=%async_computation.26 | async-start | bytes 7864320 | tf_op jit(solution)/shard_map/reduce_scatter | solution.py:368
  607.6 25.4 %slice-start.4 = ((s8[6291456]{0:T(1024)(128)(4,1)}), s8[2097152]{0:T(1024)(128)(4,1)S(1)}, s32[]{:S(2)}) async-start(s8[6291456]{0:T(1024)(128)(4,1)} %bitcast.397), calls=%async_computation.32 | async-start | bytes 4194304
  618.2 14.9 %slice-start.5 = ((s8[6291456]{0:T(1024)(128)(4,1)}), s8[4194304]{0:T(1024)(128)(4,1)S(1)}, s32[]{:S(2)}) async-start(s8[6291456]{0:T(1024)(128)(4,1)} %bitcast.397), calls=%async_computation.33 | async-start | bytes 8388608
  667.2 76.4 %all-to-all-start.8 = ((bf16[1,2,768,2048]{3,1,0,2:T(2,128)(2,1)}), bf16[1,2,768,2048]{3,1,0,2:T(2,128)(2,1)}, u32[]{:S(2)}, u32[]{:S(2)}) async-start(bf16[1,2,768,2048]{3,1,0,2:T(2,128)(2,1)} %copy.415), calls=%async_computation.8 | async-start | bytes 12582912 | tf_op jit(solution)/shard_map/all_to_all | solution.py:250
  672.0 572.6 %reduce-scatter.6.cloned.1.call-start = ((), (), s32[]{:S(2)}) async-start(), calls=%async_computation.25 | async-start | bytes 7864320 | tf_op jit(solution)/shard_map/reduce_scatter | solution.py:365
  743.6 76.5 %all-to-all-start.10 = ((bf16[1,2,768,2048]{3,1,0,2:T(2,128)(2,1)}), bf16[1,2,768,2048]{3,1,0,2:T(2,128)(2,1)}, u32[]{:S(2)}, u32[]{:S(2)}) async-start(bf16[1,2,768,2048]{3,1,0,2:T(2,128)(2,1)} %copy.419), calls=%async_computation.10 | async-start | bytes 12582912 | tf_op jit(solution)/shard_map/all_to_all | solution.py:277
  869.9 88.5 %all-to-all-start.11 = ((bf16[4,128,2048]{2,1,0:T(8,128)(2,1)}), bf16[4,128,2048]{2,1,0:T(8,128)(2,1)S(1)}, u32[]{:S(2)}, u32[]{:S(2)}) async-start(bf16[4,128,2048]{2,1,0:T(8,128)(2,1)} %broadcast_in_dim.174), calls=%async_computation.11 | async-start | bytes 4194304 | tf_op jit(solution)/shard_map/all_to_all | solution.py:71
  873.5 374.5 %reduce-scatter.4.cloned.1.call-start = ((), (), s32[]{:S(2)}) async-start(), calls=%async_computation.24 | async-start | bytes 7864320 | tf_op jit(solution)/shard_map/reduce_scatter | solution.py:362
  964.0 14.5 %slice-start = ((s8[16777216]{0:T(1024)(128)(4,1)}), s8[4194304]{0:T(1024)(128)(4,1)S(1)}, s32[]{:S(2)}) async-start(s8[16777216]{0:T(1024)(128)(4,1)} %bitcast.371), calls=%async_computation.28 | async-start | bytes 8388608
  964.0 14.4 %slice-start.1 = ((s8[16777216]{0:T(1024)(128)(4,1)}), s8[4194304]{0:T(1024)(128)(4,1)S(1)}, s32[]{:S(2)}) async-start(s8[16777216]{0:T(1024)(128)(4,1)} %bitcast.371), calls=%async_computation.29 | async-start | bytes 8388608
  964.0 15.7 %slice-start.2 = ((s8[16777216]{0:T(1024)(128)(4,1)}), s8[4194304]{0:T(1024)(128)(4,1)S(1)}, s32[]{:S(2)}) async-start(s8[16777216]{0:T(1024)(128)(4,1)} %bitcast.371), calls=%async_computation.30 | async-start | bytes 8388608
  964.0 16.9 %slice-start.3 = ((s8[16777216]{0:T(1024)(128)(4,1)}), s8[4194304]{0:T(1024)(128)(4,1)S(1)}, s32[]{:S(2)}) async-start(s8[16777216]{0:T(1024)(128)(4,1)} %bitcast.371), calls=%async_computation.31 | async-start | bytes 8388608
  980.9 13.2 copy-start.12
  980.9 13.2 copy-start.13
  1020.5 21.0 %all-to-all-start.13 = ((bf16[4,8,128,128]{2,3,0,1:T(8,128)(2,1)}), bf16[4,8,128,128]{2,3,0,1:T(8,128)(2,1)S(1)}, u32[]{:S(2)}, u32[]{:S(2)}) async-start(bf16[4,8,128,128]{2,3,0,1:T(8,128)(2,1)} %copy.435), calls=%async_computation.13 | async-start | bytes 2097152 | tf_op jit(solution)/shard_map/all_to_all | solution.py:77
  1032.6 13.2 copy-start.1
  1032.6 13.2 copy-start.48
  1032.7 13.2 copy-start.71
  1041.6 19.7 %all-to-all-start.12 = ((bf16[4,8,128,128]{2,3,0,1:T(8,128)(2,1)}), bf16[4,8,128,128]{2,3,0,1:T(8,128)(2,1)}, u32[]{:S(2)}, u32[]{:S(2)}) async-start(bf16[4,8,128,128]{2,3,0,1:T(8,128)(2,1)} %copy.430), calls=%async_computation.12 | async-start | bytes 2097152 | tf_op jit(solution)/shard_map/all_to_all | solution.py:77
  1067.6 119.1 %all-to-all-start.14 = ((bf16[4,512,1,1280]{3,1,2,0:T(8,128)(2,1)}), bf16[4,512,1,1280]{3,1,2,0:T(8,128)(2,1)}, u32[]{:S(2)}, u32[]{:S(2)}) async-start(bf16[4,512,1,1280]{3,1,2,0:T(8,128)(2,1)} %broadcast_in_dim.175), calls=%async_computation.14 | async-start | bytes 10485760 | tf_op jit(solution)/shard_map/all_to_all | solution.py:71
  1072.9 279.2 %all-reduce.4.cloned.1.call-start = ((), (), s32[]{:S(2)}) async-start(), calls=%async_computation.27 | async-start | bytes 18874368 | tf_op jit(solution)/shard_map/psum | solution.py:374
  1221.0 14.3 %all-to-all-start.17 = ((f32[8,1,512,16]{2,3,1,0:T(8,128)}), f32[8,1,512,16]{2,3,1,0:T(8,128)S(1)}, u32[]{:S(2)}, u32[]{:S(2)}) async-start(f32[8,1,512,16]{2,3,1,0:T(8,128)} %broadcast_in_dim.177), calls=%async_computation.17 | async-start | bytes 524288 | tf_op jit(solution)/shard_map/all_to_all | solution.py:71
  1235.3 28.4 %all-to-all-start.15 = ((f32[4,128,512]{2,1,0:T(8,128)}), f32[4,128,512]{2,1,0:T(8,128)S(1)}, u32[]{:S(2)}, u32[]{:S(2)}) async-start(f32[4,128,512]{2,1,0:T(8,128)} %bitcast.409), calls=%async_computation.15 | async-start | bytes 2097152 | tf_op jit(solution)/shard_map/all_to_all | solution.py:356
  1248.0 16.0 %copy-start.73 = (f32[128]{0:T(128)S(1)}, f32[128]{0:T(128)}, u32[]{:S(2)}) copy-start(f32[128]{0:T(128)} %copy-done.72) | copy-start | bytes 1540
  (62 other events, 395.2 us)
Sparse Core Ops, SparseCore 0:
  102.7 159.1 all-gather.5
  263.5 159.5 all-gather.3
  444.8 114.8 all-gather.7
  640.3 108.1 reduce-scatter.7
  750.6 111.2 reduce-scatter.5
  887.5 123.8 reduce-scatter.3
  1210.6 141.4 all-reduce.3

commit v5 on v4

--- a/solution.py
+++ b/solution.py
@@ -120,18 +120,11 @@
     offsets = jnp.arange(block_len, dtype=jnp.int32)
     local_pos = (own_blocks[:, None] * block_len + offsets[None, :]).reshape(-1)
     all_pos = (block_map[:, None] * block_len + offsets[None, :]).reshape(-1)
-    doc_rows = gather_a2a(doc_ids.astype(jnp.float32), "fsdp", fsdp_size, 0)
-    docs_query = jnp.take(doc_rows, local_pos, axis=1)
-    docs_key = jnp.take(doc_rows, all_pos, axis=1)
-    visible = (all_pos[None, None, :] <= local_pos[None, :, None]) & (
-        docs_key[:, None, :] == docs_query[:, :, None]
-    )
     cosine, sine_table = rotary(local_pos)
     hidden = hidden_in[0]
     first_scale = rms_scale(hidden)
     first_normed = hidden * first_scale
     first_input = (first_normed * attn_gain).astype(jnp.bfloat16)
-    group_input = gather_a2a(first_input, "fsdp", fsdp_size, 0)
     q_width, kv_width = heads_dev * HEAD_DIM, kv_dev * HEAD_DIM
     if share == 1:
         blocks = jnp.concatenate(
@@ -144,14 +137,30 @@
         )
         half = d_part // 2
         core = ctx_index % 2
-        mine = lax.all_to_all(
-            lax.dynamic_slice_in_dim(blocks, core * half, half, 0), "fsdp", 1, 0, tiled=True
-        ).reshape(fsdp_size, half, -1)
+        lanes = 128
+        sent_rows = jnp.moveaxis(
+            lax.dynamic_slice_in_dim(blocks, core * half, half, 0), 1, 0
+        ).reshape(fsdp_size, -1, lanes)
+        common = jnp.concatenate(
+            [first_input.reshape(-1, lanes), doc_ids.astype(jnp.bfloat16).reshape(-1, lanes)],
+            axis=0,
+        )
+        payload = jnp.concatenate(
+            [sent_rows, jnp.broadcast_to(common[None], (fsdp_size,) + common.shape)], axis=1
+        )
+        got = lax.all_to_all(payload, "fsdp", 0, 0, tiled=True)
+        w_rows = sent_rows.shape[1]
+        h_rows = tokens * D // lanes
+        mine = got[:, :w_rows].reshape(fsdp_size, half, -1)
+        group_input = got[:, w_rows : w_rows + h_rows].reshape(group_rows, D)
+        doc_rows = got[:, w_rows + h_rows :].reshape(fsdp_size, -1).astype(jnp.float32)
         other = lax.ppermute(mine, "ctx", [(i, i ^ 1) for i in range(ctx_size)])
         w_cols = jnp.where(
             core == 0, jnp.stack([mine, other], axis=1), jnp.stack([other, mine], axis=1)
         ).reshape(D, -1)
     else:
+        group_input = gather_a2a(first_input, "fsdp", fsdp_size, 0)
+        doc_rows = gather_a2a(doc_ids.astype(jnp.float32), "fsdp", fsdp_size, 0)
         kv_start = (fsdp_index // share) * HEAD_DIM
         w_cols = jnp.concatenate(
             [
@@ -165,7 +174,14 @@
             ],
             axis=1,
         )
-    w_cols, expert_gate, expert_up = lax.optimization_barrier((w_cols, expert_gate, expert_up))
+    w_cols, expert_gate, expert_up, expert_down = lax.optimization_barrier(
+        (w_cols, expert_gate, expert_up, expert_down)
+    )
+    docs_query = jnp.take(doc_rows, local_pos, axis=1)
+    docs_key = jnp.take(doc_rows, all_pos, axis=1)
+    visible = (all_pos[None, None, :] <= local_pos[None, :, None]) & (
+        docs_key[:, None, :] == docs_query[:, :, None]
+    )
     projected = matmul(group_input, w_cols)
     query_raw = projected[:, :q_width].reshape(seqs, tokens, heads_dev, HEAD_DIM)
     key_raw = projected[:, q_width : q_width + kv_width].reshape(seqs, tokens, kv_dev, HEAD_DIM)
@@ -205,7 +221,6 @@
     )
     branch_parts = matmul(attended, out_proj).reshape(seqs, tokens, D)
     branch = scatter_sum_a2a(branch_parts.astype(jnp.bfloat16), "fsdp", fsdp_size, 0)[0]
-    branch, expert_down = lax.optimization_barrier((branch, expert_down))
     middle = hidden + branch
     second_scale = rms_scale(middle)
     second_normed = middle * second_scale

time: 1390 us -> 1320 us (0.950)
  waiting for transfers between devices: 672 us -> 539 us
  blocking collectives: 113 us -> 158 us
    all_to_all x8 -> x6, waiting for transfers between devices: 299 us -> 195 us  [gather_a2a(): lax.all_to_all(rep, axis_name, 0, 0, tiled=True)]
    all_to_all x1, blocking collectives: 65.6 us -> 111 us  [per_device(): got = lax.all_to_all(payload, 'fsdp', 0, 0, tiled=True)]
    reshape x1 -> x6, local copies, waits for them, and re-layouts: 0.02 us -> 20.4 us  [the longest x1 7.82 us: per_device(): query_proj.reshape(d_part, fsdp_size, q_width)]
    all_to_all x1, waiting for transfers between devices: 63.2 us -> 44 us  [per_device(): lax.all_to_all(grad_rows[None], 'ctx', split_axis=2, concat_axis=0, tiled...]
    all_to_all x8 -> x6, starting transfers between devices: 31.9 us -> 26.2 us  [gather_a2a(): lax.all_to_all(rep, axis_name, 0, 0, tiled=True)]
  transfers between devices with their start and end apart: 24 -> 22, of which waited for: 17 -> 15; matrix products, arithmetic and copies ran while one was open for 32% -> 34% of each run, Pallas kernels for 0% -> 0%
where the time goes in v5:
time: 1320 us; the launch traced here: 1300 us
  waiting for transfers between devices  539 us (41%)
  local copies, waits for them, and re-layouts  216 us (16%)
  matrix products  191 us (14%)
  blocking collectives  158 us (12%)
  other arithmetic  121 us (9%)
  starting transfers between devices  62.1 us (5%)
  between operations  16.1 us (1%)
    all_to_all x6, waiting for transfers between devices, gather_a2a(): lax.all_to_all(rep, axis_name, 0, 0, tiled=True)  195 us
    dot_general x25, matrix products, contract(): return jnp.einsum(form, left, right, preferred_element_type=jnp.float32)  173 us
    all_to_all x1, blocking collectives, per_device(): got = lax.all_to_all(payload, 'fsdp', 0, 0, tiled=True)  111 us
    all_to_all x3, waiting for transfers between devices, scatter_sum_a2a(): got = lax.all_to_all(parts, axis_name, axis, axis, tiled=True)  104 us
    all_to_all x1, waiting for transfers between devices, per_device(): lax.all_to_all(dispatch(grad_routes), 'ctx', split_axis=0, concat_axis=2,...  64.9 us
    all_to_all x1, waiting for transfers between devices, per_device(): lax.all_to_all(dispatch(jnp.repeat(second_input, TOP, axis=0)), 'ctx', sp...  51.2 us
    all_to_all x1, waiting for transfers between devices, per_device(): lax.all_to_all(grad_rows[None], 'ctx', split_axis=2, concat_axis=0, tiled...  44 us
    psum x1, waiting for transfers between devices, per_device(): lax.psum(query_grad_part.astype(jnp.bfloat16), 'ctx').astype(jnp.float32)  43.9 us
  transfers between devices with their start and end apart: 22, of which 15 were waited for; matrix products, arithmetic and copies ran while one was open for 34% of the time, Pallas kernels for 0%

profile of v5, /device:TPU:0, one launch (start us, length us, event | category | flops | bytes accessed | tf_op | source)
XLA Modules:
  0.0 1303.4 jit_solution(4470099899393840523)
XLA Ops:
  13.2 7.8 reshape.788
  33.2 110.7 %all_to_all.130 = bf16[4,4616,128]{2,1,0:T(8,128)(2,1)S(1)} all-to-all(bf16[4,4616,128]{2,1,0:T(8,128)(2,1)S(1)} %pad_maximum_fusion), channel_id=1, replica_groups=mesh['ctx'=8,'fsdp'=4] {'fsdp'}, dimensions={0} | all-to-all | bytes 9453568 | tf_op jit(solution)/shard_map/all_to_all | solution.py:151
  155.5 7.2 maximum_select_fusion
  171.8 6.5 fusion.99
  191.5 9.1 all-to-all-done.2
  211.2 9.5 all-to-all-done.1
  224.6 9.2 fusion.98
  233.8 8.6 fusion.3
  242.5 7.9 fusion.41
  264.3 94.8 %all-to-all-done.3 = bf16[4,1,128,2048]{3,2,1,0:T(8,128)(2,1)S(1)} async-done(((bf16[4,1,128,2048]{3,2,1,0:T(8,128)(2,1)}), bf16[4,1,128,2048]{3,2,1,0:T(8,128)(2,1)S(1)}, u32[]{:S(2)}, u32[]{:S(2)}) %all-to-all-start.3) | async-done | bytes 2097184 | tf_op jit(solution)/shard_map/all_to_all | solution.py:77
  367.6 10.2 scatter_custom_fusion
  384.6 7.0 gather_fusion.2
  392.4 10.7 scatter_custom_fusion.1
  403.1 51.2 %all-to-all-done.5 = bf16[8,2,96,2048]{3,2,1,0:T(8,128)(2,1)} async-done(((bf16[8,2,96,2048]{3,2,1,0:T(8,128)(2,1)}), bf16[8,2,96,2048]{3,2,1,0:T(8,128)(2,1)}, u32[]{:S(2)}, u32[]{:S(2)}) %all-to-all-start.5) | async-done | bytes 6291488 | tf_op jit(solution)/shard_map/all_to_all | solution.py:252
  459.1 6.7 copy.359
  465.8 64.9 %all-to-all-done.7 = bf16[8,2,96,2048]{3,2,1,0:T(8,128)(2,1)} async-done(((bf16[8,2,96,2048]{3,2,1,0:T(8,128)(2,1)}), bf16[8,2,96,2048]{3,2,1,0:T(8,128)(2,1)}, u32[]{:S(2)}, u32[]{:S(2)}) %all-to-all-start.7) | async-done | bytes 6291488 | tf_op jit(solution)/shard_map/all_to_all | solution.py:277
  530.6 6.6 copy.363
  537.2 10.6 fusion.101
  547.9 10.6 fusion.100
  558.5 13.5 %multiply_convert_fusion = (bf16[2,768,768]{2,1,0:T(8,128)(2,1)}, bf16[2,768,768]{2,1,0:T(8,128)(2,1)}, bf16[2,768,768]{2,1,0:T(8,128)(2,1)S(1)}) fusion(f32[2,768,768]{2,1,0:T(8,128)} %fusion.100, f32[2,768,768]{2,1,0:T(8,128)} %fusion.101, bf16[2,768,2048]{2,1,0:T(8,128)(2,1)} %bitcast.410, bf16[2,768,2048]{2,1,0:T(8,128)(2,1)} %all-gather.8.cloned.1.call-done), kind=kOutput, calls=%fused_computation.34 | convolution fusion | flops 4850712576 | bytes 29097984 | tf_op jit(solution)/shard_map/erd,efd->erf/dot_general | solution.py:23
  573.4 7.1 convolution_convert_fusion.1
  580.5 7.9 convert_bitcast_fusion
  588.4 19.2 %copy.360 = bf16[1,2,768,2048]{3,1,0,2:T(2,128)(2,1)} copy(bf16[1,2,768,2048]{3,2,1,0:T(8,128)(2,1)S(1)} %convert_bitcast_fusion) | data formatting | bytes 12582912 | tf_op jit(solution)/shard_map/broadcast_in_dim | solution.py:265
  612.4 9.7 convolution_convert_fusion.2
  622.1 10.7 fusion.102
  632.8 9.9 fusion.10
  642.7 18.8 %copy.364 = bf16[1,2,768,2048]{3,1,0,2:T(2,128)(2,1)} copy(bf16[1,2,768,2048]{3,2,1,0:T(8,128)(2,1)S(1)} %fusion.10) | data formatting | bytes 12582912 | tf_op jit(solution)/shard_map/broadcast_in_dim | solution.py:292
  661.5 22.5 %all-to-all-done.6 = bf16[1,2,768,2048]{3,1,0,2:T(2,128)(2,1)} async-done(((bf16[1,2,768,2048]{3,1,0,2:T(2,128)(2,1)}), bf16[1,2,768,2048]{3,1,0,2:T(2,128)(2,1)}, u32[]{:S(2)}, u32[]{:S(2)}) %all-to-all-start.6) | async-done | bytes 6291488 | tf_op jit(solution)/shard_map/all_to_all | solution.py:265
  688.9 8.5 copy.361
  697.3 13.0 gather_fusion.3
  716.4 44.0 %all-to-all-done.8 = bf16[1,2,768,2048]{3,1,0,2:T(2,128)(2,1)} async-done(((bf16[1,2,768,2048]{3,1,0,2:T(2,128)(2,1)}), bf16[1,2,768,2048]{3,1,0,2:T(2,128)(2,1)}, u32[]{:S(2)}, u32[]{:S(2)}) %all-to-all-start.8) | async-done | bytes 6291488 | tf_op jit(solution)/shard_map/all_to_all | solution.py:292
  760.4 8.4 copy.365
  768.8 12.7 gather_fusion.4
  781.5 6.8 convert_reduce_fusion
  803.3 9.7 convolution_convert_fusion.3
  813.0 67.7 %all-to-all-done.9 = bf16[4,128,2048]{2,1,0:T(8,128)(2,1)} async-done(((bf16[4,128,2048]{2,1,0:T(8,128)(2,1)}), bf16[4,128,2048]{2,1,0:T(8,128)(2,1)}, u32[]{:S(2)}, u32[]{:S(2)}) %all-to-all-start.9) | async-done | bytes 2097184 | tf_op jit(solution)/shard_map/all_to_all | solution.py:71
  887.1 16.8 %fusion = (f32[4,8,128]{2,1,0:T(8,128)}, f32[4,1024,128,8]{2,1,3,0:T(8,128)}) fusion(f32[4,1,8,128,1024]{3,4,2,0,1:T(8,128)} %get-tuple-element.70, f32[4,8,128]{2,1,0:T(8,128)} %log_add_fusion, bf16[4,1024,128,1]{2,1,3,0:T(8,128)(2,1)} %bitcast.405, bf16[4,128,8,128]{3,2,1,0:T(8,128)(2,1)} %bitcast.395), kind=kOutput, calls=%fused_computation.10 | convolution fusion | flops 1086320640 | bytes 35684352 | tf_op jit(solution)/shard_map/stkgd,sjkd->skgtj/dot_general | solution.py:23
  904.0 13.2 %fusion.6 = (bf16[4,8,128,1024]{2,3,1,0:T(8,128)(2,1)}, bf16[4,8,128,1024]{2,3,1,0:T(8,128)(2,1)}) fusion(f32[4,1024,128,8]{2,1,3,0:T(8,128)} %get-tuple-element.73, f32[4,1,8,128,1024]{3,4,2,0,1:T(8,128)S(1)} %bitcast.387, f32[4,8,128]{2,1,0:T(8,128)} %get-tuple-element.72, f32[4,8,128]{2,1,0:T(8,128)} %log_add_fusion), kind=kLoop, calls=%fused_computation.20 | loop fusion | flops 20971520 | bytes 50364416 | tf_op jit(solution)/shard_map/reshape.38
  917.1 6.9 fusion.38
  924.1 12.7 copy.379
  948.8 6.4 multiply_bitcast_fusion
  1003.5 106.5 %all-to-all-done.12 = bf16[4,512,1,1280]{3,1,2,0:T(8,128)(2,1)} async-done(((bf16[4,512,1,1280]{3,1,2,0:T(8,128)(2,1)}), bf16[4,512,1,1280]{3,1,2,0:T(8,128)(2,1)}, u32[]{:S(2)}, u32[]{:S(2)}) %all-to-all-start.12) | async-done | bytes 5242912 | tf_op jit(solution)/shard_map/all_to_all | solution.py:71
  1132.0 6.6 convolution_convert_fusion
  1139.9 8.5 all_to_all.131
  1179.8 12.5 all-to-all-done.13
  1195.1 39.0 %all-reduce = (f32[2048]{0:T(1024)}, f32[128]{0:T(128)}, f32[128]{0:T(128)}, f32[2048]{0:T(1024)}) all-reduce(f32[2048]{0:T(1024)S(1)} %bitcast.454, f32[128]{0:T(128)S(1)} %bitcast_reduce_fusion, f32[128]{0:T(128)S(1)} %copy-done.70, f32[2048]{0:T(1024)S(1)} %copy-done.56), channel_id=1, replica_groups=mesh['ctx'=8,'fsdp'=4] {'ctx','fsdp'}, use_global_device_ids=true, to_apply=%region_24.26 | all-reduce | flops 4352 | bytes 34816 | tf_op jit(solution)/shard_map/psum | solution.py:395
  1236.6 43.9 %all-reduce.4.cloned.1.call-done = (bf16[512,4096]{1,0:T(8,128)(2,1)}, bf16[512,512]{1,0:T(8,128)(2,1)}, bf16[512,512]{1,0:T(8,128)(2,1)}, bf16[1024,2048]{1,0:T(8,128)(2,1)}) async-done(((bf16[512,4096]{1,0:T(8,128)(2,1)}, bf16[512,512]{1,0:T(8,128)(2,1)}, bf16[512,512]{1,0:T(8,128)(2,1)}, bf16[1024,2048]{1,0:T(8,128)(2,1)}), (bf16[512,4096]{1,0:T(8,128)(2,1)}, bf16[512,512]{1,0:T(8,128)(2,1)}, ...) | async-done | bytes 9437200 | tf_op jit(solution)/shard_map/psum | solution.py:389
  1284.8 6.8 convert_element_type.233
  (385 shorter events, 268.2 us)
Async XLA Ops:
  7.2 530.1 %all-gather.6.cloned.1.call-start = ((), (), s32[]{:S(2)}) async-start(), calls=%async_computation.20 | async-start | bytes 7864320 | tf_op jit(solution)/shard_map/all_gather | solution.py:230
  150.3 5.3 collective-permute-start
  163.5 16.0 %copy-start.40 = (f32[128,64]{0,1:T(8,128)}, f32[128,64]{0,1:T(8,128)S(1)}, u32[]{:S(2)}) copy-start(f32[128,64]{0,1:T(8,128)S(1)} %get-tuple-element.67) | copy-start | bytes 98308
  163.5 16.0 %copy-start.42 = (f32[128,64]{0,1:T(8,128)}, f32[128,64]{0,1:T(8,128)S(1)}, u32[]{:S(2)}) copy-start(f32[128,64]{0,1:T(8,128)S(1)} %get-tuple-element.68) | copy-start | bytes 98308
  163.6 44.1 %copy-start.34 = (f32[128,64]{1,0:T(8,128)}, f32[128,64]{1,0:T(8,128)S(1)}, u32[]{:S(2)}) copy-start(f32[128,64]{1,0:T(8,128)S(1)} %copy.346) | copy-start | bytes 98308
  163.7 44.0 %copy-start.36 = (f32[128,64]{1,0:T(8,128)}, f32[128,64]{1,0:T(8,128)S(1)}, u32[]{:S(2)}) copy-start(f32[128,64]{1,0:T(8,128)S(1)} %copy.347) | copy-start | bytes 98308
  180.9 19.6 %all-to-all-start.2 = ((bf16[8,4,128,128]{3,2,1,0:T(8,128)(2,1)}), bf16[8,4,128,128]{3,2,1,0:T(8,128)(2,1)}, u32[]{:S(2)}, u32[]{:S(2)}) async-start(bf16[8,4,128,128]{3,2,1,0:T(8,128)(2,1)} %broadcast_in_dim.85), calls=%async_computation.2 | async-start | bytes 2097152 | tf_op jit(solution)/shard_map/all_to_all | solution.py:71
  191.5 16.2 %copy-start.2 = (f32[64,8,8,128]{3,2,1,0:T(8,128)}, f32[64,8,8,128]{3,2,1,0:T(8,128)S(1)}, u32[]{:S(2)}) copy-start(f32[64,8,8,128]{3,2,1,0:T(8,128)S(1)} %copy.425) | copy-start | bytes 6291460
  201.8 18.9 %all-to-all-start.1 = ((bf16[8,4,128,128]{2,3,1,0:T(8,128)(2,1)}), bf16[8,4,128,128]{2,3,1,0:T(8,128)(2,1)S(1)}, u32[]{:S(2)}, u32[]{:S(2)}) async-start(bf16[8,4,128,128]{2,3,1,0:T(8,128)(2,1)} %broadcast_in_dim.79), calls=%async_computation.1 | async-start | bytes 2097152 | tf_op jit(solution)/shard_map/all_to_all | solution.py:71
  205.4 342.5 %all-gather.4.cloned.1.call-start = ((), (), s32[]{:S(2)}) async-start(), calls=%async_computation.19 | async-start | bytes 7864320 | tf_op jit(solution)/shard_map/all_gather | solution.py:229
  209.8 14.8 %copy-start.14 = (bf16[4,128,8,64]{3,1,2,0:T(8,128)(2,1)S(1)}, bf16[4,128,8,64]{3,1,2,0:T(8,128)(2,1)}, u32[]{:S(2)}) copy-start(bf16[4,128,8,64]{3,1,2,0:T(8,128)(2,1)} %get-tuple-element.58) | copy-start | bytes 1572868
  211.2 22.6 %copy-start.8 = (bf16[4,8,128,128]{3,2,1,0:T(8,128)(2,1)}, bf16[4,8,128,128]{3,2,1,0:T(8,128)(2,1)S(1)}, u32[]{:S(2)}) copy-start(bf16[4,8,128,128]{3,2,1,0:T(8,128)(2,1)S(1)} %copy.343) | copy-start | bytes 3145732
  255.1 104.1 %copy-start.60 = (bf16[512,16]{0,1:T(8,128)(2,1)S(1)}, bf16[512,16]{0,1:T(8,128)(2,1)}, u32[]{:S(2)}) copy-start(bf16[512,16]{0,1:T(8,128)(2,1)} %param.31) | copy-start | bytes 49156
  255.1 111.2 %copy-start = (f32[1,128,2048]{2,1,0:T(8,128)S(1)}, f32[1,128,2048]{2,1,0:T(8,128)}, u32[]{:S(2)}) copy-start(f32[1,128,2048]{2,1,0:T(8,128)} %param.19) | copy-start | bytes 3145732
  255.1 104.1 %all-to-all-start.3 = ((bf16[4,1,128,2048]{3,2,1,0:T(8,128)(2,1)}), bf16[4,1,128,2048]{3,2,1,0:T(8,128)(2,1)S(1)}, u32[]{:S(2)}, u32[]{:S(2)}) async-start(bf16[4,1,128,2048]{3,2,1,0:T(8,128)(2,1)} %fusion.28), calls=%async_computation.3 | async-start | bytes 4194304 | tf_op jit(solution)/shard_map/all_to_all | solution.py:77
  258.8 108.6 %copy-start.47 = (f32[2048]{0:T(1024)S(1)}, f32[2048]{0:T(1024)}, u32[]{:S(2)}) copy-start(f32[2048]{0:T(1024)} %param.30) | copy-start | bytes 24580
  360.5 17.4 %all-to-all-start.4 = ((bf16[4,512,16]{1,2,0:T(8,128)(2,1)}), bf16[4,512,16]{1,2,0:T(8,128)(2,1)S(1)}, u32[]{:S(2)}, u32[]{:S(2)}) async-start(bf16[4,512,16]{1,2,0:T(8,128)(2,1)} %broadcast_in_dim.87), calls=%async_computation.4 | async-start | bytes 131072 | tf_op jit(solution)/shard_map/all_to_all | solution.py:71
  366.5 17.2 %copy-start.61 = (f32[128]{0:T(128)}, f32[128]{0:T(128)S(1)}, u32[]{:S(2)}) copy-start(f32[128]{0:T(128)S(1)} %add_rsqrt_fusion.2) | copy-start | bytes 1540
  377.9 76.4 %all-to-all-start.5 = ((bf16[8,2,96,2048]{3,2,1,0:T(8,128)(2,1)}), bf16[8,2,96,2048]{3,2,1,0:T(8,128)(2,1)}, u32[]{:S(2)}, u32[]{:S(2)}) async-start(bf16[8,2,96,2048]{3,2,1,0:T(8,128)(2,1)} %bitcast.393), calls=%async_computation.5 | async-start | bytes 12582912 | tf_op jit(solution)/shard_map/all_to_all | solution.py:252
  382.7 175.8 %all-gather.8.cloned.1.call-start = ((), (), s32[]{:S(2)}) async-start(), calls=%async_computation.21 | async-start | bytes 7864320 | tf_op jit(solution)/shard_map/all_gather | solution.py:231
  454.3 76.4 %all-to-all-start.7 = ((bf16[8,2,96,2048]{3,2,1,0:T(8,128)(2,1)}), bf16[8,2,96,2048]{3,2,1,0:T(8,128)(2,1)}, u32[]{:S(2)}, u32[]{:S(2)}) async-start(bf16[8,2,96,2048]{3,2,1,0:T(8,128)(2,1)} %bitcast.394), calls=%async_computation.7 | async-start | bytes 12582912 | tf_op jit(solution)/shard_map/all_to_all | solution.py:277
  459.1 710.5 %reduce-scatter.8.cloned.1.call-start = ((), (), s32[]{:S(2)}) async-start(), calls=%async_computation.24 | async-start | bytes 7864320 | tf_op jit(solution)/shard_map/reduce_scatter | solution.py:383
  547.9 25.5 %slice-start.5 = ((s8[6291456]{0:T(1024)(128)(4,1)}), s8[2097152]{0:T(1024)(128)(4,1)S(1)}, s32[]{:S(2)}) async-start(s8[6291456]{0:T(1024)(128)(4,1)} %bitcast.411), calls=%async_computation.31 | async-start | bytes 4194304
  558.5 14.9 %slice-start.6 = ((s8[6291456]{0:T(1024)(128)(4,1)}), s8[4194304]{0:T(1024)(128)(4,1)S(1)}, s32[]{:S(2)}) async-start(s8[6291456]{0:T(1024)(128)(4,1)} %bitcast.411), calls=%async_computation.32 | async-start | bytes 8388608
  607.6 76.4 %all-to-all-start.6 = ((bf16[1,2,768,2048]{3,1,0,2:T(2,128)(2,1)}), bf16[1,2,768,2048]{3,1,0,2:T(2,128)(2,1)}, u32[]{:S(2)}, u32[]{:S(2)}) async-start(bf16[1,2,768,2048]{3,1,0,2:T(2,128)(2,1)} %copy.360), calls=%async_computation.6 | async-start | bytes 12582912 | tf_op jit(solution)/shard_map/all_to_all | solution.py:265
  612.3 560.8 %reduce-scatter.6.cloned.1.call-start = ((), (), s32[]{:S(2)}) async-start(), calls=%async_computation.23 | async-start | bytes 7864320 | tf_op jit(solution)/shard_map/reduce_scatter | solution.py:380
  683.9 76.5 %all-to-all-start.8 = ((bf16[1,2,768,2048]{3,1,0,2:T(2,128)(2,1)}), bf16[1,2,768,2048]{3,1,0,2:T(2,128)(2,1)}, u32[]{:S(2)}, u32[]{:S(2)}) async-start(bf16[1,2,768,2048]{3,1,0,2:T(2,128)(2,1)} %copy.364), calls=%async_computation.8 | async-start | bytes 12582912 | tf_op jit(solution)/shard_map/all_to_all | solution.py:292
  768.8 19.5 %copy-start.39 = (bf16[4,2,8,512]{3,2,0,1:T(8,128)(2,1)S(1)}, bf16[4,2,8,512]{3,2,0,1:T(8,128)(2,1)}, u32[]{:S(2)}) copy-start(bf16[4,2,8,512]{3,2,0,1:T(8,128)(2,1)} %copy-done.38) | copy-start | bytes 196612
  768.8 19.5 %copy-start.48 = (f32[2048]{0:T(1024)S(1)}, f32[2048]{0:T(1024)}, u32[]{:S(2)}) copy-start(f32[2048]{0:T(1024)} %param.30) | copy-start | bytes 24580
  794.5 86.2 %all-to-all-start.9 = ((bf16[4,128,2048]{2,1,0:T(8,128)(2,1)}), bf16[4,128,2048]{2,1,0:T(8,128)(2,1)}, u32[]{:S(2)}, u32[]{:S(2)}) async-start(bf16[4,128,2048]{2,1,0:T(8,128)(2,1)} %broadcast_in_dim.94), calls=%async_computation.9 | async-start | bytes 4194304 | tf_op jit(solution)/shard_map/all_to_all | solution.py:71
  799.6 376.9 %reduce-scatter.4.cloned.1.call-start = ((), (), s32[]{:S(2)}) async-start(), calls=%async_computation.22 | async-start | bytes 7864320 | tf_op jit(solution)/shard_map/reduce_scatter | solution.py:377
  887.1 16.8 %slice-start = ((s8[16777216]{0:T(1024)(128)(4,1)}), s8[4194304]{0:T(1024)(128)(4,1)S(1)}, s32[]{:S(2)}) async-start(s8[16777216]{0:T(1024)(128)(4,1)} %bitcast.386), calls=%async_computation.26 | async-start | bytes 8388608
  887.1 16.8 %slice-start.1 = ((s8[16777216]{0:T(1024)(128)(4,1)}), s8[4194304]{0:T(1024)(128)(4,1)S(1)}, s32[]{:S(2)}) async-start(s8[16777216]{0:T(1024)(128)(4,1)} %bitcast.386), calls=%async_computation.27 | async-start | bytes 8388608
  887.1 16.8 %slice-start.2 = ((s8[16777216]{0:T(1024)(128)(4,1)}), s8[4194304]{0:T(1024)(128)(4,1)S(1)}, s32[]{:S(2)}) async-start(s8[16777216]{0:T(1024)(128)(4,1)} %bitcast.386), calls=%async_computation.28 | async-start | bytes 8388608
  887.1 16.8 %slice-start.3 = ((s8[16777216]{0:T(1024)(128)(4,1)}), s8[4194304]{0:T(1024)(128)(4,1)S(1)}, s32[]{:S(2)}) async-start(s8[16777216]{0:T(1024)(128)(4,1)} %bitcast.386), calls=%async_computation.29 | async-start | bytes 8388608
  903.9 13.2 %copy-start.15 = (bf16[4,128,8,64]{3,1,2,0:T(8,128)(2,1)S(1)}, bf16[4,128,8,64]{3,1,2,0:T(8,128)(2,1)}, u32[]{:S(2)}) copy-start(bf16[4,128,8,64]{3,1,2,0:T(8,128)(2,1)} %get-tuple-element.58) | copy-start | bytes 1572868
  944.5 19.6 %all-to-all-start.11 = ((bf16[4,8,128,128]{2,3,0,1:T(8,128)(2,1)}), bf16[4,8,128,128]{2,3,0,1:T(8,128)(2,1)}, u32[]{:S(2)}, u32[]{:S(2)}) async-start(bf16[4,8,128,128]{2,3,0,1:T(8,128)(2,1)} %copy.380), calls=%async_computation.11 | async-start | bytes 2097152 | tf_op jit(solution)/shard_map/all_to_all | solution.py:77
  955.2 13.2 %copy-start.3 = (f32[64,8,8,128]{3,2,1,0:T(8,128)S(1)}, f32[64,8,8,128]{3,2,1,0:T(8,128)}, u32[]{:S(2)}) copy-start(f32[64,8,8,128]{3,2,1,0:T(8,128)} %copy-done.2) | copy-start | bytes 6291460
  955.2 13.2 %copy-start.46 = (f32[4,128,8]{1,2,0:T(8,128)S(1)}, f32[4,128,8]{1,2,0:T(8,128)}, u32[]{:S(2)}) copy-start(f32[4,128,8]{1,2,0:T(8,128)} %copy-done.44) | copy-start | bytes 49156
  955.2 13.2 %copy-start.67 = (f32[128]{0:T(128)S(1)}, f32[128]{0:T(128)}, u32[]{:S(2)}) copy-start(f32[128]{0:T(128)} %param.27) | copy-start | bytes 1540
  964.2 19.6 %all-to-all-start.10 = ((bf16[4,8,128,128]{2,3,0,1:T(8,128)(2,1)}), bf16[4,8,128,128]{2,3,0,1:T(8,128)(2,1)}, u32[]{:S(2)}, u32[]{:S(2)}) async-start(bf16[4,8,128,128]{2,3,0,1:T(8,128)(2,1)} %copy.375), calls=%async_computation.10 | async-start | bytes 2097152 | tf_op jit(solution)/shard_map/all_to_all | solution.py:77
  991.4 118.7 %all-to-all-start.12 = ((bf16[4,512,1,1280]{3,1,2,0:T(8,128)(2,1)}), bf16[4,512,1,1280]{3,1,2,0:T(8,128)(2,1)}, u32[]{:S(2)}, u32[]{:S(2)}) async-start(bf16[4,512,1,1280]{3,1,2,0:T(8,128)(2,1)} %broadcast_in_dim.162), calls=%async_computation.12 | async-start | bytes 10485760 | tf_op jit(solution)/shard_map/all_to_all | solution.py:71
  996.6 284.0 %all-reduce.4.cloned.1.call-start = ((), (), s32[]{:S(2)}) async-start(), calls=%async_computation.25 | async-start | bytes 18874368 | tf_op jit(solution)/shard_map/psum | solution.py:389
  1149.1 14.6 %all-to-all-start.15 = ((f32[8,1,512,16]{2,3,1,0:T(8,128)}), f32[8,1,512,16]{2,3,1,0:T(8,128)S(1)}, u32[]{:S(2)}, u32[]{:S(2)}) async-start(f32[8,1,512,16]{2,3,1,0:T(8,128)} %broadcast_in_dim.164), calls=%async_computation.15 | async-start | bytes 524288 | tf_op jit(solution)/shard_map/all_to_all | solution.py:71
  1163.7 28.5 %all-to-all-start.13 = ((f32[4,128,512]{2,1,0:T(8,128)}), f32[4,128,512]{2,1,0:T(8,128)S(1)}, u32[]{:S(2)}, u32[]{:S(2)}) async-start(f32[4,128,512]{2,1,0:T(8,128)} %bitcast.102), calls=%async_computation.13 | async-start | bytes 2097152 | tf_op jit(solution)/shard_map/all_to_all | solution.py:371
  1176.4 16.2 %copy-start.69 = (f32[128]{0:T(128)S(1)}, f32[128]{0:T(128)}, u32[]{:S(2)}) copy-start(f32[128]{0:T(128)} %copy-done.68) | copy-start | bytes 1540
  1179.8 15.3 %copy-start.56 = (f32[2048]{0:T(1024)S(1)}, f32[2048]{0:T(1024)}, u32[]{:S(2)}) copy-start(f32[2048]{0:T(1024)} %get-tuple-element.25) | copy-start | bytes 24580
  1179.8 15.3 %copy-start.70 = (f32[128]{0:T(128)S(1)}, f32[128]{0:T(128)}, u32[]{:S(2)}) copy-start(f32[128]{0:T(128)} %get-tuple-element.23) | copy-start | bytes 1540
  (56 other events, 354.4 us)
Sparse Core Ops, SparseCore 0:
  162.8 134.8 all-gather.5
  299.3 126.0 all-gather.3
  427.0 113.5 all-gather.7
  580.6 110.3 reduce-scatter.7
  693.1 114.5 reduce-scatter.5
  813.1 127.7 reduce-scatter.3
  1138.7 141.7 all-reduce.3

commit v6 on v5

--- a/solution.py
+++ b/solution.py
@@ -2,6 +2,7 @@
 import jax.numpy as jnp
 from jax import lax
 from jax.sharding import PartitionSpec as P
+
 
 D = 2048
 HEADS = 32
@@ -375,21 +376,17 @@
     grad_hidden = grad_hidden + grad_middle
     gate_grad, up_grad, down_grad = (
         lax.psum_scatter(
-            gate_grad_full.astype(jnp.bfloat16), "fsdp", scatter_dimension=1, tiled=True
-        ).astype(jnp.float32),
-        lax.psum_scatter(
-            up_grad_full.astype(jnp.bfloat16), "fsdp", scatter_dimension=1, tiled=True
-        ).astype(jnp.float32),
-        lax.psum_scatter(
-            down_grad_full.astype(jnp.bfloat16), "fsdp", scatter_dimension=1, tiled=True
-        ).astype(jnp.float32),
+            full.astype(jnp.bfloat16), "fsdp", scatter_dimension=1, tiled=True
+        ).astype(jnp.float32)
+        for full in (gate_grad_full, up_grad_full, down_grad_full)
     )
     router_shard = scatter_sum_a2a(router_grad_full, "fsdp", fsdp_size, 0)
-    query_grad, key_grad, value_grad, out_grad, router_grad = (
+    out_grad = lax.psum(out_grad_part.astype(jnp.bfloat16), "ctx").astype(jnp.float32)
+    query_grad_part, out_grad = lax.optimization_barrier((query_grad_part, out_grad))
+    query_grad, key_grad, value_grad, router_grad = (
         lax.psum(query_grad_part.astype(jnp.bfloat16), "ctx").astype(jnp.float32),
         lax.psum(key_grad_part.astype(jnp.bfloat16), "ctx").astype(jnp.float32),
         lax.psum(value_grad_part.astype(jnp.bfloat16), "ctx").astype(jnp.float32),
-        lax.psum(out_grad_part.astype(jnp.bfloat16), "ctx").astype(jnp.float32),
         jnp.sum(gather_a2a(router_shard[None], "ctx", ctx_size, 0), axis=0),
     )
     attn_gain_total, query_gain_total, key_gain_total, ffn_gain_total = lax.psum(

time: 1320 us -> 1510 us (1.14)
  waiting for transfers between devices: 539 us -> 733 us
    reduce_scatter x3, waiting for transfers between devices: 0.02 us -> 100 us  [per_device(): lax.psum_scatter(full.astype(jnp.bfloat16), 'fsdp', scatter_dimension=1,...]
    all_to_all x6, waiting for transfers between devices: 195 us -> 283 us  [gather_a2a(): lax.all_to_all(rep, axis_name, 0, 0, tiled=True)]
    all_to_all x3 -> x4, waiting for transfers between devices: 104 us -> 110 us  [scatter_sum_a2a(): got = lax.all_to_all(parts, axis_name, axis, axis, tiled=True)]
  transfers between devices with their start and end apart: 22 -> 24, of which waited for: 15 -> 15; matrix products, arithmetic and copies ran while one was open for 34% -> 26% of each run, Pallas kernels for 0% -> 0%
where the time goes in v6:
time: 1510 us; the launch traced here: 1500 us
  waiting for transfers between devices  733 us (49%)
  local copies, waits for them, and re-layouts  214 us (14%)
  matrix products  192 us (13%)
  blocking collectives  158 us (10%)
  other arithmetic  122 us (8%)
  starting transfers between devices  65.7 us (4%)
  between operations  15.7 us (1%)
    all_to_all x6, waiting for transfers between devices, gather_a2a(): lax.all_to_all(rep, axis_name, 0, 0, tiled=True)  283 us
    dot_general x25, matrix products, contract(): return jnp.einsum(form, left, right, preferred_element_type=jnp.float32)  173 us
    all_to_all x1, blocking collectives, per_device(): got = lax.all_to_all(payload, 'fsdp', 0, 0, tiled=True)  111 us
    all_to_all x4, waiting for transfers between devices, scatter_sum_a2a(): got = lax.all_to_all(parts, axis_name, axis, axis, tiled=True)  110 us
    reduce_scatter x3, waiting for transfers between devices, per_device(): lax.psum_scatter(full.astype(jnp.bfloat16), 'fsdp', scatter_dimension=1,...  100 us
    all_to_all x1, waiting for transfers between devices, per_device(): lax.all_to_all(dispatch(grad_routes), 'ctx', split_axis=0, concat_axis=2,...  64.9 us
    all_to_all x1, waiting for transfers between devices, per_device(): lax.all_to_all(dispatch(jnp.repeat(second_input, TOP, axis=0)), 'ctx', sp...  51.8 us
    psum x1, waiting for transfers between devices, per_device(): lax.psum(query_grad_part.astype(jnp.bfloat16), 'ctx').astype(jnp.float32)  47.1 us
  transfers between devices with their start and end apart: 24, of which 15 were waited for; matrix products, arithmetic and copies ran while one was open for 26% of the time, Pallas kernels for 0%

profile of v6, /device:TPU:0, one launch (start us, length us, event | category | flops | bytes accessed | tf_op | source)
XLA Modules:
  0.0 1500.3 jit_solution(14030890438357927869)
XLA Ops:
  13.2 7.8 reshape.788
  33.2 110.7 %all_to_all.130 = bf16[4,4616,128]{2,1,0:T(8,128)(2,1)S(1)} all-to-all(bf16[4,4616,128]{2,1,0:T(8,128)(2,1)S(1)} %pad_maximum_fusion), channel_id=1, replica_groups=mesh['ctx'=8,'fsdp'=4] {'fsdp'}, dimensions={0} | all-to-all | bytes 9453568 | tf_op jit(solution)/shard_map/all_to_all | solution.py:152
  155.5 7.4 maximum_select_fusion
  191.7 9.1 all-to-all-done.2
  211.7 9.2 all-to-all-done.1
  224.9 9.2 fusion.99
  234.1 8.6 fusion.3
  242.7 7.8 fusion.41
  264.6 94.8 %all-to-all-done.3 = bf16[4,1,128,2048]{3,2,1,0:T(8,128)(2,1)S(1)} async-done(((bf16[4,1,128,2048]{3,2,1,0:T(8,128)(2,1)}), bf16[4,1,128,2048]{3,2,1,0:T(8,128)(2,1)S(1)}, u32[]{:S(2)}, u32[]{:S(2)}) %all-to-all-start.3) | async-done | bytes 2097184 | tf_op jit(solution)/shard_map/all_to_all | solution.py:78
  367.6 10.2 scatter_custom_fusion
  383.9 7.0 gather_fusion.2
  391.8 10.7 scatter_custom_fusion.1
  402.4 51.8 %all-to-all-done.5 = bf16[8,2,96,2048]{3,2,1,0:T(8,128)(2,1)} async-done(((bf16[8,2,96,2048]{3,2,1,0:T(8,128)(2,1)}), bf16[8,2,96,2048]{3,2,1,0:T(8,128)(2,1)}, u32[]{:S(2)}, u32[]{:S(2)}) %all-to-all-start.5) | async-done | bytes 6291488 | tf_op jit(solution)/shard_map/all_to_all | solution.py:253
  459.4 6.7 copy.359
  466.1 64.9 %all-to-all-done.7 = bf16[8,2,96,2048]{3,2,1,0:T(8,128)(2,1)} async-done(((bf16[8,2,96,2048]{3,2,1,0:T(8,128)(2,1)}), bf16[8,2,96,2048]{3,2,1,0:T(8,128)(2,1)}, u32[]{:S(2)}, u32[]{:S(2)}) %all-to-all-start.7) | async-done | bytes 6291488 | tf_op jit(solution)/shard_map/all_to_all | solution.py:278
  531.0 6.6 copy.363
  537.6 10.3 fusion.102
  547.9 10.4 fusion.101
  558.4 13.9 multiply_convert_fusion
  572.2 7.0 convert_bitcast_fusion
  579.2 18.8 %copy.360 = bf16[1,2,768,2048]{3,1,0,2:T(2,128)(2,1)} copy(bf16[1,2,768,2048]{3,2,1,0:T(8,128)(2,1)S(1)} %convert_bitcast_fusion) | data formatting | bytes 12582912 | tf_op jit(solution)/shard_map/broadcast_in_dim | solution.py:266
  602.9 10.7 fusion.103
  613.7 9.9 fusion.10
  623.6 18.8 %copy.364 = bf16[1,2,768,2048]{3,1,0,2:T(2,128)(2,1)} copy(bf16[1,2,768,2048]{3,2,1,0:T(8,128)(2,1)S(1)} %fusion.10) | data formatting | bytes 12582912 | tf_op jit(solution)/shard_map/broadcast_in_dim | solution.py:293
  642.4 32.1 %all-to-all-done.6 = bf16[1,2,768,2048]{3,1,0,2:T(2,128)(2,1)} async-done(((bf16[1,2,768,2048]{3,1,0,2:T(2,128)(2,1)}), bf16[1,2,768,2048]{3,1,0,2:T(2,128)(2,1)}, u32[]{:S(2)}, u32[]{:S(2)}) %all-to-all-start.6) | async-done | bytes 6291488 | tf_op jit(solution)/shard_map/all_to_all | solution.py:266
  679.3 8.3 copy.361
  687.6 12.6 gather_fusion.3
  709.8 41.0 %all-to-all-done.8 = bf16[1,2,768,2048]{3,1,0,2:T(2,128)(2,1)} async-done(((bf16[1,2,768,2048]{3,1,0,2:T(2,128)(2,1)}), bf16[1,2,768,2048]{3,1,0,2:T(2,128)(2,1)}, u32[]{:S(2)}, u32[]{:S(2)}) %all-to-all-start.8) | async-done | bytes 6291488 | tf_op jit(solution)/shard_map/all_to_all | solution.py:293
  750.8 8.3 copy.365
  759.1 12.8 gather_fusion.4
  772.0 6.7 convert_reduce_fusion
  791.0 42.9 %all-to-all-done.9 = bf16[4,128,2048]{2,1,0:T(8,128)(2,1)S(1)} async-done(((bf16[4,128,2048]{2,1,0:T(8,128)(2,1)}), bf16[4,128,2048]{2,1,0:T(8,128)(2,1)S(1)}, u32[]{:S(2)}, u32[]{:S(2)}) %all-to-all-start.9) | async-done | bytes 2097184 | tf_op jit(solution)/shard_map/all_to_all | solution.py:72
  840.3 9.6 convolution_convert_fusion
  850.0 9.7 convolution_convert_fusion.1
  863.9 9.8 convolution_convert_fusion.2
  880.2 14.4 fusion
  897.2 13.4 fusion.6
  910.7 7.1 fusion.38
  917.7 12.6 copy.379
  984.6 8.1 all-to-all-done.14
  1000.5 6.7 convert_element_type.233
  1007.1 222.0 %all-to-all-done.12 = bf16[4,512,1,1280]{3,1,2,0:T(8,128)(2,1)} async-done(((bf16[4,512,1,1280]{3,1,2,0:T(8,128)(2,1)}), bf16[4,512,1,1280]{3,1,2,0:T(8,128)(2,1)}, u32[]{:S(2)}, u32[]{:S(2)}) %all-to-all-start.12) | async-done | bytes 5242912 | tf_op jit(solution)/shard_map/all_to_all | solution.py:72
  1248.0 6.6 fusion.71
  1257.3 7.0 fusion.104
  1279.7 100.2 %reduce-scatter.4.cloned.1.call-done = bf16[2,512,768]{2,1,0:T(8,128)(2,1)} async-done(((bf16[2,2048,768]{2,1,0:T(8,128)(2,1)}), bf16[2,512,768]{2,1,0:T(8,128)(2,1)}) %reduce-scatter.4.cloned.1.call-update) | async-done | bytes 1572880 | tf_op jit(solution)/shard_map/reduce_scatter | solution.py:378
  1385.8 47.0 %all-reduce = (f32[2048]{0:T(1024)}, f32[128]{0:T(128)}, f32[128]{0:T(128)}, f32[2048]{0:T(1024)}) all-reduce(f32[2048]{0:T(1024)S(1)} %bitcast.455, f32[128]{0:T(128)S(1)} %bitcast_reduce_fusion, f32[128]{0:T(128)S(1)} %get-tuple-element.27, f32[2048]{0:T(1024)S(1)} %copy-done.49), channel_id=1, replica_groups=mesh['ctx'=8,'fsdp'=4] {'ctx','fsdp'}, use_global_device_ids=true, to_apply=%region_24.26 | all-reduce | flops 4352 | bytes 34816 | tf_op jit(solution)/shard_map/psum | solution.py:392
  1435.3 47.1 %all-reduce.7.cloned.1.call-done = (bf16[512,4096]{1,0:T(8,128)(2,1)}, bf16[512,512]{1,0:T(8,128)(2,1)}, bf16[512,512]{1,0:T(8,128)(2,1)}) async-done(((bf16[512,4096]{1,0:T(8,128)(2,1)}, bf16[512,512]{1,0:T(8,128)(2,1)}, bf16[512,512]{1,0:T(8,128)(2,1)}), (bf16[512,4096]{1,0:T(8,128)(2,1)}, bf16[512,512]{1,0:T(8,128)(2,1)}, bf16[512,512]{1,0:T(8,128)(2,1)})) %all-reduce.7.cloned.1.call-update) | async-done | bytes 5242896 | tf_op jit(solution)/shard_map/psum | solution.py:387
  1486.6 6.7 convert_element_type.235
  (356 shorter events, 269.5 us)
Async XLA Ops:
  7.2 530.4 %all-gather.6.cloned.1.call-start = ((), (), s32[]{:S(2)}) async-start(), calls=%async_computation.20 | async-start | bytes 7864320 | tf_op jit(solution)/shard_map/all_gather | solution.py:231
  150.3 5.3 collective-permute-start
  163.7 16.0 %copy-start.34 = (f32[128,64]{0,1:T(8,128)}, f32[128,64]{0,1:T(8,128)S(1)}, u32[]{:S(2)}) copy-start(f32[128,64]{0,1:T(8,128)S(1)} %get-tuple-element.70) | copy-start | bytes 98308
  163.7 16.0 %copy-start.36 = (f32[128,64]{0,1:T(8,128)}, f32[128,64]{0,1:T(8,128)S(1)}, u32[]{:S(2)}) copy-start(f32[128,64]{0,1:T(8,128)S(1)} %get-tuple-element.71) | copy-start | bytes 98308
  163.8 44.3 %copy-start.30 = (f32[128,64]{1,0:T(8,128)}, f32[128,64]{1,0:T(8,128)S(1)}, u32[]{:S(2)}) copy-start(f32[128,64]{1,0:T(8,128)S(1)} %copy.346) | copy-start | bytes 98308
  163.9 44.2 %copy-start.32 = (f32[128,64]{1,0:T(8,128)}, f32[128,64]{1,0:T(8,128)S(1)}, u32[]{:S(2)}) copy-start(f32[128,64]{1,0:T(8,128)S(1)} %copy.347) | copy-start | bytes 98308
  178.6 12.4 copy-start.9
  181.2 19.6 %all-to-all-start.2 = ((bf16[8,4,128,128]{3,2,1,0:T(8,128)(2,1)}), bf16[8,4,128,128]{3,2,1,0:T(8,128)(2,1)}, u32[]{:S(2)}, u32[]{:S(2)}) async-start(bf16[8,4,128,128]{3,2,1,0:T(8,128)(2,1)} %broadcast_in_dim.85), calls=%async_computation.2 | async-start | bytes 2097152 | tf_op jit(solution)/shard_map/all_to_all | solution.py:72
  191.7 16.5 %copy-start.2 = (f32[64,8,8,128]{3,2,1,0:T(8,128)}, f32[64,8,8,128]{3,2,1,0:T(8,128)S(1)}, u32[]{:S(2)}) copy-start(f32[64,8,8,128]{3,2,1,0:T(8,128)S(1)} %copy.425) | copy-start | bytes 6291460
  202.0 18.9 %all-to-all-start.1 = ((bf16[8,4,128,128]{2,3,1,0:T(8,128)(2,1)}), bf16[8,4,128,128]{2,3,1,0:T(8,128)(2,1)S(1)}, u32[]{:S(2)}, u32[]{:S(2)}) async-start(bf16[8,4,128,128]{2,3,1,0:T(8,128)(2,1)} %broadcast_in_dim.79), calls=%async_computation.1 | async-start | bytes 2097152 | tf_op jit(solution)/shard_map/all_to_all | solution.py:72
  205.6 342.3 %all-gather.4.cloned.1.call-start = ((), (), s32[]{:S(2)}) async-start(), calls=%async_computation.19 | async-start | bytes 7864320 | tf_op jit(solution)/shard_map/all_gather | solution.py:230
  210.3 14.6 copy-start.13
  211.7 22.3 %copy-start.7 = (bf16[4,8,128,128]{3,2,1,0:T(8,128)(2,1)}, bf16[4,8,128,128]{3,2,1,0:T(8,128)(2,1)S(1)}, u32[]{:S(2)}) copy-start(bf16[4,8,128,128]{3,2,1,0:T(8,128)(2,1)S(1)} %copy.343) | copy-start | bytes 3145732
  220.9 13.1 copy-start.11
  255.3 104.1 %copy-start.51 = (bf16[512,16]{0,1:T(8,128)(2,1)S(1)}, bf16[512,16]{0,1:T(8,128)(2,1)}, u32[]{:S(2)}) copy-start(bf16[512,16]{0,1:T(8,128)(2,1)} %param.31) | copy-start | bytes 49156
  255.3 111.0 %copy-start = (f32[1,128,2048]{2,1,0:T(8,128)S(1)}, f32[1,128,2048]{2,1,0:T(8,128)}, u32[]{:S(2)}) copy-start(f32[1,128,2048]{2,1,0:T(8,128)} %param.19) | copy-start | bytes 3145732
  255.3 104.1 %all-to-all-start.3 = ((bf16[4,1,128,2048]{3,2,1,0:T(8,128)(2,1)}), bf16[4,1,128,2048]{3,2,1,0:T(8,128)(2,1)S(1)}, u32[]{:S(2)}, u32[]{:S(2)}) async-start(bf16[4,1,128,2048]{3,2,1,0:T(8,128)(2,1)} %fusion.28), calls=%async_computation.3 | async-start | bytes 4194304 | tf_op jit(solution)/shard_map/all_to_all | solution.py:78
  259.1 108.4 %copy-start.41 = (f32[2048]{0:T(1024)S(1)}, f32[2048]{0:T(1024)}, u32[]{:S(2)}) copy-start(f32[2048]{0:T(1024)} %param.30) | copy-start | bytes 24580
  360.7 17.2 %all-to-all-start.4 = ((bf16[4,512,16]{1,2,0:T(8,128)(2,1)}), bf16[4,512,16]{1,2,0:T(8,128)(2,1)S(1)}, u32[]{:S(2)}, u32[]{:S(2)}) async-start(bf16[4,512,16]{1,2,0:T(8,128)(2,1)} %broadcast_in_dim.87), calls=%async_computation.4 | async-start | bytes 131072 | tf_op jit(solution)/shard_map/all_to_all | solution.py:72
  377.9 76.3 %all-to-all-start.5 = ((bf16[8,2,96,2048]{3,2,1,0:T(8,128)(2,1)}), bf16[8,2,96,2048]{3,2,1,0:T(8,128)(2,1)}, u32[]{:S(2)}, u32[]{:S(2)}) async-start(bf16[8,2,96,2048]{3,2,1,0:T(8,128)(2,1)} %bitcast.393), calls=%async_computation.5 | async-start | bytes 12582912 | tf_op jit(solution)/shard_map/all_to_all | solution.py:253
  382.7 175.7 %all-gather.8.cloned.1.call-start = ((), (), s32[]{:S(2)}) async-start(), calls=%async_computation.21 | async-start | bytes 7864320 | tf_op jit(solution)/shard_map/all_gather | solution.py:232
  454.2 76.7 %all-to-all-start.7 = ((bf16[8,2,96,2048]{3,2,1,0:T(8,128)(2,1)}), bf16[8,2,96,2048]{3,2,1,0:T(8,128)(2,1)}, u32[]{:S(2)}, u32[]{:S(2)}) async-start(bf16[8,2,96,2048]{3,2,1,0:T(8,128)(2,1)} %bitcast.394), calls=%async_computation.7 | async-start | bytes 12582912 | tf_op jit(solution)/shard_map/all_to_all | solution.py:278
  558.3 13.9 copy-start.57
  598.0 76.5 %all-to-all-start.6 = ((bf16[1,2,768,2048]{3,1,0,2:T(2,128)(2,1)}), bf16[1,2,768,2048]{3,1,0,2:T(2,128)(2,1)}, u32[]{:S(2)}, u32[]{:S(2)}) async-start(bf16[1,2,768,2048]{3,1,0,2:T(2,128)(2,1)} %copy.360), calls=%async_computation.6 | async-start | bytes 12582912 | tf_op jit(solution)/shard_map/all_to_all | solution.py:266
  602.9 10.8 copy-start.60
  674.5 76.3 %all-to-all-start.8 = ((bf16[1,2,768,2048]{3,1,0,2:T(2,128)(2,1)}), bf16[1,2,768,2048]{3,1,0,2:T(2,128)(2,1)}, u32[]{:S(2)}, u32[]{:S(2)}) async-start(bf16[1,2,768,2048]{3,1,0,2:T(2,128)(2,1)} %copy.364), calls=%async_computation.8 | async-start | bytes 12582912 | tf_op jit(solution)/shard_map/all_to_all | solution.py:293
  783.5 50.3 %all-to-all-start.9 = ((bf16[4,128,2048]{2,1,0:T(8,128)(2,1)}), bf16[4,128,2048]{2,1,0:T(8,128)(2,1)S(1)}, u32[]{:S(2)}, u32[]{:S(2)}) async-start(bf16[4,128,2048]{2,1,0:T(8,128)(2,1)} %broadcast_in_dim.94), calls=%async_computation.9 | async-start | bytes 4194304 | tf_op jit(solution)/shard_map/all_to_all | solution.py:72
  788.6 211.9 %all-reduce.5.cloned.1.call-start = ((), (), s32[]{:S(2)}) async-start(), calls=%async_computation.22 | async-start | bytes 8388608 | tf_op jit(solution)/shard_map/psum | solution.py:384
  840.2 432.7 %reduce-scatter.8.cloned.1.call-start = ((), (), s32[]{:S(2)}) async-start(), calls=%async_computation.25 | async-start | bytes 7864320 | tf_op jit(solution)/shard_map/reduce_scatter | solution.py:378
  850.0 426.4 %reduce-scatter.6.cloned.1.call-start = ((), (), s32[]{:S(2)}) async-start(), calls=%async_computation.24 | async-start | bytes 7864320 | tf_op jit(solution)/shard_map/reduce_scatter | solution.py:378
  859.8 520.1 %reduce-scatter.4.cloned.1.call-start = ((), (), s32[]{:S(2)}) async-start(), calls=%async_computation.23 | async-start | bytes 7864320 | tf_op jit(solution)/shard_map/reduce_scatter | solution.py:378
  880.2 14.4 slice-start
  880.2 14.4 slice-start.1
  880.2 15.8 %slice-start.2 = ((s8[16777216]{0:T(1024)(128)(4,1)}), s8[4194304]{0:T(1024)(128)(4,1)S(1)}, s32[]{:S(2)}) async-start(s8[16777216]{0:T(1024)(128)(4,1)} %bitcast.386), calls=%async_computation.29 | async-start | bytes 8388608
  880.2 17.0 %slice-start.3 = ((s8[16777216]{0:T(1024)(128)(4,1)}), s8[4194304]{0:T(1024)(128)(4,1)S(1)}, s32[]{:S(2)}) async-start(s8[16777216]{0:T(1024)(128)(4,1)} %bitcast.386), calls=%async_computation.30 | async-start | bytes 8388608
  897.2 13.5 copy-start.14
  897.2 13.5 copy-start.15
  936.9 20.6 %all-to-all-start.11 = ((bf16[4,8,128,128]{2,3,0,1:T(8,128)(2,1)}), bf16[4,8,128,128]{2,3,0,1:T(8,128)(2,1)S(1)}, u32[]{:S(2)}, u32[]{:S(2)}) async-start(bf16[4,8,128,128]{2,3,0,1:T(8,128)(2,1)} %copy.380), calls=%async_computation.11 | async-start | bytes 2097152 | tf_op jit(solution)/shard_map/all_to_all | solution.py:78
  951.3 10.5 copy-start.40
  957.5 19.6 %all-to-all-start.10 = ((bf16[4,8,128,128]{2,3,0,1:T(8,128)(2,1)}), bf16[4,8,128,128]{2,3,0,1:T(8,128)(2,1)}, u32[]{:S(2)}, u32[]{:S(2)}) async-start(bf16[4,8,128,128]{2,3,0,1:T(8,128)(2,1)} %copy.375), calls=%async_computation.10 | async-start | bytes 2097152 | tf_op jit(solution)/shard_map/all_to_all | solution.py:78
  970.2 12.1 copy-start.35
  970.2 12.1 copy-start.37
  977.2 15.5 %all-to-all-start.14 = ((f32[4,512,16]{1,2,0:T(8,128)}), f32[4,512,16]{1,2,0:T(8,128)S(1)}, u32[]{:S(2)}, u32[]{:S(2)}) async-start(f32[4,512,16]{1,2,0:T(8,128)} %fusion.83), calls=%async_computation.14 | async-start | bytes 262144 | tf_op jit(solution)/shard_map/all_to_all | solution.py:78
  995.4 233.8 %all-to-all-start.12 = ((bf16[4,512,1,1280]{3,1,2,0:T(8,128)(2,1)}), bf16[4,512,1,1280]{3,1,2,0:T(8,128)(2,1)}, u32[]{:S(2)}, u32[]{:S(2)}) async-start(bf16[4,512,1,1280]{3,1,2,0:T(8,128)(2,1)} %broadcast_in_dim.162), calls=%async_computation.12 | async-start | bytes 10485760 | tf_op jit(solution)/shard_map/all_to_all | solution.py:72
  1229.9 37.4 %all-to-all-start.15 = ((f32[8,1,512,16]{2,3,1,0:T(8,128)}), f32[8,1,512,16]{2,3,1,0:T(8,128)S(1)}, u32[]{:S(2)}, u32[]{:S(2)}) async-start(f32[8,1,512,16]{2,3,1,0:T(8,128)} %broadcast_in_dim.164), calls=%async_computation.15 | async-start | bytes 524288 | tf_op jit(solution)/shard_map/all_to_all | solution.py:72
  1233.3 249.0 %all-reduce.7.cloned.1.call-start = ((), (), s32[]{:S(2)}) async-start(), calls=%async_computation.26 | async-start | bytes 10485760 | tf_op jit(solution)/shard_map/psum | solution.py:387
  1267.3 115.9 %all-to-all-start.13 = ((f32[4,128,512]{2,1,0:T(8,128)}), f32[4,128,512]{2,1,0:T(8,128)S(1)}, u32[]{:S(2)}, u32[]{:S(2)}) async-start(f32[4,128,512]{2,1,0:T(8,128)} %bitcast.417), calls=%async_computation.13 | async-start | bytes 2097152 | tf_op jit(solution)/shard_map/all_to_all | solution.py:372
  1279.7 103.8 %copy-start.56 = (f32[128]{0:T(128)S(1)}, f32[128]{0:T(128)}, u32[]{:S(2)}) copy-start(f32[128]{0:T(128)} %copy-done.55) | copy-start | bytes 1540
  (42 other events, 206.6 us)
Sparse Core Ops, SparseCore 0:
  163.1 134.8 all-gather.5
  299.6 126.0 all-gather.3
  427.2 113.5 all-gather.7
  840.4 81.1 all-reduce.4
  923.7 159.2 reduce-scatter.7
  1085.1 156.0 reduce-scatter.5
  1243.5 136.2 reduce-scatter.3
  1384.0 98.3 all-reduce.6

commit v7 on v6

--- a/solution.py
+++ b/solution.py
@@ -247,23 +247,26 @@
         buffer = jnp.zeros((experts * capacity, D), jnp.bfloat16).at[target].set(route_rows)
         return buffer.reshape(ctx_size, local_experts, capacity, D)
 
+    def to_experts(buffer):
+        got = lax.all_to_all(buffer, "ctx", 0, 0, tiled=True)
+        return got.transpose(1, 0, 2, 3).reshape(local_experts, ctx_size * capacity, D)
+
+    def from_experts(rows):
+        parts = rows.reshape(local_experts, ctx_size, capacity, D).transpose(1, 0, 2, 3)
+        back = lax.all_to_all(parts, "ctx", 0, 0, tiled=True)
+        return back.reshape(experts * capacity, D)
+
     def collect(returned):
-        return jnp.take(returned.reshape(experts * capacity, D), target, axis=0)
-
-    received = lax.all_to_all(
-        dispatch(jnp.repeat(second_input, TOP, axis=0)),
-        "ctx",
-        split_axis=0,
-        concat_axis=2,
-        tiled=True,
-    )[0]
+        return jnp.take(returned, target, axis=0)
+
+    received = to_experts(dispatch(jnp.repeat(second_input, TOP, axis=0)))
     gate_val = contract("erd,edf->erf", received, w_gate)
     up_val = contract("erd,edf->erf", received, w_up)
     gate_sig = jax.nn.sigmoid(gate_val)
     hid_low = (gate_val * gate_sig * up_val).astype(jnp.bfloat16)
     expert_out = contract("erf,efd->erd", hid_low, w_down).astype(jnp.bfloat16)
     route_out = (
-        collect(lax.all_to_all(expert_out[None], "ctx", split_axis=2, concat_axis=0, tiled=True))
+        collect(from_experts(expert_out))
         .reshape(tokens, TOP, D)
         .astype(jnp.float32)
     )
@@ -275,9 +278,7 @@
         .astype(jnp.bfloat16)
         .reshape(tokens * TOP, D)
     )
-    grad_expert = lax.all_to_all(
-        dispatch(grad_routes), "ctx", split_axis=0, concat_axis=2, tiled=True
-    )[0]
+    grad_expert = to_experts(dispatch(grad_routes))
     grad_hid = contract("erd,efd->erf", grad_expert, w_down)
     down_grad_full = contract("erf,erd->efd", hid_low, grad_expert)
     grad_gate = (grad_hid * up_val * gate_sig * (1.0 + gate_val * (1.0 - gate_sig))).astype(
@@ -289,9 +290,7 @@
     grad_rows = (
         contract("erf,edf->erd", grad_gate, w_gate) + contract("erf,edf->erd", grad_up, w_up)
     ).astype(jnp.bfloat16)
-    grad_copies = collect(
-        lax.all_to_all(grad_rows[None], "ctx", split_axis=2, concat_axis=0, tiled=True)
-    ).reshape(tokens, TOP, D)
+    grad_copies = collect(from_experts(grad_rows)).reshape(tokens, TOP, D)
     grad_chosen = route_weights * (
         grad_weights - jnp.sum(route_weights * grad_weights, axis=-1, keepdims=True)
     )
@@ -381,14 +380,12 @@
         for full in (gate_grad_full, up_grad_full, down_grad_full)
     )
     router_shard = scatter_sum_a2a(router_grad_full, "fsdp", fsdp_size, 0)
-    out_grad = lax.psum(out_grad_part.astype(jnp.bfloat16), "ctx").astype(jnp.float32)
-    query_grad_part, out_grad = lax.optimization_barrier((query_grad_part, out_grad))
-    query_grad, key_grad, value_grad, router_grad = (
-        lax.psum(query_grad_part.astype(jnp.bfloat16), "ctx").astype(jnp.float32),
-        lax.psum(key_grad_part.astype(jnp.bfloat16), "ctx").astype(jnp.float32),
-        lax.psum(value_grad_part.astype(jnp.bfloat16), "ctx").astype(jnp.float32),
-        jnp.sum(gather_a2a(router_shard[None], "ctx", ctx_size, 0), axis=0),
-    )
+    out_grad = lax.psum(out_grad_part, "ctx")
+    query_grad, key_grad, value_grad = (
+        lax.psum(part.astype(jnp.bfloat16), "ctx").astype(jnp.float32)
+        for part in (query_grad_part, key_grad_part, value_grad_part)
+    )
+    router_grad = jnp.sum(gather_a2a(router_shard[None], "ctx", ctx_size, 0), axis=0)
     attn_gain_total, query_gain_total, key_gain_total, ffn_gain_total = lax.psum(
         (attn_gain_grad, query_gain_grad, key_gain_grad, ffn_gain_grad), ("ctx", "fsdp")
     )

time: 1510 us -> 1360 us (0.901)
  waiting for transfers between devices: 733 us -> 626 us
  local copies, waits for them, and re-layouts: 214 us -> 176 us
    reduce_scatter x3, waiting for transfers between devices: 100 us -> 0.02 us  [per_device(): lax.psum_scatter(full.astype(jnp.bfloat16), 'fsdp', scatter_dimension=1,...]
    all_to_all x6, waiting for transfers between devices: 283 us -> 191 us  [gather_a2a(): lax.all_to_all(rep, axis_name, 0, 0, tiled=True)]
    psum x2, waiting for transfers between devices: 47.1 us -> 109 us  [the longest x1 109 us: per_device(): out_grad = lax.psum(out_grad_part, 'ctx')]
    broadcast_in_dim x2 -> x0, local copies, waits for them, and re-layouts: 37.6 us -> none  [the longest x1 18.8 us: per_device(): expert_out[None]]
    all_to_all x4 -> x0, local copies, waits for them, and re-layouts: 29.9 us -> none  [the longest x1 8.33 us: per_device(): lax.all_to_all(grad_rows[None], 'ctx', split_axis=2, concat_axis=0, tiled...]
    all_to_all x4, waiting for transfers between devices: 190 us -> 206 us  [the longest x2 116 us: to_experts(): got = lax.all_to_all(buffer, 'ctx', 0, 0, tiled=True)]
    all_to_all x4 -> x3, waiting for transfers between devices: 110 us -> 104 us  [scatter_sum_a2a(): got = lax.all_to_all(parts, axis_name, axis, axis, tiled=True)]
  transfers between devices with their start and end apart: 24 -> 23, of which waited for: 15 -> 14; matrix products, arithmetic and copies ran while one was open for 26% -> 31% of each run, Pallas kernels for 0% -> 0%
where the time goes in v7:
time: 1360 us; the launch traced here: 1350 us
  waiting for transfers between devices  626 us (46%)
  matrix products  193 us (14%)
  local copies, waits for them, and re-layouts  176 us (13%)
  blocking collectives  158 us (12%)
  other arithmetic  116 us (9%)
  starting transfers between devices  62.5 us (5%)
  between operations  16.1 us (1%)
    all_to_all x6, waiting for transfers between devices, gather_a2a(): lax.all_to_all(rep, axis_name, 0, 0, tiled=True)  191 us
    dot_general x25, matrix products, contract(): return jnp.einsum(form, left, right, preferred_element_type=jnp.float32)  176 us
    all_to_all x2, waiting for transfers between devices, to_experts(): got = lax.all_to_all(buffer, 'ctx', 0, 0, tiled=True)  116 us
    all_to_all x1, blocking collectives, per_device(): got = lax.all_to_all(payload, 'fsdp', 0, 0, tiled=True)  111 us
    psum x1, waiting for transfers between devices, per_device(): out_grad = lax.psum(out_grad_part, 'ctx')  109 us
    all_to_all x3, waiting for transfers between devices, scatter_sum_a2a(): got = lax.all_to_all(parts, axis_name, axis, axis, tiled=True)  104 us
    all_to_all x2, waiting for transfers between devices, from_experts(): back = lax.all_to_all(parts, 'ctx', 0, 0, tiled=True)  90.1 us
    psum x1, blocking collectives, per_device(): lax.psum((attn_gain_grad, query_gain_grad, key_gain_grad, ffn_gain_grad),...  38.8 us
  transfers between devices with their start and end apart: 23, of which 14 were waited for; matrix products, arithmetic and copies ran while one was open for 31% of the time, Pallas kernels for 0%

profile of v7, /device:TPU:0, one launch (start us, length us, event | category | flops | bytes accessed | tf_op | source)
XLA Modules:
  0.0 1347.7 jit_solution(8277800728490702078)
XLA Ops:
  13.2 7.8 reshape.796
  33.2 110.7 %all_to_all.90 = bf16[4,4616,128]{2,1,0:T(8,128)(2,1)S(1)} all-to-all(bf16[4,4616,128]{2,1,0:T(8,128)(2,1)S(1)} %pad_maximum_fusion), channel_id=1, replica_groups=mesh['ctx'=8,'fsdp'=4] {'fsdp'}, dimensions={0} | all-to-all | bytes 9453568 | tf_op jit(solution)/shard_map/all_to_all | solution.py:152
  155.5 7.2 maximum_select_fusion
  171.8 6.5 fusion.99
  191.5 9.1 all-to-all-done.2
  211.3 9.5 all-to-all-done.1
  224.7 9.2 fusion.98
  233.9 8.6 fusion.3
  242.6 7.8 fusion.40
  264.4 94.7 %all-to-all-done.3 = bf16[4,1,128,2048]{3,2,1,0:T(8,128)(2,1)S(1)} async-done(((bf16[4,1,128,2048]{3,2,1,0:T(8,128)(2,1)}), bf16[4,1,128,2048]{3,2,1,0:T(8,128)(2,1)S(1)}, u32[]{:S(2)}, u32[]{:S(2)}) %all-to-all-start.3) | async-done | bytes 2097184 | tf_op jit(solution)/shard_map/all_to_all | solution.py:78
  367.6 10.2 scatter_custom_fusion
  384.6 7.0 gather_fusion.2
  392.4 10.7 scatter_custom_fusion.1
  403.1 51.2 %all-to-all-done.5 = bf16[8,2,96,2048]{3,2,1,0:T(8,128)(2,1)} async-done(((bf16[8,2,96,2048]{3,2,1,0:T(8,128)(2,1)}), bf16[8,2,96,2048]{3,2,1,0:T(8,128)(2,1)}, u32[]{:S(2)}, u32[]{:S(2)}) %all-to-all-start.5) | async-done | bytes 6291488 | tf_op jit(solution)/shard_map/all_to_all | solution.py:251
  459.0 6.7 copy.351
  465.7 64.8 %all-to-all-done.7 = bf16[8,2,96,2048]{3,2,1,0:T(8,128)(2,1)} async-done(((bf16[8,2,96,2048]{3,2,1,0:T(8,128)(2,1)}), bf16[8,2,96,2048]{3,2,1,0:T(8,128)(2,1)}, u32[]{:S(2)}, u32[]{:S(2)}) %all-to-all-start.7) | async-done | bytes 6291488 | tf_op jit(solution)/shard_map/all_to_all | solution.py:251
  530.5 6.6 copy.354
  537.1 10.6 fusion.101
  547.7 10.6 fusion.100
  558.3 13.5 %multiply_convert_fusion = (bf16[2,768,768]{2,1,0:T(8,128)(2,1)}, bf16[2,768,768]{2,1,0:T(8,128)(2,1)}, bf16[2,768,768]{2,1,0:T(8,128)(2,1)S(1)}) fusion(f32[2,768,768]{2,1,0:T(8,128)} %fusion.100, f32[2,768,768]{2,1,0:T(8,128)} %fusion.101, bf16[2,768,2048]{2,1,0:T(8,128)(2,1)} %bitcast.404, bf16[2,768,2048]{2,1,0:T(8,128)(2,1)} %all-gather.8.cloned.1.call-done), kind=kOutput, calls=%fused_computation.34 | convolution fusion | flops 4850712576 | bytes 29097984 | tf_op jit(solution)/shard_map/erd,efd->erf/dot_general | solution.py:24
  573.2 7.0 convolution_convert_fusion.1
  580.2 8.1 convolution_convert_fusion.4
  596.3 9.7 convolution_convert_fusion.2
  606.0 10.8 fusion.102
  616.9 9.9 add_convert_fusion
  630.6 37.2 %all-to-all-done.6 = bf16[8,2,96,2048]{3,2,1,0:T(8,128)(2,1)} async-done(((bf16[8,2,96,2048]{3,2,1,0:T(8,128)(2,1)}), bf16[8,2,96,2048]{3,2,1,0:T(8,128)(2,1)}, u32[]{:S(2)}, u32[]{:S(2)}) %all-to-all-start.6) | async-done | bytes 6291488 | tf_op jit(solution)/shard_map/all_to_all | solution.py:256
  673.1 12.6 gather_fusion.3
  691.7 53.0 %all-to-all-done.8 = bf16[8,2,96,2048]{3,2,1,0:T(8,128)(2,1)} async-done(((bf16[8,2,96,2048]{3,2,1,0:T(8,128)(2,1)}), bf16[8,2,96,2048]{3,2,1,0:T(8,128)(2,1)}, u32[]{:S(2)}, u32[]{:S(2)}) %all-to-all-start.8) | async-done | bytes 6291488 | tf_op jit(solution)/shard_map/all_to_all | solution.py:256
  744.6 12.6 gather_fusion.4
  757.3 6.8 convert_reduce_fusion
  779.1 9.8 convolution_convert_fusion.3
  788.9 59.5 %all-to-all-done.9 = bf16[4,128,2048]{2,1,0:T(8,128)(2,1)} async-done(((bf16[4,128,2048]{2,1,0:T(8,128)(2,1)}), bf16[4,128,2048]{2,1,0:T(8,128)(2,1)}, u32[]{:S(2)}, u32[]{:S(2)}) %all-to-all-start.9) | async-done | bytes 2097184 | tf_op jit(solution)/shard_map/all_to_all | solution.py:72
  855.1 16.8 %fusion = (f32[4,8,128]{2,1,0:T(8,128)}, f32[4,1024,128,8]{2,1,3,0:T(8,128)}) fusion(f32[4,1,8,128,1024]{3,4,2,0,1:T(8,128)} %get-tuple-element.69, f32[4,8,128]{2,1,0:T(8,128)} %log_add_fusion, bf16[4,1024,128,1]{2,1,3,0:T(8,128)(2,1)} %bitcast.399, bf16[4,128,8,128]{3,2,1,0:T(8,128)(2,1)} %bitcast.389), kind=kOutput, calls=%fused_computation.10 | convolution fusion | flops 1086320640 | bytes 35684352 | tf_op jit(solution)/shard_map/stkgd,sjkd->skgtj/dot_general | solution.py:24
  871.9 13.2 fusion.6
  885.1 6.9 fusion.37
  892.0 12.7 copy.369
  916.9 6.4 multiply_bitcast_fusion
  926.0 6.2 all-to-all-done.11
  964.6 113.4 %all-to-all-done.12 = bf16[4,512,1,1280]{3,1,2,0:T(8,128)(2,1)} async-done(((bf16[4,512,1,1280]{3,1,2,0:T(8,128)(2,1)}), bf16[4,512,1,1280]{3,1,2,0:T(8,128)(2,1)}, u32[]{:S(2)}, u32[]{:S(2)}) %all-to-all-start.12) | async-done | bytes 5242912 | tf_op jit(solution)/shard_map/all_to_all | solution.py:72
  1100.0 6.7 convolution_convert_fusion
  1109.2 7.4 fusion.44
  1116.9 8.8 all_to_all.91
  1130.6 6.2 fusion.103
  1155.3 13.6 %all-to-all-done.13 = f32[4,128,512]{2,1,0:T(8,128)S(1)} async-done(((f32[4,128,512]{2,1,0:T(8,128)}), f32[4,128,512]{2,1,0:T(8,128)S(1)}, u32[]{:S(2)}, u32[]{:S(2)}) %all-to-all-start.13) | async-done | bytes 1048608 | tf_op jit(solution)/shard_map/all_to_all | solution.py:371
  1171.5 38.8 %all-reduce = (f32[2048]{0:T(1024)}, f32[128]{0:T(128)}, f32[128]{0:T(128)}, f32[2048]{0:T(1024)}) all-reduce(f32[2048]{0:T(1024)S(1)} %bitcast.450, f32[128]{0:T(128)S(1)} %bitcast_reduce_fusion, f32[128]{0:T(128)S(1)} %copy-done.69, f32[2048]{0:T(1024)S(1)} %copy-done.55), channel_id=1, replica_groups=mesh['ctx'=8,'fsdp'=4] {'ctx','fsdp'}, use_global_device_ids=true, to_apply=%region_24.26 | all-reduce | flops 4352 | bytes 34816 | tf_op jit(solution)/shard_map/psum | solution.py:389
  1217.0 6.7 convert_element_type.227
  1223.8 108.8 %all-reduce.5.cloned.1.call-done = f32[1024,2048]{1,0:T(8,128)} async-done(((f32[1024,2048]{1,0:T(8,128)}), f32[1024,2048]{1,0:T(8,128)}) %all-reduce.5.cloned.1.call-update) | async-done | bytes 8388624 | tf_op jit(solution)/shard_map/psum | solution.py:383
  1332.6 7.9 copy.455
  (384 shorter events, 251.4 us)
Async XLA Ops:
  7.2 529.9 %all-gather.6.cloned.1.call-start = ((), (), s32[]{:S(2)}) async-start(), calls=%async_computation.20 | async-start | bytes 7864320 | tf_op jit(solution)/shard_map/all_gather | solution.py:231
  150.3 5.3 collective-permute-start
  163.5 16.0 %copy-start.39 = (f32[128,64]{0,1:T(8,128)}, f32[128,64]{0,1:T(8,128)S(1)}, u32[]{:S(2)}) copy-start(f32[128,64]{0,1:T(8,128)S(1)} %get-tuple-element.66) | copy-start | bytes 98308
  163.5 16.0 %copy-start.41 = (f32[128,64]{0,1:T(8,128)}, f32[128,64]{0,1:T(8,128)S(1)}, u32[]{:S(2)}) copy-start(f32[128,64]{0,1:T(8,128)S(1)} %get-tuple-element.67) | copy-start | bytes 98308
  163.6 44.1 %copy-start.33 = (f32[128,64]{1,0:T(8,128)}, f32[128,64]{1,0:T(8,128)S(1)}, u32[]{:S(2)}) copy-start(f32[128,64]{1,0:T(8,128)S(1)} %copy.338) | copy-start | bytes 98308
  163.7 44.0 %copy-start.35 = (f32[128,64]{1,0:T(8,128)}, f32[128,64]{1,0:T(8,128)S(1)}, u32[]{:S(2)}) copy-start(f32[128,64]{1,0:T(8,128)S(1)} %copy.339) | copy-start | bytes 98308
  181.0 19.6 %all-to-all-start.2 = ((bf16[8,4,128,128]{3,2,1,0:T(8,128)(2,1)}), bf16[8,4,128,128]{3,2,1,0:T(8,128)(2,1)}, u32[]{:S(2)}, u32[]{:S(2)}) async-start(bf16[8,4,128,128]{3,2,1,0:T(8,128)(2,1)} %broadcast_in_dim.81), calls=%async_computation.2 | async-start | bytes 2097152 | tf_op jit(solution)/shard_map/all_to_all | solution.py:72
  191.5 16.2 %copy-start.2 = (f32[64,8,8,128]{3,2,1,0:T(8,128)}, f32[64,8,8,128]{3,2,1,0:T(8,128)S(1)}, u32[]{:S(2)}) copy-start(f32[64,8,8,128]{3,2,1,0:T(8,128)S(1)} %copy.415) | copy-start | bytes 6291460
  201.8 18.9 %all-to-all-start.1 = ((bf16[8,4,128,128]{2,3,1,0:T(8,128)(2,1)}), bf16[8,4,128,128]{2,3,1,0:T(8,128)(2,1)S(1)}, u32[]{:S(2)}, u32[]{:S(2)}) async-start(bf16[8,4,128,128]{2,3,1,0:T(8,128)(2,1)} %broadcast_in_dim.75), calls=%async_computation.1 | async-start | bytes 2097152 | tf_op jit(solution)/shard_map/all_to_all | solution.py:72
  205.4 342.3 %all-gather.4.cloned.1.call-start = ((), (), s32[]{:S(2)}) async-start(), calls=%async_computation.19 | async-start | bytes 7864320 | tf_op jit(solution)/shard_map/all_gather | solution.py:230
  209.9 14.8 %copy-start.14 = (bf16[4,128,8,64]{3,1,2,0:T(8,128)(2,1)S(1)}, bf16[4,128,8,64]{3,1,2,0:T(8,128)(2,1)}, u32[]{:S(2)}) copy-start(bf16[4,128,8,64]{3,1,2,0:T(8,128)(2,1)} %get-tuple-element.57) | copy-start | bytes 1572868
  211.2 22.6 %copy-start.8 = (bf16[4,8,128,128]{3,2,1,0:T(8,128)(2,1)}, bf16[4,8,128,128]{3,2,1,0:T(8,128)(2,1)S(1)}, u32[]{:S(2)}) copy-start(bf16[4,8,128,128]{3,2,1,0:T(8,128)(2,1)S(1)} %copy.335) | copy-start | bytes 3145732
  255.1 104.0 %copy-start.59 = (bf16[512,16]{0,1:T(8,128)(2,1)S(1)}, bf16[512,16]{0,1:T(8,128)(2,1)}, u32[]{:S(2)}) copy-start(bf16[512,16]{0,1:T(8,128)(2,1)} %param.31) | copy-start | bytes 49156
  255.1 111.2 %copy-start = (f32[1,128,2048]{2,1,0:T(8,128)S(1)}, f32[1,128,2048]{2,1,0:T(8,128)}, u32[]{:S(2)}) copy-start(f32[1,128,2048]{2,1,0:T(8,128)} %param.19) | copy-start | bytes 3145732
  255.1 104.0 %all-to-all-start.3 = ((bf16[4,1,128,2048]{3,2,1,0:T(8,128)(2,1)}), bf16[4,1,128,2048]{3,2,1,0:T(8,128)(2,1)S(1)}, u32[]{:S(2)}, u32[]{:S(2)}) async-start(bf16[4,1,128,2048]{3,2,1,0:T(8,128)(2,1)} %fusion.27), calls=%async_computation.3 | async-start | bytes 4194304 | tf_op jit(solution)/shard_map/all_to_all | solution.py:78
  258.9 108.6 %copy-start.46 = (f32[2048]{0:T(1024)S(1)}, f32[2048]{0:T(1024)}, u32[]{:S(2)}) copy-start(f32[2048]{0:T(1024)} %param.30) | copy-start | bytes 24580
  360.5 17.4 %all-to-all-start.4 = ((bf16[4,512,16]{1,2,0:T(8,128)(2,1)}), bf16[4,512,16]{1,2,0:T(8,128)(2,1)S(1)}, u32[]{:S(2)}, u32[]{:S(2)}) async-start(bf16[4,512,16]{1,2,0:T(8,128)(2,1)} %broadcast_in_dim.83), calls=%async_computation.4 | async-start | bytes 131072 | tf_op jit(solution)/shard_map/all_to_all | solution.py:72
  366.5 17.1 %copy-start.60 = (f32[128]{0:T(128)}, f32[128]{0:T(128)S(1)}, u32[]{:S(2)}) copy-start(f32[128]{0:T(128)S(1)} %add_rsqrt_fusion.2) | copy-start | bytes 1540
  377.9 76.3 %all-to-all-start.5 = ((bf16[8,2,96,2048]{3,2,1,0:T(8,128)(2,1)}), bf16[8,2,96,2048]{3,2,1,0:T(8,128)(2,1)}, u32[]{:S(2)}, u32[]{:S(2)}) async-start(bf16[8,2,96,2048]{3,2,1,0:T(8,128)(2,1)} %bitcast.385), calls=%async_computation.5 | async-start | bytes 12582912 | tf_op jit(solution)/shard_map/all_to_all | solution.py:251
  382.6 175.6 %all-gather.8.cloned.1.call-start = ((), (), s32[]{:S(2)}) async-start(), calls=%async_computation.21 | async-start | bytes 7864320 | tf_op jit(solution)/shard_map/all_gather | solution.py:232
  454.2 76.3 %all-to-all-start.7 = ((bf16[8,2,96,2048]{3,2,1,0:T(8,128)(2,1)}), bf16[8,2,96,2048]{3,2,1,0:T(8,128)(2,1)}, u32[]{:S(2)}, u32[]{:S(2)}) async-start(bf16[8,2,96,2048]{3,2,1,0:T(8,128)(2,1)} %bitcast.388), calls=%async_computation.7 | async-start | bytes 12582912 | tf_op jit(solution)/shard_map/all_to_all | solution.py:251
  459.0 686.3 %reduce-scatter.8.cloned.1.call-start = ((), (), s32[]{:S(2)}) async-start(), calls=%async_computation.25 | async-start | bytes 7864320 | tf_op jit(solution)/shard_map/reduce_scatter | solution.py:377
  547.7 25.4 %slice-start.5 = ((s8[6291456]{0:T(1024)(128)(4,1)}), s8[2097152]{0:T(1024)(128)(4,1)S(1)}, s32[]{:S(2)}) async-start(s8[6291456]{0:T(1024)(128)(4,1)} %bitcast.405), calls=%async_computation.32 | async-start | bytes 4194304
  558.3 14.9 %slice-start.6 = ((s8[6291456]{0:T(1024)(128)(4,1)}), s8[4194304]{0:T(1024)(128)(4,1)S(1)}, s32[]{:S(2)}) async-start(s8[6291456]{0:T(1024)(128)(4,1)} %bitcast.405), calls=%async_computation.33 | async-start | bytes 8388608
  591.5 76.3 %all-to-all-start.6 = ((bf16[8,2,96,2048]{3,2,1,0:T(8,128)(2,1)}), bf16[8,2,96,2048]{3,2,1,0:T(8,128)(2,1)}, u32[]{:S(2)}, u32[]{:S(2)}) async-start(bf16[8,2,96,2048]{3,2,1,0:T(8,128)(2,1)} %bitcast.387), calls=%async_computation.6 | async-start | bytes 12582912 | tf_op jit(solution)/shard_map/all_to_all | solution.py:256
  596.2 552.5 %reduce-scatter.6.cloned.1.call-start = ((), (), s32[]{:S(2)}) async-start(), calls=%async_computation.24 | async-start | bytes 7864320 | tf_op jit(solution)/shard_map/reduce_scatter | solution.py:377
  667.8 76.8 %all-to-all-start.8 = ((bf16[8,2,96,2048]{3,2,1,0:T(8,128)(2,1)}), bf16[8,2,96,2048]{3,2,1,0:T(8,128)(2,1)}, u32[]{:S(2)}, u32[]{:S(2)}) async-start(bf16[8,2,96,2048]{3,2,1,0:T(8,128)(2,1)} %bitcast.386), calls=%async_computation.8 | async-start | bytes 12582912 | tf_op jit(solution)/shard_map/all_to_all | solution.py:256
  744.6 19.5 %copy-start.38 = (bf16[4,2,8,512]{3,2,0,1:T(8,128)(2,1)S(1)}, bf16[4,2,8,512]{3,2,0,1:T(8,128)(2,1)}, u32[]{:S(2)}) copy-start(bf16[4,2,8,512]{3,2,0,1:T(8,128)(2,1)} %copy-done.37) | copy-start | bytes 196612
  744.6 19.5 %copy-start.47 = (f32[2048]{0:T(1024)S(1)}, f32[2048]{0:T(1024)}, u32[]{:S(2)}) copy-start(f32[2048]{0:T(1024)} %param.30) | copy-start | bytes 24580
  770.3 78.1 %all-to-all-start.9 = ((bf16[4,128,2048]{2,1,0:T(8,128)(2,1)}), bf16[4,128,2048]{2,1,0:T(8,128)(2,1)}, u32[]{:S(2)}, u32[]{:S(2)}) async-start(bf16[4,128,2048]{2,1,0:T(8,128)(2,1)} %broadcast_in_dim.88), calls=%async_computation.9 | async-start | bytes 4194304 | tf_op jit(solution)/shard_map/all_to_all | solution.py:72
  775.4 376.6 %reduce-scatter.4.cloned.1.call-start = ((), (), s32[]{:S(2)}) async-start(), calls=%async_computation.23 | async-start | bytes 7864320 | tf_op jit(solution)/shard_map/reduce_scatter | solution.py:377
  855.1 16.8 %slice-start = ((s8[16777216]{0:T(1024)(128)(4,1)}), s8[4194304]{0:T(1024)(128)(4,1)S(1)}, s32[]{:S(2)}) async-start(s8[16777216]{0:T(1024)(128)(4,1)} %bitcast.380), calls=%async_computation.27 | async-start | bytes 8388608
  855.1 16.8 %slice-start.1 = ((s8[16777216]{0:T(1024)(128)(4,1)}), s8[4194304]{0:T(1024)(128)(4,1)S(1)}, s32[]{:S(2)}) async-start(s8[16777216]{0:T(1024)(128)(4,1)} %bitcast.380), calls=%async_computation.28 | async-start | bytes 8388608
  855.1 16.8 %slice-start.2 = ((s8[16777216]{0:T(1024)(128)(4,1)}), s8[4194304]{0:T(1024)(128)(4,1)S(1)}, s32[]{:S(2)}) async-start(s8[16777216]{0:T(1024)(128)(4,1)} %bitcast.380), calls=%async_computation.29 | async-start | bytes 8388608
  855.1 16.8 %slice-start.3 = ((s8[16777216]{0:T(1024)(128)(4,1)}), s8[4194304]{0:T(1024)(128)(4,1)S(1)}, s32[]{:S(2)}) async-start(s8[16777216]{0:T(1024)(128)(4,1)} %bitcast.380), calls=%async_computation.30 | async-start | bytes 8388608
  912.6 19.7 %all-to-all-start.11 = ((bf16[4,8,128,128]{2,3,0,1:T(8,128)(2,1)}), bf16[4,8,128,128]{2,3,0,1:T(8,128)(2,1)}, u32[]{:S(2)}, u32[]{:S(2)}) async-start(bf16[4,8,128,128]{2,3,0,1:T(8,128)(2,1)} %copy.370), calls=%async_computation.11 | async-start | bytes 2097152 | tf_op jit(solution)/shard_map/all_to_all | solution.py:78
  923.3 13.2 copy-start.3
  923.3 13.2 copy-start.45
  923.3 13.2 copy-start.66
  932.2 19.6 %all-to-all-start.10 = ((bf16[4,8,128,128]{2,3,0,1:T(8,128)(2,1)}), bf16[4,8,128,128]{2,3,0,1:T(8,128)(2,1)}, u32[]{:S(2)}, u32[]{:S(2)}) async-start(bf16[4,8,128,128]{2,3,0,1:T(8,128)(2,1)} %copy.365), calls=%async_computation.10 | async-start | bytes 2097152 | tf_op jit(solution)/shard_map/all_to_all | solution.py:78
  959.5 118.5 %all-to-all-start.12 = ((bf16[4,512,1,1280]{3,1,2,0:T(8,128)(2,1)}), bf16[4,512,1,1280]{3,1,2,0:T(8,128)(2,1)}, u32[]{:S(2)}, u32[]{:S(2)}) async-start(bf16[4,512,1,1280]{3,1,2,0:T(8,128)(2,1)} %broadcast_in_dim.89), calls=%async_computation.12 | async-start | bytes 10485760 | tf_op jit(solution)/shard_map/all_to_all | solution.py:72
  964.6 248.2 %all-reduce.7.cloned.1.call-start = ((), (), s32[]{:S(2)}) async-start(), calls=%async_computation.26 | async-start | bytes 10485760 | tf_op jit(solution)/shard_map/psum | solution.py:385
  1106.7 225.9 %all-reduce.5.cloned.1.call-start = ((), (), s32[]{:S(2)}) async-start(), calls=%async_computation.22 | async-start | bytes 16777216 | tf_op jit(solution)/shard_map/psum | solution.py:383
  1126.4 12.5 all-to-all-start.15
  1138.9 30.0 %all-to-all-start.13 = ((f32[4,128,512]{2,1,0:T(8,128)}), f32[4,128,512]{2,1,0:T(8,128)S(1)}, u32[]{:S(2)}, u32[]{:S(2)}) async-start(f32[4,128,512]{2,1,0:T(8,128)} %bitcast.98), calls=%async_computation.13 | async-start | bytes 2097152 | tf_op jit(solution)/shard_map/all_to_all | solution.py:371
  1152.0 17.2 %copy-start.68 = (f32[128]{0:T(128)S(1)}, f32[128]{0:T(128)}, u32[]{:S(2)}) copy-start(f32[128]{0:T(128)} %copy-done.67) | copy-start | bytes 1540
  1155.3 16.1 %copy-start.55 = (f32[2048]{0:T(1024)S(1)}, f32[2048]{0:T(1024)}, u32[]{:S(2)}) copy-start(f32[2048]{0:T(1024)} %get-tuple-element.25) | copy-start | bytes 24580
  1155.3 16.1 %copy-start.69 = (f32[128]{0:T(128)S(1)}, f32[128]{0:T(128)}, u32[]{:S(2)}) copy-start(f32[128]{0:T(128)} %get-tuple-element.23) | copy-start | bytes 1540
  (56 other events, 355.0 us)
Sparse Core Ops, SparseCore 0:
  162.8 134.8 all-gather.5
  299.3 126.1 all-gather.3
  427.0 113.5 all-gather.7
  580.3 110.3 reduce-scatter.7
  692.8 136.2 reduce-scatter.5
  831.3 121.0 reduce-scatter.3
  1106.8 95.3 all-reduce.6
  1206.3 126.2 all-reduce.4

commit v8 on v7

--- a/solution.py
+++ b/solution.py
@@ -142,19 +142,15 @@
         sent_rows = jnp.moveaxis(
             lax.dynamic_slice_in_dim(blocks, core * half, half, 0), 1, 0
         ).reshape(fsdp_size, -1, lanes)
-        common = jnp.concatenate(
-            [first_input.reshape(-1, lanes), doc_ids.astype(jnp.bfloat16).reshape(-1, lanes)],
-            axis=0,
-        )
+        common = doc_ids.astype(jnp.bfloat16).reshape(-1, lanes)
         payload = jnp.concatenate(
             [sent_rows, jnp.broadcast_to(common[None], (fsdp_size,) + common.shape)], axis=1
         )
         got = lax.all_to_all(payload, "fsdp", 0, 0, tiled=True)
         w_rows = sent_rows.shape[1]
-        h_rows = tokens * D // lanes
         mine = got[:, :w_rows].reshape(fsdp_size, half, -1)
-        group_input = got[:, w_rows : w_rows + h_rows].reshape(group_rows, D)
-        doc_rows = got[:, w_rows + h_rows :].reshape(fsdp_size, -1).astype(jnp.float32)
+        doc_rows = got[:, w_rows:].reshape(fsdp_size, -1).astype(jnp.float32)
+        group_input = lax.all_gather(first_input, "fsdp", axis=0, tiled=True)
         other = lax.ppermute(mine, "ctx", [(i, i ^ 1) for i in range(ctx_size)])
         w_cols = jnp.where(
             core == 0, jnp.stack([mine, other], axis=1), jnp.stack([other, mine], axis=1)

time: 1360 us -> 1320 us (0.971)
  blocking collectives: 158 us -> 47.3 us
  waiting for transfers between devices: 626 us -> 694 us
    all_to_all x1 -> x0, blocking collectives: 111 us -> none  [per_device(): got = lax.all_to_all(payload, 'fsdp', 0, 0, tiled=True)]
    all_to_all x0 -> x1, waiting for transfers between devices: none -> 59.5 us  [per_device(): got = lax.all_to_all(payload, 'fsdp', 0, 0, tiled=True)]
    all_to_all x3, waiting for transfers between devices: 104 us -> 72 us  [scatter_sum_a2a(): got = lax.all_to_all(parts, axis_name, axis, axis, tiled=True)]
    all_gather x0 -> x1, waiting for transfers between devices: none -> 24.6 us  [per_device(): group_input = lax.all_gather(first_input, 'fsdp', axis=0, tiled=True)]
    all_gather x1, waiting for transfers between devices: 0.01 us -> 22.9 us  [per_device(): lax.all_gather(expert_down, 'fsdp', axis=1, tiled=True)]
  transfers between devices with their start and end apart: 23 -> 25, of which waited for: 14 -> 16; matrix products, arithmetic and copies ran while one was open for 31% -> 33% of each run, Pallas kernels for 0% -> 0%
where the time goes in v8:
time: 1320 us; the launch traced here: 1310 us
  waiting for transfers between devices  694 us (53%)
  matrix products  192 us (15%)
  local copies, waits for them, and re-layouts  176 us (13%)
  other arithmetic  120 us (9%)
  starting transfers between devices  67.9 us (5%)
  blocking collectives  47.3 us (4%)
  between operations  15.6 us (1%)
    all_to_all x6, waiting for transfers between devices, gather_a2a(): lax.all_to_all(rep, axis_name, 0, 0, tiled=True)  189 us
    dot_general x25, matrix products, contract(): return jnp.einsum(form, left, right, preferred_element_type=jnp.float32)  175 us
    all_to_all x2, waiting for transfers between devices, to_experts(): got = lax.all_to_all(buffer, 'ctx', 0, 0, tiled=True)  116 us
    psum x1, waiting for transfers between devices, per_device(): out_grad = lax.psum(out_grad_part, 'ctx')  105 us
    all_to_all x2, waiting for transfers between devices, from_experts(): back = lax.all_to_all(parts, 'ctx', 0, 0, tiled=True)  90.2 us
    all_to_all x3, waiting for transfers between devices, scatter_sum_a2a(): got = lax.all_to_all(parts, axis_name, axis, axis, tiled=True)  72 us
    all_to_all x1, waiting for transfers between devices, per_device(): got = lax.all_to_all(payload, 'fsdp', 0, 0, tiled=True)  59.5 us
    psum x1, blocking collectives, per_device(): lax.psum((attn_gain_grad, query_gain_grad, key_gain_grad, ffn_gain_grad),...  38.9 us
  transfers between devices with their start and end apart: 25, of which 16 were waited for; matrix products, arithmetic and copies ran while one was open for 33% of the time, Pallas kernels for 0%

profile of v8, /device:TPU:0, one launch (start us, length us, event | category | flops | bytes accessed | tf_op | source)
XLA Modules:
  0.0 1312.9 jit_solution(14403360446594547965)
XLA Ops:
  22.4 6.3 all-to-all-start
  28.9 59.5 %all-to-all-done = bf16[4,2568,128]{2,1,0:T(8,128)(2,1)} async-done(((bf16[4,2568,128]{2,1,0:T(8,128)(2,1)}), bf16[4,2568,128]{2,1,0:T(8,128)(2,1)}, u32[]{:S(2)}, u32[]{:S(2)}) %all-to-all-start) | async-done | bytes 2629664 | tf_op jit(solution)/shard_map/all_to_all | solution.py:149
  91.8 6.2 reshape.788
  99.1 6.2 stack_reshape.4
  105.3 7.4 maximum_select_fusion
  119.5 24.6 %all-gather.5.cloned.1.call-done = bf16[512,2048]{1,0:T(8,128)(2,1)} async-done(((bf16[128,2048]{1,0:T(8,128)(2,1)}), bf16[512,2048]{1,0:T(8,128)(2,1)}) %all-gather.5.cloned.1.call-update) | async-done | bytes 2097168 | tf_op jit(solution)/shard_map/all_gather | solution.py:153
  186.9 7.1 all-to-all-done.1
  199.2 9.3 fusion.92
  208.5 8.6 fusion.3
  217.1 7.9 fusion.40
  239.9 64.6 %all-to-all-done.3 = bf16[4,1,128,2048]{3,2,1,0:T(8,128)(2,1)} async-done(((bf16[4,1,128,2048]{3,2,1,0:T(8,128)(2,1)}), bf16[4,1,128,2048]{3,2,1,0:T(8,128)(2,1)}, u32[]{:S(2)}, u32[]{:S(2)}) %all-to-all-start.3) | async-done | bytes 2097184 | tf_op jit(solution)/shard_map/all_to_all | solution.py:78
  312.2 10.2 scatter_custom_fusion
  329.0 7.0 gather_fusion.2
  336.8 10.7 scatter_custom_fusion.1
  347.5 51.3 %all-to-all-done.5 = bf16[8,2,96,2048]{3,2,1,0:T(8,128)(2,1)} async-done(((bf16[8,2,96,2048]{3,2,1,0:T(8,128)(2,1)}), bf16[8,2,96,2048]{3,2,1,0:T(8,128)(2,1)}, u32[]{:S(2)}, u32[]{:S(2)}) %all-to-all-start.5) | async-done | bytes 6291488 | tf_op jit(solution)/shard_map/all_to_all | solution.py:247
  403.6 6.6 copy.362
  410.2 64.9 %all-to-all-done.7 = bf16[8,2,96,2048]{3,2,1,0:T(8,128)(2,1)} async-done(((bf16[8,2,96,2048]{3,2,1,0:T(8,128)(2,1)}), bf16[8,2,96,2048]{3,2,1,0:T(8,128)(2,1)}, u32[]{:S(2)}, u32[]{:S(2)}) %all-to-all-start.7) | async-done | bytes 6291488 | tf_op jit(solution)/shard_map/all_to_all | solution.py:247
  475.2 6.7 copy.365
  481.8 10.6 fusion.95
  492.5 10.6 fusion.94
  503.1 22.9 %all-gather.11.cloned.1.call-done = bf16[2,768,2048]{2,1,0:T(8,128)(2,1)} async-done(((bf16[2,192,2048]{2,1,0:T(8,128)(2,1)}), bf16[2,768,2048]{2,1,0:T(8,128)(2,1)}) %all-gather.11.cloned.1.call-update) | async-done | bytes 6291472 | tf_op jit(solution)/shard_map/all_gather | solution.py:228
  526.0 13.5 %multiply_convert_fusion = (bf16[2,768,768]{2,1,0:T(8,128)(2,1)}, bf16[2,768,768]{2,1,0:T(8,128)(2,1)}, bf16[2,768,768]{2,1,0:T(8,128)(2,1)S(1)}) fusion(f32[2,768,768]{2,1,0:T(8,128)} %fusion.94, f32[2,768,768]{2,1,0:T(8,128)} %fusion.95, bf16[2,768,2048]{2,1,0:T(8,128)(2,1)} %bitcast.406, bf16[2,768,2048]{2,1,0:T(8,128)(2,1)} %all-gather.11.cloned.1.call-done), kind=kOutput, calls=%fused_computation.33 | convolution fusion | flops 4850712576 | bytes 29097984 | tf_op jit(solution)/shard_map/erd,efd->erf/dot_general | solution.py:24
  540.8 7.0 convolution_convert_fusion.1
  547.8 8.1 convolution_convert_fusion.4
  563.9 9.8 convolution_convert_fusion.2
  573.7 10.7 fusion.96
  584.4 9.9 add_convert_fusion
  598.2 37.3 %all-to-all-done.6 = bf16[8,2,96,2048]{3,2,1,0:T(8,128)(2,1)} async-done(((bf16[8,2,96,2048]{3,2,1,0:T(8,128)(2,1)}), bf16[8,2,96,2048]{3,2,1,0:T(8,128)(2,1)}, u32[]{:S(2)}, u32[]{:S(2)}) %all-to-all-start.6) | async-done | bytes 6291488 | tf_op jit(solution)/shard_map/all_to_all | solution.py:252
  640.7 12.5 gather_fusion.3
  659.3 53.0 %all-to-all-done.8 = bf16[8,2,96,2048]{3,2,1,0:T(8,128)(2,1)} async-done(((bf16[8,2,96,2048]{3,2,1,0:T(8,128)(2,1)}), bf16[8,2,96,2048]{3,2,1,0:T(8,128)(2,1)}, u32[]{:S(2)}, u32[]{:S(2)}) %all-to-all-start.8) | async-done | bytes 6291488 | tf_op jit(solution)/shard_map/all_to_all | solution.py:252
  712.3 12.6 gather_fusion.4
  724.9 6.9 convert_reduce_fusion
  744.5 9.7 convolution_convert_fusion.3
  754.2 60.4 %all-to-all-done.9 = bf16[4,128,2048]{2,1,0:T(8,128)(2,1)S(1)} async-done(((bf16[4,128,2048]{2,1,0:T(8,128)(2,1)}), bf16[4,128,2048]{2,1,0:T(8,128)(2,1)S(1)}, u32[]{:S(2)}, u32[]{:S(2)}) %all-to-all-start.9) | async-done | bytes 2097184 | tf_op jit(solution)/shard_map/all_to_all | solution.py:72
  821.2 16.1 %fusion = (f32[4,8,128]{2,1,0:T(8,128)S(1)}, f32[4,1024,128,8]{2,1,3,0:T(8,128)}) fusion(f32[4,1,8,128,1024]{3,4,2,0,1:T(8,128)} %get-tuple-element.69, f32[4,8,128]{2,1,0:T(8,128)S(1)} %log_add_fusion, bf16[4,1024,128,1]{2,1,3,0:T(8,128)(2,1)} %bitcast.401, bf16[4,128,8,128]{3,2,1,0:T(8,128)(2,1)} %bitcast.393), kind=kOutput, calls=%fused_computation.10 | convolution fusion | flops 1086320640 | bytes 35684352 | tf_op jit(solution)/shard_map/stkgd,sjkd->skgtj/dot_general | solution.py:24
  837.4 13.1 fusion.6
  856.5 12.8 copy.380
  881.4 6.5 multiply_bitcast_fusion
  933.5 115.0 %all-to-all-done.12 = bf16[4,512,1,1280]{3,1,2,0:T(8,128)(2,1)} async-done(((bf16[4,512,1,1280]{3,1,2,0:T(8,128)(2,1)}), bf16[4,512,1,1280]{3,1,2,0:T(8,128)(2,1)}, u32[]{:S(2)}, u32[]{:S(2)}) %all-to-all-start.12) | async-done | bytes 5242912 | tf_op jit(solution)/shard_map/all_to_all | solution.py:72
  1053.2 6.2 copy.384
  1065.8 6.9 convolution_convert_fusion
  1075.8 8.0 fusion.44
  1084.0 8.3 all_to_all.90
  1121.2 14.7 %all-to-all-done.13 = f32[4,128,512]{2,1,0:T(8,128)} async-done(((f32[4,128,512]{2,1,0:T(8,128)}), f32[4,128,512]{2,1,0:T(8,128)}, u32[]{:S(2)}, u32[]{:S(2)}) %all-to-all-start.13) | async-done | bytes 1048608 | tf_op jit(solution)/shard_map/all_to_all | solution.py:367
  1140.6 38.9 %all-reduce = (f32[2048]{0:T(1024)}, f32[128]{0:T(128)}, f32[128]{0:T(128)}, f32[2048]{0:T(1024)}) all-reduce(f32[2048]{0:T(1024)S(1)} %bitcast.455, f32[128]{0:T(128)S(1)} %bitcast_reduce_fusion, f32[128]{0:T(128)S(1)} %copy-done.57, f32[2048]{0:T(1024)S(1)} %copy-done.46), channel_id=1, replica_groups=mesh['ctx'=8,'fsdp'=4] {'ctx','fsdp'}, use_global_device_ids=true, to_apply=%region_24.26 | all-reduce | flops 4352 | bytes 34816 | tf_op jit(solution)/shard_map/psum | solution.py:385
  1186.7 6.7 convert_element_type.226
  1193.4 104.6 %all-reduce.5.cloned.1.call-done = f32[1024,2048]{1,0:T(8,128)} async-done(((f32[1024,2048]{1,0:T(8,128)}), f32[1024,2048]{1,0:T(8,128)}) %all-reduce.5.cloned.1.call-update) | async-done | bytes 8388624 | tf_op jit(solution)/shard_map/psum | solution.py:379
  1298.1 7.9 copy.473
  (355 shorter events, 270.9 us)
Async XLA Ops:
  22.4 66.1 %all-to-all-start = ((bf16[4,2568,128]{2,1,0:T(8,128)(2,1)}), bf16[4,2568,128]{2,1,0:T(8,128)(2,1)}, u32[]{:S(2)}, u32[]{:S(2)}) async-start(bf16[4,2568,128]{2,1,0:T(8,128)(2,1)} %pad_maximum_fusion), calls=%async_computation | async-start | bytes 5259264 | tf_op jit(solution)/shard_map/all_to_all | solution.py:149
  28.7 115.3 %all-gather.5.cloned.1.call-start = ((), (), s32[]{:S(2)}) async-start(), calls=%async_computation.19 | async-start | bytes 2621440 | tf_op jit(solution)/shard_map/all_gather | solution.py:153
  28.9 69.1 %copy-start.55 = (f32[128]{0:T(128)}, f32[128]{0:T(128)S(1)}, u32[]{:S(2)}) copy-start(f32[128]{0:T(128)S(1)} %add_rsqrt_fusion.3) | copy-start | bytes 1540
  28.9 69.1 %copy-start.41 = (f32[2048]{0:T(1024)S(1)}, f32[2048]{0:T(1024)}, u32[]{:S(2)}) copy-start(f32[2048]{0:T(1024)} %param.23) | copy-start | bytes 24580
  98.0 7.2 collective-permute-start
  99.0 382.8 %all-gather.9.cloned.1.call-start = ((), (), s32[]{:S(2)}) async-start(), calls=%async_computation.21 | async-start | bytes 7864320 | tf_op jit(solution)/shard_map/all_gather | solution.py:227
  113.5 39.1 %copy-start.31 = (f32[128,64]{0,1:T(8,128)}, f32[128,64]{0,1:T(8,128)S(1)}, u32[]{:S(2)}) copy-start(f32[128,64]{0,1:T(8,128)S(1)} %get-tuple-element.66) | copy-start | bytes 98308
  113.5 39.1 %copy-start.33 = (f32[128,64]{0,1:T(8,128)}, f32[128,64]{0,1:T(8,128)S(1)}, u32[]{:S(2)}) copy-start(f32[128,64]{0,1:T(8,128)S(1)} %get-tuple-element.67) | copy-start | bytes 98308
  113.6 69.8 %copy-start.25 = (f32[128,64]{1,0:T(8,128)}, f32[128,64]{1,0:T(8,128)S(1)}, u32[]{:S(2)}) copy-start(f32[128,64]{1,0:T(8,128)S(1)} %copy.349) | copy-start | bytes 98308
  113.7 69.7 %copy-start.27 = (f32[128,64]{1,0:T(8,128)}, f32[128,64]{1,0:T(8,128)S(1)}, u32[]{:S(2)}) copy-start(f32[128,64]{1,0:T(8,128)S(1)} %copy.350) | copy-start | bytes 98308
  115.4 28.7 %copy-start.24 = (f32[4,8,128]{0,2,1:T(8,128)}, f32[4,8,128]{0,2,1:T(8,128)S(1)}, u32[]{:S(2)}) copy-start(f32[4,8,128]{0,2,1:T(8,128)S(1)} %copy.341) | copy-start | bytes 49156
  119.5 33.0 %copy-start.53 = (f32[128]{0:T(128)S(1)}, f32[128]{0:T(128)}, u32[]{:S(2)}) copy-start(f32[128]{0:T(128)} %param.28) | copy-start | bytes 1540
  154.0 19.0 %all-to-all-start.2 = ((bf16[8,4,128,128]{3,2,1,0:T(8,128)(2,1)}), bf16[8,4,128,128]{3,2,1,0:T(8,128)(2,1)S(1)}, u32[]{:S(2)}, u32[]{:S(2)}) async-start(bf16[8,4,128,128]{3,2,1,0:T(8,128)(2,1)} %broadcast_in_dim.84), calls=%async_computation.2 | async-start | bytes 2097152 | tf_op jit(solution)/shard_map/all_to_all | solution.py:72
  174.3 19.6 %all-to-all-start.1 = ((bf16[8,4,128,128]{2,3,1,0:T(8,128)(2,1)}), bf16[8,4,128,128]{2,3,1,0:T(8,128)(2,1)}, u32[]{:S(2)}, u32[]{:S(2)}) async-start(bf16[8,4,128,128]{2,3,1,0:T(8,128)(2,1)} %broadcast_in_dim.78), calls=%async_computation.1 | async-start | bytes 2097152 | tf_op jit(solution)/shard_map/all_to_all | solution.py:72
  178.6 313.9 %all-gather.7.cloned.1.call-start = ((), (), s32[]{:S(2)}) async-start(), calls=%async_computation.20 | async-start | bytes 7864320 | tf_op jit(solution)/shard_map/all_gather | solution.py:226
  186.9 21.6 %copy-start.8 = (bf16[4,8,128,128]{3,2,1,0:T(8,128)(2,1)}, bf16[4,8,128,128]{3,2,1,0:T(8,128)(2,1)S(1)}, u32[]{:S(2)}) copy-start(bf16[4,8,128,128]{3,2,1,0:T(8,128)(2,1)S(1)} %copy.346) | copy-start | bytes 3145732
  229.7 74.7 %copy-start.49 = (bf16[512,16]{0,1:T(8,128)(2,1)S(1)}, bf16[512,16]{0,1:T(8,128)(2,1)}, u32[]{:S(2)}) copy-start(bf16[512,16]{0,1:T(8,128)(2,1)} %param.31) | copy-start | bytes 49156
  229.7 74.7 %all-to-all-start.3 = ((bf16[4,1,128,2048]{3,2,1,0:T(8,128)(2,1)}), bf16[4,1,128,2048]{3,2,1,0:T(8,128)(2,1)}, u32[]{:S(2)}, u32[]{:S(2)}) async-start(bf16[4,1,128,2048]{3,2,1,0:T(8,128)(2,1)} %fusion.27), calls=%async_computation.3 | async-start | bytes 4194304 | tf_op jit(solution)/shard_map/all_to_all | solution.py:78
  234.3 77.7 %copy-start.37 = (f32[2048]{0:T(1024)S(1)}, f32[2048]{0:T(1024)}, u32[]{:S(2)}) copy-start(f32[2048]{0:T(1024)} %param.30) | copy-start | bytes 24580
  305.1 17.4 %all-to-all-start.4 = ((bf16[4,512,16]{1,2,0:T(8,128)(2,1)}), bf16[4,512,16]{1,2,0:T(8,128)(2,1)S(1)}, u32[]{:S(2)}, u32[]{:S(2)}) async-start(bf16[4,512,16]{1,2,0:T(8,128)(2,1)} %broadcast_in_dim.86), calls=%async_computation.4 | async-start | bytes 131072 | tf_op jit(solution)/shard_map/all_to_all | solution.py:72
  311.1 16.9 %copy-start.50 = (f32[128]{0:T(128)}, f32[128]{0:T(128)S(1)}, u32[]{:S(2)}) copy-start(f32[128]{0:T(128)S(1)} %add_rsqrt_fusion.2) | copy-start | bytes 1540
  322.5 76.3 %all-to-all-start.5 = ((bf16[8,2,96,2048]{3,2,1,0:T(8,128)(2,1)}), bf16[8,2,96,2048]{3,2,1,0:T(8,128)(2,1)}, u32[]{:S(2)}, u32[]{:S(2)}) async-start(bf16[8,2,96,2048]{3,2,1,0:T(8,128)(2,1)} %bitcast.388), calls=%async_computation.5 | async-start | bytes 12582912 | tf_op jit(solution)/shard_map/all_to_all | solution.py:247
  327.2 198.7 %all-gather.11.cloned.1.call-start = ((), (), s32[]{:S(2)}) async-start(), calls=%async_computation.22 | async-start | bytes 7864320 | tf_op jit(solution)/shard_map/all_gather | solution.py:228
  398.8 76.3 %all-to-all-start.7 = ((bf16[8,2,96,2048]{3,2,1,0:T(8,128)(2,1)}), bf16[8,2,96,2048]{3,2,1,0:T(8,128)(2,1)}, u32[]{:S(2)}, u32[]{:S(2)}) async-start(bf16[8,2,96,2048]{3,2,1,0:T(8,128)(2,1)} %bitcast.391), calls=%async_computation.7 | async-start | bytes 12582912 | tf_op jit(solution)/shard_map/all_to_all | solution.py:247
  403.6 707.5 %reduce-scatter.8.cloned.1.call-start = ((), (), s32[]{:S(2)}) async-start(), calls=%async_computation.26 | async-start | bytes 7864320 | tf_op jit(solution)/shard_map/reduce_scatter | solution.py:373
  492.5 48.4 %slice-start.4 = ((s8[6291456]{0:T(1024)(128)(4,1)}), s8[2097152]{0:T(1024)(128)(4,1)S(1)}, s32[]{:S(2)}) async-start(s8[6291456]{0:T(1024)(128)(4,1)} %bitcast.407), calls=%async_computation.32 | async-start | bytes 4194304
  526.0 14.9 %slice-start.5 = ((s8[6291456]{0:T(1024)(128)(4,1)}), s8[4194304]{0:T(1024)(128)(4,1)S(1)}, s32[]{:S(2)}) async-start(s8[6291456]{0:T(1024)(128)(4,1)} %bitcast.407), calls=%async_computation.33 | async-start | bytes 8388608
  559.1 76.3 %all-to-all-start.6 = ((bf16[8,2,96,2048]{3,2,1,0:T(8,128)(2,1)}), bf16[8,2,96,2048]{3,2,1,0:T(8,128)(2,1)}, u32[]{:S(2)}, u32[]{:S(2)}) async-start(bf16[8,2,96,2048]{3,2,1,0:T(8,128)(2,1)} %bitcast.390), calls=%async_computation.6 | async-start | bytes 12582912 | tf_op jit(solution)/shard_map/all_to_all | solution.py:252
  563.9 550.6 %reduce-scatter.6.cloned.1.call-start = ((), (), s32[]{:S(2)}) async-start(), calls=%async_computation.25 | async-start | bytes 7864320 | tf_op jit(solution)/shard_map/reduce_scatter | solution.py:373
  635.5 76.8 %all-to-all-start.8 = ((bf16[8,2,96,2048]{3,2,1,0:T(8,128)(2,1)}), bf16[8,2,96,2048]{3,2,1,0:T(8,128)(2,1)}, u32[]{:S(2)}, u32[]{:S(2)}) async-start(bf16[8,2,96,2048]{3,2,1,0:T(8,128)(2,1)} %bitcast.389), calls=%async_computation.8 | async-start | bytes 12582912 | tf_op jit(solution)/shard_map/all_to_all | solution.py:252
  712.3 19.6 %copy-start.30 = (bf16[4,2,8,512]{3,2,0,1:T(8,128)(2,1)S(1)}, bf16[4,2,8,512]{3,2,0,1:T(8,128)(2,1)}, u32[]{:S(2)}) copy-start(bf16[4,2,8,512]{3,2,0,1:T(8,128)(2,1)} %copy-done.29) | copy-start | bytes 196612
  712.3 19.6 %copy-start.38 = (f32[2048]{0:T(1024)S(1)}, f32[2048]{0:T(1024)}, u32[]{:S(2)}) copy-start(f32[2048]{0:T(1024)} %param.30) | copy-start | bytes 24580
  738.0 76.6 %all-to-all-start.9 = ((bf16[4,128,2048]{2,1,0:T(8,128)(2,1)}), bf16[4,128,2048]{2,1,0:T(8,128)(2,1)S(1)}, u32[]{:S(2)}, u32[]{:S(2)}) async-start(bf16[4,128,2048]{2,1,0:T(8,128)(2,1)} %broadcast_in_dim.91), calls=%async_computation.9 | async-start | bytes 4194304 | tf_op jit(solution)/shard_map/all_to_all | solution.py:72
  741.6 376.2 %reduce-scatter.4.cloned.1.call-start = ((), (), s32[]{:S(2)}) async-start(), calls=%async_computation.24 | async-start | bytes 7864320 | tf_op jit(solution)/shard_map/reduce_scatter | solution.py:373
  821.2 16.2 %slice-start = ((s8[16777216]{0:T(1024)(128)(4,1)}), s8[4194304]{0:T(1024)(128)(4,1)S(1)}, s32[]{:S(2)}) async-start(s8[16777216]{0:T(1024)(128)(4,1)} %bitcast.383), calls=%async_computation.28 | async-start | bytes 8388608
  821.2 16.2 %slice-start.1 = ((s8[16777216]{0:T(1024)(128)(4,1)}), s8[4194304]{0:T(1024)(128)(4,1)S(1)}, s32[]{:S(2)}) async-start(s8[16777216]{0:T(1024)(128)(4,1)} %bitcast.383), calls=%async_computation.29 | async-start | bytes 8388608
  821.2 16.2 %slice-start.2 = ((s8[16777216]{0:T(1024)(128)(4,1)}), s8[4194304]{0:T(1024)(128)(4,1)S(1)}, s32[]{:S(2)}) async-start(s8[16777216]{0:T(1024)(128)(4,1)} %bitcast.383), calls=%async_computation.30 | async-start | bytes 8388608
  821.2 16.2 %slice-start.3 = ((s8[16777216]{0:T(1024)(128)(4,1)}), s8[4194304]{0:T(1024)(128)(4,1)S(1)}, s32[]{:S(2)}) async-start(s8[16777216]{0:T(1024)(128)(4,1)} %bitcast.383), calls=%async_computation.31 | async-start | bytes 8388608
  877.1 19.6 %all-to-all-start.11 = ((bf16[4,8,128,128]{2,3,0,1:T(8,128)(2,1)}), bf16[4,8,128,128]{2,3,0,1:T(8,128)(2,1)}, u32[]{:S(2)}, u32[]{:S(2)}) async-start(bf16[4,8,128,128]{2,3,0,1:T(8,128)(2,1)} %copy.381), calls=%async_computation.11 | async-start | bytes 2097152 | tf_op jit(solution)/shard_map/all_to_all | solution.py:78
  896.8 19.7 %all-to-all-start.10 = ((bf16[4,8,128,128]{2,3,0,1:T(8,128)(2,1)}), bf16[4,8,128,128]{2,3,0,1:T(8,128)(2,1)}, u32[]{:S(2)}, u32[]{:S(2)}) async-start(bf16[4,8,128,128]{2,3,0,1:T(8,128)(2,1)} %copy.376), calls=%async_computation.10 | async-start | bytes 2097152 | tf_op jit(solution)/shard_map/all_to_all | solution.py:78
  928.4 120.1 %all-to-all-start.12 = ((bf16[4,512,1,1280]{3,1,2,0:T(8,128)(2,1)}), bf16[4,512,1,1280]{3,1,2,0:T(8,128)(2,1)}, u32[]{:S(2)}, u32[]{:S(2)}) async-start(bf16[4,512,1,1280]{3,1,2,0:T(8,128)(2,1)} %broadcast_in_dim.156), calls=%async_computation.12 | async-start | bytes 10485760 | tf_op jit(solution)/shard_map/all_to_all | solution.py:72
  933.5 248.9 %all-reduce.7.cloned.1.call-start = ((), (), s32[]{:S(2)}) async-start(), calls=%async_computation.27 | async-start | bytes 10485760 | tf_op jit(solution)/shard_map/psum | solution.py:381
  1072.6 225.4 %all-reduce.5.cloned.1.call-start = ((), (), s32[]{:S(2)}) async-start(), calls=%async_computation.23 | async-start | bytes 16777216 | tf_op jit(solution)/shard_map/psum | solution.py:379
  1093.1 11.7 all-to-all-start.15
  1104.8 31.1 %all-to-all-start.13 = ((f32[4,128,512]{2,1,0:T(8,128)}), f32[4,128,512]{2,1,0:T(8,128)}, u32[]{:S(2)}, u32[]{:S(2)}) async-start(f32[4,128,512]{2,1,0:T(8,128)} %bitcast.96), calls=%async_computation.13 | async-start | bytes 2097152 | tf_op jit(solution)/shard_map/all_to_all | solution.py:367
  1117.9 19.6 %copy-start.56 = (f32[128]{0:T(128)S(1)}, f32[128]{0:T(128)}, u32[]{:S(2)}) copy-start(f32[128]{0:T(128)} %copy-done.55) | copy-start | bytes 1540
  1121.2 19.5 %copy-start.46 = (f32[2048]{0:T(1024)S(1)}, f32[2048]{0:T(1024)}, u32[]{:S(2)}) copy-start(f32[2048]{0:T(1024)} %get-tuple-element.25) | copy-start | bytes 24580
  1121.2 19.5 %copy-start.57 = (f32[128]{0:T(128)S(1)}, f32[128]{0:T(128)}, u32[]{:S(2)}) copy-start(f32[128]{0:T(128)} %get-tuple-element.23) | copy-start | bytes 1540
  (45 other events, 310.3 us)
Sparse Core Ops, SparseCore 0:
  99.1 44.9 all-gather.4
  145.6 148.9 all-gather.8
  296.2 114.8 all-gather.6
  412.5 113.4 all-gather.10
  548.0 108.9 reduce-scatter.7
  659.1 136.2 reduce-scatter.5
  797.7 121.0 reduce-scatter.3
  1072.8 94.9 all-reduce.6
  1171.8 126.1 all-reduce.4

commit v9 on v8

--- a/solution.py
+++ b/solution.py
@@ -209,8 +209,8 @@
     peak = jnp.max(scores, axis=-1, keepdims=True)
     expo = jnp.exp(scores - peak)
     total = jnp.sum(expo, axis=-1, keepdims=True)
-    probs = (expo / total).astype(jnp.bfloat16)
-    log_sums = peak + jnp.log(total)
+    probs_full = expo / total
+    probs = probs_full.astype(jnp.bfloat16)
     attended = (
         contract("skgtj,sjkd->stkgd", probs, values_all)
         .astype(jnp.bfloat16)
@@ -222,12 +222,19 @@
     second_scale = rms_scale(middle)
     second_normed = middle * second_scale
     second_input = (second_normed * ffn_gain).astype(jnp.bfloat16)
-    w_gate, w_up, w_down, w_router = (
-        lax.all_gather(expert_gate, "fsdp", axis=1, tiled=True),
-        lax.all_gather(expert_up, "fsdp", axis=1, tiled=True),
-        lax.all_gather(expert_down, "fsdp", axis=1, tiled=True),
-        gather_a2a(router_proj, "fsdp", fsdp_size, 0),
-    )
+    shards = (expert_gate, expert_up, expert_down)
+    packed = jnp.concatenate([w.reshape(w.shape[0], -1, 128) for w in shards], axis=1)
+    gathered = lax.all_gather(packed, "fsdp", axis=0, tiled=False)
+    unpacked, offset = [], 0
+    for w in shards:
+        size = w.shape[1] * w.shape[2] // 128
+        piece = gathered[:, :, offset : offset + size].reshape((fsdp_size,) + w.shape)
+        unpacked.append(
+            jnp.moveaxis(piece, 0, 1).reshape(w.shape[0], fsdp_size * w.shape[1], w.shape[2])
+        )
+        offset += size
+    w_gate, w_up, w_down = unpacked
+    w_router = gather_a2a(router_proj, "fsdp", fsdp_size, 0)
     logits = matmul(second_input, w_router)
     route_ids = routes[0]
     chosen = jnp.take_along_axis(logits, route_ids, axis=1)
@@ -304,7 +311,7 @@
     grad_attended = contract("td,qd->tq", grad_branch, out_proj).astype(jnp.bfloat16)
     grad_groups = grad_attended.reshape(seqs, tokens, kv_dev, group_dev, HEAD_DIM)
 
-    probs_back = jnp.exp(masked_scores() - log_sums)
+    probs_back = probs_full
     grad_probs = contract("stkgd,sjkd->skgtj", grad_groups, values_all)
     delta = jnp.sum(probs_back * grad_probs, axis=-1, keepdims=True)
     grad_scores = (probs_back * (grad_probs - delta)).astype(jnp.bfloat16)
@@ -369,12 +376,25 @@
     )[0]
     grad_hidden, attn_gain_grad = norm_back(grad_first, first_normed, first_scale, attn_gain)
     grad_hidden = grad_hidden + grad_middle
-    gate_grad, up_grad, down_grad = (
-        lax.psum_scatter(
-            full.astype(jnp.bfloat16), "fsdp", scatter_dimension=1, tiled=True
-        ).astype(jnp.float32)
-        for full in (gate_grad_full, up_grad_full, down_grad_full)
-    )
+
+    def by_owner(full):
+        count, rows, cols = full.shape
+        part = full.astype(jnp.bfloat16).reshape(count, fsdp_size, rows // fsdp_size, cols)
+        return jnp.moveaxis(part, 1, 0).reshape(fsdp_size, count, -1, 128)
+
+    fulls = (gate_grad_full, up_grad_full, down_grad_full)
+    summed = lax.psum_scatter(
+        jnp.concatenate([by_owner(g) for g in fulls], axis=2),
+        "fsdp",
+        scatter_dimension=0,
+        tiled=True,
+    )[0]
+    owned, offset = [], 0
+    for shard in shards:
+        size = shard.shape[1] * shard.shape[2] // 128
+        owned.append(summed[:, offset : offset + size].reshape(shard.shape).astype(jnp.float32))
+        offset += size
+    gate_grad, up_grad, down_grad = owned
     router_shard = scatter_sum_a2a(router_grad_full, "fsdp", fsdp_size, 0)
     out_grad = lax.psum(out_grad_part, "ctx")
     query_grad, key_grad, value_grad = (

time: 1320 us -> 1680 us (1.27)
  waiting for transfers between devices: 694 us -> 851 us
  local copies, waits for them, and re-layouts: 176 us -> 316 us
  blocking collectives: 47.3 us -> 110 us
  other arithmetic: 120 us -> 143 us
  matrix products: 192 us -> 171 us
    reduce_scatter x3 -> x1, waiting for transfers between devices: 0.02 us -> 188 us  [per_device(): lax.psum_scatter(jnp.concatenate([by_owner(g) for g in fulls], axis=2), '...]
    reshape x0 -> x12, local copies, waits for them, and re-layouts: none -> 90.4 us  [the longest x6 46 us: per_device(): piece = gathered[:, :, offset:offset + size].reshape((fsdp_size,) + w.shape)]
    all_to_all x1 -> x0, waiting for transfers between devices: 59.5 us -> none  [per_device(): got = lax.all_to_all(payload, 'fsdp', 0, 0, tiled=True)]
    all_to_all x1, blocking collectives: 8.32 us -> 65.8 us  [per_device(): got = lax.all_to_all(payload, 'fsdp', 0, 0, tiled=True)]
    all_to_all x6, waiting for transfers between devices: 189 us -> 146 us  [gather_a2a(): lax.all_to_all(rep, axis_name, 0, 0, tiled=True)]
    all_to_all x1, waiting for transfers between devices: 14.7 us -> 52.1 us  [per_device(): lax.all_to_all(grad_first_cols.reshape(seqs, tokens, d_part), 'fsdp', 0,...]
    all_to_all x3 -> x4, waiting for transfers between devices: 72 us -> 106 us  [scatter_sum_a2a(): got = lax.all_to_all(parts, axis_name, axis, axis, tiled=True)]
    all_to_all x2, waiting for transfers between devices: 90.2 us -> 120 us  [from_experts(): back = lax.all_to_all(parts, 'ctx', 0, 0, tiled=True)]
  transfers between devices with their start and end apart: 25 -> 21, of which waited for: 16 -> 16; matrix products, arithmetic and copies ran while one was open for 33% -> 24% of each run, Pallas kernels for 0% -> 0%
where the time goes in v9:
time: 1680 us; the launch traced here: 1670 us
  waiting for transfers between devices  851 us (51%)
  local copies, waits for them, and re-layouts  316 us (19%)
  matrix products  171 us (10%)
  other arithmetic  143 us (9%)
  blocking collectives  110 us (7%)
  starting transfers between devices  67.8 us (4%)
    reduce_scatter x1, waiting for transfers between devices, per_device(): lax.psum_scatter(jnp.concatenate([by_owner(g) for g in fulls], axis=2), '...  188 us
    dot_general x25, matrix products, contract(): return jnp.einsum(form, left, right, preferred_element_type=jnp.float32)  153 us
    all_to_all x6, waiting for transfers between devices, gather_a2a(): lax.all_to_all(rep, axis_name, 0, 0, tiled=True)  146 us
    all_to_all x2, waiting for transfers between devices, from_experts(): back = lax.all_to_all(parts, 'ctx', 0, 0, tiled=True)  120 us
    all_to_all x2, waiting for transfers between devices, to_experts(): got = lax.all_to_all(buffer, 'ctx', 0, 0, tiled=True)  117 us
    psum x1, waiting for transfers between devices, per_device(): out_grad = lax.psum(out_grad_part, 'ctx')  114 us
    all_to_all x4, waiting for transfers between devices, scatter_sum_a2a(): got = lax.all_to_all(parts, axis_name, axis, axis, tiled=True)  106 us
    all_to_all x1, blocking collectives, per_device(): got = lax.all_to_all(payload, 'fsdp', 0, 0, tiled=True)  65.8 us
  transfers between devices with their start and end apart: 21, of which 16 were waited for; matrix products, arithmetic and copies ran while one was open for 24% of the time, Pallas kernels for 0%

profile of v9, /device:TPU:0, one launch (start us, length us, event | category | flops | bytes accessed | tf_op | source)
XLA Modules:
  0.0 1674.0 jit_solution(3072470205935598029)
XLA Ops:
  24.5 65.8 %all_to_all.90 = bf16[4,2568,128]{2,1,0:T(8,128)(2,1)S(1)} all-to-all(bf16[4,2568,128]{2,1,0:T(8,128)(2,1)S(1)} %pad_maximum_fusion.2), channel_id=1, replica_groups=mesh['ctx'=8,'fsdp'=4] {'fsdp'}, dimensions={0} | all-to-all | bytes 5259264 | tf_op jit(solution)/shard_map/all_to_all | solution.py:149
  108.1 7.4 maximum_select_fusion
  126.1 8.5 pad_maximum_fusion.1
  138.0 8.6 all-gather.4.cloned.1.call-done
  189.3 7.4 all-to-all-done.1
  201.8 9.4 fusion.5
  211.2 9.3 fusion.4
  220.6 8.3 convert_bitcast_fusion
  248.1 99.6 %all-to-all-done.3 = bf16[4,1,128,2048]{3,2,1,0:T(8,128)(2,1)} async-done(((bf16[4,1,128,2048]{3,2,1,0:T(8,128)(2,1)}), bf16[4,1,128,2048]{3,2,1,0:T(8,128)(2,1)}, u32[]{:S(2)}, u32[]{:S(2)}) %all-to-all-start.3) | async-done | bytes 2097184 | tf_op jit(solution)/shard_map/all_to_all | solution.py:78
  355.2 10.2 scatter_custom_fusion
  373.0 7.0 gather_fusion.2
  380.8 10.6 scatter_custom_fusion.1
  391.4 52.0 %all-to-all-done.5 = bf16[8,2,96,2048]{3,2,1,0:T(8,128)(2,1)} async-done(((bf16[8,2,96,2048]{3,2,1,0:T(8,128)(2,1)}), bf16[8,2,96,2048]{3,2,1,0:T(8,128)(2,1)}, u32[]{:S(2)}, u32[]{:S(2)}) %all-to-all-start.5) | async-done | bytes 6291488 | tf_op jit(solution)/shard_map/all_to_all | solution.py:254
  454.8 65.0 %all-to-all-done.7 = bf16[8,2,96,2048]{3,2,1,0:T(8,128)(2,1)} async-done(((bf16[8,2,96,2048]{3,2,1,0:T(8,128)(2,1)}), bf16[8,2,96,2048]{3,2,1,0:T(8,128)(2,1)}, u32[]{:S(2)}, u32[]{:S(2)}) %all-to-all-start.7) | async-done | bytes 6291488 | tf_op jit(solution)/shard_map/all_to_all | solution.py:254
  526.5 16.1 fusion.87
  542.5 11.6 reshape.953
  559.9 11.6 reshape.954
  576.8 9.8 fusion.90
  593.2 10.3 reshape.955
  606.9 15.4 multiply_convert_fusion
  622.3 10.7 fusion.92
  633.0 9.9 add_convert_fusion
  651.5 7.9 convolution_convert_fusion.4
  662.6 60.5 %all-to-all-done.8 = bf16[8,2,96,2048]{3,2,1,0:T(8,128)(2,1)} async-done(((bf16[8,2,96,2048]{3,2,1,0:T(8,128)(2,1)}), bf16[8,2,96,2048]{3,2,1,0:T(8,128)(2,1)}, u32[]{:S(2)}, u32[]{:S(2)}) %all-to-all-start.8) | async-done | bytes 6291488 | tf_op jit(solution)/shard_map/all_to_all | solution.py:259
  728.3 12.4 gather_fusion.4
  740.7 59.1 %all-to-all-done.6 = bf16[8,2,96,2048]{3,2,1,0:T(8,128)(2,1)} async-done(((bf16[8,2,96,2048]{3,2,1,0:T(8,128)(2,1)}), bf16[8,2,96,2048]{3,2,1,0:T(8,128)(2,1)}, u32[]{:S(2)}, u32[]{:S(2)}) %all-to-all-start.6) | async-done | bytes 6291488 | tf_op jit(solution)/shard_map/all_to_all | solution.py:259
  799.8 12.4 gather_fusion.3
  812.3 7.8 convert_reduce_fusion
  838.5 12.3 copy.419
  853.0 30.9 %all-to-all-done.9 = bf16[4,128,2048]{2,1,0:T(8,128)(2,1)} async-done(((bf16[4,128,2048]{2,1,0:T(8,128)(2,1)}), bf16[4,128,2048]{2,1,0:T(8,128)(2,1)}, u32[]{:S(2)}, u32[]{:S(2)}) %all-to-all-start.9) | async-done | bytes 2097184 | tf_op jit(solution)/shard_map/all_to_all | solution.py:72
  897.8 12.1 fusion
  909.9 12.8 fusion.6
  963.4 10.1 convolution_convert_fusion.1
  973.5 104.1 %all-to-all-done.12 = bf16[4,512,1,1280]{3,1,2,0:T(8,128)(2,1)} async-done(((bf16[4,512,1,1280]{3,1,2,0:T(8,128)(2,1)}), bf16[4,512,1,1280]{3,1,2,0:T(8,128)(2,1)}, u32[]{:S(2)}, u32[]{:S(2)}) %all-to-all-start.12) | async-done | bytes 5242912 | tf_op jit(solution)/shard_map/all_to_all | solution.py:72
  1090.2 6.9 convolution_convert_fusion
  1099.8 9.9 convolution_convert_fusion.2
  1109.7 10.6 reshape.870
  1120.3 11.6 reshape.868
  1131.9 9.8 convolution_convert_fusion.3
  1141.7 11.7 reshape.866
  1153.4 15.1 pad_maximum_fusion
  1168.5 17.8 %copy.466 = bf16[4,2,9216,128]{3,2,1,0:T(8,128)(2,1)} copy(bf16[4,2,9216,128]{3,2,0,1:T(8,128)(2,1)} %pad_maximum_fusion) | data formatting | bytes 37748736 | tf_op jit(solution)/shard_map/concatenate | solution.py:387
  1203.1 7.4 fusion.39
  1224.8 52.1 %all-to-all-done.13 = f32[4,128,512]{2,1,0:T(8,128)} async-done(((f32[4,128,512]{2,1,0:T(8,128)}), f32[4,128,512]{2,1,0:T(8,128)}, u32[]{:S(2)}, u32[]{:S(2)}) %all-to-all-start.13) | async-done | bytes 1048608 | tf_op jit(solution)/shard_map/all_to_all | solution.py:374
  1281.7 43.8 %all-reduce = (f32[2048]{0:T(1024)}, f32[128]{0:T(128)}, f32[128]{0:T(128)}, f32[2048]{0:T(1024)}) all-reduce(f32[2048]{0:T(1024)S(1)} %bitcast.507, f32[128]{0:T(128)S(1)} %bitcast_reduce_fusion, f32[128]{0:T(128)S(1)} %get-tuple-element.23, f32[2048]{0:T(1024)S(1)} %copy-done.55), channel_id=1, replica_groups=mesh['ctx'=8,'fsdp'=4] {'ctx','fsdp'}, use_global_device_ids=true, to_apply=%region_24.26 | all-reduce | flops 4352 | bytes 34816 | tf_op jit(solution)/shard_map/psum | solution.py:405
  1337.4 188.2 %reduce-scatter.2.cloned.1.call-done = bf16[1,2,9216,128]{3,2,1,0:T(8,128)(2,1)} async-done(((bf16[4,2,9216,128]{3,2,1,0:T(8,128)(2,1)}), bf16[1,2,9216,128]{3,2,1,0:T(8,128)(2,1)}) %reduce-scatter.2.cloned.1.call-update) | async-done | bytes 4718608 | tf_op jit(solution)/shard_map/reduce_scatter | solution.py:386
  1545.7 113.7 %all-reduce.5.cloned.1.call-done = f32[1024,2048]{1,0:T(8,128)} async-done(((f32[1024,2048]{1,0:T(8,128)}), f32[1024,2048]{1,0:T(8,128)}) %all-reduce.5.cloned.1.call-update) | async-done | bytes 8388624 | tf_op jit(solution)/shard_map/psum | solution.py:399
  1659.3 7.9 copy.519
  (365 shorter events, 345.3 us)
Async XLA Ops:
  7.2 139.4 %all-gather.4.cloned.1.call-start = ((), (), s32[]{:S(2)}) async-start(), calls=%async_computation.17 | async-start | bytes 2621440 | tf_op jit(solution)/shard_map/all_gather | solution.py:153
  91.8 7.9 copy-start.2
  93.4 8.4 copy-start.67
  99.7 8.5 collective-permute-start
  101.3 425.1 %all-gather.6.cloned.1.call-start = ((), (), s32[]{:S(2)}) async-start(), calls=%async_computation.20 | async-start | bytes 23592960 | tf_op jit(solution)/shard_map/all_gather | solution.py:227
  135.3 19.8 %copy-start.34 = (f32[128,64]{0,1:T(8,128)}, f32[128,64]{0,1:T(8,128)S(1)}, u32[]{:S(2)}) copy-start(f32[128,64]{0,1:T(8,128)S(1)} %get-tuple-element.70) | copy-start | bytes 98308
  135.3 19.8 %copy-start.36 = (f32[128,64]{0,1:T(8,128)}, f32[128,64]{0,1:T(8,128)S(1)}, u32[]{:S(2)}) copy-start(f32[128,64]{0,1:T(8,128)S(1)} %get-tuple-element.71) | copy-start | bytes 98308
  135.4 50.4 %copy-start.28 = (f32[128,64]{1,0:T(8,128)}, f32[128,64]{1,0:T(8,128)S(1)}, u32[]{:S(2)}) copy-start(f32[128,64]{1,0:T(8,128)S(1)} %copy.386) | copy-start | bytes 98308
  135.5 50.3 %copy-start.30 = (f32[128,64]{1,0:T(8,128)}, f32[128,64]{1,0:T(8,128)S(1)}, u32[]{:S(2)}) copy-start(f32[128,64]{1,0:T(8,128)S(1)} %copy.385) | copy-start | bytes 98308
  136.7 9.8 copy-start.27
  138.0 17.0 %copy-start.61 = (f32[128]{0:T(128)S(1)}, f32[128]{0:T(128)}, u32[]{:S(2)}) copy-start(f32[128]{0:T(128)} %param.28) | copy-start | bytes 1540
  156.5 19.2 %all-to-all-start.2 = ((bf16[8,4,128,128]{3,2,1,0:T(8,128)(2,1)}), bf16[8,4,128,128]{3,2,1,0:T(8,128)(2,1)S(1)}, u32[]{:S(2)}, u32[]{:S(2)}) async-start(bf16[8,4,128,128]{3,2,1,0:T(8,128)(2,1)} %broadcast_in_dim.80), calls=%async_computation.2 | async-start | bytes 2097152 | tf_op jit(solution)/shard_map/all_to_all | solution.py:72
  168.7 51.9 %copy-start.8 = (pred[4,128,1024]{1,2,0:T(8,128)(4,1)}, pred[4,128,1024]{1,2,0:T(8,128)(4,1)S(1)}, u32[]{:S(2)}) copy-start(pred[4,128,1024]{1,2,0:T(8,128)(4,1)S(1)} %compare_and_fusion) | copy-start | bytes 1572868
  175.7 10.1 copy-start.24
  177.0 19.6 %all-to-all-start.1 = ((bf16[8,4,128,128]{2,3,1,0:T(8,128)(2,1)}), bf16[8,4,128,128]{2,3,1,0:T(8,128)(2,1)}, u32[]{:S(2)}, u32[]{:S(2)}) async-start(bf16[8,4,128,128]{2,3,1,0:T(8,128)(2,1)} %broadcast_in_dim.74), calls=%async_computation.1 | async-start | bytes 2097152 | tf_op jit(solution)/shard_map/all_to_all | solution.py:72
  189.2 21.9 %copy-start.10 = (bf16[4,8,128,128]{3,2,1,0:T(8,128)(2,1)}, bf16[4,8,128,128]{3,2,1,0:T(8,128)(2,1)S(1)}, u32[]{:S(2)}) copy-start(bf16[4,8,128,128]{3,2,1,0:T(8,128)(2,1)S(1)} %copy.382) | copy-start | bytes 3145732
  211.2 9.4 copy-start.43
  220.5 8.4 copy-start.48
  220.6 8.4 copy-start.22
  238.0 109.8 %copy-start.57 = (bf16[512,16]{0,1:T(8,128)(2,1)S(1)}, bf16[512,16]{0,1:T(8,128)(2,1)}, u32[]{:S(2)}) copy-start(bf16[512,16]{0,1:T(8,128)(2,1)} %param.31) | copy-start | bytes 49156
  238.0 109.8 %all-to-all-start.3 = ((bf16[4,1,128,2048]{3,2,1,0:T(8,128)(2,1)}), bf16[4,1,128,2048]{3,2,1,0:T(8,128)(2,1)}, u32[]{:S(2)}, u32[]{:S(2)}) async-start(bf16[4,1,128,2048]{3,2,1,0:T(8,128)(2,1)} %fusion.25), calls=%async_computation.3 | async-start | bytes 4194304 | tf_op jit(solution)/shard_map/all_to_all | solution.py:78
  242.6 112.4 %copy-start.45 = (f32[2048]{0:T(1024)S(1)}, f32[2048]{0:T(1024)}, u32[]{:S(2)}) copy-start(f32[2048]{0:T(1024)} %param.30) | copy-start | bytes 24580
  348.4 18.2 %all-to-all-start.4 = ((bf16[4,512,16]{1,2,0:T(8,128)(2,1)}), bf16[4,512,16]{1,2,0:T(8,128)(2,1)S(1)}, u32[]{:S(2)}, u32[]{:S(2)}) async-start(bf16[4,512,16]{1,2,0:T(8,128)(2,1)} %broadcast_in_dim.82), calls=%async_computation.4 | async-start | bytes 131072 | tf_op jit(solution)/shard_map/all_to_all | solution.py:72
  354.1 17.9 %copy-start.58 = (f32[128]{0:T(128)}, f32[128]{0:T(128)S(1)}, u32[]{:S(2)}) copy-start(f32[128]{0:T(128)S(1)} %add_rsqrt_fusion.2) | copy-start | bytes 1540
  366.6 76.7 %all-to-all-start.5 = ((bf16[8,2,96,2048]{3,2,1,0:T(8,128)(2,1)}), bf16[8,2,96,2048]{3,2,1,0:T(8,128)(2,1)}, u32[]{:S(2)}, u32[]{:S(2)}) async-start(bf16[8,2,96,2048]{3,2,1,0:T(8,128)(2,1)} %bitcast.430), calls=%async_computation.5 | async-start | bytes 12582912 | tf_op jit(solution)/shard_map/all_to_all | solution.py:254
  443.3 76.5 %all-to-all-start.7 = ((bf16[8,2,96,2048]{3,2,1,0:T(8,128)(2,1)}), bf16[8,2,96,2048]{3,2,1,0:T(8,128)(2,1)}, u32[]{:S(2)}, u32[]{:S(2)}) async-start(bf16[8,2,96,2048]{3,2,1,0:T(8,128)(2,1)} %bitcast.432), calls=%async_computation.7 | async-start | bytes 12582912 | tf_op jit(solution)/shard_map/all_to_all | solution.py:254
  571.5 15.1 slice-start
  574.8 11.7 copy-start.19
  576.8 9.8 slice-start.1
  606.9 15.4 copy-start.17
  622.3 10.7 copy-start.68
  646.8 76.3 %all-to-all-start.8 = ((bf16[8,2,96,2048]{3,2,1,0:T(8,128)(2,1)}), bf16[8,2,96,2048]{3,2,1,0:T(8,128)(2,1)}, u32[]{:S(2)}, u32[]{:S(2)}) async-start(bf16[8,2,96,2048]{3,2,1,0:T(8,128)(2,1)} %bitcast.433), calls=%async_computation.8 | async-start | bytes 12582912 | tf_op jit(solution)/shard_map/all_to_all | solution.py:259
  723.1 76.7 %all-to-all-start.6 = ((bf16[8,2,96,2048]{3,2,1,0:T(8,128)(2,1)}), bf16[8,2,96,2048]{3,2,1,0:T(8,128)(2,1)}, u32[]{:S(2)}, u32[]{:S(2)}) async-start(bf16[8,2,96,2048]{3,2,1,0:T(8,128)(2,1)} %bitcast.431), calls=%async_computation.6 | async-start | bytes 12582912 | tf_op jit(solution)/shard_map/all_to_all | solution.py:259
  833.8 50.1 %all-to-all-start.9 = ((bf16[4,128,2048]{2,1,0:T(8,128)(2,1)}), bf16[4,128,2048]{2,1,0:T(8,128)(2,1)}, u32[]{:S(2)}, u32[]{:S(2)}) async-start(bf16[4,128,2048]{2,1,0:T(8,128)(2,1)} %broadcast_in_dim.87), calls=%async_computation.9 | async-start | bytes 4194304 | tf_op jit(solution)/shard_map/all_to_all | solution.py:72
  892.5 40.1 %all-to-all-start.11 = ((bf16[4,8,128,128]{2,3,0,1:T(8,128)(2,1)}), bf16[4,8,128,128]{2,3,0,1:T(8,128)(2,1)}, u32[]{:S(2)}, u32[]{:S(2)}) async-start(bf16[4,8,128,128]{2,3,0,1:T(8,128)(2,1)} %copy.420), calls=%async_computation.11 | async-start | bytes 2097152 | tf_op jit(solution)/shard_map/all_to_all | solution.py:78
  909.9 12.8 copy-start.14
  909.9 12.8 copy-start.15
  932.7 19.8 %all-to-all-start.10 = ((bf16[4,8,128,128]{2,3,0,1:T(8,128)(2,1)}), bf16[4,8,128,128]{2,3,0,1:T(8,128)(2,1)S(1)}, u32[]{:S(2)}, u32[]{:S(2)}) async-start(bf16[4,8,128,128]{2,3,0,1:T(8,128)(2,1)} %copy.415), calls=%async_computation.10 | async-start | bytes 2097152 | tf_op jit(solution)/shard_map/all_to_all | solution.py:78
  958.3 119.4 %all-to-all-start.12 = ((bf16[4,512,1,1280]{3,1,2,0:T(8,128)(2,1)}), bf16[4,512,1,1280]{3,1,2,0:T(8,128)(2,1)}, u32[]{:S(2)}, u32[]{:S(2)}) async-start(bf16[4,512,1,1280]{3,1,2,0:T(8,128)(2,1)} %broadcast_in_dim.88), calls=%async_computation.12 | async-start | bytes 10485760 | tf_op jit(solution)/shard_map/all_to_all | solution.py:72
  963.4 365.0 %all-reduce.7.cloned.1.call-start = ((), (), s32[]{:S(2)}) async-start(), calls=%async_computation.21 | async-start | bytes 10485760 | tf_op jit(solution)/shard_map/psum | solution.py:401
  1099.7 425.8 %reduce-scatter.2.cloned.1.call-start = ((), (), s32[]{:S(2)}) async-start(), calls=%async_computation.19 | async-start | bytes 23592960 | tf_op jit(solution)/shard_map/reduce_scatter | solution.py:386
  1188.9 9.2 all-to-all-start.14
  1198.9 19.5 %all-to-all-start.15 = ((f32[8,1,512,16]{2,3,1,0:T(8,128)}), f32[8,1,512,16]{2,3,1,0:T(8,128)S(1)}, u32[]{:S(2)}, u32[]{:S(2)}) async-start(f32[8,1,512,16]{2,3,1,0:T(8,128)} %broadcast_in_dim.90), calls=%async_computation.15 | async-start | bytes 524288 | tf_op jit(solution)/shard_map/all_to_all | solution.py:72
  1202.9 456.5 %all-reduce.5.cloned.1.call-start = ((), (), s32[]{:S(2)}) async-start(), calls=%async_computation.18 | async-start | bytes 16777216 | tf_op jit(solution)/shard_map/psum | solution.py:399
  1218.4 61.4 %copy-start.65 = (f32[128]{0:T(128)S(1)}, f32[128]{0:T(128)}, u32[]{:S(2)}) copy-start(f32[128]{0:T(128)} %copy-done.64) | copy-start | bytes 1540
  1218.4 58.5 %all-to-all-start.13 = ((f32[4,128,512]{2,1,0:T(8,128)}), f32[4,128,512]{2,1,0:T(8,128)}, u32[]{:S(2)}, u32[]{:S(2)}) async-start(f32[4,128,512]{2,1,0:T(8,128)} %bitcast.469), calls=%async_computation.13 | async-start | bytes 2097152 | tf_op jit(solution)/shard_map/all_to_all | solution.py:374
  1222.8 58.9 %copy-start.55 = (f32[2048]{0:T(1024)S(1)}, f32[2048]{0:T(1024)}, u32[]{:S(2)}) copy-start(f32[2048]{0:T(1024)} %get-tuple-element.25) | copy-start | bytes 24580
  1328.4 7.9 copy-start.38
  (44 other events, 202.3 us)
Sparse Core Ops, SparseCore 0:
  101.4 45.0 all-gather.3
  148.1 367.5 all-gather.5
  1099.9 91.6 all-reduce.6
  1193.7 331.7 reduce-scatter.1
  1529.4 129.8 all-reduce.4

commit v10 on v8

--- a/solution.py
+++ b/solution.py
@@ -209,8 +209,8 @@
     peak = jnp.max(scores, axis=-1, keepdims=True)
     expo = jnp.exp(scores - peak)
     total = jnp.sum(expo, axis=-1, keepdims=True)
-    probs = (expo / total).astype(jnp.bfloat16)
-    log_sums = peak + jnp.log(total)
+    probs_full = expo / total
+    probs = probs_full.astype(jnp.bfloat16)
     attended = (
         contract("skgtj,sjkd->stkgd", probs, values_all)
         .astype(jnp.bfloat16)
@@ -222,9 +222,10 @@
     second_scale = rms_scale(middle)
     second_normed = middle * second_scale
     second_input = (second_normed * ffn_gain).astype(jnp.bfloat16)
+    gate_up = lax.all_gather(jnp.stack([expert_gate, expert_up]), "fsdp", axis=2, tiled=True)
     w_gate, w_up, w_down, w_router = (
-        lax.all_gather(expert_gate, "fsdp", axis=1, tiled=True),
-        lax.all_gather(expert_up, "fsdp", axis=1, tiled=True),
+        gate_up[0],
+        gate_up[1],
         lax.all_gather(expert_down, "fsdp", axis=1, tiled=True),
         gather_a2a(router_proj, "fsdp", fsdp_size, 0),
     )
@@ -304,7 +305,7 @@
     grad_attended = contract("td,qd->tq", grad_branch, out_proj).astype(jnp.bfloat16)
     grad_groups = grad_attended.reshape(seqs, tokens, kv_dev, group_dev, HEAD_DIM)
 
-    probs_back = jnp.exp(masked_scores() - log_sums)
+    probs_back = probs_full
     grad_probs = contract("stkgd,sjkd->skgtj", grad_groups, values_all)
     delta = jnp.sum(probs_back * grad_probs, axis=-1, keepdims=True)
     grad_scores = (probs_back * (grad_probs - delta)).astype(jnp.bfloat16)
@@ -369,12 +370,16 @@
     )[0]
     grad_hidden, attn_gain_grad = norm_back(grad_first, first_normed, first_scale, attn_gain)
     grad_hidden = grad_hidden + grad_middle
-    gate_grad, up_grad, down_grad = (
-        lax.psum_scatter(
-            full.astype(jnp.bfloat16), "fsdp", scatter_dimension=1, tiled=True
-        ).astype(jnp.float32)
-        for full in (gate_grad_full, up_grad_full, down_grad_full)
-    )
+    down_grad = lax.psum_scatter(
+        down_grad_full.astype(jnp.bfloat16), "fsdp", scatter_dimension=1, tiled=True
+    ).astype(jnp.float32)
+    gate_up_grad = lax.psum_scatter(
+        jnp.stack([gate_grad_full, up_grad_full]).astype(jnp.bfloat16),
+        "fsdp",
+        scatter_dimension=2,
+        tiled=True,
+    ).astype(jnp.float32)
+    gate_grad, up_grad = gate_up_grad[0], gate_up_grad[1]
     router_shard = scatter_sum_a2a(router_grad_full, "fsdp", fsdp_size, 0)
     out_grad = lax.psum(out_grad_part, "ctx")
     query_grad, key_grad, value_grad = (

time: 1320 us -> 1530 us (1.16)
  waiting for transfers between devices: 694 us -> 886 us
  matrix products: 192 us -> 175 us
    reduce_scatter x3 -> x2, waiting for transfers between devices: 0.02 us -> 156 us  [the longest x1 156 us: per_device(): lax.psum_scatter(jnp.stack([gate_grad_full, up_grad_full]).astype(jnp.bfl...]
    all_to_all x3 -> x4, waiting for transfers between devices: 72 us -> 105 us  [scatter_sum_a2a(): got = lax.all_to_all(parts, axis_name, axis, axis, tiled=True)]
    all_gather x1, waiting for transfers between devices: 22.9 us -> 0.01 us  [per_device(): lax.all_gather(expert_down, 'fsdp', axis=1, tiled=True)]
    dot_general x25, matrix products: 175 us -> 153 us  [contract(): return jnp.einsum(form, left, right, preferred_element_type=jnp.float32)]
    psum x1, waiting for transfers between devices: 105 us -> 126 us  [per_device(): out_grad = lax.psum(out_grad_part, 'ctx')]
    another operation x6 -> x9, other arithmetic: 19.9 us -> 35.8 us
  transfers between devices with their start and end apart: 25 -> 24, of which waited for: 16 -> 16; matrix products, arithmetic and copies ran while one was open for 33% -> 26% of each run, Pallas kernels for 0% -> 0%
where the time goes in v10:
time: 1530 us; the launch traced here: 1510 us
  waiting for transfers between devices  886 us (58%)
  local copies, waits for them, and re-layouts  182 us (12%)
  matrix products  175 us (11%)
  other arithmetic  132 us (9%)
  starting transfers between devices  75.4 us (5%)
  blocking collectives  47.1 us (3%)
  between operations  15.7 us (1%)
    all_to_all x6, waiting for transfers between devices, gather_a2a(): lax.all_to_all(rep, axis_name, 0, 0, tiled=True)  185 us
    reduce_scatter x1, waiting for transfers between devices, per_device(): lax.psum_scatter(jnp.stack([gate_grad_full, up_grad_full]).astype(jnp.bfl...  156 us
    dot_general x25, matrix products, contract(): return jnp.einsum(form, left, right, preferred_element_type=jnp.float32)  153 us
    psum x1, waiting for transfers between devices, per_device(): out_grad = lax.psum(out_grad_part, 'ctx')  126 us
    all_to_all x2, waiting for transfers between devices, to_experts(): got = lax.all_to_all(buffer, 'ctx', 0, 0, tiled=True)  115 us
    all_to_all x4, waiting for transfers between devices, scatter_sum_a2a(): got = lax.all_to_all(parts, axis_name, axis, axis, tiled=True)  105 us
    all_to_all x2, waiting for transfers between devices, from_experts(): back = lax.all_to_all(parts, 'ctx', 0, 0, tiled=True)  95.7 us
    all_to_all x1, waiting for transfers between devices, per_device(): got = lax.all_to_all(payload, 'fsdp', 0, 0, tiled=True)  59.5 us
  transfers between devices with their start and end apart: 24, of which 16 were waited for; matrix products, arithmetic and copies ran while one was open for 26% of the time, Pallas kernels for 0%

profile of v10, /device:TPU:0, one launch (start us, length us, event | category | flops | bytes accessed | tf_op | source)
XLA Modules:
  0.0 1512.7 jit_solution(13704886682449176957)
XLA Ops:
  22.4 6.3 all-to-all-start
  28.9 59.5 %all-to-all-done = bf16[4,2568,128]{2,1,0:T(8,128)(2,1)} async-done(((bf16[4,2568,128]{2,1,0:T(8,128)(2,1)}), bf16[4,2568,128]{2,1,0:T(8,128)(2,1)}, u32[]{:S(2)}, u32[]{:S(2)}) %all-to-all-start) | async-done | bytes 2629664 | tf_op jit(solution)/shard_map/all_to_all | solution.py:149
  91.8 6.2 reshape.772
  100.6 6.2 stack_reshape.4
  106.9 8.0 maximum_select_fusion
  122.0 22.1 %all-gather.4.cloned.1.call-done = bf16[512,2048]{1,0:T(8,128)(2,1)} async-done(((bf16[128,2048]{1,0:T(8,128)(2,1)}), bf16[512,2048]{1,0:T(8,128)(2,1)}) %all-gather.4.cloned.1.call-update) | async-done | bytes 2097168 | tf_op jit(solution)/shard_map/all_gather | solution.py:153
  144.1 6.0 fusion.92
  186.8 7.4 all-to-all-done.1
  199.3 9.2 fusion.5
  208.5 9.4 fusion.4
  218.0 8.3 convert_bitcast_fusion
  245.5 98.5 %all-to-all-done.3 = bf16[4,1,128,2048]{3,2,1,0:T(8,128)(2,1)} async-done(((bf16[4,1,128,2048]{3,2,1,0:T(8,128)(2,1)}), bf16[4,1,128,2048]{3,2,1,0:T(8,128)(2,1)}, u32[]{:S(2)}, u32[]{:S(2)}) %all-to-all-start.3) | async-done | bytes 2097184 | tf_op jit(solution)/shard_map/all_to_all | solution.py:78
  351.6 10.2 scatter_custom_fusion
  369.1 7.4 gather_fusion.2
  377.3 10.6 scatter_custom_fusion.1
  387.9 50.2 %all-to-all-done.5 = bf16[8,2,96,2048]{3,2,1,0:T(8,128)(2,1)} async-done(((bf16[8,2,96,2048]{3,2,1,0:T(8,128)(2,1)}), bf16[8,2,96,2048]{3,2,1,0:T(8,128)(2,1)}, u32[]{:S(2)}, u32[]{:S(2)}) %all-to-all-start.5) | async-done | bytes 6291488 | tf_op jit(solution)/shard_map/all_to_all | solution.py:248
  443.1 6.6 copy.362
  449.8 64.9 %all-to-all-done.7 = bf16[8,2,96,2048]{3,2,1,0:T(8,128)(2,1)} async-done(((bf16[8,2,96,2048]{3,2,1,0:T(8,128)(2,1)}), bf16[8,2,96,2048]{3,2,1,0:T(8,128)(2,1)}, u32[]{:S(2)}, u32[]{:S(2)}) %all-to-all-start.7) | async-done | bytes 6291488 | tf_op jit(solution)/shard_map/all_to_all | solution.py:248
  514.7 6.6 copy.365
  521.3 10.5 fusion.11
  533.0 6.6 fusion.9
  539.7 13.9 multiply_convert_fusion
  553.6 7.0 convolution_convert_fusion.2
  568.9 10.7 fusion.8
  579.6 9.9 add_convert_fusion
  593.4 47.1 %all-to-all-done.6 = bf16[8,2,96,2048]{3,2,1,0:T(8,128)(2,1)} async-done(((bf16[8,2,96,2048]{3,2,1,0:T(8,128)(2,1)}), bf16[8,2,96,2048]{3,2,1,0:T(8,128)(2,1)}, u32[]{:S(2)}, u32[]{:S(2)}) %all-to-all-start.6) | async-done | bytes 6291488 | tf_op jit(solution)/shard_map/all_to_all | solution.py:253
  645.3 12.4 gather_fusion.3
  668.3 48.5 %all-to-all-done.8 = bf16[8,2,96,2048]{3,2,1,0:T(8,128)(2,1)} async-done(((bf16[8,2,96,2048]{3,2,1,0:T(8,128)(2,1)}), bf16[8,2,96,2048]{3,2,1,0:T(8,128)(2,1)}, u32[]{:S(2)}, u32[]{:S(2)}) %all-to-all-start.8) | async-done | bytes 6291488 | tf_op jit(solution)/shard_map/all_to_all | solution.py:253
  716.8 12.6 gather_fusion.4
  729.4 6.7 convert_reduce_fusion
  748.5 12.2 copy.380
  760.8 9.7 convolution_convert_fusion.1
  770.5 57.4 %all-to-all-done.9 = bf16[4,128,2048]{2,1,0:T(8,128)(2,1)S(1)} async-done(((bf16[4,128,2048]{2,1,0:T(8,128)(2,1)}), bf16[4,128,2048]{2,1,0:T(8,128)(2,1)S(1)}, u32[]{:S(2)}, u32[]{:S(2)}) %all-to-all-start.9) | async-done | bytes 2097184 | tf_op jit(solution)/shard_map/all_to_all | solution.py:72
  845.8 11.7 fusion
  857.5 12.8 fusion.6
  912.1 6.3 all-to-all-start.12
  918.3 114.3 %all-to-all-done.12 = bf16[4,512,1,1280]{3,1,2,0:T(8,128)(2,1)} async-done(((bf16[4,512,1,1280]{3,1,2,0:T(8,128)(2,1)}), bf16[4,512,1,1280]{3,1,2,0:T(8,128)(2,1)}, u32[]{:S(2)}, u32[]{:S(2)}) %all-to-all-start.12) | async-done | bytes 5242912 | tf_op jit(solution)/shard_map/all_to_all | solution.py:72
  1037.3 6.2 copy.384
  1049.9 6.8 convolution_convert_fusion
  1056.8 8.3 convert_bitcast_fusion.1
  1065.2 10.7 convert_bitcast_fusion.2
  1098.1 7.4 fusion.43
  1123.3 21.2 %all-to-all-done.13 = f32[4,128,512]{2,1,0:T(8,128)} async-done(((f32[4,128,512]{2,1,0:T(8,128)}), f32[4,128,512]{2,1,0:T(8,128)}, u32[]{:S(2)}, u32[]{:S(2)}) %all-to-all-start.13) | async-done | bytes 1048608 | tf_op jit(solution)/shard_map/all_to_all | solution.py:368
  1149.4 47.1 %all-reduce = (f32[2048]{0:T(1024)}, f32[128]{0:T(128)}, f32[128]{0:T(128)}, f32[2048]{0:T(1024)}) all-reduce(f32[2048]{0:T(1024)S(1)} %bitcast.477, f32[128]{0:T(128)S(1)} %bitcast_reduce_fusion, f32[128]{0:T(128)S(1)} %get-tuple-element.23, f32[2048]{0:T(1024)S(1)} %copy-done.51), channel_id=1, replica_groups=mesh['ctx'=8,'fsdp'=4] {'ctx','fsdp'}, use_global_device_ids=true, to_apply=%region_24.26 | all-reduce | flops 4352 | bytes 34816 | tf_op jit(solution)/shard_map/psum | solution.py:390
  1203.5 6.7 convert_element_type.215
  1210.2 156.2 %reduce-scatter.3.cloned.1.call-done = bf16[2,2,512,768]{3,2,1,0:T(8,128)(2,1)} async-done(((bf16[2,2,2048,768]{3,2,1,0:T(8,128)(2,1)}), bf16[2,2,512,768]{3,2,1,0:T(8,128)(2,1)}) %reduce-scatter.3.cloned.1.call-update) | async-done | bytes 3145744 | tf_op jit(solution)/shard_map/reduce_scatter | solution.py:376
  1372.2 125.6 %all-reduce.5.cloned.1.call-done = f32[1024,2048]{1,0:T(8,128)} async-done(((f32[1024,2048]{1,0:T(8,128)}), f32[1024,2048]{1,0:T(8,128)}) %all-reduce.5.cloned.1.call-update) | async-done | bytes 8388624 | tf_op jit(solution)/shard_map/psum | solution.py:384
  1497.8 7.9 copy.473
  (348 shorter events, 278.7 us)
Async XLA Ops:
  22.4 66.1 %all-to-all-start = ((bf16[4,2568,128]{2,1,0:T(8,128)(2,1)}), bf16[4,2568,128]{2,1,0:T(8,128)(2,1)}, u32[]{:S(2)}, u32[]{:S(2)}) async-start(bf16[4,2568,128]{2,1,0:T(8,128)(2,1)} %pad_maximum_fusion.2), calls=%async_computation | async-start | bytes 5259264 | tf_op jit(solution)/shard_map/all_to_all | solution.py:149
  28.7 115.4 %all-gather.4.cloned.1.call-start = ((), (), s32[]{:S(2)}) async-start(), calls=%async_computation.18 | async-start | bytes 2621440 | tf_op jit(solution)/shard_map/all_gather | solution.py:153
  28.9 69.1 %copy-start.59 = (f32[128]{0:T(128)}, f32[128]{0:T(128)S(1)}, u32[]{:S(2)}) copy-start(f32[128]{0:T(128)S(1)} %add_rsqrt_fusion.3) | copy-start | bytes 1540
  28.9 69.1 %copy-start.46 = (f32[2048]{0:T(1024)S(1)}, f32[2048]{0:T(1024)}, u32[]{:S(2)}) copy-start(f32[2048]{0:T(1024)} %param.23) | copy-start | bytes 24580
  98.0 8.8 collective-permute-start
  99.0 422.3 %all-gather.6.cloned.1.call-start = ((), (), s32[]{:S(2)}) async-start(), calls=%async_computation.19 | async-start | bytes 15728640 | tf_op jit(solution)/shard_map/all_gather | solution.py:225
  100.4 52.1 %copy-start.34 = (f32[128,64]{0,1:T(8,128)}, f32[128,64]{0,1:T(8,128)S(1)}, u32[]{:S(2)}) copy-start(f32[128,64]{0,1:T(8,128)S(1)} %get-tuple-element.66) | copy-start | bytes 98308
  100.4 52.1 %copy-start.36 = (f32[128,64]{0,1:T(8,128)}, f32[128,64]{0,1:T(8,128)S(1)}, u32[]{:S(2)}) copy-start(f32[128,64]{0,1:T(8,128)S(1)} %get-tuple-element.67) | copy-start | bytes 98308
  116.9 66.4 %copy-start.30 = (f32[128,64]{1,0:T(8,128)}, f32[128,64]{1,0:T(8,128)S(1)}, u32[]{:S(2)}) copy-start(f32[128,64]{1,0:T(8,128)S(1)} %copy.349) | copy-start | bytes 98308
  117.0 66.3 %copy-start.32 = (f32[128,64]{1,0:T(8,128)}, f32[128,64]{1,0:T(8,128)S(1)}, u32[]{:S(2)}) copy-start(f32[128,64]{1,0:T(8,128)S(1)} %copy.350) | copy-start | bytes 98308
  118.0 26.1 %copy-start.29 = (f32[4,8,128]{0,2,1:T(8,128)}, f32[4,8,128]{0,2,1:T(8,128)S(1)}, u32[]{:S(2)}) copy-start(f32[4,8,128]{0,2,1:T(8,128)S(1)} %copy.341) | copy-start | bytes 49156
  122.0 30.4 %copy-start.56 = (f32[128]{0:T(128)S(1)}, f32[128]{0:T(128)}, u32[]{:S(2)}) copy-start(f32[128]{0:T(128)} %param.28) | copy-start | bytes 1540
  153.9 19.0 %all-to-all-start.2 = ((bf16[8,4,128,128]{3,2,1,0:T(8,128)(2,1)}), bf16[8,4,128,128]{3,2,1,0:T(8,128)(2,1)S(1)}, u32[]{:S(2)}, u32[]{:S(2)}) async-start(bf16[8,4,128,128]{3,2,1,0:T(8,128)(2,1)} %broadcast_in_dim.80), calls=%async_computation.2 | async-start | bytes 2097152 | tf_op jit(solution)/shard_map/all_to_all | solution.py:72
  162.4 55.6 %copy-start.7 = (pred[4,128,1024]{1,2,0:T(8,128)(4,1)}, pred[4,128,1024]{1,2,0:T(8,128)(4,1)S(1)}, u32[]{:S(2)}) copy-start(pred[4,128,1024]{1,2,0:T(8,128)(4,1)S(1)} %compare_and_fusion) | copy-start | bytes 1572868
  174.3 19.8 %all-to-all-start.1 = ((bf16[8,4,128,128]{2,3,1,0:T(8,128)(2,1)}), bf16[8,4,128,128]{2,3,1,0:T(8,128)(2,1)}, u32[]{:S(2)}, u32[]{:S(2)}) async-start(bf16[8,4,128,128]{2,3,1,0:T(8,128)(2,1)} %broadcast_in_dim.74), calls=%async_computation.1 | async-start | bytes 2097152 | tf_op jit(solution)/shard_map/all_to_all | solution.py:72
  186.7 21.8 %copy-start.9 = (bf16[4,8,128,128]{3,2,1,0:T(8,128)(2,1)}, bf16[4,8,128,128]{3,2,1,0:T(8,128)(2,1)S(1)}, u32[]{:S(2)}) copy-start(bf16[4,8,128,128]{3,2,1,0:T(8,128)(2,1)S(1)} %copy.346) | copy-start | bytes 3145732
  235.4 108.6 %copy-start.53 = (bf16[512,16]{0,1:T(8,128)(2,1)S(1)}, bf16[512,16]{0,1:T(8,128)(2,1)}, u32[]{:S(2)}) copy-start(bf16[512,16]{0,1:T(8,128)(2,1)} %param.31) | copy-start | bytes 49156
  235.4 108.6 %all-to-all-start.3 = ((bf16[4,1,128,2048]{3,2,1,0:T(8,128)(2,1)}), bf16[4,1,128,2048]{3,2,1,0:T(8,128)(2,1)}, u32[]{:S(2)}, u32[]{:S(2)}) async-start(bf16[4,1,128,2048]{3,2,1,0:T(8,128)(2,1)} %fusion.29), calls=%async_computation.3 | async-start | bytes 4194304 | tf_op jit(solution)/shard_map/all_to_all | solution.py:78
  240.0 111.4 %copy-start.42 = (f32[2048]{0:T(1024)S(1)}, f32[2048]{0:T(1024)}, u32[]{:S(2)}) copy-start(f32[2048]{0:T(1024)} %param.30) | copy-start | bytes 24580
  344.6 17.2 %all-to-all-start.4 = ((bf16[4,512,16]{1,2,0:T(8,128)(2,1)}), bf16[4,512,16]{1,2,0:T(8,128)(2,1)S(1)}, u32[]{:S(2)}, u32[]{:S(2)}) async-start(bf16[4,512,16]{1,2,0:T(8,128)(2,1)} %broadcast_in_dim.82), calls=%async_computation.4 | async-start | bytes 131072 | tf_op jit(solution)/shard_map/all_to_all | solution.py:72
  351.4 385.9 %copy-start.5 = (f32[128,2048]{1,0:T(8,128)}, f32[128,2048]{1,0:T(8,128)S(1)}, u32[]{:S(2)}) copy-start(f32[128,2048]{1,0:T(8,128)S(1)} %get-tuple-element.43) | copy-start | bytes 3145732
  351.4 385.9 %copy-start.54 = (f32[128]{0:T(128)}, f32[128]{0:T(128)S(1)}, u32[]{:S(2)}) copy-start(f32[128]{0:T(128)S(1)} %add_rsqrt_fusion.2) | copy-start | bytes 1540
  361.8 76.3 %all-to-all-start.5 = ((bf16[8,2,96,2048]{3,2,1,0:T(8,128)(2,1)}), bf16[8,2,96,2048]{3,2,1,0:T(8,128)(2,1)}, u32[]{:S(2)}, u32[]{:S(2)}) async-start(bf16[8,2,96,2048]{3,2,1,0:T(8,128)(2,1)} %bitcast.410), calls=%async_computation.5 | async-start | bytes 12582912 | tf_op jit(solution)/shard_map/all_to_all | solution.py:248
  366.6 173.1 %all-gather.8.cloned.1.call-start = ((), (), s32[]{:S(2)}) async-start(), calls=%async_computation.20 | async-start | bytes 7864320 | tf_op jit(solution)/shard_map/all_gather | solution.py:229
  438.1 76.6 %all-to-all-start.7 = ((bf16[8,2,96,2048]{3,2,1,0:T(8,128)(2,1)}), bf16[8,2,96,2048]{3,2,1,0:T(8,128)(2,1)}, u32[]{:S(2)}, u32[]{:S(2)}) async-start(bf16[8,2,96,2048]{3,2,1,0:T(8,128)(2,1)} %bitcast.412), calls=%async_computation.7 | async-start | bytes 12582912 | tf_op jit(solution)/shard_map/all_to_all | solution.py:248
  521.3 11.7 copy-start.61
  539.6 13.9 copy-start.62
  563.7 76.8 %all-to-all-start.6 = ((bf16[8,2,96,2048]{3,2,1,0:T(8,128)(2,1)}), bf16[8,2,96,2048]{3,2,1,0:T(8,128)(2,1)}, u32[]{:S(2)}, u32[]{:S(2)}) async-start(bf16[8,2,96,2048]{3,2,1,0:T(8,128)(2,1)} %bitcast.413), calls=%async_computation.6 | async-start | bytes 12582912 | tf_op jit(solution)/shard_map/all_to_all | solution.py:253
  568.9 10.7 copy-start.65
  640.5 76.3 %all-to-all-start.8 = ((bf16[8,2,96,2048]{3,2,1,0:T(8,128)(2,1)}), bf16[8,2,96,2048]{3,2,1,0:T(8,128)(2,1)}, u32[]{:S(2)}, u32[]{:S(2)}) async-start(bf16[8,2,96,2048]{3,2,1,0:T(8,128)(2,1)} %bitcast.411), calls=%async_computation.8 | async-start | bytes 12582912 | tf_op jit(solution)/shard_map/all_to_all | solution.py:253
  663.8 72.4 %copy-start.48 = (bf16[128,1,16]{0,2,1:T(8,128)(2,1)}, bf16[128,1,16]{0,2,1:T(8,128)(2,1)S(1)}, u32[]{:S(2)}) copy-start(bf16[128,1,16]{0,2,1:T(8,128)(2,1)S(1)} %copy.404) | copy-start | bytes 12292
  741.0 86.8 %all-to-all-start.9 = ((bf16[4,128,2048]{2,1,0:T(8,128)(2,1)}), bf16[4,128,2048]{2,1,0:T(8,128)(2,1)S(1)}, u32[]{:S(2)}, u32[]{:S(2)}) async-start(bf16[4,128,2048]{2,1,0:T(8,128)(2,1)} %broadcast_in_dim.87), calls=%async_computation.9 | async-start | bytes 4194304 | tf_op jit(solution)/shard_map/all_to_all | solution.py:72
  746.1 373.8 %reduce-scatter.5.cloned.1.call-start = ((), (), s32[]{:S(2)}) async-start(), calls=%async_computation.23 | async-start | bytes 7864320 | tf_op jit(solution)/shard_map/reduce_scatter | solution.py:373
  840.4 39.9 %all-to-all-start.11 = ((bf16[4,8,128,128]{2,3,0,1:T(8,128)(2,1)}), bf16[4,8,128,128]{2,3,0,1:T(8,128)(2,1)}, u32[]{:S(2)}, u32[]{:S(2)}) async-start(bf16[4,8,128,128]{2,3,0,1:T(8,128)(2,1)} %copy.381), calls=%async_computation.11 | async-start | bytes 2097152 | tf_op jit(solution)/shard_map/all_to_all | solution.py:78
  857.5 12.9 copy-start.14
  857.5 12.9 copy-start.15
  880.4 20.2 %all-to-all-start.10 = ((bf16[4,8,128,128]{2,3,0,1:T(8,128)(2,1)}), bf16[4,8,128,128]{2,3,0,1:T(8,128)(2,1)}, u32[]{:S(2)}, u32[]{:S(2)}) async-start(bf16[4,8,128,128]{2,3,0,1:T(8,128)(2,1)} %copy.376), calls=%async_computation.10 | async-start | bytes 2097152 | tf_op jit(solution)/shard_map/all_to_all | solution.py:78
  894.4 11.1 copy-start.52
  894.4 11.1 copy-start.57
  912.1 120.6 %all-to-all-start.12 = ((bf16[4,512,1,1280]{3,1,2,0:T(8,128)(2,1)}), bf16[4,512,1,1280]{3,1,2,0:T(8,128)(2,1)}, u32[]{:S(2)}, u32[]{:S(2)}) async-start(bf16[4,512,1,1280]{3,1,2,0:T(8,128)(2,1)} %broadcast_in_dim.88), calls=%async_computation.12 | async-start | bytes 10485760 | tf_op jit(solution)/shard_map/all_to_all | solution.py:72
  918.3 280.9 %all-reduce.7.cloned.1.call-start = ((), (), s32[]{:S(2)}) async-start(), calls=%async_computation.24 | async-start | bytes 10485760 | tf_op jit(solution)/shard_map/psum | solution.py:386
  1056.8 309.7 %reduce-scatter.3.cloned.1.call-start = ((), (), s32[]{:S(2)}) async-start(), calls=%async_computation.22 | async-start | bytes 15728640 | tf_op jit(solution)/shard_map/reduce_scatter | solution.py:376
  1084.3 9.2 all-to-all-start.14
  1094.2 19.2 %all-to-all-start.15 = ((f32[8,1,512,16]{2,3,1,0:T(8,128)}), f32[8,1,512,16]{2,3,1,0:T(8,128)S(1)}, u32[]{:S(2)}, u32[]{:S(2)}) async-start(f32[8,1,512,16]{2,3,1,0:T(8,128)} %broadcast_in_dim.90), calls=%async_computation.15 | async-start | bytes 524288 | tf_op jit(solution)/shard_map/all_to_all | solution.py:72
  1098.1 399.7 %all-reduce.5.cloned.1.call-start = ((), (), s32[]{:S(2)}) async-start(), calls=%async_computation.21 | async-start | bytes 16777216 | tf_op jit(solution)/shard_map/psum | solution.py:384
  1113.4 31.1 %all-to-all-start.13 = ((f32[4,128,512]{2,1,0:T(8,128)}), f32[4,128,512]{2,1,0:T(8,128)}, u32[]{:S(2)}, u32[]{:S(2)}) async-start(f32[4,128,512]{2,1,0:T(8,128)} %bitcast.99), calls=%async_computation.13 | async-start | bytes 2097152 | tf_op jit(solution)/shard_map/all_to_all | solution.py:368
  1117.9 28.3 %copy-start.60 = (f32[128]{0:T(128)S(1)}, f32[128]{0:T(128)}, u32[]{:S(2)}) copy-start(f32[128]{0:T(128)} %copy-done.59) | copy-start | bytes 1540
  1123.3 26.0 %copy-start.51 = (f32[2048]{0:T(1024)S(1)}, f32[2048]{0:T(1024)}, u32[]{:S(2)}) copy-start(f32[2048]{0:T(1024)} %get-tuple-element.25) | copy-start | bytes 24580
  (43 other events, 242.5 us)
Sparse Core Ops, SparseCore 0:
  99.1 44.9 all-gather.3
  146.2 263.1 all-gather.5
  411.0 113.4 all-gather.7
  770.6 120.5 reduce-scatter.4
  1056.9 94.2 all-reduce.6
  1153.4 213.0 reduce-scatter.2
  1370.5 127.2 all-reduce.4

commit v11 on v8

--- a/solution.py
+++ b/solution.py
@@ -209,8 +209,8 @@
     peak = jnp.max(scores, axis=-1, keepdims=True)
     expo = jnp.exp(scores - peak)
     total = jnp.sum(expo, axis=-1, keepdims=True)
-    probs = (expo / total).astype(jnp.bfloat16)
-    log_sums = peak + jnp.log(total)
+    probs_full = expo / total
+    probs = probs_full.astype(jnp.bfloat16)
     attended = (
         contract("skgtj,sjkd->stkgd", probs, values_all)
         .astype(jnp.bfloat16)
@@ -304,7 +304,7 @@
     grad_attended = contract("td,qd->tq", grad_branch, out_proj).astype(jnp.bfloat16)
     grad_groups = grad_attended.reshape(seqs, tokens, kv_dev, group_dev, HEAD_DIM)
 
-    probs_back = jnp.exp(masked_scores() - log_sums)
+    probs_back = probs_full
     grad_probs = contract("stkgd,sjkd->skgtj", grad_groups, values_all)
     delta = jnp.sum(probs_back * grad_probs, axis=-1, keepdims=True)
     grad_scores = (probs_back * (grad_probs - delta)).astype(jnp.bfloat16)
@@ -365,8 +365,8 @@
         + contract("tq,dq->td", value_all, value_proj)
     )
     grad_first = lax.all_to_all(
-        grad_first_cols.reshape(seqs, tokens, d_part), "fsdp", 0, 2, tiled=True
-    )[0]
+        grad_first_cols.reshape(seqs, tokens, d_part).astype(jnp.bfloat16), "fsdp", 0, 2, tiled=True
+    )[0].astype(jnp.float32)
     grad_hidden, attn_gain_grad = norm_back(grad_first, first_normed, first_scale, attn_gain)
     grad_hidden = grad_hidden + grad_middle
     gate_grad, up_grad, down_grad = (

time: 1320 us -> 1310 us (level)
    psum x1, waiting for transfers between devices: 105 us -> 119 us  [per_device(): out_grad = lax.psum(out_grad_part, 'ctx')]
    another operation x6 -> x7, other arithmetic: 19.9 us -> 30.5 us
  transfers between devices with their start and end apart: 25 -> 25, of which waited for: 16 -> 15; matrix products, arithmetic and copies ran while one was open for 33% -> 31% of each run, Pallas kernels for 0% -> 0%
where the time goes in v11:
time: 1310 us; the launch traced here: 1300 us
  waiting for transfers between devices  701 us (54%)
  matrix products  181 us (14%)
  local copies, waits for them, and re-layouts  164 us (13%)
  other arithmetic  121 us (9%)
  starting transfers between devices  67.7 us (5%)
  blocking collectives  47.6 us (4%)
  between operations  15.5 us (1%)
    all_to_all x6, waiting for transfers between devices, gather_a2a(): lax.all_to_all(rep, axis_name, 0, 0, tiled=True)  180 us
    dot_general x25, matrix products, contract(): return jnp.einsum(form, left, right, preferred_element_type=jnp.float32)  164 us
    all_to_all x2, waiting for transfers between devices, to_experts(): got = lax.all_to_all(buffer, 'ctx', 0, 0, tiled=True)  126 us
    psum x1, waiting for transfers between devices, per_device(): out_grad = lax.psum(out_grad_part, 'ctx')  119 us
    all_to_all x2, waiting for transfers between devices, from_experts(): back = lax.all_to_all(parts, 'ctx', 0, 0, tiled=True)  90.3 us
    all_to_all x3, waiting for transfers between devices, scatter_sum_a2a(): got = lax.all_to_all(parts, axis_name, axis, axis, tiled=True)  78.3 us
    all_to_all x1, waiting for transfers between devices, per_device(): got = lax.all_to_all(payload, 'fsdp', 0, 0, tiled=True)  59.5 us
    psum x1, blocking collectives, per_device(): lax.psum((attn_gain_grad, query_gain_grad, key_gain_grad, ffn_gain_grad),...  39.1 us
  transfers between devices with their start and end apart: 25, of which 15 were waited for; matrix products, arithmetic and copies ran while one was open for 31% of the time, Pallas kernels for 0%

profile of v11, /device:TPU:0, one launch (start us, length us, event | category | flops | bytes accessed | tf_op | source)
XLA Modules:
  0.0 1297.3 jit_solution(17635337693789623597)
XLA Ops:
  21.7 6.3 all-to-all-start
  28.2 59.5 %all-to-all-done = bf16[4,2568,128]{2,1,0:T(8,128)(2,1)} async-done(((bf16[4,2568,128]{2,1,0:T(8,128)(2,1)}), bf16[4,2568,128]{2,1,0:T(8,128)(2,1)}, u32[]{:S(2)}, u32[]{:S(2)}) %all-to-all-start) | async-done | bytes 2629664 | tf_op jit(solution)/shard_map/all_to_all | solution.py:149
  91.2 6.2 reshape.777
  98.4 6.2 stack_reshape.4
  104.6 7.4 maximum_select_fusion
  119.0 24.4 %all-gather.5.cloned.1.call-done = bf16[512,2048]{1,0:T(8,128)(2,1)} async-done(((bf16[128,2048]{1,0:T(8,128)(2,1)}), bf16[512,2048]{1,0:T(8,128)(2,1)}) %all-gather.5.cloned.1.call-update) | async-done | bytes 2097168 | tf_op jit(solution)/shard_map/all_gather | solution.py:153
  143.4 6.0 fusion.89
  179.3 9.7 fusion.5
  189.0 9.4 fusion.4
  198.4 10.5 convert_bitcast_fusion
  237.9 67.2 %all-to-all-done.3 = bf16[4,1,128,2048]{3,2,1,0:T(8,128)(2,1)} async-done(((bf16[4,1,128,2048]{3,2,1,0:T(8,128)(2,1)}), bf16[4,1,128,2048]{3,2,1,0:T(8,128)(2,1)}, u32[]{:S(2)}, u32[]{:S(2)}) %all-to-all-start.3) | async-done | bytes 2097184 | tf_op jit(solution)/shard_map/all_to_all | solution.py:78
  308.0 7.0 gather_fusion.2
  315.9 11.0 scatter_custom_fusion.1
  332.4 10.2 scatter_custom_fusion
  342.7 60.6 %all-to-all-done.7 = bf16[8,2,96,2048]{3,2,1,0:T(8,128)(2,1)} async-done(((bf16[8,2,96,2048]{3,2,1,0:T(8,128)(2,1)}), bf16[8,2,96,2048]{3,2,1,0:T(8,128)(2,1)}, u32[]{:S(2)}, u32[]{:S(2)}) %all-to-all-start.7) | async-done | bytes 6291488 | tf_op jit(solution)/shard_map/all_to_all | solution.py:247
  408.0 6.5 copy.365
  414.6 65.0 %all-to-all-done.5 = bf16[8,2,96,2048]{3,2,1,0:T(8,128)(2,1)} async-done(((bf16[8,2,96,2048]{3,2,1,0:T(8,128)(2,1)}), bf16[8,2,96,2048]{3,2,1,0:T(8,128)(2,1)}, u32[]{:S(2)}, u32[]{:S(2)}) %all-to-all-start.5) | async-done | bytes 6291488 | tf_op jit(solution)/shard_map/all_to_all | solution.py:247
  479.6 6.5 copy.362
  486.1 10.5 fusion.91
  496.7 10.4 fusion.90
  507.0 18.6 %all-gather.11.cloned.1.call-done = bf16[2,768,2048]{2,1,0:T(8,128)(2,1)} async-done(((bf16[2,192,2048]{2,1,0:T(8,128)(2,1)}), bf16[2,768,2048]{2,1,0:T(8,128)(2,1)}) %all-gather.11.cloned.1.call-update) | async-done | bytes 6291472 | tf_op jit(solution)/shard_map/all_gather | solution.py:228
  525.6 13.4 %multiply_convert_fusion = (bf16[2,768,768]{2,1,0:T(8,128)(2,1)}, bf16[2,768,768]{2,1,0:T(8,128)(2,1)}, bf16[2,768,768]{2,1,0:T(8,128)(2,1)S(1)}) fusion(f32[2,768,768]{2,1,0:T(8,128)} %fusion.90, f32[2,768,768]{2,1,0:T(8,128)} %fusion.91, bf16[2,768,2048]{2,1,0:T(8,128)(2,1)} %bitcast.411, bf16[2,768,2048]{2,1,0:T(8,128)(2,1)} %all-gather.11.cloned.1.call-done), kind=kOutput, calls=%fused_computation.30 | convolution fusion | flops 4850712576 | bytes 29097984 | tf_op jit(solution)/shard_map/erd,efd->erf/dot_general | solution.py:24
  540.5 9.8 convolution_convert_fusion.1
  550.3 8.1 convolution_convert_fusion.4
  566.5 9.8 convolution_convert_fusion.3
  576.3 10.7 fusion.92
  587.0 9.9 add_convert_fusion
  600.8 37.2 %all-to-all-done.6 = bf16[8,2,96,2048]{3,2,1,0:T(8,128)(2,1)} async-done(((bf16[8,2,96,2048]{3,2,1,0:T(8,128)(2,1)}), bf16[8,2,96,2048]{3,2,1,0:T(8,128)(2,1)}, u32[]{:S(2)}, u32[]{:S(2)}) %all-to-all-start.6) | async-done | bytes 6291488 | tf_op jit(solution)/shard_map/all_to_all | solution.py:252
  643.1 12.4 gather_fusion.3
  661.6 53.1 %all-to-all-done.8 = bf16[8,2,96,2048]{3,2,1,0:T(8,128)(2,1)} async-done(((bf16[8,2,96,2048]{3,2,1,0:T(8,128)(2,1)}), bf16[8,2,96,2048]{3,2,1,0:T(8,128)(2,1)}, u32[]{:S(2)}, u32[]{:S(2)}) %all-to-all-start.8) | async-done | bytes 6291488 | tf_op jit(solution)/shard_map/all_to_all | solution.py:252
  714.6 12.8 gather_fusion.4
  727.5 6.9 convert_reduce_fusion
  746.3 12.3 copy.380
  758.6 9.6 convolution_convert_fusion.2
  768.2 49.0 %all-to-all-done.9 = bf16[4,128,2048]{2,1,0:T(8,128)(2,1)} async-done(((bf16[4,128,2048]{2,1,0:T(8,128)(2,1)}), bf16[4,128,2048]{2,1,0:T(8,128)(2,1)}, u32[]{:S(2)}, u32[]{:S(2)}) %all-to-all-start.9) | async-done | bytes 2097184 | tf_op jit(solution)/shard_map/all_to_all | solution.py:72
  822.9 11.8 fusion
  834.7 13.2 %fusion.6 = bf16[4,8,128,1024]{2,3,1,0:T(8,128)(2,1)S(1)} fusion(f32[4,1024,128,8]{2,1,3,0:T(8,128)} %get-tuple-element.70, f32[4,8,128]{2,1,0:T(8,128)S(1)} %get-tuple-element.69, f32[4,8,128]{2,1,0:T(8,128)S(1)} %copy-done.43, f32[4,8,128]{2,1,0:T(8,128)S(1)} %copy-done.40, f32[4,1024,128,8]{2,1,3,0:T(8,128)} %get-tuple-element.67, ...), kind=kLoop, calls=%fused_computation.18 | loop fusion | flops 29360128 | bytes 42516480 | tf_op jit(solution)/shard_map/reshape.33
  889.0 6.4 all-to-all-done.11
  907.4 125.2 %all-to-all-done.12 = bf16[4,512,1,1280]{3,1,2,0:T(8,128)(2,1)} async-done(((bf16[4,512,1,1280]{3,1,2,0:T(8,128)(2,1)}), bf16[4,512,1,1280]{3,1,2,0:T(8,128)(2,1)}, u32[]{:S(2)}, u32[]{:S(2)}) %all-to-all-start.12) | async-done | bytes 5242912 | tf_op jit(solution)/shard_map/all_to_all | solution.py:72
  1037.2 6.2 copy.384
  1050.0 6.7 convolution_convert_fusion
  1059.5 7.8 fusion.40
  1068.1 8.5 all_to_all.84
  1080.9 6.0 fusion.93
  1113.2 39.1 %all-reduce = (f32[2048]{0:T(1024)}, f32[128]{0:T(128)}, f32[128]{0:T(128)}, f32[2048]{0:T(1024)}) all-reduce(f32[2048]{0:T(1024)S(1)} %bitcast.460, f32[128]{0:T(128)S(1)} %bitcast_reduce_fusion, f32[128]{0:T(128)S(1)} %get-tuple-element.23, f32[2048]{0:T(1024)S(1)} %get-tuple-element.25), channel_id=1, replica_groups=mesh['ctx'=8,'fsdp'=4] {'ctx','fsdp'}, use_global_device_ids=true, to_apply=%region_24.26 | all-reduce | flops 4352 | bytes 34816 | tf_op jit(solution)/shard_map/psum | solution.py:385
  1154.7 6.8 convert_element_type.254
  1163.7 118.9 %all-reduce.5.cloned.1.call-done = f32[1024,2048]{1,0:T(8,128)} async-done(((f32[1024,2048]{1,0:T(8,128)}), f32[1024,2048]{1,0:T(8,128)}) %all-reduce.5.cloned.1.call-update) | async-done | bytes 8388624 | tf_op jit(solution)/shard_map/psum | solution.py:379
  1282.7 7.9 copy.473
  (336 shorter events, 242.9 us)
Async XLA Ops:
  18.2 9.9 copy-start.1
  21.7 66.1 %all-to-all-start = ((bf16[4,2568,128]{2,1,0:T(8,128)(2,1)}), bf16[4,2568,128]{2,1,0:T(8,128)(2,1)}, u32[]{:S(2)}, u32[]{:S(2)}) async-start(bf16[4,2568,128]{2,1,0:T(8,128)(2,1)} %pad_maximum_fusion), calls=%async_computation | async-start | bytes 5259264 | tf_op jit(solution)/shard_map/all_to_all | solution.py:149
  28.1 115.3 %all-gather.5.cloned.1.call-start = ((), (), s32[]{:S(2)}) async-start(), calls=%async_computation.19 | async-start | bytes 2621440 | tf_op jit(solution)/shard_map/all_gather | solution.py:153
  28.2 69.1 %copy-start.51 = (f32[128]{0:T(128)}, f32[128]{0:T(128)S(1)}, u32[]{:S(2)}) copy-start(f32[128]{0:T(128)S(1)} %add_rsqrt_fusion.3) | copy-start | bytes 1540
  28.2 69.1 %copy-start.44 = (f32[2048]{0:T(1024)S(1)}, f32[2048]{0:T(1024)}, u32[]{:S(2)}) copy-start(f32[2048]{0:T(1024)} %param.23) | copy-start | bytes 24580
  97.3 7.2 collective-permute-start
  98.3 387.8 %all-gather.9.cloned.1.call-start = ((), (), s32[]{:S(2)}) async-start(), calls=%async_computation.21 | async-start | bytes 7864320 | tf_op jit(solution)/shard_map/all_gather | solution.py:227
  112.8 39.8 %copy-start.31 = (f32[128,64]{0,1:T(8,128)}, f32[128,64]{0,1:T(8,128)S(1)}, u32[]{:S(2)}) copy-start(f32[128,64]{0,1:T(8,128)S(1)} %get-tuple-element.64) | copy-start | bytes 98308
  112.8 39.8 %copy-start.33 = (f32[128,64]{0,1:T(8,128)}, f32[128,64]{0,1:T(8,128)S(1)}, u32[]{:S(2)}) copy-start(f32[128,64]{0,1:T(8,128)S(1)} %get-tuple-element.65) | copy-start | bytes 98308
  112.9 52.2 %copy-start.25 = (f32[128,64]{1,0:T(8,128)}, f32[128,64]{1,0:T(8,128)S(1)}, u32[]{:S(2)}) copy-start(f32[128,64]{1,0:T(8,128)S(1)} %copy.349) | copy-start | bytes 98308
  113.0 52.1 %copy-start.27 = (f32[128,64]{1,0:T(8,128)}, f32[128,64]{1,0:T(8,128)S(1)}, u32[]{:S(2)}) copy-start(f32[128,64]{1,0:T(8,128)S(1)} %copy.350) | copy-start | bytes 98308
  119.0 79.4 %copy-start.5 = (pred[4,128,1024]{1,2,0:T(8,128)(4,1)}, pred[4,128,1024]{1,2,0:T(8,128)(4,1)S(1)}, u32[]{:S(2)}) copy-start(pred[4,128,1024]{1,2,0:T(8,128)(4,1)S(1)} %compare_and_fusion) | copy-start | bytes 1572868
  154.0 19.0 %all-to-all-start.2 = ((bf16[8,4,128,128]{3,2,1,0:T(8,128)(2,1)}), bf16[8,4,128,128]{3,2,1,0:T(8,128)(2,1)S(1)}, u32[]{:S(2)}, u32[]{:S(2)}) async-start(bf16[8,4,128,128]{3,2,1,0:T(8,128)(2,1)} %broadcast_in_dim.80), calls=%async_computation.2 | async-start | bytes 2097152 | tf_op jit(solution)/shard_map/all_to_all | solution.py:72
  157.7 339.0 %all-gather.7.cloned.1.call-start = ((), (), s32[]{:S(2)}) async-start(), calls=%async_computation.20 | async-start | bytes 7864320 | tf_op jit(solution)/shard_map/all_gather | solution.py:226
  174.4 34.6 %all-to-all-start.1 = ((bf16[8,4,128,128]{2,3,1,0:T(8,128)(2,1)}), bf16[8,4,128,128]{2,3,1,0:T(8,128)(2,1)S(1)}, u32[]{:S(2)}, u32[]{:S(2)}) async-start(bf16[8,4,128,128]{2,3,1,0:T(8,128)(2,1)} %broadcast_in_dim.74), calls=%async_computation.1 | async-start | bytes 2097152 | tf_op jit(solution)/shard_map/all_to_all | solution.py:72
  179.3 9.7 copy-start.7
  189.0 9.4 copy-start.39
  198.4 10.5 copy-start.42
  198.4 10.5 copy-start.48
  208.9 13.4 %copy-start.11 = (bf16[8,4,128,128]{2,3,1,0:T(8,128)(2,1)}, bf16[8,4,128,128]{2,3,1,0:T(8,128)(2,1)S(1)}, u32[]{:S(2)}) copy-start(bf16[8,4,128,128]{2,3,1,0:T(8,128)(2,1)S(1)} %all-to-all-done.1) | copy-start | bytes 3145732
  209.6 17.4 %all-to-all-start.4 = ((bf16[4,512,16]{1,2,0:T(8,128)(2,1)}), bf16[4,512,16]{1,2,0:T(8,128)(2,1)S(1)}, u32[]{:S(2)}, u32[]{:S(2)}) async-start(bf16[4,512,16]{1,2,0:T(8,128)(2,1)} %broadcast_in_dim.82), calls=%async_computation.4 | async-start | bytes 131072 | tf_op jit(solution)/shard_map/all_to_all | solution.py:72
  227.0 78.1 %all-to-all-start.3 = ((bf16[4,1,128,2048]{3,2,1,0:T(8,128)(2,1)}), bf16[4,1,128,2048]{3,2,1,0:T(8,128)(2,1)}, u32[]{:S(2)}, u32[]{:S(2)}) async-start(bf16[4,1,128,2048]{3,2,1,0:T(8,128)(2,1)} %fusion.25), calls=%async_computation.3 | async-start | bytes 4194304 | tf_op jit(solution)/shard_map/all_to_all | solution.py:78
  232.2 75.5 %copy-start.41 = (f32[2048]{0:T(1024)S(1)}, f32[2048]{0:T(1024)}, u32[]{:S(2)}) copy-start(f32[2048]{0:T(1024)} %param.30) | copy-start | bytes 24580
  237.9 69.8 %copy-start.29 = (bf16[4,2,8,512]{3,2,0,1:T(8,128)(2,1)}, bf16[4,2,8,512]{3,2,0,1:T(8,128)(2,1)S(1)}, u32[]{:S(2)}) copy-start(bf16[4,2,8,512]{3,2,0,1:T(8,128)(2,1)S(1)} %copy.428) | copy-start | bytes 196612
  326.8 76.4 %all-to-all-start.7 = ((bf16[8,2,96,2048]{3,2,1,0:T(8,128)(2,1)}), bf16[8,2,96,2048]{3,2,1,0:T(8,128)(2,1)}, u32[]{:S(2)}, u32[]{:S(2)}) async-start(bf16[8,2,96,2048]{3,2,1,0:T(8,128)(2,1)} %bitcast.397), calls=%async_computation.7 | async-start | bytes 12582912 | tf_op jit(solution)/shard_map/all_to_all | solution.py:247
  331.7 194.0 %all-gather.11.cloned.1.call-start = ((), (), s32[]{:S(2)}) async-start(), calls=%async_computation.22 | async-start | bytes 7864320 | tf_op jit(solution)/shard_map/all_gather | solution.py:228
  403.2 76.3 %all-to-all-start.5 = ((bf16[8,2,96,2048]{3,2,1,0:T(8,128)(2,1)}), bf16[8,2,96,2048]{3,2,1,0:T(8,128)(2,1)}, u32[]{:S(2)}, u32[]{:S(2)}) async-start(bf16[8,2,96,2048]{3,2,1,0:T(8,128)(2,1)} %bitcast.398), calls=%async_computation.5 | async-start | bytes 12582912 | tf_op jit(solution)/shard_map/all_to_all | solution.py:247
  408.0 686.0 %reduce-scatter.8.cloned.1.call-start = ((), (), s32[]{:S(2)}) async-start(), calls=%async_computation.26 | async-start | bytes 7864320 | tf_op jit(solution)/shard_map/reduce_scatter | solution.py:373
  561.6 76.4 %all-to-all-start.6 = ((bf16[8,2,96,2048]{3,2,1,0:T(8,128)(2,1)}), bf16[8,2,96,2048]{3,2,1,0:T(8,128)(2,1)}, u32[]{:S(2)}, u32[]{:S(2)}) async-start(bf16[8,2,96,2048]{3,2,1,0:T(8,128)(2,1)} %bitcast.396), calls=%async_computation.6 | async-start | bytes 12582912 | tf_op jit(solution)/shard_map/all_to_all | solution.py:252
  566.4 531.0 %reduce-scatter.4.cloned.1.call-start = ((), (), s32[]{:S(2)}) async-start(), calls=%async_computation.24 | async-start | bytes 7864320 | tf_op jit(solution)/shard_map/reduce_scatter | solution.py:373
  576.3 10.8 copy-start.57
  638.0 76.6 %all-to-all-start.8 = ((bf16[8,2,96,2048]{3,2,1,0:T(8,128)(2,1)}), bf16[8,2,96,2048]{3,2,1,0:T(8,128)(2,1)}, u32[]{:S(2)}, u32[]{:S(2)}) async-start(bf16[8,2,96,2048]{3,2,1,0:T(8,128)(2,1)} %bitcast.395), calls=%async_computation.8 | async-start | bytes 12582912 | tf_op jit(solution)/shard_map/all_to_all | solution.py:252
  740.1 77.2 %all-to-all-start.9 = ((bf16[4,128,2048]{2,1,0:T(8,128)(2,1)}), bf16[4,128,2048]{2,1,0:T(8,128)(2,1)}, u32[]{:S(2)}, u32[]{:S(2)}) async-start(bf16[4,128,2048]{2,1,0:T(8,128)(2,1)} %broadcast_in_dim.87), calls=%async_computation.9 | async-start | bytes 4194304 | tf_op jit(solution)/shard_map/all_to_all | solution.py:72
  744.5 356.3 %reduce-scatter.6.cloned.1.call-start = ((), (), s32[]{:S(2)}) async-start(), calls=%async_computation.25 | async-start | bytes 7864320 | tf_op jit(solution)/shard_map/reduce_scatter | solution.py:373
  834.7 13.2 %copy-start.13 = (bf16[4,128,8,64]{3,1,2,0:T(8,128)(2,1)S(1)}, bf16[4,128,8,64]{3,1,2,0:T(8,128)(2,1)}, u32[]{:S(2)}) copy-start(bf16[4,128,8,64]{3,1,2,0:T(8,128)(2,1)} %get-tuple-element.55) | copy-start | bytes 1572868
  834.7 13.2 %copy-start.14 = (bf16[4,128,8,64]{3,1,2,0:T(8,128)(2,1)S(1)}, bf16[4,128,8,64]{3,1,2,0:T(8,128)(2,1)}, u32[]{:S(2)}) copy-start(bf16[4,128,8,64]{3,1,2,0:T(8,128)(2,1)} %get-tuple-element.56) | copy-start | bytes 1572868
  856.5 19.7 %all-to-all-start.10 = ((bf16[4,8,128,128]{2,3,0,1:T(8,128)(2,1)}), bf16[4,8,128,128]{2,3,0,1:T(8,128)(2,1)}, u32[]{:S(2)}, u32[]{:S(2)}) async-start(bf16[4,8,128,128]{2,3,0,1:T(8,128)(2,1)} %copy.376), calls=%async_computation.10 | async-start | bytes 2097152 | tf_op jit(solution)/shard_map/all_to_all | solution.py:78
  876.1 19.3 %all-to-all-start.11 = ((bf16[4,8,128,128]{2,3,0,1:T(8,128)(2,1)}), bf16[4,8,128,128]{2,3,0,1:T(8,128)(2,1)S(1)}, u32[]{:S(2)}, u32[]{:S(2)}) async-start(bf16[4,8,128,128]{2,3,0,1:T(8,128)(2,1)} %copy.381), calls=%async_computation.11 | async-start | bytes 2097152 | tf_op jit(solution)/shard_map/all_to_all | solution.py:78
  884.5 11.2 copy-start.47
  884.5 11.2 copy-start.50
  902.3 130.3 %all-to-all-start.12 = ((bf16[4,512,1,1280]{3,1,2,0:T(8,128)(2,1)}), bf16[4,512,1,1280]{3,1,2,0:T(8,128)(2,1)}, u32[]{:S(2)}, u32[]{:S(2)}) async-start(bf16[4,512,1,1280]{3,1,2,0:T(8,128)(2,1)} %broadcast_in_dim.88), calls=%async_computation.12 | async-start | bytes 10485760 | tf_op jit(solution)/shard_map/all_to_all | solution.py:72
  907.3 247.4 %all-reduce.7.cloned.1.call-start = ((), (), s32[]{:S(2)}) async-start(), calls=%async_computation.27 | async-start | bytes 10485760 | tf_op jit(solution)/shard_map/psum | solution.py:381
  1045.2 11.5 copy-start.15
  1056.7 225.9 %all-reduce.5.cloned.1.call-start = ((), (), s32[]{:S(2)}) async-start(), calls=%async_computation.23 | async-start | bytes 16777216 | tf_op jit(solution)/shard_map/psum | solution.py:379
  1077.3 11.6 all-to-all-start.15
  1088.8 19.7 %all-to-all-start.13 = ((bf16[4,128,512]{2,1,0:T(8,128)(2,1)}), bf16[4,128,512]{2,1,0:T(8,128)(2,1)}, u32[]{:S(2)}, u32[]{:S(2)}) async-start(bf16[4,128,512]{2,1,0:T(8,128)(2,1)} %bitcast.95), calls=%async_computation.13 | async-start | bytes 1048576 | tf_op jit(solution)/shard_map/all_to_all | solution.py:367
  1097.5 12.3 copy-start.52
  1154.7 7.9 copy-start.35
  (36 other events, 164.4 us)
Sparse Core Ops, SparseCore 0:
  98.5 44.9 all-gather.4
  145.0 150.6 all-gather.8
  297.2 113.4 all-gather.6
  412.1 113.5 all-gather.10
  550.5 109.0 reduce-scatter.7
  661.7 135.7 reduce-scatter.3
  799.8 155.0 reduce-scatter.5
  1056.8 95.4 all-reduce.6
  1156.4 126.2 all-reduce.4
